TPU v7x, 32 devices: a whole 2x2x4 slice. The times are simulated.
32 devices in a mesh: groups: 2 (over x), src: 16 (over z, y, core).
Axes of the slice: x: 2, y: 2, z: 4, core: 2. Of those that a mesh axis runs over, the one named last changes fastest.
Arguments:
- perambulator: bfloat16 [32, 5, 2, 512, 512], P(('groups', 'src')), parts along dimension 0, may hold values from -0.1875 to 0.1875
- source_meson: bfloat16 [32, 2, 128, 128], P(('groups', 'src')), parts along dimension 0, may hold values from -0.375 to 0.375
- sink_meson: bfloat16 [32, 2, 128, 128], P(('groups', 'src')), parts along dimension 0, may hold values from -0.375 to 0.375
- gamma_order: int32 [2, 4], replicated, may hold values from 0 to 3, each once within a row
- gamma_phase: int32 [2, 4], replicated, may hold values from 0 to 3
- diagram_blocks: int32 [2, 8192], P(None, 'src'), may hold values from 0 to 79
- diagram_codes: int32 [8192], P('src'), may hold values from 0 to 3
Outputs:
- box_traces: float32 [2, 16384], P(None, ('groups', 'src')), parts along dimension 1
There are 2 independent parts, one for each index of `groups`. A program takes and returns all parts, laid end to end along the dimension named above; an argument that names none is the same for every part. Nothing has to cross between parts.
Inputs may be any that keep to these rules, and one draw needn't show every extreme that they name: `gamma_order`: each row is an ordering of the 4 spins.
All inputs are finite; a program needn't handle non-finite values.
Results may differ from a plain program's by a relative error of at most 0.0079.
Values may be sent and summed in bfloat16 or wider, within the bound.
No kernel may reach another device: no remote copies, remote signals or barrier semaphores. Data moves between devices by JAX's collectives and lax.ppermute only.
A program may use at most 192 MiB of HBM per device.

v0:
```python
import jax
import jax.numpy as jnp
from jax import lax
from jax.experimental import pallas as pl
from jax.experimental.pallas import tpu as pltpu
from jax.sharding import PartitionSpec as P


def shifted(block, axis, distance):
    devices = range(lax.axis_size(axis))
    route = [((i - distance) % len(devices), i) for i in devices]
    return lax.ppermute(block, axis, route)


def gamma_parts(order_row, phase_row):
    spins = order_row.shape[0]
    chosen = (order_row[:, None] == jnp.arange(spins, dtype=jnp.int32)[None, :]).astype(jnp.float32)
    cosine = ((phase_row == 0).astype(jnp.float32) - (phase_row == 2).astype(jnp.float32))[:, None] * chosen
    sine = ((phase_row == 1).astype(jnp.float32) - (phase_row == 3).astype(jnp.float32))[:, None] * chosen
    return cosine, sine


def dressing_matrix(elemental, order_row, phase_row):
    cosine, sine = gamma_parts(order_row, phase_row)
    meson = elemental.astype(jnp.float32)
    kron_re = jnp.kron(cosine, meson[0]) - jnp.kron(sine, meson[1])
    kron_im = jnp.kron(cosine, meson[1]) + jnp.kron(sine, meson[0])
    top = jnp.concatenate([kron_re, -kron_im], axis=1)
    bottom = jnp.concatenate([kron_im, kron_re], axis=1)
    return jnp.concatenate([top, bottom], axis=0).astype(jnp.bfloat16)


def dress(weights, tile_pair):
    order = tile_pair.shape[-1]
    stacked = tile_pair.reshape(2 * order, order)
    out = jnp.dot(weights, stacked, preferred_element_type=jnp.float32)
    return out.astype(jnp.bfloat16).reshape(2, order, order)


def loop_kernel(forward_ref, backward_ref, out_ref):
    fr = forward_ref[0, 0]
    fi = forward_ref[0, 1]
    br = backward_ref[0, 0]
    bi = backward_ref[0, 1]
    shares = out_ref.shape[0]
    rows = out_ref.shape[3]
    real = jnp.dot(fr, br, preferred_element_type=jnp.float32) - jnp.dot(fi, bi, preferred_element_type=jnp.float32)
    imag = jnp.dot(fr, bi, preferred_element_type=jnp.float32) + jnp.dot(fi, br, preferred_element_type=jnp.float32)
    out_ref[:, 0, 0] = real.astype(out_ref.dtype).reshape(shares, rows, real.shape[-1])
    out_ref[:, 0, 1] = imag.astype(out_ref.dtype).reshape(shares, rows, imag.shape[-1])


def open_loops(forward, backward, shares):
    window, _, order, _ = forward.shape
    rows = order // shares
    tile = pl.BlockSpec((1, 2, order, order), lambda s: (s, 0, 0, 0))
    return pl.pallas_call(
        loop_kernel,
        grid=(window,),
        in_specs=[tile, tile],
        out_specs=pl.BlockSpec((shares, 1, 2, rows, order), lambda s: (0, s, 0, 0, 0)),
        out_shape=jax.ShapeDtypeStruct((shares, window, 2, rows, order), jnp.bfloat16),
        compiler_params=pltpu.CompilerParams(vmem_limit_bytes=48 * 1024 * 1024),
        cost_estimate=pl.CostEstimate(
            flops=8 * window * order ** 3, transcendentals=0, bytes_accessed=6 * window * order * order * 2
        ),
    )(forward, backward)


def inner_product(left, right):
    return lax.dot_general(left, right, (((1,), (1,)), ((), ())), preferred_element_type=jnp.float32)


def all_sum(table, axis):
    n = lax.axis_size(axis)
    if n & (n - 1):
        return lax.psum(table, axis)
    bit = 1
    while bit < n:
        table = table + lax.ppermute(table, axis, [(i, i ^ bit) for i in range(n)])
        bit *= 2
    return table


def select_diagrams(trace_table, block_pairs, codes):
    signs = 1 - 2 * (codes % 2)
    scales = 1 + codes // 2
    weight = (signs * scales).astype(jnp.float32)
    return trace_table[:, block_pairs[0], block_pairs[1]] * weight[None, :]


def per_device(
    perambulator, source_meson, sink_meson, gamma_order, gamma_phase, diagram_blocks, diagram_codes
):
    window = perambulator.shape[1]
    half_window = window // 2
    shares = lax.axis_size("src")
    sink_weights = dressing_matrix(sink_meson[0], gamma_order[1], gamma_phase[1])
    backward = [dress(sink_weights, perambulator[0, position]) for position in range(window)]
    mirrored = {0: backward[half_window]}
    for offset in range(1, half_window + 1):
        for direction in (1, -1):
            separation = direction * offset
            mirrored[separation] = shifted(backward[half_window - separation], "src", -separation)
    source_weights = dressing_matrix(source_meson[0], gamma_order[0], gamma_phase[0])
    forward = jnp.stack([dress(source_weights, perambulator[0, position]) for position in range(window)])
    partners = jnp.stack([mirrored[position - half_window] for position in range(window)])
    loops = open_loops(forward, partners, shares)
    slices = lax.all_to_all(loops, "src", split_axis=0, concat_axis=0, tiled=True)
    block_count = slices.shape[0] * slices.shape[1]
    real_flat = slices[:, :, 0].reshape(block_count, -1)
    imag_flat = slices[:, :, 1].reshape(block_count, -1)
    trace_table = jnp.stack(
        [
            inner_product(real_flat, real_flat) - inner_product(imag_flat, imag_flat),
            inner_product(real_flat, imag_flat) + inner_product(imag_flat, real_flat),
        ]
    )
    summed = all_sum(trace_table, "src")
    return select_diagrams(summed, diagram_blocks, diagram_codes)


def solution(mesh):
    placed = (
        P(("groups", "src"), None, None, None, None),
        P(("groups", "src"), None, None, None),
        P(("groups", "src"), None, None, None),
        P(),
        P(),
        P(None, "src"),
        P("src"),
    )
    return jax.shard_map(
        per_device,
        mesh=mesh,
        in_specs=placed,
        out_specs=P(None, ("groups", "src")),
        check_vma=False,
    )
```

profile of v0, /device:TPU:0, one launch (start us, length us, event | category | flops | bytes accessed | tf_op | source)
XLA Modules:
  0.0 240.1 jit_solution(6225665843069887849)
XLA Ops:
  0.0 0.8 slice_bitcast_fusion.4
  0.9 0.9 fusion.25
  1.7 0.8 convert_element_type.121
  2.6 0.1 fusion.15
  2.7 0.8 negate_convert_fusion
  3.5 0.1 copy.27
  3.6 0.1 copy.26
  3.7 0.1 copy.28
  3.8 0.3 fusion.30
  4.1 1.2 convolution_convert_fusion
  5.4 6.1 %collective-permute-start.3 = (bf16[2,512,512]{2,1,0:T(8,128)(2,1)S(1)}, bf16[2,512,512]{2,1,0:T(8,128)(2,1)S(1)}, u32[]{:S(2)}, u32[]{:S(2)}) collective-permute-start(bf16[2,512,512]{2,1,0:T(8,128)(2,1)S(1)} %bitcast.169), channel_id=1, source_target_pairs={{2,0},{3,1},{4,2},{5,3},{6,4},{7,5},{8,6},{9,7},{10,8},{11,9},{12,... | collective-permute-start | bytes 3145736 | tf_op jit(solution)/shard_map/ppermute | solution.py:12
  11.4 1.2 convolution_convert_fusion.3
  12.7 0.1 collective-permute-start.1
  12.7 1.2 convolution_convert_fusion.1
  14.0 4.5 %collective-permute-start.2 = (bf16[2,512,512]{2,1,0:T(8,128)(2,1)S(1)}, bf16[2,512,512]{2,1,0:T(8,128)(2,1)S(1)}, u32[]{:S(2)}, u32[]{:S(2)}) collective-permute-start(bf16[2,512,512]{2,1,0:T(8,128)(2,1)S(1)} %bitcast.170), channel_id=1, source_target_pairs={{1,0},{2,1},{3,2},{4,3},{5,4},{6,5},{7,6},{8,7},{9,8},{10,9},{11,1... | collective-permute-start | bytes 3145736 | tf_op jit(solution)/shard_map/ppermute | solution.py:12
  18.5 1.2 convolution_convert_fusion.4
  19.7 0.1 collective-permute-start
  19.8 0.8 negate_convert_fusion.1
  20.7 0.1 copy.30
  20.8 0.1 copy.29
  20.8 0.1 copy.31
  20.9 1.2 convolution_convert_fusion.2
  22.2 1.2 convolution_convert_fusion.7
  23.4 1.2 convolution_convert_fusion.5
  24.7 1.2 convolution_convert_fusion.8
  25.9 1.2 convolution_convert_fusion.9
  27.2 0.1 constant_dynamic-update-slice_fusion.4
  27.2 0.1 constant_dynamic-update-slice_fusion.3
  27.3 1.2 convolution_convert_fusion.6
  28.6 0.1 constant_dynamic-update-slice_fusion.2
  28.6 0.1 constant_dynamic-update-slice_fusion.1
  28.7 0.1 constant_dynamic-update-slice_fusion.forward_ref
  28.8 36.7 %collective-permute-done = bf16[2,512,512]{2,1,0:T(8,128)(2,1)S(1)} collective-permute-done((bf16[2,512,512]{2,1,0:T(8,128)(2,1)S(1)}, bf16[2,512,512]{2,1,0:T(8,128)(2,1)S(1)}, u32[]{:S(2)}, u32[]{:S(2)}) %collective-permute-start) | collective-permute-done | bytes 1048608 | tf_op jit(solution)/shard_map/ppermute | solution.py:12
  65.5 0.1 bitcast_dynamic-update-slice_fusion.3
  65.6 0.0 collective-permute-done.1
  65.6 0.1 bitcast_dynamic-update-slice_fusion.2
  65.7 0.1 constant_dynamic-update-slice_fusion.5
  65.7 0.0 collective-permute-done.2
  65.8 0.1 bitcast_dynamic-update-slice_fusion.1
  65.9 0.1 bitcast_dynamic-update-slice_fusion.backward_ref
  65.9 2.4 copy-done.1
  68.3 8.6 %shard_map.73 = bf16[16,5,2,32,512]{4,3,2,1,0:T(8,128)(2,1)S(1)} custom-call(bf16[5,2,512,512]{3,2,1,0:T(8,128)(2,1)} %copy-done.2, bf16[5,2,512,512]{3,2,1,0:T(8,128)(2,1)} %copy-done.1), custom_call_target="tpu_custom_call" | custom-call | flops 5368709120 | bytes 15728640 | tf_op jit(solution)/shard_map/pallas_call | solution.py:57
  76.9 133.5 %all_to_all.5 = bf16[16,5,2,32,512]{4,3,2,1,0:T(8,128)(2,1)S(1)} all-to-all(bf16[16,5,2,32,512]{4,3,2,1,0:T(8,128)(2,1)S(1)} %shard_map.73), channel_id=1, replica_groups=mesh['groups'=2,'src'=16] {'src'}, dimensions={0} | all-to-all | bytes 10485760 | tf_op jit(solution)/shard_map/all_to_all | solution.py:109
  210.3 0.8 fusion.29
  211.2 1.6 copy.19
  212.8 1.6 copy.18
  214.5 0.8 fusion.31
  215.3 0.8 fusion.32
  216.2 0.8 fusion
  217.0 0.0 copy-start.4
  217.0 0.0 copy-start.5
  217.0 0.8 fusion.1
  217.9 0.8 collective-permute-start.4
  218.7 0.9 collective-permute-done.4
  219.7 1.3 collective-permute-start.5
  221.0 3.4 %collective-permute-done.5 = f32[2,80,80]{2,1,0:T(8,128)S(1)} collective-permute-done((f32[2,80,80]{2,1,0:T(8,128)S(1)}, f32[2,80,80]{2,1,0:T(8,128)S(1)}, u32[]{:S(2)}, u32[]{:S(2)}) %collective-permute-start.5) | collective-permute-done | bytes 51232 | tf_op jit(solution)/shard_map/ppermute | solution.py:80
  224.5 1.9 collective-permute-start.6
  226.4 2.6 %collective-permute-done.6 = f32[2,80,80]{2,1,0:T(8,128)S(1)} collective-permute-done((f32[2,80,80]{2,1,0:T(8,128)S(1)}, f32[2,80,80]{2,1,0:T(8,128)S(1)}, u32[]{:S(2)}, u32[]{:S(2)}) %collective-permute-start.6) | collective-permute-done | bytes 51232 | tf_op jit(solution)/shard_map/ppermute | solution.py:80
  229.0 2.7 %collective-permute-start.7 = (f32[2,80,80]{2,1,0:T(8,128)S(1)}, f32[2,80,80]{2,1,0:T(8,128)S(1)}, u32[]{:S(2)}, u32[]{:S(2)}) collective-permute-start(f32[2,80,80]{2,1,0:T(8,128)S(1)} %add.64), channel_id=1, source_target_pairs={{0,8},{1,9},{2,10},{3,11},{4,12},{5,13},{6,14},{7,15},{8,0},{9,1},... | collective-permute-start | bytes 153608 | tf_op jit(solution)/shard_map/ppermute | solution.py:80
  231.7 2.7 %collective-permute-done.7 = f32[2,80,80]{2,1,0:T(8,128)S(1)} collective-permute-done((f32[2,80,80]{2,1,0:T(8,128)S(1)}, f32[2,80,80]{2,1,0:T(8,128)S(1)}, u32[]{:S(2)}, u32[]{:S(2)}) %collective-permute-start.7) | collective-permute-done | bytes 51232 | tf_op jit(solution)/shard_map/ppermute | solution.py:80
  234.4 1.1 copy.10
  235.5 3.7 %gather_fusion = f32[512,2]{1,0:T(8,128)S(1)} fusion(f32[2,80,80]{0,2,1:T(8,128)S(1)} %copy.10, s32[512]{0:T(512)S(1)} %bitcast.114), kind=kCustom, calls=%fused_computation | custom fusion | bytes 12288 | tf_op jit(solution)/shard_map/gather | solution.py:89
  239.2 0.1 multiply_bitcast_fusion
  239.3 0.7 copy.11
  (20 shorter events, 0.1 us)
Async XLA Ops:
  0.0 3.8 %copy-start = (bf16[1,5,2,512,512]{4,3,2,1,0:T(8,128)(2,1)S(1)}, bf16[1,5,2,512,512]{4,3,2,1,0:T(8,128)(2,1)}, u32[]{:S(2)}) copy-start(bf16[1,5,2,512,512]{4,3,2,1,0:T(8,128)(2,1)} %param.7) | copy-start | bytes 15728644
  5.4 60.5 %collective-permute-start.3 = (bf16[2,512,512]{2,1,0:T(8,128)(2,1)S(1)}, bf16[2,512,512]{2,1,0:T(8,128)(2,1)S(1)}, u32[]{:S(2)}, u32[]{:S(2)}) collective-permute-start(bf16[2,512,512]{2,1,0:T(8,128)(2,1)S(1)} %bitcast.169), channel_id=1, source_target_pairs={{2,0},{3,1},{4,2},{5,3},{6,4},{7,5},{8,6},{9,7},{10,8},{11,9},{12,... | collective-permute-start | bytes 3145736 | tf_op jit(solution)/shard_map/ppermute | solution.py:12
  12.7 52.9 %collective-permute-start.1 = (bf16[2,512,512]{2,1,0:T(8,128)(2,1)S(1)}, bf16[2,512,512]{2,1,0:T(8,128)(2,1)S(1)}, u32[]{:S(2)}, u32[]{:S(2)}) collective-permute-start(bf16[2,512,512]{2,1,0:T(8,128)(2,1)S(1)} %bitcast.171), channel_id=1, source_target_pairs={{15,0},{0,1},{1,2},{2,3},{3,4},{4,5},{5,6},{6,7},{7,8},{8,9},{9,10... | collective-permute-start | bytes 3145736 | tf_op jit(solution)/shard_map/ppermute | solution.py:12
  14.0 51.8 %collective-permute-start.2 = (bf16[2,512,512]{2,1,0:T(8,128)(2,1)S(1)}, bf16[2,512,512]{2,1,0:T(8,128)(2,1)S(1)}, u32[]{:S(2)}, u32[]{:S(2)}) collective-permute-start(bf16[2,512,512]{2,1,0:T(8,128)(2,1)S(1)} %bitcast.170), channel_id=1, source_target_pairs={{1,0},{2,1},{3,2},{4,3},{5,4},{6,5},{7,6},{8,7},{9,8},{10,9},{11,1... | collective-permute-start | bytes 3145736 | tf_op jit(solution)/shard_map/ppermute | solution.py:12
  18.5 1.3 copy-start.3
  19.7 45.8 %collective-permute-start = (bf16[2,512,512]{2,1,0:T(8,128)(2,1)S(1)}, bf16[2,512,512]{2,1,0:T(8,128)(2,1)S(1)}, u32[]{:S(2)}, u32[]{:S(2)}) collective-permute-start(bf16[2,512,512]{2,1,0:T(8,128)(2,1)S(1)} %bitcast.172), channel_id=1, source_target_pairs={{14,0},{15,1},{0,2},{1,3},{2,4},{3,5},{4,6},{5,7},{6,8},{7,9},{8,1... | collective-permute-start | bytes 3145736 | tf_op jit(solution)/shard_map/ppermute | solution.py:12
  28.8 37.0 %copy-start.2 = (bf16[5,2,512,512]{3,2,1,0:T(8,128)(2,1)}, bf16[5,2,512,512]{3,2,1,0:T(8,128)(2,1)S(1)}, u32[]{:S(2)}) copy-start(bf16[5,2,512,512]{3,2,1,0:T(8,128)(2,1)S(1)} %constant_dynamic-update-slice_fusion.forward_ref) | copy-start | bytes 15728644
  65.9 2.4 copy-start.1
  217.0 9.4 %copy-start.4 = (s32[2,512]{1,0:T(2,128)S(1)}, s32[2,512]{1,0:T(2,128)}, u32[]{:S(2)}) copy-start(s32[2,512]{1,0:T(2,128)} %param.12) | copy-start | bytes 12292
  217.0 14.7 %copy-start.5 = (s32[512]{0:T(512)S(1)}, s32[512]{0:T(512)}, u32[]{:S(2)}) copy-start(s32[512]{0:T(512)} %param.13) | copy-start | bytes 6148
  217.9 1.8 collective-permute-start.4
  219.7 4.8 %collective-permute-start.5 = (f32[2,80,80]{2,1,0:T(8,128)S(1)}, f32[2,80,80]{2,1,0:T(8,128)S(1)}, u32[]{:S(2)}, u32[]{:S(2)}) collective-permute-start(f32[2,80,80]{2,1,0:T(8,128)S(1)} %fusion.28), channel_id=1, source_target_pairs={{0,2},{1,3},{2,0},{3,1},{4,6},{5,7},{6,4},{7,5},{8,10},{9,11},{10,... | collective-permute-start | bytes 153608 | tf_op jit(solution)/shard_map/ppermute | solution.py:80
  224.5 4.5 %collective-permute-start.6 = (f32[2,80,80]{2,1,0:T(8,128)S(1)}, f32[2,80,80]{2,1,0:T(8,128)S(1)}, u32[]{:S(2)}, u32[]{:S(2)}) collective-permute-start(f32[2,80,80]{2,1,0:T(8,128)S(1)} %fusion.51), channel_id=1, source_target_pairs={{0,4},{1,5},{2,6},{3,7},{4,0},{5,1},{6,2},{7,3},{8,12},{9,13},{10,... | collective-permute-start | bytes 153608 | tf_op jit(solution)/shard_map/ppermute | solution.py:80
  229.0 5.4 %collective-permute-start.7 = (f32[2,80,80]{2,1,0:T(8,128)S(1)}, f32[2,80,80]{2,1,0:T(8,128)S(1)}, u32[]{:S(2)}, u32[]{:S(2)}) collective-permute-start(f32[2,80,80]{2,1,0:T(8,128)S(1)} %add.64), channel_id=1, source_target_pairs={{0,8},{1,9},{2,10},{3,11},{4,12},{5,13},{6,14},{7,15},{8,0},{9,1},... | collective-permute-start | bytes 153608 | tf_op jit(solution)/shard_map/ppermute | solution.py:80
where the time goes:
time: 240 us
  blocking collectives  133 us (55%)
  waiting for transfers between devices  46.3 us (19%)
  starting transfers between devices  17.4 us (7%)
  matrix products  15.7 us (7%)
  local copies, waits for them, and re-layouts  14.4 us (6%)
  Pallas kernels  8.58 us (4%)
  other arithmetic  3.69 us (2%)
    all_to_all x1, blocking collectives, per_device(): lax.all_to_all(loops, 'src', split_axis=0, concat_axis=0, tiled=True)  133 us
    ppermute x4, waiting for transfers between devices, shifted(): return lax.ppermute(block, axis, route)  36.7 us
    dot_general x10, matrix products, dress(): out = jnp.dot(weights, stacked, preferred_element_type=jnp.float32)  12.4 us
    ppermute x4, starting transfers between devices, shifted(): return lax.ppermute(block, axis, route)  10.7 us
    ppermute x4, waiting for transfers between devices, all_sum(): table = table + lax.ppermute(table, axis, [(i, i ^ bit) for i in range(n)])  9.62 us
    pallas_call x1, Pallas kernels, open_loops(): pl.pallas_call(loop_kernel, grid=(window,), in_specs=[tile, tile], out_sp...  8.58 us
    ppermute x4, starting transfers between devices, all_sum(): table = table + lax.ppermute(table, axis, [(i, i ^ bit) for i in range(n)])  6.78 us
    unnamed x28, local copies, waits for them, and re-layouts  6.71 us
  transfers between devices with their start and end apart: 8, of which 5 were waited for; matrix products, arithmetic and copies ran while one was open for 5% of the time, Pallas kernels for 0%

commit v1 on v0

--- a/solution.py
+++ b/solution.py
@@ -89,12 +89,23 @@
     return trace_table[:, block_pairs[0], block_pairs[1]] * weight[None, :]
 
 
+def exchange_rows(loops, axis):
+    n = lax.axis_size(axis)
+    me = lax.axis_index(axis)
+    pieces = [lax.dynamic_index_in_dim(loops, me, 0, keepdims=False)]
+    for k in range(1, n):
+        chunk = lax.dynamic_index_in_dim(loops, (me + k) % n, 0, keepdims=False)
+        pieces.append(lax.ppermute(chunk, axis, [(i, (i + k) % n) for i in range(n)]))
+    return jnp.stack(pieces)
+
+
 def per_device(
     perambulator, source_meson, sink_meson, gamma_order, gamma_phase, diagram_blocks, diagram_codes
 ):
     window = perambulator.shape[1]
     half_window = window // 2
     shares = lax.axis_size("src")
+    me = lax.axis_index("src")
     sink_weights = dressing_matrix(sink_meson[0], gamma_order[1], gamma_phase[1])
     backward = [dress(sink_weights, perambulator[0, position]) for position in range(window)]
     mirrored = {0: backward[half_window]}
@@ -103,10 +114,15 @@
             separation = direction * offset
             mirrored[separation] = shifted(backward[half_window - separation], "src", -separation)
     source_weights = dressing_matrix(source_meson[0], gamma_order[0], gamma_phase[0])
-    forward = jnp.stack([dress(source_weights, perambulator[0, position]) for position in range(window)])
-    partners = jnp.stack([mirrored[position - half_window] for position in range(window)])
-    loops = open_loops(forward, partners, shares)
-    slices = lax.all_to_all(loops, "src", split_axis=0, concat_axis=0, tiled=True)
+    forward = [dress(source_weights, perambulator[0, position]) for position in range(window)]
+    first = open_loops(forward[half_window][None], mirrored[0][None], shares)
+    others = [position for position in range(window) if position != half_window]
+    rest = open_loops(
+        jnp.stack([forward[position] for position in others]),
+        jnp.stack([mirrored[position - half_window] for position in others]),
+        shares,
+    )
+    slices = jnp.concatenate([exchange_rows(first, "src"), exchange_rows(rest, "src")], axis=1)
     block_count = slices.shape[0] * slices.shape[1]
     real_flat = slices[:, :, 0].reshape(block_count, -1)
     imag_flat = slices[:, :, 1].reshape(block_count, -1)
@@ -116,6 +132,13 @@
             inner_product(real_flat, imag_flat) + inner_product(imag_flat, real_flat),
         ]
     )
+    positions = [half_window] + others
+    slot_of_position = [positions.index(position) for position in range(window)]
+    block = jnp.arange(block_count, dtype=jnp.int32)
+    source_time = block // window
+    slot = jnp.asarray(slot_of_position, jnp.int32)[block % window]
+    canonical = ((me - source_time) % shares) * window + slot
+    trace_table = trace_table[:, canonical][:, :, canonical]
     summed = all_sum(trace_table, "src")
     return select_diagrams(summed, diagram_blocks, diagram_codes)
 

time: 240 us -> 296 us (1.23)
  waiting for transfers between devices: 46.3 us -> 184 us
  blocking collectives: 133 us -> 0 us
  starting transfers between devices: 17.4 us -> 56.5 us
  other arithmetic: 3.69 us -> 9.62 us
  local copies, waits for them, and re-layouts: 14.4 us -> 19.4 us
    ppermute x0 -> x30, waiting for transfers between devices: none -> 173 us  [exchange_rows(): lax.ppermute(chunk, axis, [(i, (i + k) % n) for i in range(n)])]
    all_to_all x1 -> x0, blocking collectives: 133 us -> none  [per_device(): lax.all_to_all(loops, 'src', split_axis=0, concat_axis=0, tiled=True)]
    ppermute x0 -> x30, starting transfers between devices: none -> 43.5 us  [exchange_rows(): lax.ppermute(chunk, axis, [(i, (i + k) % n) for i in range(n)])]
    ppermute x4, waiting for transfers between devices: 36.7 us -> 0.01 us  [shifted(): return lax.ppermute(block, axis, route)]
    another operation x2 -> x4, other arithmetic: 1.66 us -> 6.21 us  [the longest x1 2.28 us: per_device(): jnp.stack([forward[position] for position in others])]
    ppermute x4, starting transfers between devices: 10.7 us -> 6.32 us  [shifted(): return lax.ppermute(block, axis, route)]
    unnamed x28 -> x58, local copies, waits for them, and re-layouts: 6.71 us -> 8.88 us
    pallas_call x1 -> x2, Pallas kernels: 8.58 us -> 8.34 us  [open_loops(): pl.pallas_call(loop_kernel, grid=(window,), in_specs=[tile, tile], out_sp...]
  transfers between devices with their start and end apart: 8 -> 38, of which waited for: 5 -> 22; matrix products, arithmetic and copies ran while one was open for 5% -> 5% of each run, Pallas kernels for 0% -> 2%
where the time goes in v1:
time: 296 us
  waiting for transfers between devices  184 us (62%)
  starting transfers between devices  56.5 us (19%)
  local copies, waits for them, and re-layouts  19.4 us (7%)
  matrix products  17.7 us (6%)
  other arithmetic  9.62 us (3%)
  Pallas kernels  8.34 us (3%)
    ppermute x30, waiting for transfers between devices, exchange_rows(): lax.ppermute(chunk, axis, [(i, (i + k) % n) for i in range(n)])  173 us
    ppermute x30, starting transfers between devices, exchange_rows(): lax.ppermute(chunk, axis, [(i, (i + k) % n) for i in range(n)])  43.5 us
    dot_general x10, matrix products, dress(): out = jnp.dot(weights, stacked, preferred_element_type=jnp.float32)  14.4 us
    ppermute x4, waiting for transfers between devices, all_sum(): table = table + lax.ppermute(table, axis, [(i, i ^ bit) for i in range(n)])  11 us
    unnamed x58, local copies, waits for them, and re-layouts  8.88 us
    pallas_call x2, Pallas kernels, open_loops(): pl.pallas_call(loop_kernel, grid=(window,), in_specs=[tile, tile], out_sp...  8.34 us
    ppermute x4, starting transfers between devices, all_sum(): table = table + lax.ppermute(table, axis, [(i, i ^ bit) for i in range(n)])  6.64 us
    ppermute x4, starting transfers between devices, shifted(): return lax.ppermute(block, axis, route)  6.32 us
  transfers between devices with their start and end apart: 38, of which 22 were waited for; matrix products, arithmetic and copies ran while one was open for 5% of the time, Pallas kernels for 2%

profile of v1, /device:TPU:0, one launch (start us, length us, event | category | flops | bytes accessed | tf_op | source)
XLA Modules:
  0.0 296.2 jit_solution(7267933553961818136)
XLA Ops:
  1.5 0.8 convert_element_type.111
  2.4 0.9 convert_element_type.117
  3.3 0.8 negate_convert_fusion
  4.2 0.9 copy.30
  5.1 0.9 copy.29
  5.9 0.9 copy.31
  6.8 0.8 negate_convert_fusion.1
  7.6 0.9 copy.33
  8.5 0.9 copy.32
  9.4 0.9 copy.34
  10.3 1.9 fusion.34
  12.2 3.2 %convolution_convert_fusion.8 = bf16[1024,512]{1,0:T(8,128)(2,1)S(1)} fusion(bf16[1024,512]{1,0:T(8,128)(2,1)} %bitcast.254, bf16[512,512]{1,0:T(8,128)(2,1)} %bitcast.274, bf16[512,512]{1,0:T(8,128)(2,1)} %bitcast.269, bf16[512,512]{1,0:T(8,128)(2,1)} %bitcast.264), kind=kOutput, calls=%fused_computation.19 | convolution fusion | flops 1082654720 | bytes 3670016 | tf_op jit(solution)/shard_map/dot_general | solution.py:36
  15.5 1.2 convolution_convert_fusion.9
  16.8 1.2 shard_map.82
  18.2 5.0 %collective-permute-start.9 = (bf16[1,2,32,512]{3,2,1,0:T(8,128)(2,1)S(1)}, bf16[1,2,32,512]{3,2,1,0:T(8,128)(2,1)S(1)}, u32[]{:S(2)}, u32[]{:S(2)}) collective-permute-start(bf16[1,2,32,512]{3,2,1,0:T(8,128)(2,1)S(1)} %get-tuple-element.33), channel_id=1, source_target_pairs={{0,10},{1,11},{2,12},{3,13},{4,14},{5,15},{6,0},{7,1},{8,2},{9,3},... | collective-permute-start | bytes 196616 | tf_op jit(solution)/shard_map/ppermute | solution.py:98
  23.3 2.1 collective-permute-start.7
  26.0 1.0 collective-permute-start
  27.0 1.2 convolution_convert_fusion.1
  28.3 1.2 convolution_convert_fusion.6
  29.5 1.2 convolution_convert_fusion
  30.8 1.2 convolution_convert_fusion.7
  32.0 1.2 convolution_convert_fusion.2
  33.3 1.2 convolution_convert_fusion.5
  34.5 1.2 convolution_convert_fusion.3
  35.8 1.2 convolution_convert_fusion.4
  37.0 2.3 pad_maximum_fusion.forward_ref
  39.3 1.4 collective-permute-start.1
  40.7 5.9 %collective-permute-done.1 = bf16[1,2,32,512]{3,2,1,0:T(8,128)(2,1)S(1)} collective-permute-done((bf16[1,2,32,512]{3,2,1,0:T(8,128)(2,1)S(1)}, bf16[1,2,32,512]{3,2,1,0:T(8,128)(2,1)S(1)}, u32[]{:S(2)}, u32[]{:S(2)}) %collective-permute-start.1) | collective-permute-done | bytes 65568 | tf_op jit(solution)/shard_map/ppermute | solution.py:98
  46.6 5.5 %collective-permute-done.2 = bf16[1,2,32,512]{3,2,1,0:T(8,128)(2,1)S(1)} collective-permute-done((bf16[1,2,32,512]{3,2,1,0:T(8,128)(2,1)S(1)}, bf16[1,2,32,512]{3,2,1,0:T(8,128)(2,1)S(1)}, u32[]{:S(2)}, u32[]{:S(2)}) %collective-permute-start.2) | collective-permute-done | bytes 65568 | tf_op jit(solution)/shard_map/ppermute | solution.py:98
  52.1 6.6 %collective-permute-done.3 = bf16[1,2,32,512]{3,2,1,0:T(8,128)(2,1)S(1)} collective-permute-done((bf16[1,2,32,512]{3,2,1,0:T(8,128)(2,1)S(1)}, bf16[1,2,32,512]{3,2,1,0:T(8,128)(2,1)S(1)}, u32[]{:S(2)}, u32[]{:S(2)}) %collective-permute-start.3) | collective-permute-done | bytes 65568 | tf_op jit(solution)/shard_map/ppermute | solution.py:98
  58.7 5.5 %collective-permute-done.4 = bf16[1,2,32,512]{3,2,1,0:T(8,128)(2,1)S(1)} collective-permute-done((bf16[1,2,32,512]{3,2,1,0:T(8,128)(2,1)S(1)}, bf16[1,2,32,512]{3,2,1,0:T(8,128)(2,1)S(1)}, u32[]{:S(2)}, u32[]{:S(2)}) %collective-permute-start.4) | collective-permute-done | bytes 65568 | tf_op jit(solution)/shard_map/ppermute | solution.py:98
  64.2 6.1 %collective-permute-done.5 = bf16[1,2,32,512]{3,2,1,0:T(8,128)(2,1)S(1)} collective-permute-done((bf16[1,2,32,512]{3,2,1,0:T(8,128)(2,1)S(1)}, bf16[1,2,32,512]{3,2,1,0:T(8,128)(2,1)S(1)}, u32[]{:S(2)}, u32[]{:S(2)}) %collective-permute-start.5) | collective-permute-done | bytes 65568 | tf_op jit(solution)/shard_map/ppermute | solution.py:98
  70.4 4.8 %collective-permute-start.18 = (bf16[2,512,512]{2,1,0:T(8,128)(2,1)S(1)}, bf16[2,512,512]{2,1,0:T(8,128)(2,1)S(1)}, u32[]{:S(2)}, u32[]{:S(2)}) collective-permute-start(bf16[2,512,512]{2,1,0:T(8,128)(2,1)S(1)} %bitcast.297), channel_id=1, source_target_pairs={{2,0},{3,1},{4,2},{5,3},{6,4},{7,5},{8,6},{9,7},{10,8},{11,9},{12,... | collective-permute-start | bytes 3145736 | tf_op jit(solution)/shard_map/ppermute | solution.py:12
  75.1 1.5 collective-permute-start.17
  76.7 34.3 %collective-permute-done.10 = bf16[1,2,32,512]{3,2,1,0:T(8,128)(2,1)S(1)} collective-permute-done((bf16[1,2,32,512]{3,2,1,0:T(8,128)(2,1)S(1)}, bf16[1,2,32,512]{3,2,1,0:T(8,128)(2,1)S(1)}, u32[]{:S(2)}, u32[]{:S(2)}) %collective-permute-start.10) | collective-permute-done | bytes 65568 | tf_op jit(solution)/shard_map/ppermute | solution.py:98
  111.0 4.6 %collective-permute-done.11 = bf16[1,2,32,512]{3,2,1,0:T(8,128)(2,1)S(1)} collective-permute-done((bf16[1,2,32,512]{3,2,1,0:T(8,128)(2,1)S(1)}, bf16[1,2,32,512]{3,2,1,0:T(8,128)(2,1)S(1)}, u32[]{:S(2)}, u32[]{:S(2)}) %collective-permute-start.11) | collective-permute-done | bytes 65568 | tf_op jit(solution)/shard_map/ppermute | solution.py:98
  115.6 14.7 %collective-permute-done.12 = bf16[1,2,32,512]{3,2,1,0:T(8,128)(2,1)S(1)} collective-permute-done((bf16[1,2,32,512]{3,2,1,0:T(8,128)(2,1)S(1)}, bf16[1,2,32,512]{3,2,1,0:T(8,128)(2,1)S(1)}, u32[]{:S(2)}, u32[]{:S(2)}) %collective-permute-start.12) | collective-permute-done | bytes 65568 | tf_op jit(solution)/shard_map/ppermute | solution.py:98
  130.9 2.3 pad_maximum_fusion.1.backward_ref
  133.1 7.1 %shard_map.83 = bf16[16,4,2,32,512]{4,3,2,1,0:T(8,128)(2,1)S(1)} custom-call(bf16[4,2,512,512]{3,2,1,0:T(8,128)(2,1)} %pad_maximum_fusion.forward_ref, bf16[4,2,512,512]{3,2,1,0:T(8,128)(2,1)} %pad_maximum_fusion.1.backward_ref), custom_call_target="tpu_custom_call" | custom-call | flops 4294967296 | bytes 12582912 | tf_op jit(solution)/shard_map/pallas_call | solution.py:57
  140.8 11.5 %collective-permute-start.19 = (bf16[4,2,32,512]{3,2,1,0:T(8,128)(2,1)S(1)}, bf16[4,2,32,512]{3,2,1,0:T(8,128)(2,1)S(1)}, u32[]{:S(2)}, u32[]{:S(2)}) collective-permute-start(bf16[4,2,32,512]{3,2,1,0:T(8,128)(2,1)S(1)} %get-tuple-element.26), channel_id=1, source_target_pairs={{0,1},{1,2},{2,3},{3,4},{4,5},{5,6},{6,7},{7,8},{8,9},{9,10},{10,1... | collective-permute-start | bytes 786440 | tf_op jit(solution)/shard_map/ppermute | solution.py:98
  153.1 4.2 %collective-permute-start.33 = (bf16[4,2,32,512]{3,2,1,0:T(8,128)(2,1)S(1)}, bf16[4,2,32,512]{3,2,1,0:T(8,128)(2,1)S(1)}, u32[]{:S(2)}, u32[]{:S(2)}) collective-permute-start(bf16[4,2,32,512]{3,2,1,0:T(8,128)(2,1)S(1)} %get-tuple-element.12), channel_id=1, source_target_pairs={{0,15},{1,0},{2,1},{3,2},{4,3},{5,4},{6,5},{7,6},{8,7},{9,8},{10,9... | collective-permute-start | bytes 786440 | tf_op jit(solution)/shard_map/ppermute | solution.py:98
  157.3 1.8 collective-permute-start.21
  159.0 11.9 %collective-permute-done.20 = bf16[4,2,32,512]{3,2,1,0:T(8,128)(2,1)S(1)} collective-permute-done((bf16[4,2,32,512]{3,2,1,0:T(8,128)(2,1)S(1)}, bf16[4,2,32,512]{3,2,1,0:T(8,128)(2,1)S(1)}, u32[]{:S(2)}, u32[]{:S(2)}) %collective-permute-start.20) | collective-permute-done | bytes 262176 | tf_op jit(solution)/shard_map/ppermute | solution.py:98
  171.1 4.8 %collective-permute-done.21 = bf16[4,2,32,512]{3,2,1,0:T(8,128)(2,1)S(1)} collective-permute-done((bf16[4,2,32,512]{3,2,1,0:T(8,128)(2,1)S(1)}, bf16[4,2,32,512]{3,2,1,0:T(8,128)(2,1)S(1)}, u32[]{:S(2)}, u32[]{:S(2)}) %collective-permute-start.21) | collective-permute-done | bytes 262176 | tf_op jit(solution)/shard_map/ppermute | solution.py:98
  175.9 3.9 %collective-permute-start.23 = (bf16[4,2,32,512]{3,2,1,0:T(8,128)(2,1)S(1)}, bf16[4,2,32,512]{3,2,1,0:T(8,128)(2,1)S(1)}, u32[]{:S(2)}, u32[]{:S(2)}) collective-permute-start(bf16[4,2,32,512]{3,2,1,0:T(8,128)(2,1)S(1)} %get-tuple-element.22), channel_id=1, source_target_pairs={{0,5},{1,6},{2,7},{3,8},{4,9},{5,10},{6,11},{7,12},{8,13},{9,14},{... | collective-permute-start | bytes 786440 | tf_op jit(solution)/shard_map/ppermute | solution.py:98
  179.9 6.2 %collective-permute-start.24 = (bf16[4,2,32,512]{3,2,1,0:T(8,128)(2,1)S(1)}, bf16[4,2,32,512]{3,2,1,0:T(8,128)(2,1)S(1)}, u32[]{:S(2)}, u32[]{:S(2)}) collective-permute-start(bf16[4,2,32,512]{3,2,1,0:T(8,128)(2,1)S(1)} %get-tuple-element.21), channel_id=1, source_target_pairs={{0,6},{1,7},{2,8},{3,9},{4,10},{5,11},{6,12},{7,13},{8,14},{9,15},... | collective-permute-start | bytes 786440 | tf_op jit(solution)/shard_map/ppermute | solution.py:98
  186.1 20.4 %collective-permute-done.23 = bf16[4,2,32,512]{3,2,1,0:T(8,128)(2,1)S(1)} collective-permute-done((bf16[4,2,32,512]{3,2,1,0:T(8,128)(2,1)S(1)}, bf16[4,2,32,512]{3,2,1,0:T(8,128)(2,1)S(1)}, u32[]{:S(2)}, u32[]{:S(2)}) %collective-permute-start.23) | collective-permute-done | bytes 262176 | tf_op jit(solution)/shard_map/ppermute | solution.py:98
  206.7 21.0 %collective-permute-done.25 = bf16[4,2,32,512]{3,2,1,0:T(8,128)(2,1)S(1)} collective-permute-done((bf16[4,2,32,512]{3,2,1,0:T(8,128)(2,1)S(1)}, bf16[4,2,32,512]{3,2,1,0:T(8,128)(2,1)S(1)}, u32[]{:S(2)}, u32[]{:S(2)}) %collective-permute-start.25) | collective-permute-done | bytes 262176 | tf_op jit(solution)/shard_map/ppermute | solution.py:98
  228.7 11.5 %collective-permute-done.27 = bf16[4,2,32,512]{3,2,1,0:T(8,128)(2,1)S(1)} collective-permute-done((bf16[4,2,32,512]{3,2,1,0:T(8,128)(2,1)S(1)}, bf16[4,2,32,512]{3,2,1,0:T(8,128)(2,1)S(1)}, u32[]{:S(2)}, u32[]{:S(2)}) %collective-permute-start.27) | collective-permute-done | bytes 262176 | tf_op jit(solution)/shard_map/ppermute | solution.py:98
  240.3 3.6 %collective-permute-start.30 = (bf16[4,2,32,512]{3,2,1,0:T(8,128)(2,1)S(1)}, bf16[4,2,32,512]{3,2,1,0:T(8,128)(2,1)S(1)}, u32[]{:S(2)}, u32[]{:S(2)}) collective-permute-start(bf16[4,2,32,512]{3,2,1,0:T(8,128)(2,1)S(1)} %get-tuple-element.15), channel_id=1, source_target_pairs={{0,12},{1,13},{2,14},{3,15},{4,0},{5,1},{6,2},{7,3},{8,4},{9,5},{1... | collective-permute-start | bytes 786440 | tf_op jit(solution)/shard_map/ppermute | solution.py:98
  243.8 4.4 %collective-permute-done.29 = bf16[4,2,32,512]{3,2,1,0:T(8,128)(2,1)S(1)} collective-permute-done((bf16[4,2,32,512]{3,2,1,0:T(8,128)(2,1)S(1)}, bf16[4,2,32,512]{3,2,1,0:T(8,128)(2,1)S(1)}, u32[]{:S(2)}, u32[]{:S(2)}) %collective-permute-start.29) | collective-permute-done | bytes 262176 | tf_op jit(solution)/shard_map/ppermute | solution.py:98
  248.3 15.5 %collective-permute-done.30 = bf16[4,2,32,512]{3,2,1,0:T(8,128)(2,1)S(1)} collective-permute-done((bf16[4,2,32,512]{3,2,1,0:T(8,128)(2,1)S(1)}, bf16[4,2,32,512]{3,2,1,0:T(8,128)(2,1)S(1)}, u32[]{:S(2)}, u32[]{:S(2)}) %collective-permute-start.30) | collective-permute-done | bytes 262176 | tf_op jit(solution)/shard_map/ppermute | solution.py:98
  264.4 1.6 copy.22
  266.0 1.6 copy.21
  269.3 0.8 fusion.1
  270.2 0.8 fusion.2
  272.6 1.3 collective-permute-done.34
  273.9 3.6 %collective-permute-start.35 = (f32[2,80,80]{1,0,2:T(2,128)S(1)}, f32[2,80,80]{1,0,2:T(2,128)S(1)}, u32[]{:S(2)}, u32[]{:S(2)}) collective-permute-start(f32[2,80,80]{1,0,2:T(2,128)S(1)} %bitcast_add_fusion), channel_id=1, source_target_pairs={{0,2},{1,3},{2,0},{3,1},{4,6},{5,7},{6,4},{7,5},{8,10},{9,11},{10,... | collective-permute-start | bytes 153608 | tf_op jit(solution)/shard_map/ppermute | solution.py:80
  277.5 2.8 collective-permute-done.35
  280.5 4.4 %collective-permute-done.36 = f32[2,80,80]{1,0,2:T(2,128)S(1)} collective-permute-done((f32[2,80,80]{1,0,2:T(2,128)S(1)}, f32[2,80,80]{1,0,2:T(2,128)S(1)}, u32[]{:S(2)}, u32[]{:S(2)}) %collective-permute-start.36) | collective-permute-done | bytes 51232 | tf_op jit(solution)/shard_map/ppermute | solution.py:80
  284.9 2.9 collective-permute-start.37
  287.8 2.5 collective-permute-done.37
  290.4 1.3 copy.13
  291.7 3.7 %gather_fusion.2 = f32[512,2]{1,0:T(8,128)S(1)} fusion(f32[2,80,80]{0,2,1:T(8,128)S(1)} %copy.13, s32[512]{0:T(512)S(1)} %bitcast.237), kind=kCustom, calls=%fused_computation.2 | custom fusion | bytes 12288 | tf_op jit(solution)/shard_map/gather | solution.py:89
  (120 shorter events, 11.0 us)
Async XLA Ops:
  4.2 6.1 %copy-start = (bf16[1,5,2,512,512]{4,3,2,1,0:T(8,128)(2,1)S(1)}, bf16[1,5,2,512,512]{4,3,2,1,0:T(8,128)(2,1)}, u32[]{:S(2)}) copy-start(bf16[1,5,2,512,512]{4,3,2,1,0:T(8,128)(2,1)} %param.8) | copy-start | bytes 15728644
  12.2 3.3 %copy-start.2 = (bf16[1,1,2,512,512]{4,3,2,1,0:T(8,128)(2,1)S(1)}, bf16[1,1,2,512,512]{4,3,2,1,0:T(8,128)(2,1)}, u32[]{:S(2)}) copy-start(bf16[1,1,2,512,512]{4,3,2,1,0:T(8,128)(2,1)} %get-tuple-element.9) | copy-start | bytes 3145732
  12.2 3.3 %copy-start.6 = (bf16[64,8,4,128]{3,1,2,0:T(8,128)(2,1)S(1)}, bf16[64,8,4,128]{3,1,2,0:T(8,128)(2,1)}, u32[]{:S(2)}) copy-start(bf16[64,8,4,128]{3,1,2,0:T(8,128)(2,1)} %copy.33) | copy-start | bytes 1572868
  12.2 3.3 %copy-start.7 = (bf16[64,8,4,128]{3,1,2,0:T(8,128)(2,1)S(1)}, bf16[64,8,4,128]{3,1,2,0:T(8,128)(2,1)}, u32[]{:S(2)}) copy-start(bf16[64,8,4,128]{3,1,2,0:T(8,128)(2,1)} %copy.32) | copy-start | bytes 1572868
  12.2 3.3 %copy-start.8 = (bf16[64,8,4,128]{3,1,2,0:T(8,128)(2,1)S(1)}, bf16[64,8,4,128]{3,1,2,0:T(8,128)(2,1)}, u32[]{:S(2)}) copy-start(bf16[64,8,4,128]{3,1,2,0:T(8,128)(2,1)} %copy.34) | copy-start | bytes 1572868
  16.7 10.3 %copy-start.1 = (bf16[1,1,2,512,512]{4,3,2,1,0:T(8,128)(2,1)S(1)}, bf16[1,1,2,512,512]{4,3,2,1,0:T(8,128)(2,1)}, u32[]{:S(2)}) copy-start(bf16[1,1,2,512,512]{4,3,2,1,0:T(8,128)(2,1)} %get-tuple-element.8) | copy-start | bytes 3145732
  16.7 10.3 %copy-start.3 = (bf16[64,8,4,128]{3,1,2,0:T(8,128)(2,1)S(1)}, bf16[64,8,4,128]{3,1,2,0:T(8,128)(2,1)}, u32[]{:S(2)}) copy-start(bf16[64,8,4,128]{3,1,2,0:T(8,128)(2,1)} %copy.30) | copy-start | bytes 1572868
  16.7 10.3 %copy-start.4 = (bf16[64,8,4,128]{3,1,2,0:T(8,128)(2,1)S(1)}, bf16[64,8,4,128]{3,1,2,0:T(8,128)(2,1)}, u32[]{:S(2)}) copy-start(bf16[64,8,4,128]{3,1,2,0:T(8,128)(2,1)} %copy.29) | copy-start | bytes 1572868
  16.7 10.3 %copy-start.5 = (bf16[64,8,4,128]{3,1,2,0:T(8,128)(2,1)S(1)}, bf16[64,8,4,128]{3,1,2,0:T(8,128)(2,1)}, u32[]{:S(2)}) copy-start(bf16[64,8,4,128]{3,1,2,0:T(8,128)(2,1)} %copy.31) | copy-start | bytes 1572868
  18.2 58.4 %collective-permute-start.9 = (bf16[1,2,32,512]{3,2,1,0:T(8,128)(2,1)S(1)}, bf16[1,2,32,512]{3,2,1,0:T(8,128)(2,1)S(1)}, u32[]{:S(2)}, u32[]{:S(2)}) collective-permute-start(bf16[1,2,32,512]{3,2,1,0:T(8,128)(2,1)S(1)} %get-tuple-element.33), channel_id=1, source_target_pairs={{0,10},{1,11},{2,12},{3,13},{4,14},{5,15},{6,0},{7,1},{8,2},{9,3},... | collective-permute-start | bytes 196616 | tf_op jit(solution)/shard_map/ppermute | solution.py:98
  23.3 51.9 %collective-permute-start.8 = (bf16[1,2,32,512]{3,2,1,0:T(8,128)(2,1)S(1)}, bf16[1,2,32,512]{3,2,1,0:T(8,128)(2,1)S(1)}, u32[]{:S(2)}, u32[]{:S(2)}) collective-permute-start(bf16[1,2,32,512]{3,2,1,0:T(8,128)(2,1)S(1)} %get-tuple-element.34), channel_id=1, source_target_pairs={{0,9},{1,10},{2,11},{3,12},{4,13},{5,14},{6,15},{7,0},{8,1},{9,2},... | collective-permute-start | bytes 196616 | tf_op jit(solution)/shard_map/ppermute | solution.py:98
  23.3 47.1 %collective-permute-start.7 = (bf16[1,2,32,512]{3,2,1,0:T(8,128)(2,1)S(1)}, bf16[1,2,32,512]{3,2,1,0:T(8,128)(2,1)S(1)}, u32[]{:S(2)}, u32[]{:S(2)}) collective-permute-start(bf16[1,2,32,512]{3,2,1,0:T(8,128)(2,1)S(1)} %get-tuple-element.35), channel_id=1, source_target_pairs={{0,8},{1,9},{2,10},{3,11},{4,12},{5,13},{6,14},{7,15},{8,0},{9,1},... | collective-permute-start | bytes 196616 | tf_op jit(solution)/shard_map/ppermute | solution.py:98
  25.3 44.9 %collective-permute-start.6 = (bf16[1,2,32,512]{3,2,1,0:T(8,128)(2,1)S(1)}, bf16[1,2,32,512]{3,2,1,0:T(8,128)(2,1)S(1)}, u32[]{:S(2)}, u32[]{:S(2)}) collective-permute-start(bf16[1,2,32,512]{3,2,1,0:T(8,128)(2,1)S(1)} %get-tuple-element.36), channel_id=1, source_target_pairs={{0,7},{1,8},{2,9},{3,10},{4,11},{5,12},{6,13},{7,14},{8,15},{9,0},... | collective-permute-start | bytes 196616 | tf_op jit(solution)/shard_map/ppermute | solution.py:98
  26.0 13.3 %collective-permute-start = (bf16[1,2,32,512]{3,2,1,0:T(8,128)(2,1)S(1)}, bf16[1,2,32,512]{3,2,1,0:T(8,128)(2,1)S(1)}, u32[]{:S(2)}, u32[]{:S(2)}) collective-permute-start(bf16[1,2,32,512]{3,2,1,0:T(8,128)(2,1)S(1)} %get-tuple-element.42), channel_id=1, source_target_pairs={{0,1},{1,2},{2,3},{3,4},{4,5},{5,6},{6,7},{7,8},{8,9},{9,10},{10,1... | collective-permute-start | bytes 196616 | tf_op jit(solution)/shard_map/ppermute | solution.py:98
  39.3 7.3 %collective-permute-start.1 = (bf16[1,2,32,512]{3,2,1,0:T(8,128)(2,1)S(1)}, bf16[1,2,32,512]{3,2,1,0:T(8,128)(2,1)S(1)}, u32[]{:S(2)}, u32[]{:S(2)}) collective-permute-start(bf16[1,2,32,512]{3,2,1,0:T(8,128)(2,1)S(1)} %get-tuple-element.41), channel_id=1, source_target_pairs={{0,2},{1,3},{2,4},{3,5},{4,6},{5,7},{6,8},{7,9},{8,10},{9,11},{10,... | collective-permute-start | bytes 196616 | tf_op jit(solution)/shard_map/ppermute | solution.py:98
  46.6 5.5 %collective-permute-start.2 = (bf16[1,2,32,512]{3,2,1,0:T(8,128)(2,1)S(1)}, bf16[1,2,32,512]{3,2,1,0:T(8,128)(2,1)S(1)}, u32[]{:S(2)}, u32[]{:S(2)}) collective-permute-start(bf16[1,2,32,512]{3,2,1,0:T(8,128)(2,1)S(1)} %get-tuple-element.40), channel_id=1, source_target_pairs={{0,3},{1,4},{2,5},{3,6},{4,7},{5,8},{6,9},{7,10},{8,11},{9,12},{10... | collective-permute-start | bytes 196616 | tf_op jit(solution)/shard_map/ppermute | solution.py:98
  52.1 6.6 %collective-permute-start.3 = (bf16[1,2,32,512]{3,2,1,0:T(8,128)(2,1)S(1)}, bf16[1,2,32,512]{3,2,1,0:T(8,128)(2,1)S(1)}, u32[]{:S(2)}, u32[]{:S(2)}) collective-permute-start(bf16[1,2,32,512]{3,2,1,0:T(8,128)(2,1)S(1)} %get-tuple-element.39), channel_id=1, source_target_pairs={{0,4},{1,5},{2,6},{3,7},{4,8},{5,9},{6,10},{7,11},{8,12},{9,13},{1... | collective-permute-start | bytes 196616 | tf_op jit(solution)/shard_map/ppermute | solution.py:98
  58.7 5.5 %collective-permute-start.4 = (bf16[1,2,32,512]{3,2,1,0:T(8,128)(2,1)S(1)}, bf16[1,2,32,512]{3,2,1,0:T(8,128)(2,1)S(1)}, u32[]{:S(2)}, u32[]{:S(2)}) collective-permute-start(bf16[1,2,32,512]{3,2,1,0:T(8,128)(2,1)S(1)} %get-tuple-element.38), channel_id=1, source_target_pairs={{0,5},{1,6},{2,7},{3,8},{4,9},{5,10},{6,11},{7,12},{8,13},{9,14},{... | collective-permute-start | bytes 196616 | tf_op jit(solution)/shard_map/ppermute | solution.py:98
  64.2 6.1 %collective-permute-start.5 = (bf16[1,2,32,512]{3,2,1,0:T(8,128)(2,1)S(1)}, bf16[1,2,32,512]{3,2,1,0:T(8,128)(2,1)S(1)}, u32[]{:S(2)}, u32[]{:S(2)}) collective-permute-start(bf16[1,2,32,512]{3,2,1,0:T(8,128)(2,1)S(1)} %get-tuple-element.37), channel_id=1, source_target_pairs={{0,6},{1,7},{2,8},{3,9},{4,10},{5,11},{6,12},{7,13},{8,14},{9,15},... | collective-permute-start | bytes 196616 | tf_op jit(solution)/shard_map/ppermute | solution.py:98
  70.2 60.1 %collective-permute-start.15 = (bf16[2,512,512]{2,1,0:T(8,128)(2,1)S(1)}, bf16[2,512,512]{2,1,0:T(8,128)(2,1)S(1)}, u32[]{:S(2)}, u32[]{:S(2)}) collective-permute-start(bf16[2,512,512]{2,1,0:T(8,128)(2,1)S(1)} %bitcast.299), channel_id=1, source_target_pairs={{14,0},{15,1},{0,2},{1,3},{2,4},{3,5},{4,6},{5,7},{6,8},{7,9},{8,1... | collective-permute-start | bytes 3145736 | tf_op jit(solution)/shard_map/ppermute | solution.py:12
  70.3 60.6 %collective-permute-start.16 = (bf16[2,512,512]{2,1,0:T(8,128)(2,1)S(1)}, bf16[2,512,512]{2,1,0:T(8,128)(2,1)S(1)}, u32[]{:S(2)}, u32[]{:S(2)}) collective-permute-start(bf16[2,512,512]{2,1,0:T(8,128)(2,1)S(1)} %bitcast.298), channel_id=1, source_target_pairs={{15,0},{0,1},{1,2},{2,3},{3,4},{4,5},{5,6},{6,7},{7,8},{8,9},{9,10... | collective-permute-start | bytes 3145736 | tf_op jit(solution)/shard_map/ppermute | solution.py:12
  70.4 60.5 %collective-permute-start.18 = (bf16[2,512,512]{2,1,0:T(8,128)(2,1)S(1)}, bf16[2,512,512]{2,1,0:T(8,128)(2,1)S(1)}, u32[]{:S(2)}, u32[]{:S(2)}) collective-permute-start(bf16[2,512,512]{2,1,0:T(8,128)(2,1)S(1)} %bitcast.297), channel_id=1, source_target_pairs={{2,0},{3,1},{4,2},{5,3},{6,4},{7,5},{8,6},{9,7},{10,8},{11,9},{12,... | collective-permute-start | bytes 3145736 | tf_op jit(solution)/shard_map/ppermute | solution.py:12
  75.1 55.7 %collective-permute-start.17 = (bf16[2,512,512]{2,1,0:T(8,128)(2,1)S(1)}, bf16[2,512,512]{2,1,0:T(8,128)(2,1)S(1)}, u32[]{:S(2)}, u32[]{:S(2)}) collective-permute-start(bf16[2,512,512]{2,1,0:T(8,128)(2,1)S(1)} %bitcast.296), channel_id=1, source_target_pairs={{1,0},{2,1},{3,2},{4,3},{5,4},{6,5},{7,6},{8,7},{9,8},{10,9},{11,1... | collective-permute-start | bytes 3145736 | tf_op jit(solution)/shard_map/ppermute | solution.py:12
  76.6 34.3 %collective-permute-start.10 = (bf16[1,2,32,512]{3,2,1,0:T(8,128)(2,1)S(1)}, bf16[1,2,32,512]{3,2,1,0:T(8,128)(2,1)S(1)}, u32[]{:S(2)}, u32[]{:S(2)}) collective-permute-start(bf16[1,2,32,512]{3,2,1,0:T(8,128)(2,1)S(1)} %get-tuple-element.32), channel_id=1, source_target_pairs={{0,11},{1,12},{2,13},{3,14},{4,15},{5,0},{6,1},{7,2},{8,3},{9,4},{... | collective-permute-start | bytes 196616 | tf_op jit(solution)/shard_map/ppermute | solution.py:98
  111.0 4.6 %collective-permute-start.11 = (bf16[1,2,32,512]{3,2,1,0:T(8,128)(2,1)S(1)}, bf16[1,2,32,512]{3,2,1,0:T(8,128)(2,1)S(1)}, u32[]{:S(2)}, u32[]{:S(2)}) collective-permute-start(bf16[1,2,32,512]{3,2,1,0:T(8,128)(2,1)S(1)} %get-tuple-element.31), channel_id=1, source_target_pairs={{0,12},{1,13},{2,14},{3,15},{4,0},{5,1},{6,2},{7,3},{8,4},{9,5},{1... | collective-permute-start | bytes 196616 | tf_op jit(solution)/shard_map/ppermute | solution.py:98
  115.6 14.7 %collective-permute-start.12 = (bf16[1,2,32,512]{3,2,1,0:T(8,128)(2,1)S(1)}, bf16[1,2,32,512]{3,2,1,0:T(8,128)(2,1)S(1)}, u32[]{:S(2)}, u32[]{:S(2)}) collective-permute-start(bf16[1,2,32,512]{3,2,1,0:T(8,128)(2,1)S(1)} %get-tuple-element.30), channel_id=1, source_target_pairs={{0,13},{1,14},{2,15},{3,0},{4,1},{5,2},{6,3},{7,4},{8,5},{9,6},{10... | collective-permute-start | bytes 196616 | tf_op jit(solution)/shard_map/ppermute | solution.py:98
  130.3 22.7 %collective-permute-start.14 = (bf16[1,2,32,512]{3,2,1,0:T(8,128)(2,1)S(1)}, bf16[1,2,32,512]{3,2,1,0:T(8,128)(2,1)S(1)}, u32[]{:S(2)}, u32[]{:S(2)}) collective-permute-start(bf16[1,2,32,512]{3,2,1,0:T(8,128)(2,1)S(1)} %get-tuple-element.28), channel_id=1, source_target_pairs={{0,15},{1,0},{2,1},{3,2},{4,3},{5,4},{6,5},{7,6},{8,7},{9,8},{10,9... | collective-permute-start | bytes 196616 | tf_op jit(solution)/shard_map/ppermute | solution.py:98
  130.3 21.9 %collective-permute-start.13 = (bf16[1,2,32,512]{3,2,1,0:T(8,128)(2,1)S(1)}, bf16[1,2,32,512]{3,2,1,0:T(8,128)(2,1)S(1)}, u32[]{:S(2)}, u32[]{:S(2)}) collective-permute-start(bf16[1,2,32,512]{3,2,1,0:T(8,128)(2,1)S(1)} %get-tuple-element.29), channel_id=1, source_target_pairs={{0,14},{1,15},{2,0},{3,1},{4,2},{5,3},{6,4},{7,5},{8,6},{9,7},{10,... | collective-permute-start | bytes 196616 | tf_op jit(solution)/shard_map/ppermute | solution.py:98
  140.8 16.5 %collective-permute-start.19 = (bf16[4,2,32,512]{3,2,1,0:T(8,128)(2,1)S(1)}, bf16[4,2,32,512]{3,2,1,0:T(8,128)(2,1)S(1)}, u32[]{:S(2)}, u32[]{:S(2)}) collective-permute-start(bf16[4,2,32,512]{3,2,1,0:T(8,128)(2,1)S(1)} %get-tuple-element.26), channel_id=1, source_target_pairs={{0,1},{1,2},{2,3},{3,4},{4,5},{5,6},{6,7},{7,8},{8,9},{9,10},{10,1... | collective-permute-start | bytes 786440 | tf_op jit(solution)/shard_map/ppermute | solution.py:98
  152.3 18.7 %collective-permute-start.20 = (bf16[4,2,32,512]{3,2,1,0:T(8,128)(2,1)S(1)}, bf16[4,2,32,512]{3,2,1,0:T(8,128)(2,1)S(1)}, u32[]{:S(2)}, u32[]{:S(2)}) collective-permute-start(bf16[4,2,32,512]{3,2,1,0:T(8,128)(2,1)S(1)} %get-tuple-element.25), channel_id=1, source_target_pairs={{0,2},{1,3},{2,4},{3,5},{4,6},{5,7},{6,8},{7,9},{8,10},{9,11},{10,... | collective-permute-start | bytes 786440 | tf_op jit(solution)/shard_map/ppermute | solution.py:98
  153.1 110.8 %collective-permute-start.33 = (bf16[4,2,32,512]{3,2,1,0:T(8,128)(2,1)S(1)}, bf16[4,2,32,512]{3,2,1,0:T(8,128)(2,1)S(1)}, u32[]{:S(2)}, u32[]{:S(2)}) collective-permute-start(bf16[4,2,32,512]{3,2,1,0:T(8,128)(2,1)S(1)} %get-tuple-element.12), channel_id=1, source_target_pairs={{0,15},{1,0},{2,1},{3,2},{4,3},{5,4},{6,5},{7,6},{8,7},{9,8},{10,9... | collective-permute-start | bytes 786440 | tf_op jit(solution)/shard_map/ppermute | solution.py:98
  157.2 106.6 %collective-permute-start.32 = (bf16[4,2,32,512]{3,2,1,0:T(8,128)(2,1)S(1)}, bf16[4,2,32,512]{3,2,1,0:T(8,128)(2,1)S(1)}, u32[]{:S(2)}, u32[]{:S(2)}) collective-permute-start(bf16[4,2,32,512]{3,2,1,0:T(8,128)(2,1)S(1)} %get-tuple-element.13), channel_id=1, source_target_pairs={{0,14},{1,15},{2,0},{3,1},{4,2},{5,3},{6,4},{7,5},{8,6},{9,7},{10,... | collective-permute-start | bytes 786440 | tf_op jit(solution)/shard_map/ppermute | solution.py:98
  157.2 106.5 %collective-permute-start.31 = (bf16[4,2,32,512]{3,2,1,0:T(8,128)(2,1)S(1)}, bf16[4,2,32,512]{3,2,1,0:T(8,128)(2,1)S(1)}, u32[]{:S(2)}, u32[]{:S(2)}) collective-permute-start(bf16[4,2,32,512]{3,2,1,0:T(8,128)(2,1)S(1)} %get-tuple-element.14), channel_id=1, source_target_pairs={{0,13},{1,14},{2,15},{3,0},{4,1},{5,2},{6,3},{7,4},{8,5},{9,6},{10... | collective-permute-start | bytes 786440 | tf_op jit(solution)/shard_map/ppermute | solution.py:98
  157.3 18.7 %collective-permute-start.21 = (bf16[4,2,32,512]{3,2,1,0:T(8,128)(2,1)S(1)}, bf16[4,2,32,512]{3,2,1,0:T(8,128)(2,1)S(1)}, u32[]{:S(2)}, u32[]{:S(2)}) collective-permute-start(bf16[4,2,32,512]{3,2,1,0:T(8,128)(2,1)S(1)} %get-tuple-element.24), channel_id=1, source_target_pairs={{0,3},{1,4},{2,5},{3,6},{4,7},{5,8},{6,9},{7,10},{8,11},{9,12},{10... | collective-permute-start | bytes 786440 | tf_op jit(solution)/shard_map/ppermute | solution.py:98
  170.9 9.0 %collective-permute-start.22 = (bf16[4,2,32,512]{3,2,1,0:T(8,128)(2,1)S(1)}, bf16[4,2,32,512]{3,2,1,0:T(8,128)(2,1)S(1)}, u32[]{:S(2)}, u32[]{:S(2)}) collective-permute-start(bf16[4,2,32,512]{3,2,1,0:T(8,128)(2,1)S(1)} %get-tuple-element.23), channel_id=1, source_target_pairs={{0,4},{1,5},{2,6},{3,7},{4,8},{5,9},{6,10},{7,11},{8,12},{9,13},{1... | collective-permute-start | bytes 786440 | tf_op jit(solution)/shard_map/ppermute | solution.py:98
  175.9 30.5 %collective-permute-start.23 = (bf16[4,2,32,512]{3,2,1,0:T(8,128)(2,1)S(1)}, bf16[4,2,32,512]{3,2,1,0:T(8,128)(2,1)S(1)}, u32[]{:S(2)}, u32[]{:S(2)}) collective-permute-start(bf16[4,2,32,512]{3,2,1,0:T(8,128)(2,1)S(1)} %get-tuple-element.22), channel_id=1, source_target_pairs={{0,5},{1,6},{2,7},{3,8},{4,9},{5,10},{6,11},{7,12},{8,13},{9,14},{... | collective-permute-start | bytes 786440 | tf_op jit(solution)/shard_map/ppermute | solution.py:98
  179.9 26.8 %collective-permute-start.24 = (bf16[4,2,32,512]{3,2,1,0:T(8,128)(2,1)S(1)}, bf16[4,2,32,512]{3,2,1,0:T(8,128)(2,1)S(1)}, u32[]{:S(2)}, u32[]{:S(2)}) collective-permute-start(bf16[4,2,32,512]{3,2,1,0:T(8,128)(2,1)S(1)} %get-tuple-element.21), channel_id=1, source_target_pairs={{0,6},{1,7},{2,8},{3,9},{4,10},{5,11},{6,12},{7,13},{8,14},{9,15},... | collective-permute-start | bytes 786440 | tf_op jit(solution)/shard_map/ppermute | solution.py:98
  206.5 21.2 %collective-permute-start.25 = (bf16[4,2,32,512]{3,2,1,0:T(8,128)(2,1)S(1)}, bf16[4,2,32,512]{3,2,1,0:T(8,128)(2,1)S(1)}, u32[]{:S(2)}, u32[]{:S(2)}) collective-permute-start(bf16[4,2,32,512]{3,2,1,0:T(8,128)(2,1)S(1)} %get-tuple-element.20), channel_id=1, source_target_pairs={{0,7},{1,8},{2,9},{3,10},{4,11},{5,12},{6,13},{7,14},{8,15},{9,0},... | collective-permute-start | bytes 786440 | tf_op jit(solution)/shard_map/ppermute | solution.py:98
  206.7 21.3 %collective-permute-start.26 = (bf16[4,2,32,512]{3,2,1,0:T(8,128)(2,1)S(1)}, bf16[4,2,32,512]{3,2,1,0:T(8,128)(2,1)S(1)}, u32[]{:S(2)}, u32[]{:S(2)}) collective-permute-start(bf16[4,2,32,512]{3,2,1,0:T(8,128)(2,1)S(1)} %get-tuple-element.19), channel_id=1, source_target_pairs={{0,8},{1,9},{2,10},{3,11},{4,12},{5,13},{6,14},{7,15},{8,0},{9,1},... | collective-permute-start | bytes 786440 | tf_op jit(solution)/shard_map/ppermute | solution.py:98
  227.7 12.5 %collective-permute-start.27 = (bf16[4,2,32,512]{3,2,1,0:T(8,128)(2,1)S(1)}, bf16[4,2,32,512]{3,2,1,0:T(8,128)(2,1)S(1)}, u32[]{:S(2)}, u32[]{:S(2)}) collective-permute-start(bf16[4,2,32,512]{3,2,1,0:T(8,128)(2,1)S(1)} %get-tuple-element.18), channel_id=1, source_target_pairs={{0,9},{1,10},{2,11},{3,12},{4,13},{5,14},{6,15},{7,0},{8,1},{9,2},... | collective-permute-start | bytes 786440 | tf_op jit(solution)/shard_map/ppermute | solution.py:98
  228.0 12.3 %collective-permute-start.28 = (bf16[4,2,32,512]{3,2,1,0:T(8,128)(2,1)S(1)}, bf16[4,2,32,512]{3,2,1,0:T(8,128)(2,1)S(1)}, u32[]{:S(2)}, u32[]{:S(2)}) collective-permute-start(bf16[4,2,32,512]{3,2,1,0:T(8,128)(2,1)S(1)} %get-tuple-element.17), channel_id=1, source_target_pairs={{0,10},{1,11},{2,12},{3,13},{4,14},{5,15},{6,0},{7,1},{8,2},{9,3},... | collective-permute-start | bytes 786440 | tf_op jit(solution)/shard_map/ppermute | solution.py:98
  240.2 8.0 %collective-permute-start.29 = (bf16[4,2,32,512]{3,2,1,0:T(8,128)(2,1)S(1)}, bf16[4,2,32,512]{3,2,1,0:T(8,128)(2,1)S(1)}, u32[]{:S(2)}, u32[]{:S(2)}) collective-permute-start(bf16[4,2,32,512]{3,2,1,0:T(8,128)(2,1)S(1)} %get-tuple-element.16), channel_id=1, source_target_pairs={{0,11},{1,12},{2,13},{3,14},{4,15},{5,0},{6,1},{7,2},{8,3},{9,4},{... | collective-permute-start | bytes 786440 | tf_op jit(solution)/shard_map/ppermute | solution.py:98
  240.3 23.5 %collective-permute-start.30 = (bf16[4,2,32,512]{3,2,1,0:T(8,128)(2,1)S(1)}, bf16[4,2,32,512]{3,2,1,0:T(8,128)(2,1)S(1)}, u32[]{:S(2)}, u32[]{:S(2)}) collective-permute-start(bf16[4,2,32,512]{3,2,1,0:T(8,128)(2,1)S(1)} %get-tuple-element.15), channel_id=1, source_target_pairs={{0,12},{1,13},{2,14},{3,15},{4,0},{5,1},{6,2},{7,3},{8,4},{9,5},{1... | collective-permute-start | bytes 786440 | tf_op jit(solution)/shard_map/ppermute | solution.py:98
  270.1 10.3 %copy-start.9 = (s32[2,512]{1,0:T(2,128)S(1)}, s32[2,512]{1,0:T(2,128)}, u32[]{:S(2)}) copy-start(s32[2,512]{1,0:T(2,128)} %param.13) | copy-start | bytes 12292
  270.2 17.6 %copy-start.10 = (s32[512]{0:T(512)S(1)}, s32[512]{0:T(512)}, u32[]{:S(2)}) copy-start(s32[512]{0:T(512)} %param.14) | copy-start | bytes 6148
  272.5 1.3 collective-permute-start.34
  273.9 6.4 %collective-permute-start.35 = (f32[2,80,80]{1,0,2:T(2,128)S(1)}, f32[2,80,80]{1,0,2:T(2,128)S(1)}, u32[]{:S(2)}, u32[]{:S(2)}) collective-permute-start(f32[2,80,80]{1,0,2:T(2,128)S(1)} %bitcast_add_fusion), channel_id=1, source_target_pairs={{0,2},{1,3},{2,0},{3,1},{4,6},{5,7},{6,4},{7,5},{8,10},{9,11},{10,... | collective-permute-start | bytes 153608 | tf_op jit(solution)/shard_map/ppermute | solution.py:80
  280.3 4.5 %collective-permute-start.36 = (f32[2,80,80]{1,0,2:T(2,128)S(1)}, f32[2,80,80]{1,0,2:T(2,128)S(1)}, u32[]{:S(2)}, u32[]{:S(2)}) collective-permute-start(f32[2,80,80]{1,0,2:T(2,128)S(1)} %add.364), channel_id=1, source_target_pairs={{0,4},{1,5},{2,6},{3,7},{4,0},{5,1},{6,2},{7,3},{8,12},{9,13},{10,... | collective-permute-start | bytes 153608 | tf_op jit(solution)/shard_map/ppermute | solution.py:80
  284.9 5.5 %collective-permute-start.37 = (f32[2,80,80]{1,0,2:T(2,128)S(1)}, f32[2,80,80]{1,0,2:T(2,128)S(1)}, u32[]{:S(2)}, u32[]{:S(2)}) collective-permute-start(f32[2,80,80]{1,0,2:T(2,128)S(1)} %add.365), channel_id=1, source_target_pairs={{0,8},{1,9},{2,10},{3,11},{4,12},{5,13},{6,14},{7,15},{8,0},{9,1},... | collective-permute-start | bytes 153608 | tf_op jit(solution)/shard_map/ppermute | solution.py:80

commit v2 on v0

--- a/solution.py
+++ b/solution.py
@@ -103,10 +103,19 @@
             separation = direction * offset
             mirrored[separation] = shifted(backward[half_window - separation], "src", -separation)
     source_weights = dressing_matrix(source_meson[0], gamma_order[0], gamma_phase[0])
-    forward = jnp.stack([dress(source_weights, perambulator[0, position]) for position in range(window)])
-    partners = jnp.stack([mirrored[position - half_window] for position in range(window)])
-    loops = open_loops(forward, partners, shares)
-    slices = lax.all_to_all(loops, "src", split_axis=0, concat_axis=0, tiled=True)
+    centre = open_loops(dress(source_weights, perambulator[0, half_window])[None], mirrored[0][None], shares)
+    centre_slices = lax.all_to_all(centre, "src", split_axis=0, concat_axis=0, tiled=True)
+    centre_slices, tiles = lax.optimization_barrier((centre_slices, perambulator[0]))
+    others = [position for position in range(window) if position != half_window]
+    rest = open_loops(
+        jnp.stack([dress(source_weights, tiles[position]) for position in others]),
+        jnp.stack([mirrored[position - half_window] for position in others]),
+        shares,
+    )
+    rest_slices = lax.all_to_all(rest, "src", split_axis=0, concat_axis=0, tiled=True)
+    slices = jnp.concatenate(
+        [rest_slices[:, :half_window], centre_slices, rest_slices[:, half_window:]], axis=1
+    )
     block_count = slices.shape[0] * slices.shape[1]
     real_flat = slices[:, :, 0].reshape(block_count, -1)
     imag_flat = slices[:, :, 1].reshape(block_count, -1)

time: 240 us -> 239 us (level)
  blocking collectives: 133 us -> 95.1 us
  waiting for transfers between devices: 46.3 us -> 68.8 us
  other arithmetic: 3.69 us -> 10.1 us
  matrix products: 15.7 us -> 19.3 us
  starting transfers between devices: 17.4 us -> 20.9 us
    all_to_all x1, blocking collectives: 133 us -> 95.1 us  [per_device(): lax.all_to_all(rest, 'src', split_axis=0, concat_axis=0, tiled=True)]
    ppermute x4, waiting for transfers between devices: 36.7 us -> 59.1 us  [shifted(): return lax.ppermute(block, axis, route)]
    all_to_all x0 -> x1, starting transfers between devices: none -> 6.15 us  [per_device(): lax.all_to_all(centre, 'src', split_axis=0, concat_axis=0, tiled=True)]
    another operation x2 -> x4, other arithmetic: 1.66 us -> 7.45 us  [the longest x1 3.48 us: per_device(): jnp.stack([mirrored[position - half_window] for position in others])]
    dot_general x10, matrix products: 12.4 us -> 16 us  [dress(): out = jnp.dot(weights, stacked, preferred_element_type=jnp.float32)]
    slice x0 -> x2, local copies, waits for them, and re-layouts: none -> 3.06 us  [the longest x1 2.56 us: per_device(): tiles[position]]
    ppermute x4, starting transfers between devices: 10.7 us -> 8 us  [shifted(): return lax.ppermute(block, axis, route)]
    unnamed x28 -> x40, local copies, waits for them, and re-layouts: 6.71 us -> 4.15 us
  transfers between devices with their start and end apart: 8 -> 9, of which waited for: 5 -> 8; matrix products, arithmetic and copies ran while one was open for 5% -> 6% of each run, Pallas kernels for 0% -> 1%
where the time goes in v2:
time: 239 us; the launch traced here: 238 us
  blocking collectives  95.1 us (40%)
  waiting for transfers between devices  68.8 us (29%)
  starting transfers between devices  20.9 us (9%)
  matrix products  19.3 us (8%)
  local copies, waits for them, and re-layouts  14.4 us (6%)
  other arithmetic  10.1 us (4%)
  Pallas kernels  9.3 us (4%)
    all_to_all x1, blocking collectives, per_device(): lax.all_to_all(rest, 'src', split_axis=0, concat_axis=0, tiled=True)  95.1 us
    ppermute x4, waiting for transfers between devices, shifted(): return lax.ppermute(block, axis, route)  59.1 us
    dot_general x10, matrix products, dress(): out = jnp.dot(weights, stacked, preferred_element_type=jnp.float32)  16 us
    ppermute x4, waiting for transfers between devices, all_sum(): table = table + lax.ppermute(table, axis, [(i, i ^ bit) for i in range(n)])  9.7 us
    pallas_call x2, Pallas kernels, open_loops(): pl.pallas_call(loop_kernel, grid=(window,), in_specs=[tile, tile], out_sp...  9.3 us
    ppermute x4, starting transfers between devices, shifted(): return lax.ppermute(block, axis, route)  8 us
    ppermute x4, starting transfers between devices, all_sum(): table = table + lax.ppermute(table, axis, [(i, i ^ bit) for i in range(n)])  6.7 us
    all_to_all x1, starting transfers between devices, per_device(): lax.all_to_all(centre, 'src', split_axis=0, concat_axis=0, tiled=True)  6.15 us
  transfers between devices with their start and end apart: 9, of which 8 were waited for; matrix products, arithmetic and copies ran while one was open for 6% of the time, Pallas kernels for 1%

profile of v2, /device:TPU:0, one launch (start us, length us, event | category | flops | bytes accessed | tf_op | source)
XLA Modules:
  0.0 238.3 jit_solution(5159115089297631979)
XLA Ops:
  0.0 0.8 fusion.25
  0.8 0.8 slice_bitcast_fusion.4
  1.5 1.0 convert_element_type.117
  2.5 0.1 fusion.15
  2.6 0.8 negate_convert_fusion
  3.5 0.1 copy.26
  3.6 0.1 copy.27
  3.7 0.1 copy.28
  3.7 0.3 copy-done
  4.0 0.5 fusion.30
  4.5 2.2 convolution_convert_fusion.3
  6.7 3.0 %collective-permute-start = (bf16[2,512,512]{2,1,0:T(8,128)(2,1)}, bf16[2,512,512]{2,1,0:T(8,128)(2,1)}, u32[]{:S(2)}, u32[]{:S(2)}) collective-permute-start(bf16[2,512,512]{2,1,0:T(8,128)(2,1)} %bitcast.23), channel_id=1, source_target_pairs={{14,0},{15,1},{0,2},{1,3},{2,4},{3,5},{4,6},{5,7},{6,8},{7,9},{8,1... | collective-permute-start | bytes 3145736 | tf_op jit(solution)/shard_map/ppermute | solution.py:12
  9.7 2.2 convolution_convert_fusion.2
  11.9 0.0 collective-permute-start.1
  11.9 0.0 copy-start.13
  11.9 1.2 convolution_convert_fusion.8
  13.2 0.8 negate_convert_fusion.1
  14.1 0.1 copy.29
  14.2 0.1 copy.30
  14.3 0.1 copy.31
  14.3 1.2 convolution_convert_fusion.9
  15.6 2.2 shard_map.73
  17.8 6.2 %all-to-all-start = ((bf16[16,1,2,32,512]{4,3,2,1,0:T(8,128)(2,1)}), bf16[16,1,2,32,512]{4,3,2,1,0:T(8,128)(2,1)S(1)}, u32[]{:S(2)}, u32[]{:S(2)}) async-start(bf16[16,1,2,32,512]{4,3,2,1,0:T(8,128)(2,1)} %shard_map.73), calls=%async_computation | async-start | bytes 2097152 | tf_op jit(solution)/shard_map/all_to_all | solution.py:107
  24.0 2.9 %convolution_convert_fusion.1 = bf16[1024,512]{1,0:T(8,128)(2,1)S(1)} fusion(bf16[1024,512]{1,0:T(8,128)(2,1)S(1)} %bitcast.128, bf16[512,512]{1,0:T(8,128)(2,1)} %bitcast.171, bf16[512,512]{1,0:T(8,128)(2,1)} %bitcast.161, bf16[512,512]{1,0:T(8,128)(2,1)} %bitcast.166), kind=kOutput, calls=%fused_computation.7 | convolution fusion | flops 1082654720 | bytes 3670016 | tf_op jit(solution)/shard_map/dot_general | solution.py:36
  26.9 4.4 %collective-permute-start.2 = (bf16[2,512,512]{2,1,0:T(8,128)(2,1)S(1)}, bf16[2,512,512]{2,1,0:T(8,128)(2,1)S(1)}, u32[]{:S(2)}, u32[]{:S(2)}) collective-permute-start(bf16[2,512,512]{2,1,0:T(8,128)(2,1)S(1)} %bitcast.173), channel_id=1, source_target_pairs={{1,0},{2,1},{3,2},{4,3},{5,4},{6,5},{7,6},{8,7},{9,8},{10,9},{11,1... | collective-permute-start | bytes 3145736 | tf_op jit(solution)/shard_map/ppermute | solution.py:12
  31.3 1.2 convolution_convert_fusion
  32.6 0.6 collective-permute-start.3
  33.2 5.5 %collective-permute-done = bf16[2,512,512]{2,1,0:T(8,128)(2,1)} collective-permute-done((bf16[2,512,512]{2,1,0:T(8,128)(2,1)}, bf16[2,512,512]{2,1,0:T(8,128)(2,1)}, u32[]{:S(2)}, u32[]{:S(2)}) %collective-permute-start) | collective-permute-done | bytes 1048608 | tf_op jit(solution)/shard_map/ppermute | solution.py:12
  38.7 17.4 %collective-permute-done.1 = bf16[2,512,512]{2,1,0:T(8,128)(2,1)} collective-permute-done((bf16[2,512,512]{2,1,0:T(8,128)(2,1)}, bf16[2,512,512]{2,1,0:T(8,128)(2,1)}, u32[]{:S(2)}, u32[]{:S(2)}) %collective-permute-start.1) | collective-permute-done | bytes 1048608 | tf_op jit(solution)/shard_map/ppermute | solution.py:12
  56.1 8.6 %collective-permute-done.2 = bf16[2,512,512]{2,1,0:T(8,128)(2,1)S(1)} collective-permute-done((bf16[2,512,512]{2,1,0:T(8,128)(2,1)S(1)}, bf16[2,512,512]{2,1,0:T(8,128)(2,1)S(1)}, u32[]{:S(2)}, u32[]{:S(2)}) %collective-permute-start.2) | collective-permute-done | bytes 1048608 | tf_op jit(solution)/shard_map/ppermute | solution.py:12
  64.7 27.6 %collective-permute-done.3 = bf16[2,512,512]{2,1,0:T(8,128)(2,1)S(1)} collective-permute-done((bf16[2,512,512]{2,1,0:T(8,128)(2,1)S(1)}, bf16[2,512,512]{2,1,0:T(8,128)(2,1)S(1)}, u32[]{:S(2)}, u32[]{:S(2)}) %collective-permute-start.3) | collective-permute-done | bytes 1048608 | tf_op jit(solution)/shard_map/ppermute | solution.py:12
  92.3 3.5 %pad_maximum_fusion.2.backward_ref = bf16[4,2,512,512]{3,2,1,0:T(8,128)(2,1)} fusion(bf16[1,2,512,512]{3,2,1,0:T(8,128)(2,1)S(1)} %bitcast.134, bf16[1,2,512,512]{3,2,1,0:T(8,128)(2,1)S(1)} %bitcast.133, bf16[1,2,512,512]{3,2,1,0:T(8,128)(2,1)} %bitcast.27, bf16[1,2,512,512]{3,2,1,0:T(8,128)(2,1)} %bitcast.24), kind=kLoop, calls=%fused_computation.3 | loop fusion | flops 6291456 | bytes 8388608 | tf_op jit(solution)/shard_map/stack | solution.py:112
  95.8 2.6 %fusion.31 = (bf16[1,2,512,512]{3,2,1,0:T(8,128)(2,1)S(1)}, bf16[1,2,512,512]{3,2,1,0:T(8,128)(2,1)S(1)}, bf16[1,2,512,512]{3,2,1,0:T(8,128)(2,1)S(1)}, bf16[1,2,512,512]{3,2,1,0:T(8,128)(2,1)S(1)}) fusion(bf16[5,2,512,512]{3,2,1,0:T(8,128)(2,1)} %bitcast.118), kind=kLoop, calls=%fused_computation.87 | loop fusion | bytes 8388608 | tf_op jit(solution)/shard_map/slice | solution.py:111
  98.4 0.0 copy-done.6
  98.4 1.2 convolution_convert_fusion.7
  99.6 1.2 convolution_convert_fusion.6
  100.9 1.2 convolution_convert_fusion.5
  102.1 1.2 convolution_convert_fusion.4
  103.4 2.3 pad_maximum_fusion.1.forward_ref
  105.7 7.1 %shard_map.74 = bf16[16,4,2,32,512]{4,3,2,1,0:T(8,128)(2,1)S(1)} custom-call(bf16[4,2,512,512]{3,2,1,0:T(8,128)(2,1)} %pad_maximum_fusion.1.forward_ref, bf16[4,2,512,512]{3,2,1,0:T(8,128)(2,1)} %pad_maximum_fusion.2.backward_ref), custom_call_target="tpu_custom_call" | custom-call | flops 4294967296 | bytes 12582912 | tf_op jit(solution)/shard_map/pallas_call | solution.py:57
  112.8 95.1 %all_to_all.10 = bf16[16,4,2,32,512]{4,3,2,1,0:T(8,128)(2,1)S(1)} all-to-all(bf16[16,4,2,32,512]{4,3,2,1,0:T(8,128)(2,1)S(1)} %shard_map.74), channel_id=1, replica_groups=mesh['groups'=2,'src'=16] {'src'}, dimensions={0} | all-to-all | bytes 8388608 | tf_op jit(solution)/shard_map/all_to_all | solution.py:115
  207.9 0.5 fusion.32
  208.4 0.6 pad_maximum_fusion
  209.0 0.4 fusion.29
  209.4 1.6 copy.18
  211.1 0.8 fusion.33
  211.9 1.6 copy.19
  213.6 0.8 fusion.34
  214.4 0.8 fusion.1
  215.2 0.0 copy-start.14
  215.3 0.0 copy-start.15
  215.3 0.8 fusion
  216.1 0.8 collective-permute-start.4
  217.0 0.9 collective-permute-done.4
  217.9 1.3 collective-permute-start.5
  219.2 3.4 %collective-permute-done.5 = f32[2,80,80]{2,1,0:T(8,128)S(1)} collective-permute-done((f32[2,80,80]{2,1,0:T(8,128)S(1)}, f32[2,80,80]{2,1,0:T(8,128)S(1)}, u32[]{:S(2)}, u32[]{:S(2)}) %collective-permute-start.5) | collective-permute-done | bytes 51232 | tf_op jit(solution)/shard_map/ppermute | solution.py:80
  222.7 1.9 collective-permute-start.6
  224.6 2.6 %collective-permute-done.6 = f32[2,80,80]{2,1,0:T(8,128)S(1)} collective-permute-done((f32[2,80,80]{2,1,0:T(8,128)S(1)}, f32[2,80,80]{2,1,0:T(8,128)S(1)}, u32[]{:S(2)}, u32[]{:S(2)}) %collective-permute-start.6) | collective-permute-done | bytes 51232 | tf_op jit(solution)/shard_map/ppermute | solution.py:80
  227.2 2.6 %collective-permute-start.7 = (f32[2,80,80]{2,1,0:T(8,128)S(1)}, f32[2,80,80]{2,1,0:T(8,128)S(1)}, u32[]{:S(2)}, u32[]{:S(2)}) collective-permute-start(f32[2,80,80]{2,1,0:T(8,128)S(1)} %add.64), channel_id=1, source_target_pairs={{0,8},{1,9},{2,10},{3,11},{4,12},{5,13},{6,14},{7,15},{8,0},{9,1},... | collective-permute-start | bytes 153608 | tf_op jit(solution)/shard_map/ppermute | solution.py:80
  229.9 2.8 %collective-permute-done.7 = f32[2,80,80]{2,1,0:T(8,128)S(1)} collective-permute-done((f32[2,80,80]{2,1,0:T(8,128)S(1)}, f32[2,80,80]{2,1,0:T(8,128)S(1)}, u32[]{:S(2)}, u32[]{:S(2)}) %collective-permute-start.7) | collective-permute-done | bytes 51232 | tf_op jit(solution)/shard_map/ppermute | solution.py:80
  232.6 1.1 copy.10
  233.8 3.7 %gather_fusion = f32[512,2]{1,0:T(8,128)S(1)} fusion(f32[2,80,80]{0,2,1:T(8,128)S(1)} %copy.10, s32[512]{0:T(512)S(1)} %bitcast.117), kind=kCustom, calls=%fused_computation | custom fusion | bytes 12288 | tf_op jit(solution)/shard_map/gather | solution.py:89
  237.5 0.1 multiply_bitcast_fusion
  237.6 0.7 copy.11
  (38 shorter events, 0.2 us)
Async XLA Ops:
  1.5 2.5 %copy-start = (bf16[1,5,2,512,512]{4,3,2,1,0:T(8,128)(2,1)S(1)}, bf16[1,5,2,512,512]{4,3,2,1,0:T(8,128)(2,1)}, u32[]{:S(2)}) copy-start(bf16[1,5,2,512,512]{4,3,2,1,0:T(8,128)(2,1)} %param.7) | copy-start | bytes 15728644
  3.5 8.4 %copy-start.7 = (bf16[64,8,4,128]{3,1,2,0:T(8,128)(2,1)}, bf16[64,8,4,128]{3,1,2,0:T(8,128)(2,1)S(1)}, u32[]{:S(2)}) copy-start(bf16[64,8,4,128]{3,1,2,0:T(8,128)(2,1)S(1)} %copy.26) | copy-start | bytes 1572868
  3.6 8.3 %copy-start.9 = (bf16[64,8,4,128]{3,1,2,0:T(8,128)(2,1)}, bf16[64,8,4,128]{3,1,2,0:T(8,128)(2,1)S(1)}, u32[]{:S(2)}) copy-start(bf16[64,8,4,128]{3,1,2,0:T(8,128)(2,1)S(1)} %copy.27) | copy-start | bytes 1572868
  4.0 7.9 %copy-start.11 = (bf16[64,8,4,128]{3,1,2,0:T(8,128)(2,1)}, bf16[64,8,4,128]{3,1,2,0:T(8,128)(2,1)S(1)}, u32[]{:S(2)}) copy-start(bf16[64,8,4,128]{3,1,2,0:T(8,128)(2,1)S(1)} %copy.28) | copy-start | bytes 1572868
  6.7 32.0 %collective-permute-start = (bf16[2,512,512]{2,1,0:T(8,128)(2,1)}, bf16[2,512,512]{2,1,0:T(8,128)(2,1)}, u32[]{:S(2)}, u32[]{:S(2)}) collective-permute-start(bf16[2,512,512]{2,1,0:T(8,128)(2,1)} %bitcast.23), channel_id=1, source_target_pairs={{14,0},{15,1},{0,2},{1,3},{2,4},{3,5},{4,6},{5,7},{6,8},{7,9},{8,1... | collective-permute-start | bytes 3145736 | tf_op jit(solution)/shard_map/ppermute | solution.py:12
  11.9 44.2 %collective-permute-start.1 = (bf16[2,512,512]{2,1,0:T(8,128)(2,1)}, bf16[2,512,512]{2,1,0:T(8,128)(2,1)}, u32[]{:S(2)}, u32[]{:S(2)}) collective-permute-start(bf16[2,512,512]{2,1,0:T(8,128)(2,1)} %bitcast.26), channel_id=1, source_target_pairs={{15,0},{0,1},{1,2},{2,3},{3,4},{4,5},{5,6},{6,7},{7,8},{8,9},{9,10... | collective-permute-start | bytes 3145736 | tf_op jit(solution)/shard_map/ppermute | solution.py:12
  11.9 1.3 copy-start.13
  14.1 1.5 copy-start.1
  14.2 1.4 copy-start.3
  14.3 1.3 copy-start.5
  17.8 77.9 %all-to-all-start = ((bf16[16,1,2,32,512]{4,3,2,1,0:T(8,128)(2,1)}), bf16[16,1,2,32,512]{4,3,2,1,0:T(8,128)(2,1)S(1)}, u32[]{:S(2)}, u32[]{:S(2)}) async-start(bf16[16,1,2,32,512]{4,3,2,1,0:T(8,128)(2,1)} %shard_map.73), calls=%async_computation | async-start | bytes 2097152 | tf_op jit(solution)/shard_map/all_to_all | solution.py:107
  24.0 7.3 %copy-start.8 = (bf16[64,8,4,128]{3,1,2,0:T(8,128)(2,1)S(1)}, bf16[64,8,4,128]{3,1,2,0:T(8,128)(2,1)}, u32[]{:S(2)}) copy-start(bf16[64,8,4,128]{3,1,2,0:T(8,128)(2,1)} %copy-done.7) | copy-start | bytes 1572868
  24.0 7.3 %copy-start.10 = (bf16[64,8,4,128]{3,1,2,0:T(8,128)(2,1)S(1)}, bf16[64,8,4,128]{3,1,2,0:T(8,128)(2,1)}, u32[]{:S(2)}) copy-start(bf16[64,8,4,128]{3,1,2,0:T(8,128)(2,1)} %copy-done.9) | copy-start | bytes 1572868
  24.0 7.3 %copy-start.12 = (bf16[64,8,4,128]{3,1,2,0:T(8,128)(2,1)S(1)}, bf16[64,8,4,128]{3,1,2,0:T(8,128)(2,1)}, u32[]{:S(2)}) copy-start(bf16[64,8,4,128]{3,1,2,0:T(8,128)(2,1)} %copy-done.11) | copy-start | bytes 1572868
  26.9 37.7 %collective-permute-start.2 = (bf16[2,512,512]{2,1,0:T(8,128)(2,1)S(1)}, bf16[2,512,512]{2,1,0:T(8,128)(2,1)S(1)}, u32[]{:S(2)}, u32[]{:S(2)}) collective-permute-start(bf16[2,512,512]{2,1,0:T(8,128)(2,1)S(1)} %bitcast.173), channel_id=1, source_target_pairs={{1,0},{2,1},{3,2},{4,3},{5,4},{6,5},{7,6},{8,7},{9,8},{10,9},{11,1... | collective-permute-start | bytes 3145736 | tf_op jit(solution)/shard_map/ppermute | solution.py:12
  32.6 59.7 %collective-permute-start.3 = (bf16[2,512,512]{2,1,0:T(8,128)(2,1)S(1)}, bf16[2,512,512]{2,1,0:T(8,128)(2,1)S(1)}, u32[]{:S(2)}, u32[]{:S(2)}) collective-permute-start(bf16[2,512,512]{2,1,0:T(8,128)(2,1)S(1)} %bitcast.174), channel_id=1, source_target_pairs={{2,0},{3,1},{4,2},{5,3},{6,4},{7,5},{8,6},{9,7},{10,8},{11,9},{12,... | collective-permute-start | bytes 3145736 | tf_op jit(solution)/shard_map/ppermute | solution.py:12
  95.8 2.6 %copy-start.2 = (bf16[64,8,4,128]{3,1,2,0:T(8,128)(2,1)S(1)}, bf16[64,8,4,128]{3,1,2,0:T(8,128)(2,1)}, u32[]{:S(2)}) copy-start(bf16[64,8,4,128]{3,1,2,0:T(8,128)(2,1)} %copy-done.1) | copy-start | bytes 1572868
  95.8 2.6 %copy-start.4 = (bf16[64,8,4,128]{3,1,2,0:T(8,128)(2,1)S(1)}, bf16[64,8,4,128]{3,1,2,0:T(8,128)(2,1)}, u32[]{:S(2)}) copy-start(bf16[64,8,4,128]{3,1,2,0:T(8,128)(2,1)} %copy-done.3) | copy-start | bytes 1572868
  95.8 2.6 %copy-start.6 = (bf16[64,8,4,128]{3,1,2,0:T(8,128)(2,1)S(1)}, bf16[64,8,4,128]{3,1,2,0:T(8,128)(2,1)}, u32[]{:S(2)}) copy-start(bf16[64,8,4,128]{3,1,2,0:T(8,128)(2,1)} %copy-done.5) | copy-start | bytes 1572868
  215.2 9.4 %copy-start.14 = (s32[2,512]{1,0:T(2,128)S(1)}, s32[2,512]{1,0:T(2,128)}, u32[]{:S(2)}) copy-start(s32[2,512]{1,0:T(2,128)} %param.12) | copy-start | bytes 12292
  215.3 14.6 %copy-start.15 = (s32[512]{0:T(512)S(1)}, s32[512]{0:T(512)}, u32[]{:S(2)}) copy-start(s32[512]{0:T(512)} %param.13) | copy-start | bytes 6148
  216.1 1.8 collective-permute-start.4
  217.9 4.8 %collective-permute-start.5 = (f32[2,80,80]{2,1,0:T(8,128)S(1)}, f32[2,80,80]{2,1,0:T(8,128)S(1)}, u32[]{:S(2)}, u32[]{:S(2)}) collective-permute-start(f32[2,80,80]{2,1,0:T(8,128)S(1)} %fusion.28), channel_id=1, source_target_pairs={{0,2},{1,3},{2,0},{3,1},{4,6},{5,7},{6,4},{7,5},{8,10},{9,11},{10,... | collective-permute-start | bytes 153608 | tf_op jit(solution)/shard_map/ppermute | solution.py:80
  222.7 4.5 %collective-permute-start.6 = (f32[2,80,80]{2,1,0:T(8,128)S(1)}, f32[2,80,80]{2,1,0:T(8,128)S(1)}, u32[]{:S(2)}, u32[]{:S(2)}) collective-permute-start(f32[2,80,80]{2,1,0:T(8,128)S(1)} %fusion.53), channel_id=1, source_target_pairs={{0,4},{1,5},{2,6},{3,7},{4,0},{5,1},{6,2},{7,3},{8,12},{9,13},{10,... | collective-permute-start | bytes 153608 | tf_op jit(solution)/shard_map/ppermute | solution.py:80
  227.2 5.4 %collective-permute-start.7 = (f32[2,80,80]{2,1,0:T(8,128)S(1)}, f32[2,80,80]{2,1,0:T(8,128)S(1)}, u32[]{:S(2)}, u32[]{:S(2)}) collective-permute-start(f32[2,80,80]{2,1,0:T(8,128)S(1)} %add.64), channel_id=1, source_target_pairs={{0,8},{1,9},{2,10},{3,11},{4,12},{5,13},{6,14},{7,15},{8,0},{9,1},... | collective-permute-start | bytes 153608 | tf_op jit(solution)/shard_map/ppermute | solution.py:80

commit v3 on v2

--- a/solution.py
+++ b/solution.py
@@ -67,6 +67,34 @@
     )(forward, backward)
 
 
+def rest_loop_kernel(*refs):
+    forward_ref, partner_refs, out_ref = refs[0], refs[1:-1], refs[-1]
+    step = pl.program_id(0)
+    for index, partner_ref in enumerate(partner_refs):
+
+        @pl.when(step == index)
+        def _():
+            loop_kernel(forward_ref, partner_ref, out_ref)
+
+
+def rest_loops(forward, partners, shares):
+    window, _, order, _ = forward.shape
+    rows = order // shares
+    tile = pl.BlockSpec((1, 2, order, order), lambda s: (s, 0, 0, 0))
+    whole = pl.BlockSpec((1, 2, order, order), lambda s: (0, 0, 0, 0))
+    return pl.pallas_call(
+        rest_loop_kernel,
+        grid=(window,),
+        in_specs=[tile] + [whole] * len(partners),
+        out_specs=pl.BlockSpec((shares, 1, 2, rows, order), lambda s: (0, s, 0, 0, 0)),
+        out_shape=jax.ShapeDtypeStruct((shares, window, 2, rows, order), jnp.bfloat16),
+        compiler_params=pltpu.CompilerParams(vmem_limit_bytes=48 * 1024 * 1024),
+        cost_estimate=pl.CostEstimate(
+            flops=8 * window * order ** 3, transcendentals=0, bytes_accessed=6 * window * order * order * 2
+        ),
+    )(forward, *[partner[None] for partner in partners])
+
+
 def inner_product(left, right):
     return lax.dot_general(left, right, (((1,), (1,)), ((), ())), preferred_element_type=jnp.float32)
 
@@ -75,10 +103,15 @@
     n = lax.axis_size(axis)
     if n & (n - 1):
         return lax.psum(table, axis)
-    bit = 1
-    while bit < n:
-        table = table + lax.ppermute(table, axis, [(i, i ^ bit) for i in range(n)])
-        bit *= 2
+    stride = 1
+    while stride < n:
+        radix = 4 if n % (stride * 4) == 0 else 2
+        received = [
+            lax.ppermute(table, axis, [(i, i ^ (digit * stride)) for i in range(n)]) for digit in range(1, radix)
+        ]
+        for part in received:
+            table = table + part
+        stride *= radix
     return table
 
 
@@ -97,19 +130,20 @@
     shares = lax.axis_size("src")
     sink_weights = dressing_matrix(sink_meson[0], gamma_order[1], gamma_phase[1])
     backward = [dress(sink_weights, perambulator[0, position]) for position in range(window)]
+    source_weights = dressing_matrix(source_meson[0], gamma_order[0], gamma_phase[0])
+    centre = open_loops(dress(source_weights, perambulator[0, half_window])[None], backward[half_window][None], shares)
+    centre, backward = lax.optimization_barrier((centre, backward))
     mirrored = {0: backward[half_window]}
     for offset in range(1, half_window + 1):
         for direction in (1, -1):
             separation = direction * offset
             mirrored[separation] = shifted(backward[half_window - separation], "src", -separation)
-    source_weights = dressing_matrix(source_meson[0], gamma_order[0], gamma_phase[0])
-    centre = open_loops(dress(source_weights, perambulator[0, half_window])[None], mirrored[0][None], shares)
     centre_slices = lax.all_to_all(centre, "src", split_axis=0, concat_axis=0, tiled=True)
-    centre_slices, tiles = lax.optimization_barrier((centre_slices, perambulator[0]))
+    centre_slices, mirrored = lax.optimization_barrier((centre_slices, mirrored))
     others = [position for position in range(window) if position != half_window]
-    rest = open_loops(
-        jnp.stack([dress(source_weights, tiles[position]) for position in others]),
-        jnp.stack([mirrored[position - half_window] for position in others]),
+    rest = rest_loops(
+        jnp.stack([dress(source_weights, perambulator[0, position]) for position in others]),
+        [mirrored[position - half_window] for position in others],
         shares,
     )
     rest_slices = lax.all_to_all(rest, "src", split_axis=0, concat_axis=0, tiled=True)

time: 239 us -> 242 us (1.013)
  waiting for transfers between devices: 68.8 us -> 74.4 us
  other arithmetic: 10.1 us -> 7.68 us
    pallas_call x0 -> x1, Pallas kernels: none -> 8.09 us  [rest_loops(): pl.pallas_call(rest_loop_kernel, grid=(window,), in_specs=[tile] + [whole...]
    pallas_call x2 -> x1, Pallas kernels: 9.3 us -> 2.22 us  [open_loops(): pl.pallas_call(loop_kernel, grid=(window,), in_specs=[tile, tile], out_sp...]
    another operation x4 -> x3, other arithmetic: 7.45 us -> 3.99 us  [the longest x1 2.32 us: per_device(): jnp.stack([dress(source_weights, perambulator[0, position]) for position...]
    ppermute x4, waiting for transfers between devices: 59.1 us -> 62.5 us  [shifted(): return lax.ppermute(block, axis, route)]
    slice x2 -> x1, local copies, waits for them, and re-layouts: 3.02 us -> 0.34 us  [per_device(): perambulator[0, half_window]]
    dot_general x10, matrix products: 16 us -> 18.4 us  [dress(): out = jnp.dot(weights, stacked, preferred_element_type=jnp.float32)]
    ppermute x4 -> x6, waiting for transfers between devices: 9.7 us -> 11.2 us  [all_sum(): lax.ppermute(table, axis, [(i, i ^ digit * stride) for i in range(n)])]
    ppermute x4 -> x6, starting transfers between devices: 6.7 us -> 6.72 us  [all_sum(): lax.ppermute(table, axis, [(i, i ^ digit * stride) for i in range(n)])]
  transfers between devices with their start and end apart: 9 -> 11, of which waited for: 8 -> 7; matrix products, arithmetic and copies ran while one was open for 6% -> 4% of each run, Pallas kernels for 1% -> 0%
where the time goes in v3:
time: 242 us
  blocking collectives  95.9 us (40%)
  waiting for transfers between devices  74.4 us (31%)
  matrix products  21.7 us (9%)
  starting transfers between devices  19 us (8%)
  local copies, waits for them, and re-layouts  12.1 us (5%)
  Pallas kernels  10.3 us (4%)
  other arithmetic  7.68 us (3%)
    all_to_all x1, blocking collectives, per_device(): lax.all_to_all(rest, 'src', split_axis=0, concat_axis=0, tiled=True)  95.9 us
    ppermute x4, waiting for transfers between devices, shifted(): return lax.ppermute(block, axis, route)  62.5 us
    dot_general x10, matrix products, dress(): out = jnp.dot(weights, stacked, preferred_element_type=jnp.float32)  18.4 us
    ppermute x6, waiting for transfers between devices, all_sum(): lax.ppermute(table, axis, [(i, i ^ digit * stride) for i in range(n)])  11.2 us
    pallas_call x1, Pallas kernels, rest_loops(): pl.pallas_call(rest_loop_kernel, grid=(window,), in_specs=[tile] + [whole...  8.09 us
    ppermute x4, starting transfers between devices, shifted(): return lax.ppermute(block, axis, route)  7.78 us
    ppermute x6, starting transfers between devices, all_sum(): lax.ppermute(table, axis, [(i, i ^ digit * stride) for i in range(n)])  6.72 us
  transfers between devices with their start and end apart: 11, of which 7 were waited for; matrix products, arithmetic and copies ran while one was open for 4% of the time, Pallas kernels for 0%

profile of v3, /device:TPU:0, one launch (start us, length us, event | category | flops | bytes accessed | tf_op | source)
XLA Modules:
  0.0 241.6 jit_solution(9006749107382505786)
XLA Ops:
  0.0 0.8 fusion.25
  0.8 0.8 slice_bitcast_fusion.4
  1.5 1.0 convert_element_type.111
  2.5 0.1 fusion.15
  2.6 0.8 negate_convert_fusion.1
  3.5 0.1 copy.29
  3.6 0.1 copy.30
  3.7 0.1 copy.31
  3.7 0.3 copy-done
  4.0 0.3 fusion.29
  4.4 0.5 copy-done.14
  5.0 0.8 negate_convert_fusion
  5.8 0.1 copy.28
  5.9 0.1 copy.26
  6.0 0.1 copy.27
  6.1 1.2 convolution_convert_fusion.4
  7.3 2.3 convolution_convert_fusion.3
  9.6 2.2 convolution_convert_fusion.2
  11.8 2.2 convolution_convert_fusion.1
  14.1 2.3 convolution_convert_fusion
  16.3 1.2 convolution_convert_fusion.5
  17.6 2.2 shard_map.73
  19.8 3.0 %collective-permute-start = (bf16[2,512,512]{2,1,0:T(8,128)(2,1)}, bf16[2,512,512]{2,1,0:T(8,128)(2,1)S(1)}, u32[]{:S(2)}, u32[]{:S(2)}) collective-permute-start(bf16[2,512,512]{2,1,0:T(8,128)(2,1)} %bitcast.24), channel_id=1, source_target_pairs={{14,0},{15,1},{0,2},{1,3},{2,4},{3,5},{4,6},{5,7},{6,8},{7,9},{8,1... | collective-permute-start | bytes 3145736 | tf_op jit(solution)/shard_map/ppermute | solution.py:12
  22.8 0.0 collective-permute-start.1
  22.8 4.4 %collective-permute-start.2 = (bf16[2,512,512]{2,1,0:T(8,128)(2,1)}, bf16[2,512,512]{2,1,0:T(8,128)(2,1)S(1)}, u32[]{:S(2)}, u32[]{:S(2)}) collective-permute-start(bf16[2,512,512]{2,1,0:T(8,128)(2,1)} %bitcast.22), channel_id=1, source_target_pairs={{1,0},{2,1},{3,2},{4,3},{5,4},{6,5},{7,6},{8,7},{9,8},{10,9},{11,1... | collective-permute-start | bytes 3145736 | tf_op jit(solution)/shard_map/ppermute | solution.py:12
  27.2 0.4 collective-permute-start.3
  27.6 4.5 %all-to-all-start = ((bf16[16,1,2,32,512]{4,3,2,1,0:T(8,128)(2,1)}), bf16[16,1,2,32,512]{4,3,2,1,0:T(8,128)(2,1)}, u32[]{:S(2)}, u32[]{:S(2)}) async-start(bf16[16,1,2,32,512]{4,3,2,1,0:T(8,128)(2,1)} %shard_map.73), calls=%async_computation | async-start | bytes 2097152 | tf_op jit(solution)/shard_map/all_to_all | solution.py:141
  32.1 3.2 %convolution_convert_fusion.9 = bf16[1024,512]{1,0:T(8,128)(2,1)S(1)} fusion(bf16[1024,512]{1,0:T(8,128)(2,1)} %bitcast.131, bf16[512,512]{1,0:T(8,128)(2,1)} %bitcast.149, bf16[512,512]{1,0:T(8,128)(2,1)} %bitcast.139, bf16[512,512]{1,0:T(8,128)(2,1)} %bitcast.144), kind=kOutput, calls=%fused_computation.14 | convolution fusion | flops 1082654720 | bytes 3670016 | tf_op jit(solution)/shard_map/dot_general | solution.py:36
  35.5 1.2 convolution_convert_fusion.8
  36.7 1.2 convolution_convert_fusion.7
  38.0 1.2 convolution_convert_fusion.6
  39.2 2.3 pad_maximum_fusion.1.refs_0_
  41.5 47.2 %collective-permute-done = bf16[2,512,512]{2,1,0:T(8,128)(2,1)S(1)} collective-permute-done((bf16[2,512,512]{2,1,0:T(8,128)(2,1)}, bf16[2,512,512]{2,1,0:T(8,128)(2,1)S(1)}, u32[]{:S(2)}, u32[]{:S(2)}) %collective-permute-start) | collective-permute-done | bytes 1048608 | tf_op jit(solution)/shard_map/ppermute | solution.py:12
  88.8 0.0 collective-permute-done.1
  88.8 0.0 collective-permute-done.2
  88.8 15.3 %collective-permute-done.3 = bf16[2,512,512]{2,1,0:T(8,128)(2,1)} collective-permute-done((bf16[2,512,512]{2,1,0:T(8,128)(2,1)}, bf16[2,512,512]{2,1,0:T(8,128)(2,1)}, u32[]{:S(2)}, u32[]{:S(2)}) %collective-permute-start.3) | collective-permute-done | bytes 1048608 | tf_op jit(solution)/shard_map/ppermute | solution.py:12
  104.0 0.7 all-to-all-done
  104.7 8.1 %shard_map.74 = bf16[16,4,2,32,512]{4,3,2,1,0:T(8,128)(2,1)} custom-call(bf16[4,2,512,512]{3,2,1,0:T(8,128)(2,1)} %pad_maximum_fusion.1.refs_0_, bf16[1,2,512,512]{3,2,1,0:T(8,128)(2,1)S(1)} %bitcast.104, bf16[1,2,512,512]{3,2,1,0:T(8,128)(2,1)S(1)} %bitcast.105, bf16[1,2,512,512]{3,2,1,0:T(8,128)(2,1)S(1)} %bitcast.106, ...), custom_call_target="tpu_custom_call" | custom-call | flops 4294967296 | bytes 12582912 | tf_op jit(solution)/shard_map/pallas_call | solution.py:85
  112.8 95.9 %all_to_all.10 = bf16[16,4,2,32,512]{4,3,2,1,0:T(8,128)(2,1)S(1)} all-to-all(bf16[16,4,2,32,512]{4,3,2,1,0:T(8,128)(2,1)} %shard_map.74), channel_id=1, replica_groups=mesh['groups'=2,'src'=16] {'src'}, dimensions={0} | all-to-all | bytes 8388608 | tf_op jit(solution)/shard_map/all_to_all | solution.py:149
  208.8 0.3 fusion.30
  209.1 1.6 pad_maximum_fusion
  210.8 0.4 fusion.28
  211.2 1.6 copy.18
  212.9 0.8 fusion.31
  213.7 1.6 copy.19
  215.3 0.8 fusion.32
  216.2 0.8 fusion.1
  217.0 0.0 copy-start.15
  217.0 0.0 copy-start.16
  217.0 0.8 fusion
  217.9 0.8 collective-permute-start.4
  218.7 1.3 collective-permute-start.5
  220.0 0.2 collective-permute-start.6
  220.2 3.2 %collective-permute-done.5 = f32[2,80,80]{2,1,0:T(8,128)S(1)} collective-permute-done((f32[2,80,80]{2,1,0:T(8,128)S(1)}, f32[2,80,80]{2,1,0:T(8,128)S(1)}, u32[]{:S(2)}, u32[]{:S(2)}) %collective-permute-start.5) | collective-permute-done | bytes 51232 | tf_op jit(solution)/shard_map/ppermute | solution.py:110
  223.4 1.3 collective-permute-done.6
  224.7 1.6 collective-permute-start.7
  226.3 1.6 collective-permute-start.8
  227.9 1.3 collective-permute-start.9
  229.2 0.1 collective-permute-done.7
  229.3 6.6 %collective-permute-done.8 = f32[2,80,80]{2,1,0:T(8,128)S(1)} collective-permute-done((f32[2,80,80]{2,1,0:T(8,128)S(1)}, f32[2,80,80]{2,1,0:T(8,128)S(1)}, u32[]{:S(2)}, u32[]{:S(2)}) %collective-permute-start.8) | collective-permute-done | bytes 51232 | tf_op jit(solution)/shard_map/ppermute | solution.py:110
  235.9 1.1 copy.10
  237.1 3.7 %gather_fusion = f32[512,2]{1,0:T(8,128)S(1)} fusion(f32[2,80,80]{0,2,1:T(8,128)S(1)} %copy.10, s32[512]{0:T(512)S(1)} %bitcast.115), kind=kCustom, calls=%fused_computation | custom fusion | bytes 12288 | tf_op jit(solution)/shard_map/gather | solution.py:122
  240.7 0.1 multiply_bitcast_fusion
  240.9 0.7 copy.11
  (40 shorter events, 0.2 us)
Async XLA Ops:
  1.5 2.5 %copy-start = (bf16[1,5,2,512,512]{4,3,2,1,0:T(8,128)(2,1)S(1)}, bf16[1,5,2,512,512]{4,3,2,1,0:T(8,128)(2,1)}, u32[]{:S(2)}) copy-start(bf16[1,5,2,512,512]{4,3,2,1,0:T(8,128)(2,1)} %param.7) | copy-start | bytes 15728644
  3.5 12.8 %copy-start.8 = (bf16[64,8,4,128]{3,1,2,0:T(8,128)(2,1)}, bf16[64,8,4,128]{3,1,2,0:T(8,128)(2,1)S(1)}, u32[]{:S(2)}) copy-start(bf16[64,8,4,128]{3,1,2,0:T(8,128)(2,1)S(1)} %copy.29) | copy-start | bytes 1572868
  3.6 12.7 %copy-start.10 = (bf16[64,8,4,128]{3,1,2,0:T(8,128)(2,1)}, bf16[64,8,4,128]{3,1,2,0:T(8,128)(2,1)S(1)}, u32[]{:S(2)}) copy-start(bf16[64,8,4,128]{3,1,2,0:T(8,128)(2,1)S(1)} %copy.30) | copy-start | bytes 1572868
  4.0 12.3 %copy-start.12 = (bf16[64,8,4,128]{3,1,2,0:T(8,128)(2,1)}, bf16[64,8,4,128]{3,1,2,0:T(8,128)(2,1)S(1)}, u32[]{:S(2)}) copy-start(bf16[64,8,4,128]{3,1,2,0:T(8,128)(2,1)S(1)} %copy.31) | copy-start | bytes 1572868
  4.0 0.9 copy-start.14
  4.9 2.4 copy-start.7
  4.9 4.7 %copy-start.5 = (bf16[1,1,2,512,512]{4,3,2,1,0:T(8,128)(2,1)}, bf16[1,1,2,512,512]{4,3,2,1,0:T(8,128)(2,1)S(1)}, u32[]{:S(2)}) copy-start(bf16[1,1,2,512,512]{4,3,2,1,0:T(8,128)(2,1)S(1)} %get-tuple-element.29) | copy-start | bytes 3145732
  4.9 6.9 %copy-start.3 = (bf16[1,1,2,512,512]{4,3,2,1,0:T(8,128)(2,1)}, bf16[1,1,2,512,512]{4,3,2,1,0:T(8,128)(2,1)S(1)}, u32[]{:S(2)}) copy-start(bf16[1,1,2,512,512]{4,3,2,1,0:T(8,128)(2,1)S(1)} %get-tuple-element.28) | copy-start | bytes 3145732
  4.9 9.1 %copy-start.1 = (bf16[1,1,2,512,512]{4,3,2,1,0:T(8,128)(2,1)}, bf16[1,1,2,512,512]{4,3,2,1,0:T(8,128)(2,1)S(1)}, u32[]{:S(2)}) copy-start(bf16[1,1,2,512,512]{4,3,2,1,0:T(8,128)(2,1)S(1)} %get-tuple-element.31) | copy-start | bytes 3145732
  19.8 69.0 %collective-permute-start = (bf16[2,512,512]{2,1,0:T(8,128)(2,1)}, bf16[2,512,512]{2,1,0:T(8,128)(2,1)S(1)}, u32[]{:S(2)}, u32[]{:S(2)}) collective-permute-start(bf16[2,512,512]{2,1,0:T(8,128)(2,1)} %bitcast.24), channel_id=1, source_target_pairs={{14,0},{15,1},{0,2},{1,3},{2,4},{3,5},{4,6},{5,7},{6,8},{7,9},{8,1... | collective-permute-start | bytes 3145736 | tf_op jit(solution)/shard_map/ppermute | solution.py:12
  22.8 66.0 %collective-permute-start.1 = (bf16[2,512,512]{2,1,0:T(8,128)(2,1)}, bf16[2,512,512]{2,1,0:T(8,128)(2,1)S(1)}, u32[]{:S(2)}, u32[]{:S(2)}) collective-permute-start(bf16[2,512,512]{2,1,0:T(8,128)(2,1)} %bitcast.23), channel_id=1, source_target_pairs={{15,0},{0,1},{1,2},{2,3},{3,4},{4,5},{5,6},{6,7},{7,8},{8,9},{9,10... | collective-permute-start | bytes 3145736 | tf_op jit(solution)/shard_map/ppermute | solution.py:12
  22.8 66.0 %collective-permute-start.2 = (bf16[2,512,512]{2,1,0:T(8,128)(2,1)}, bf16[2,512,512]{2,1,0:T(8,128)(2,1)S(1)}, u32[]{:S(2)}, u32[]{:S(2)}) collective-permute-start(bf16[2,512,512]{2,1,0:T(8,128)(2,1)} %bitcast.22), channel_id=1, source_target_pairs={{1,0},{2,1},{3,2},{4,3},{5,4},{6,5},{7,6},{8,7},{9,8},{10,9},{11,1... | collective-permute-start | bytes 3145736 | tf_op jit(solution)/shard_map/ppermute | solution.py:12
  27.2 76.8 %collective-permute-start.3 = (bf16[2,512,512]{2,1,0:T(8,128)(2,1)}, bf16[2,512,512]{2,1,0:T(8,128)(2,1)}, u32[]{:S(2)}, u32[]{:S(2)}) collective-permute-start(bf16[2,512,512]{2,1,0:T(8,128)(2,1)} %bitcast.21), channel_id=1, source_target_pairs={{2,0},{3,1},{4,2},{5,3},{6,4},{7,5},{8,6},{9,7},{10,8},{11,9},{12,... | collective-permute-start | bytes 3145736 | tf_op jit(solution)/shard_map/ppermute | solution.py:12
  27.6 77.2 %all-to-all-start = ((bf16[16,1,2,32,512]{4,3,2,1,0:T(8,128)(2,1)}), bf16[16,1,2,32,512]{4,3,2,1,0:T(8,128)(2,1)}, u32[]{:S(2)}, u32[]{:S(2)}) async-start(bf16[16,1,2,32,512]{4,3,2,1,0:T(8,128)(2,1)} %shard_map.73), calls=%async_computation | async-start | bytes 2097152 | tf_op jit(solution)/shard_map/all_to_all | solution.py:141
  32.1 3.3 %copy-start.6 = (bf16[1,1,2,512,512]{4,3,2,1,0:T(8,128)(2,1)S(1)}, bf16[1,1,2,512,512]{4,3,2,1,0:T(8,128)(2,1)}, u32[]{:S(2)}) copy-start(bf16[1,1,2,512,512]{4,3,2,1,0:T(8,128)(2,1)} %copy-done.5) | copy-start | bytes 3145732
  32.1 3.3 %copy-start.9 = (bf16[64,8,4,128]{3,1,2,0:T(8,128)(2,1)S(1)}, bf16[64,8,4,128]{3,1,2,0:T(8,128)(2,1)}, u32[]{:S(2)}) copy-start(bf16[64,8,4,128]{3,1,2,0:T(8,128)(2,1)} %copy-done.8) | copy-start | bytes 1572868
  32.1 3.3 %copy-start.11 = (bf16[64,8,4,128]{3,1,2,0:T(8,128)(2,1)S(1)}, bf16[64,8,4,128]{3,1,2,0:T(8,128)(2,1)}, u32[]{:S(2)}) copy-start(bf16[64,8,4,128]{3,1,2,0:T(8,128)(2,1)} %copy-done.10) | copy-start | bytes 1572868
  32.1 3.3 %copy-start.13 = (bf16[64,8,4,128]{3,1,2,0:T(8,128)(2,1)S(1)}, bf16[64,8,4,128]{3,1,2,0:T(8,128)(2,1)}, u32[]{:S(2)}) copy-start(bf16[64,8,4,128]{3,1,2,0:T(8,128)(2,1)} %copy-done.12) | copy-start | bytes 1572868
  35.4 1.3 copy-start.4
  36.7 1.3 copy-start.2
  217.0 3.2 %copy-start.15 = (s32[2,512]{1,0:T(2,128)S(1)}, s32[2,512]{1,0:T(2,128)}, u32[]{:S(2)}) copy-start(s32[2,512]{1,0:T(2,128)} %param.12) | copy-start | bytes 12292
  217.0 12.2 %copy-start.16 = (s32[512]{0:T(512)S(1)}, s32[512]{0:T(512)}, u32[]{:S(2)}) copy-start(s32[512]{0:T(512)} %param.13) | copy-start | bytes 6148
  217.9 2.3 collective-permute-start.4
  218.7 4.7 %collective-permute-start.5 = (f32[2,80,80]{2,1,0:T(8,128)S(1)}, f32[2,80,80]{2,1,0:T(8,128)S(1)}, u32[]{:S(2)}, u32[]{:S(2)}) collective-permute-start(f32[2,80,80]{2,1,0:T(8,128)S(1)} %pad_maximum_fusion.2), channel_id=1, source_target_pairs={{0,2},{1,3},{2,0},{3,1},{4,6},{5,7},{6,4},{7,5},{8,10},{9,11},{10,... | collective-permute-start | bytes 153608 | tf_op jit(solution)/shard_map/ppermute | solution.py:110
  220.0 4.7 %collective-permute-start.6 = (f32[2,80,80]{2,1,0:T(8,128)S(1)}, f32[2,80,80]{2,1,0:T(8,128)S(1)}, u32[]{:S(2)}, u32[]{:S(2)}) collective-permute-start(f32[2,80,80]{2,1,0:T(8,128)S(1)} %pad_maximum_fusion.2), channel_id=1, source_target_pairs={{0,3},{1,2},{2,1},{3,0},{4,7},{5,6},{6,5},{7,4},{8,11},{9,10},{10,... | collective-permute-start | bytes 153608 | tf_op jit(solution)/shard_map/ppermute | solution.py:110
  224.7 4.6 %collective-permute-start.7 = (f32[2,80,80]{2,1,0:T(8,128)S(1)}, f32[2,80,80]{2,1,0:T(8,128)S(1)}, u32[]{:S(2)}, u32[]{:S(2)}) collective-permute-start(f32[2,80,80]{2,1,0:T(8,128)S(1)} %add_add_fusion.1), channel_id=1, source_target_pairs={{0,4},{1,5},{2,6},{3,7},{4,0},{5,1},{6,2},{7,3},{8,12},{9,13},{10,... | collective-permute-start | bytes 153608 | tf_op jit(solution)/shard_map/ppermute | solution.py:110
  226.3 9.5 %collective-permute-start.8 = (f32[2,80,80]{2,1,0:T(8,128)S(1)}, f32[2,80,80]{2,1,0:T(8,128)S(1)}, u32[]{:S(2)}, u32[]{:S(2)}) collective-permute-start(f32[2,80,80]{2,1,0:T(8,128)S(1)} %add_add_fusion.1), channel_id=1, source_target_pairs={{0,8},{1,9},{2,10},{3,11},{4,12},{5,13},{6,14},{7,15},{8,0},{9,1},... | collective-permute-start | bytes 153608 | tf_op jit(solution)/shard_map/ppermute | solution.py:110
  227.9 8.0 %collective-permute-start.9 = (f32[2,80,80]{2,1,0:T(8,128)S(1)}, f32[2,80,80]{2,1,0:T(8,128)S(1)}, u32[]{:S(2)}, u32[]{:S(2)}) collective-permute-start(f32[2,80,80]{2,1,0:T(8,128)S(1)} %add_add_fusion.1), channel_id=1, source_target_pairs={{0,12},{1,13},{2,14},{3,15},{4,8},{5,9},{6,10},{7,11},{8,4},{9,5},... | collective-permute-start | bytes 153608 | tf_op jit(solution)/shard_map/ppermute | solution.py:110

commit v4 on v3

--- a/solution.py
+++ b/solution.py
@@ -1,4 +1,5 @@
 import jax
+import numpy as np
 import jax.numpy as jnp
 from jax import lax
 from jax.experimental import pallas as pl
@@ -22,12 +23,16 @@
 
 def dressing_matrix(elemental, order_row, phase_row):
     cosine, sine = gamma_parts(order_row, phase_row)
-    meson = elemental.astype(jnp.float32)
-    kron_re = jnp.kron(cosine, meson[0]) - jnp.kron(sine, meson[1])
-    kron_im = jnp.kron(cosine, meson[1]) + jnp.kron(sine, meson[0])
-    top = jnp.concatenate([kron_re, -kron_im], axis=1)
-    bottom = jnp.concatenate([kron_im, kron_re], axis=1)
-    return jnp.concatenate([top, bottom], axis=0).astype(jnp.bfloat16)
+    real, imag = elemental[0].astype(jnp.float32), elemental[1].astype(jnp.float32)
+    plain = jnp.stack([jnp.stack([real, -imag], 1), jnp.stack([imag, real], 1)], 0)
+    turned = jnp.stack([jnp.stack([-imag, -real], 1), jnp.stack([real, -imag], 1)], 0)
+    spins = cosine.shape[0]
+    weights = (
+        cosine[None, :, None, None, :, None] * plain[:, None, :, :, None, :]
+        + sine[None, :, None, None, :, None] * turned[:, None, :, :, None, :]
+    )
+    size = 2 * spins * real.shape[0]
+    return weights.reshape(size, size).astype(jnp.bfloat16)
 
 
 def dress(weights, tile_pair):
@@ -68,31 +73,32 @@
 
 
 def rest_loop_kernel(*refs):
-    forward_ref, partner_refs, out_ref = refs[0], refs[1:-1], refs[-1]
+    count = (len(refs) - 1) // 2
+    forward_refs, partner_refs, out_ref = refs[:count], refs[count:-1], refs[-1]
     step = pl.program_id(0)
-    for index, partner_ref in enumerate(partner_refs):
+    for index in range(count):
 
         @pl.when(step == index)
         def _():
-            loop_kernel(forward_ref, partner_ref, out_ref)
-
-
-def rest_loops(forward, partners, shares):
-    window, _, order, _ = forward.shape
+            loop_kernel(forward_refs[index], partner_refs[index], out_ref)
+
+
+def rest_loops(forwards, partners, shares):
+    count = len(forwards)
+    _, order, _ = forwards[0].shape
     rows = order // shares
-    tile = pl.BlockSpec((1, 2, order, order), lambda s: (s, 0, 0, 0))
     whole = pl.BlockSpec((1, 2, order, order), lambda s: (0, 0, 0, 0))
     return pl.pallas_call(
         rest_loop_kernel,
-        grid=(window,),
-        in_specs=[tile] + [whole] * len(partners),
+        grid=(count,),
+        in_specs=[whole] * (2 * count),
         out_specs=pl.BlockSpec((shares, 1, 2, rows, order), lambda s: (0, s, 0, 0, 0)),
-        out_shape=jax.ShapeDtypeStruct((shares, window, 2, rows, order), jnp.bfloat16),
-        compiler_params=pltpu.CompilerParams(vmem_limit_bytes=48 * 1024 * 1024),
+        out_shape=jax.ShapeDtypeStruct((shares, count, 2, rows, order), jnp.bfloat16),
+        compiler_params=pltpu.CompilerParams(vmem_limit_bytes=56 * 1024 * 1024),
         cost_estimate=pl.CostEstimate(
-            flops=8 * window * order ** 3, transcendentals=0, bytes_accessed=6 * window * order * order * 2
+            flops=8 * count * order ** 3, transcendentals=0, bytes_accessed=6 * count * order * order * 2
         ),
-    )(forward, *[partner[None] for partner in partners])
+    )(*[tile[None] for tile in forwards], *[tile[None] for tile in partners])
 
 
 def inner_product(left, right):
@@ -128,28 +134,32 @@
     window = perambulator.shape[1]
     half_window = window // 2
     shares = lax.axis_size("src")
-    sink_weights = dressing_matrix(sink_meson[0], gamma_order[1], gamma_phase[1])
-    backward = [dress(sink_weights, perambulator[0, position]) for position in range(window)]
-    source_weights = dressing_matrix(source_meson[0], gamma_order[0], gamma_phase[0])
-    centre = open_loops(dress(source_weights, perambulator[0, half_window])[None], backward[half_window][None], shares)
-    centre, backward = lax.optimization_barrier((centre, backward))
-    mirrored = {0: backward[half_window]}
+    tiles = perambulator[0]
+    mesons = jnp.stack([source_meson[0], sink_meson[0]])
+    received = {}
     for offset in range(1, half_window + 1):
-        for direction in (1, -1):
-            separation = direction * offset
-            mirrored[separation] = shifted(backward[half_window - separation], "src", -separation)
+        received[offset] = (
+            shifted(tiles[half_window - offset], "src", -offset),
+            shifted(mesons, "src", -offset),
+        )
+    source_own = dressing_matrix(mesons[0], gamma_order[0], gamma_phase[0])
+    sink_own = dressing_matrix(mesons[1], gamma_order[1], gamma_phase[1])
+    centre = open_loops(
+        dress(source_own, tiles[half_window])[None], dress(sink_own, tiles[half_window])[None], shares
+    )
     centre_slices = lax.all_to_all(centre, "src", split_axis=0, concat_axis=0, tiled=True)
-    centre_slices, mirrored = lax.optimization_barrier((centre_slices, mirrored))
-    others = [position for position in range(window) if position != half_window]
-    rest = rest_loops(
-        jnp.stack([dress(source_weights, perambulator[0, position]) for position in others]),
-        [mirrored[position - half_window] for position in others],
-        shares,
-    )
+    forwards, partners = [], []
+    own_forward = {offset: dress(source_own, tiles[half_window + offset]) for offset in received}
+    own_backward = {offset: dress(sink_own, tiles[half_window + offset]) for offset in received}
+    centre_slices, received = lax.optimization_barrier((centre_slices, received))
+    for offset, (tile, partner_mesons) in received.items():
+        source_partner = dressing_matrix(partner_mesons[0], gamma_order[0], gamma_phase[0])
+        sink_partner = dressing_matrix(partner_mesons[1], gamma_order[1], gamma_phase[1])
+        forwards += [own_forward[offset], dress(source_partner, tile)]
+        partners += [dress(sink_partner, tile), own_backward[offset]]
+    rest = rest_loops(forwards, partners, shares)
     rest_slices = lax.all_to_all(rest, "src", split_axis=0, concat_axis=0, tiled=True)
-    slices = jnp.concatenate(
-        [rest_slices[:, :half_window], centre_slices, rest_slices[:, half_window:]], axis=1
-    )
+    slices = jnp.concatenate([centre_slices, rest_slices], axis=1)
     block_count = slices.shape[0] * slices.shape[1]
     real_flat = slices[:, :, 0].reshape(block_count, -1)
     imag_flat = slices[:, :, 1].reshape(block_count, -1)
@@ -159,6 +169,14 @@
             inner_product(real_flat, imag_flat) + inner_product(imag_flat, real_flat),
         ]
     )
+    place = np.zeros(block_count, np.int32)
+    for source in range(shares):
+        place[source * window + half_window] = source * window
+        for offset in range(1, half_window + 1):
+            place[source * window + half_window + offset] = source * window + 2 * offset - 1
+            place[((source + offset) % shares) * window + half_window - offset] = source * window + 2 * offset
+    canonical = jnp.asarray(place)
+    trace_table = trace_table[:, canonical][:, :, canonical]
     summed = all_sum(trace_table, "src")
     return select_diagrams(summed, diagram_blocks, diagram_codes)
 

time: 242 us -> 281 us (1.16)
  blocking collectives: 95.9 us -> 0 us
  waiting for transfers between devices: 74.4 us -> 126 us
  local copies, waits for them, and re-layouts: 12.1 us -> 50.5 us
  starting transfers between devices: 19 us -> 45 us
  matrix products: 21.7 us -> 30.9 us
  other arithmetic: 7.68 us -> 14.9 us
    all_to_all x1 -> x0, blocking collectives: 95.9 us -> none  [per_device(): lax.all_to_all(rest, 'src', split_axis=0, concat_axis=0, tiled=True)]
    all_to_all x0 -> x1, waiting for transfers between devices: none -> 76.6 us  [per_device(): lax.all_to_all(rest, 'src', split_axis=0, concat_axis=0, tiled=True)]
    ppermute x4, waiting for transfers between devices: 62.5 us -> 37.6 us  [shifted(): return lax.ppermute(block, axis, route)]
    convert_element_type x0 -> x6, local copies, waits for them, and re-layouts: none -> 19.8 us  [dressing_matrix(): return weights.reshape(size, size).astype(jnp.bfloat16)]
    ppermute x6, starting transfers between devices: 6.72 us -> 19.2 us  [all_sum(): lax.ppermute(table, axis, [(i, i ^ digit * stride) for i in range(n)])]
    all_to_all x0 -> x1, starting transfers between devices: none -> 11.9 us  [per_device(): lax.all_to_all(rest, 'src', split_axis=0, concat_axis=0, tiled=True)]
    convert_element_type x2 -> x8, other arithmetic: 1.01 us -> 11.8 us  [the longest x4 10.2 us: dressing_matrix(): return weights.reshape(size, size).astype(jnp.bfloat16)]
    dot_general x10, matrix products: 18.4 us -> 27.5 us  [dress(): out = jnp.dot(weights, stacked, preferred_element_type=jnp.float32)]
  transfers between devices with their start and end apart: 11 -> 12, of which waited for: 7 -> 9; matrix products, arithmetic and copies ran while one was open for 4% -> 4% of each run, Pallas kernels for 0% -> 0%
where the time goes in v4:
time: 281 us; the launch traced here: 280 us
  waiting for transfers between devices  126 us (45%)
  local copies, waits for them, and re-layouts  50.5 us (18%)
  starting transfers between devices  45 us (16%)
  matrix products  30.9 us (11%)
  other arithmetic  14.9 us (5%)
  Pallas kernels  11.8 us (4%)
    all_to_all x1, waiting for transfers between devices, per_device(): lax.all_to_all(rest, 'src', split_axis=0, concat_axis=0, tiled=True)  76.6 us
    ppermute x4, waiting for transfers between devices, shifted(): return lax.ppermute(block, axis, route)  37.6 us
    dot_general x10, matrix products, dress(): out = jnp.dot(weights, stacked, preferred_element_type=jnp.float32)  27.5 us
    convert_element_type x6, local copies, waits for them, and re-layouts, dressing_matrix(): return weights.reshape(size, size).astype(jnp.bfloat16)  19.8 us
    ppermute x6, starting transfers between devices, all_sum(): lax.ppermute(table, axis, [(i, i ^ digit * stride) for i in range(n)])  19.2 us
    ppermute x6, waiting for transfers between devices, all_sum(): lax.ppermute(table, axis, [(i, i ^ digit * stride) for i in range(n)])  12.1 us
    all_to_all x1, starting transfers between devices, per_device(): lax.all_to_all(rest, 'src', split_axis=0, concat_axis=0, tiled=True)  11.9 us
    convert_element_type x4, other arithmetic, dressing_matrix(): return weights.reshape(size, size).astype(jnp.bfloat16)  10.2 us
  transfers between devices with their start and end apart: 12, of which 9 were waited for; matrix products, arithmetic and copies ran while one was open for 4% of the time, Pallas kernels for 0%

profile of v4, /device:TPU:0, one launch (start us, length us, event | category | flops | bytes accessed | tf_op | source)
XLA Modules:
  0.0 279.8 jit_solution(8175729601472168757)
XLA Ops:
  0.0 0.8 fusion.3
  0.8 0.8 bitcast_convert_fusion.11
  1.6 0.8 fusion.5
  2.4 0.8 bitcast_convert_fusion.9
  3.2 0.8 slice_bitcast_fusion.2
  3.9 0.8 fusion.35
  5.8 1.2 add_convert_fusion.5
  6.9 2.7 convert_element_type.420
  9.6 1.1 add_convert_fusion.4
  10.8 2.7 convert_element_type.431
  13.5 4.7 %fusion.39 = (bf16[1,1,2,512,512]{4,3,2,1,0:T(8,128)(2,1)}, bf16[2,512,512]{2,1,0:T(8,128)(2,1)}, bf16[2,512,512]{2,1,0:T(8,128)(2,1)}, bf16[1,1,2,512,512]{4,3,2,1,0:T(8,128)(2,1)S(1)}, bf16[1,1,2,512,512]{4,3,2,1,0:T(8,128)(2,1)}) fusion(bf16[1,5,2,512,512]{4,3,2,1,0:T(8,128)(2,1)} %param.8), kind=kLoop, calls=%fused_computation.133 | loop fusion | bytes 10485760 | tf_op jit(solution)/shard_map/slice | solution.py:152
  18.2 1.2 convolution_convert_fusion.8
  19.8 1.2 convolution_convert_fusion.9
  21.1 2.2 shard_map.82
  23.3 7.4 %all-to-all-start = ((bf16[16,1,2,32,512]{4,3,2,1,0:T(8,128)(2,1)}), bf16[16,1,2,32,512]{4,3,2,1,0:T(8,128)(2,1)S(1)}, u32[]{:S(2)}, u32[]{:S(2)}) async-start(bf16[16,1,2,32,512]{4,3,2,1,0:T(8,128)(2,1)} %shard_map.82), calls=%async_computation | async-start | bytes 2097152 | tf_op jit(solution)/shard_map/all_to_all | solution.py:150
  30.7 4.7 %collective-permute-start.3 = (bf16[2,2,128,128]{3,2,1,0:T(8,128)(2,1)S(1)}, bf16[2,2,128,128]{3,2,1,0:T(8,128)(2,1)S(1)}, u32[]{:S(2)}, u32[]{:S(2)}) collective-permute-start(bf16[2,2,128,128]{3,2,1,0:T(8,128)(2,1)S(1)} %constant_dynamic-update-slice_fusion), channel_id=1, source_target_pairs={{2,0},{3,1},{4,2},{5,3},{6,4},{7,5},{8,6},{9,7},{10,8},{11,9},{12,... | collective-permute-start | bytes 393224 | tf_op jit(solution)/shard_map/ppermute | solution.py:13
  35.4 1.4 collective-permute-start.2
  37.3 4.2 %convolution_convert_fusion = bf16[1024,512]{1,0:T(8,128)(2,1)} fusion(bf16[1024,1024]{1,0:T(8,128)(2,1)} %convert_element_type.431, bf16[1024,512]{1,0:T(8,128)(2,1)} %bitcast.193), kind=kOutput, calls=%fused_computation.9 | convolution fusion | flops 1074266112 | bytes 4194304 | tf_op jit(solution)/shard_map/dot_general | solution.py:41
  41.4 2.2 convolution_convert_fusion.5
  43.6 2.2 convolution_convert_fusion.2
  45.9 2.3 convolution_convert_fusion.7
  48.2 3.5 %collective-permute-done.3 = bf16[2,2,128,128]{3,2,1,0:T(8,128)(2,1)S(1)} collective-permute-done((bf16[2,2,128,128]{3,2,1,0:T(8,128)(2,1)S(1)}, bf16[2,2,128,128]{3,2,1,0:T(8,128)(2,1)S(1)}, u32[]{:S(2)}, u32[]{:S(2)}) %collective-permute-start.3) | collective-permute-done | bytes 131104 | tf_op jit(solution)/shard_map/ppermute | solution.py:13
  51.7 2.8 %collective-permute-done.1 = bf16[2,2,128,128]{3,2,1,0:T(8,128)(2,1)S(1)} collective-permute-done((bf16[2,2,128,128]{3,2,1,0:T(8,128)(2,1)S(1)}, bf16[2,2,128,128]{3,2,1,0:T(8,128)(2,1)S(1)}, u32[]{:S(2)}, u32[]{:S(2)}) %collective-permute-start.1) | collective-permute-done | bytes 131104 | tf_op jit(solution)/shard_map/ppermute | solution.py:13
  54.5 21.0 %collective-permute-done.2 = bf16[2,512,512]{2,1,0:T(8,128)(2,1)S(1)} collective-permute-done((bf16[2,512,512]{2,1,0:T(8,128)(2,1)}, bf16[2,512,512]{2,1,0:T(8,128)(2,1)S(1)}, u32[]{:S(2)}, u32[]{:S(2)}) %collective-permute-start.2) | collective-permute-done | bytes 1048608 | tf_op jit(solution)/shard_map/ppermute | solution.py:13
  75.5 1.0 copy-done.12
  76.5 10.3 %collective-permute-done = bf16[2,512,512]{2,1,0:T(8,128)(2,1)} collective-permute-done((bf16[2,512,512]{2,1,0:T(8,128)(2,1)}, bf16[2,512,512]{2,1,0:T(8,128)(2,1)}, u32[]{:S(2)}, u32[]{:S(2)}) %collective-permute-start) | collective-permute-done | bytes 1048608 | tf_op jit(solution)/shard_map/ppermute | solution.py:13
  87.1 0.9 copy.32
  88.1 0.9 copy.33
  89.0 0.9 copy.34
  90.9 3.5 %add_convert_fusion.2 = (bf16[2,4,128,2,4,128]{5,4,3,2,1,0:T(4,128)(2,1)}, bf16[2,4,128,2,4,128]{5,4,3,2,1,0:T(4,128)(2,1)S(1)}) fusion(f32[2,128,2,128]{3,2,1,0:T(2,128)S(1)} %copy.30, f32[2,128,2,128]{3,2,1,0:T(2,128)S(1)} %copy.29, f32[4,4]{1,0:T(4,128)S(1)} %get-tuple-element.90, f32[4,4]{1,0:T(4,128)S(1)} %get-tuple-element.91, ...), kind=kLoop, calls=%fused_computation.5 | loop fusion | flops 8388608 | bytes 5243008 | tf_op jit(solution)/shard_map/convert_element_type | solution.py:35
  94.5 4.4 %convert_element_type.447 = bf16[1024,1024]{1,0:T(8,128)(2,1)} reshape(bf16[2,4,128,2,4,128]{5,4,3,2,1,0:T(4,128)(2,1)} %get-tuple-element.78) | data formatting | bytes 4194304 | tf_op jit(solution)/shard_map/convert_element_type | solution.py:35
  98.9 2.7 convert_element_type.439
  101.6 4.4 %add_convert_fusion = (bf16[2,4,128,2,4,128]{5,4,3,2,1,0:T(4,128)(2,1)}, bf16[2,4,128,2,4,128]{5,4,3,2,1,0:T(4,128)(2,1)S(1)}) fusion(f32[2,128,2,128]{3,2,1,0:T(2,128)} %copy.34, f32[2,128,2,128]{3,2,1,0:T(2,128)} %copy.33, f32[4,4]{1,0:T(4,128)S(1)} %get-tuple-element.87, f32[4,4]{1,0:T(4,128)S(1)} %get-tuple-element.86, f32[2,128,2,128]{3,2,1,0:T(2,128)} %copy.32, ...), kind=kLoop, calls=%fused_computation.3 | loop fusion | flops 8388608 | bytes 5243008 | tf_op jit(solution)/shard_map/convert_element_type | solution.py:35
  105.9 4.5 %convert_element_type.462 = bf16[1024,1024]{1,0:T(8,128)(2,1)} reshape(bf16[2,4,128,2,4,128]{5,4,3,2,1,0:T(4,128)(2,1)} %get-tuple-element.76) | data formatting | bytes 4194304 | tf_op jit(solution)/shard_map/convert_element_type | solution.py:35
  110.4 4.2 %convolution_convert_fusion.4 = bf16[1024,512]{1,0:T(8,128)(2,1)} fusion(bf16[1024,1024]{1,0:T(8,128)(2,1)} %convert_element_type.447, bf16[1024,512]{1,0:T(8,128)(2,1)} %bitcast.206), kind=kOutput, calls=%fused_computation.13 | convolution fusion | flops 1074266112 | bytes 4194304 | tf_op jit(solution)/shard_map/dot_general | solution.py:41
  114.7 2.2 convolution_convert_fusion.1
  116.9 2.7 convert_element_type.454
  119.6 4.2 %convolution_convert_fusion.6 = bf16[1024,512]{1,0:T(8,128)(2,1)} fusion(bf16[1024,1024]{1,0:T(8,128)(2,1)} %convert_element_type.439, bf16[1024,512]{1,0:T(8,128)(2,1)} %bitcast.34), kind=kOutput, calls=%fused_computation.15 | convolution fusion | flops 1074266112 | bytes 4194304 | tf_op jit(solution)/shard_map/dot_general | solution.py:41
  123.9 3.5 %convolution_convert_fusion.3 = bf16[1024,512]{1,0:T(8,128)(2,1)} fusion(bf16[1024,1024]{1,0:T(8,128)(2,1)S(1)} %copy-done.4, bf16[1024,512]{1,0:T(8,128)(2,1)} %bitcast.34), kind=kOutput, calls=%fused_computation.12 | convolution fusion | flops 1074266112 | bytes 4194304 | tf_op jit(solution)/shard_map/dot_general | solution.py:41
  127.3 9.5 %shard_map.83 = bf16[16,4,2,32,512]{4,3,2,1,0:T(8,128)(2,1)} custom-call(bf16[1,2,512,512]{3,2,1,0:T(8,128)(2,1)} %bitcast.211, bf16[1,2,512,512]{3,2,1,0:T(8,128)(2,1)} %bitcast.214, bf16[1,2,512,512]{3,2,1,0:T(8,128)(2,1)} %bitcast.209, bf16[1,2,512,512]{3,2,1,0:T(8,128)(2,1)} %bitcast.212, bf16[1,2,512,512]{3,2,1,0:T(8,128)(2,1)} %bitcast.215, ...), custom_call_target="tpu_custom_call" | custom-call | flops 4294967296 | bytes 12582912 | tf_op jit(solution)/shard_map/pallas_call | solution.py:91
  136.9 11.9 %all-to-all-start.1 = ((bf16[16,4,2,32,512]{4,3,2,1,0:T(8,128)(2,1)}), bf16[16,4,2,32,512]{4,3,2,1,0:T(8,128)(2,1)}, u32[]{:S(2)}, u32[]{:S(2)}) async-start(bf16[16,4,2,32,512]{4,3,2,1,0:T(8,128)(2,1)} %shard_map.83), calls=%async_computation.1 | async-start | bytes 8388608 | tf_op jit(solution)/shard_map/all_to_all | solution.py:161
  148.8 1.1 constant_dynamic-update-slice_fusion.3
  149.8 76.6 %all-to-all-done.1 = bf16[16,4,2,32,512]{4,3,2,1,0:T(8,128)(2,1)} async-done(((bf16[16,4,2,32,512]{4,3,2,1,0:T(8,128)(2,1)}), bf16[16,4,2,32,512]{4,3,2,1,0:T(8,128)(2,1)}, u32[]{:S(2)}, u32[]{:S(2)}) %all-to-all-start.1) | async-done | bytes 4194336 | tf_op jit(solution)/shard_map/all_to_all | solution.py:161
  226.4 4.8 %constant_dynamic-update-slice_fusion.2 = bf16[16,5,2,32,512]{4,3,2,1,0:T(8,128)(2,1)} fusion(bf16[16,5,2,32,512]{4,3,2,1,0:T(8,128)(2,1)} %constant_dynamic-update-slice_fusion.3, bf16[16,4,2,32,512]{4,3,2,1,0:T(8,128)(2,1)} %all-to-all-done.1), kind=kLoop, calls=%fused_computation.87 | loop fusion | bytes 8388608 | tf_op jit(solution)/shard_map/concatenate | solution.py:162
  231.2 3.0 %fusion.38 = (bf16[16,5,1,32,512]{4,3,2,1,0:T(8,128)(2,1)S(1)}, bf16[16,5,1,32,512]{4,3,2,1,0:T(8,128)(2,1)S(1)}) fusion(bf16[16,5,2,32,512]{4,3,2,1,0:T(8,128)(2,1)} %constant_dynamic-update-slice_fusion.2), kind=kLoop, calls=%fused_computation.132 | loop fusion | bytes 10485760 | tf_op jit(solution)/shard_map/slice | solution.py:165
  234.2 1.6 copy.40
  235.9 1.6 copy.39
  237.5 0.8 fusion.40
  238.3 0.8 fusion.41
  239.2 0.8 fusion
  240.0 0.8 fusion.1
  241.0 0.7 gather_fusion
  241.7 0.7 gather_fusion.1
  242.4 6.2 %collective-permute-start.5 = (f32[2,80,80]{1,0,2:T(2,128)S(1)}, f32[2,80,80]{1,0,2:T(2,128)S(1)}, u32[]{:S(2)}, u32[]{:S(2)}) collective-permute-start(f32[2,80,80]{1,0,2:T(2,128)S(1)} %bitcast.199), channel_id=1, source_target_pairs={{0,2},{1,3},{2,0},{3,1},{4,6},{5,7},{6,4},{7,5},{8,10},{9,11},{10,... | collective-permute-start | bytes 153608 | tf_op jit(solution)/shard_map/ppermute | solution.py:116
  248.7 0.5 collective-permute-start.4
  249.2 2.7 collective-permute-done.5
  251.9 1.8 collective-permute-done.6
  253.8 11.8 %collective-permute-start.9 = (f32[2,80,80]{1,0,2:T(2,128)S(1)}, f32[2,80,80]{1,0,2:T(2,128)S(1)}, u32[]{:S(2)}, u32[]{:S(2)}) collective-permute-start(f32[2,80,80]{1,0,2:T(2,128)S(1)} %add_add_fusion.1), channel_id=1, source_target_pairs={{0,12},{1,13},{2,14},{3,15},{4,8},{5,9},{6,10},{7,11},{8,4},{9,5},... | collective-permute-start | bytes 153608 | tf_op jit(solution)/shard_map/ppermute | solution.py:116
  265.6 0.6 collective-permute-start.8
  266.3 2.5 collective-permute-done.9
  268.8 5.2 %collective-permute-done.8 = f32[2,80,80]{1,0,2:T(2,128)S(1)} collective-permute-done((f32[2,80,80]{1,0,2:T(2,128)S(1)}, f32[2,80,80]{1,0,2:T(2,128)S(1)}, u32[]{:S(2)}, u32[]{:S(2)}) %collective-permute-start.8) | collective-permute-done | bytes 51232 | tf_op jit(solution)/shard_map/ppermute | solution.py:116
  273.9 1.3 copy.37
  275.2 3.7 %gather_fusion.2 = f32[512,2]{1,0:T(8,128)S(1)} fusion(f32[2,80,80]{0,2,1:T(8,128)S(1)} %copy.37, s32[512]{0:T(512)S(1)} %bitcast.188), kind=kCustom, calls=%fused_computation.2 | custom fusion | bytes 12288 | tf_op jit(solution)/shard_map/gather | solution.py:128
  279.1 0.7 copy.38
  (71 shorter events, 3.7 us)
Async XLA Ops:
  13.5 4.7 %copy-start.1 = (bf16[1024,1024]{1,0:T(8,128)(2,1)S(1)}, bf16[1024,1024]{1,0:T(8,128)(2,1)}, u32[]{:S(2)}) copy-start(bf16[1024,1024]{1,0:T(8,128)(2,1)} %convert_element_type.431) | copy-start | bytes 6291460
  18.2 1.6 copy-start
  21.0 9.6 %copy-start.7 = (bf16[1,2,128,128]{3,2,1,0:T(8,128)(2,1)S(1)}, bf16[1,2,128,128]{3,2,1,0:T(8,128)(2,1)}, u32[]{:S(2)}) copy-start(bf16[1,2,128,128]{3,2,1,0:T(8,128)(2,1)} %param.9) | copy-start | bytes 196612
  21.0 9.7 %copy-start.8 = (bf16[1,2,128,128]{3,2,1,0:T(8,128)(2,1)S(1)}, bf16[1,2,128,128]{3,2,1,0:T(8,128)(2,1)}, u32[]{:S(2)}) copy-start(bf16[1,2,128,128]{3,2,1,0:T(8,128)(2,1)} %param.10) | copy-start | bytes 196612
  23.3 63.5 %all-to-all-start = ((bf16[16,1,2,32,512]{4,3,2,1,0:T(8,128)(2,1)}), bf16[16,1,2,32,512]{4,3,2,1,0:T(8,128)(2,1)S(1)}, u32[]{:S(2)}, u32[]{:S(2)}) async-start(bf16[16,1,2,32,512]{4,3,2,1,0:T(8,128)(2,1)} %shard_map.82), calls=%async_computation | async-start | bytes 2097152 | tf_op jit(solution)/shard_map/all_to_all | solution.py:150
  30.7 21.0 %collective-permute-start.3 = (bf16[2,2,128,128]{3,2,1,0:T(8,128)(2,1)S(1)}, bf16[2,2,128,128]{3,2,1,0:T(8,128)(2,1)S(1)}, u32[]{:S(2)}, u32[]{:S(2)}) collective-permute-start(bf16[2,2,128,128]{3,2,1,0:T(8,128)(2,1)S(1)} %constant_dynamic-update-slice_fusion), channel_id=1, source_target_pairs={{2,0},{3,1},{4,2},{5,3},{6,4},{7,5},{8,6},{9,7},{10,8},{11,9},{12,... | collective-permute-start | bytes 393224 | tf_op jit(solution)/shard_map/ppermute | solution.py:13
  35.4 19.1 %collective-permute-start.1 = (bf16[2,2,128,128]{3,2,1,0:T(8,128)(2,1)S(1)}, bf16[2,2,128,128]{3,2,1,0:T(8,128)(2,1)S(1)}, u32[]{:S(2)}, u32[]{:S(2)}) collective-permute-start(bf16[2,2,128,128]{3,2,1,0:T(8,128)(2,1)S(1)} %constant_dynamic-update-slice_fusion), channel_id=1, source_target_pairs={{1,0},{2,1},{3,2},{4,3},{5,4},{6,5},{7,6},{8,7},{9,8},{10,9},{11,1... | collective-permute-start | bytes 393224 | tf_op jit(solution)/shard_map/ppermute | solution.py:13
  35.4 40.0 %collective-permute-start.2 = (bf16[2,512,512]{2,1,0:T(8,128)(2,1)}, bf16[2,512,512]{2,1,0:T(8,128)(2,1)S(1)}, u32[]{:S(2)}, u32[]{:S(2)}) collective-permute-start(bf16[2,512,512]{2,1,0:T(8,128)(2,1)} %get-tuple-element.18), channel_id=1, source_target_pairs={{2,0},{3,1},{4,2},{5,3},{6,4},{7,5},{8,6},{9,7},{10,8},{11,9},{12,... | collective-permute-start | bytes 3145736 | tf_op jit(solution)/shard_map/ppermute | solution.py:13
  36.9 49.8 %collective-permute-start = (bf16[2,512,512]{2,1,0:T(8,128)(2,1)}, bf16[2,512,512]{2,1,0:T(8,128)(2,1)}, u32[]{:S(2)}, u32[]{:S(2)}) collective-permute-start(bf16[2,512,512]{2,1,0:T(8,128)(2,1)} %get-tuple-element.19), channel_id=1, source_target_pairs={{1,0},{2,1},{3,2},{4,3},{5,4},{6,5},{7,6},{8,7},{9,8},{10,9},{11,1... | collective-permute-start | bytes 3145736 | tf_op jit(solution)/shard_map/ppermute | solution.py:13
  37.3 4.2 %copy-start.6 = (bf16[1,1,2,512,512]{4,3,2,1,0:T(8,128)(2,1)S(1)}, bf16[1,1,2,512,512]{4,3,2,1,0:T(8,128)(2,1)}, u32[]{:S(2)}) copy-start(bf16[1,1,2,512,512]{4,3,2,1,0:T(8,128)(2,1)} %get-tuple-element.17) | copy-start | bytes 3145732
  41.4 2.2 copy-start.2
  41.4 2.2 copy-start.5
  75.5 1.0 copy-start.12
  110.4 4.2 %copy-start.3 = (bf16[1024,1024]{1,0:T(8,128)(2,1)S(1)}, bf16[1024,1024]{1,0:T(8,128)(2,1)}, u32[]{:S(2)}) copy-start(bf16[1024,1024]{1,0:T(8,128)(2,1)} %convert_element_type.462) | copy-start | bytes 6291460
  110.4 4.2 %copy-start.13 = (bf16[2,512,512]{2,1,0:T(8,128)(2,1)S(1)}, bf16[2,512,512]{2,1,0:T(8,128)(2,1)}, u32[]{:S(2)}) copy-start(bf16[2,512,512]{2,1,0:T(8,128)(2,1)} %copy-done.12) | copy-start | bytes 3145732
  119.6 4.3 %copy-start.4 = (bf16[1024,1024]{1,0:T(8,128)(2,1)S(1)}, bf16[1024,1024]{1,0:T(8,128)(2,1)}, u32[]{:S(2)}) copy-start(bf16[1024,1024]{1,0:T(8,128)(2,1)} %convert_element_type.454) | copy-start | bytes 6291460
  136.9 11.9 %copy-start.11 = (s32[80]{0:T(128)S(1)}, s32[80]{0:T(128)}, u32[]{:S(2)}) copy-start(s32[80]{0:T(128)} %constant.66) | copy-start | bytes 964
  136.9 89.5 %all-to-all-start.1 = ((bf16[16,4,2,32,512]{4,3,2,1,0:T(8,128)(2,1)}), bf16[16,4,2,32,512]{4,3,2,1,0:T(8,128)(2,1)}, u32[]{:S(2)}, u32[]{:S(2)}) async-start(bf16[16,4,2,32,512]{4,3,2,1,0:T(8,128)(2,1)} %shard_map.83), calls=%async_computation.1 | async-start | bytes 8388608 | tf_op jit(solution)/shard_map/all_to_all | solution.py:161
  240.0 9.2 %copy-start.9 = (s32[2,512]{1,0:T(2,128)S(1)}, s32[2,512]{1,0:T(2,128)}, u32[]{:S(2)}) copy-start(s32[2,512]{1,0:T(2,128)} %param.13) | copy-start | bytes 12292
  240.0 26.2 %copy-start.10 = (s32[512]{0:T(512)S(1)}, s32[512]{0:T(512)}, u32[]{:S(2)}) copy-start(s32[512]{0:T(512)} %param.14) | copy-start | bytes 6148
  242.4 9.5 %collective-permute-start.5 = (f32[2,80,80]{1,0,2:T(2,128)S(1)}, f32[2,80,80]{1,0,2:T(2,128)S(1)}, u32[]{:S(2)}, u32[]{:S(2)}) collective-permute-start(f32[2,80,80]{1,0,2:T(2,128)S(1)} %bitcast.199), channel_id=1, source_target_pairs={{0,2},{1,3},{2,0},{3,1},{4,6},{5,7},{6,4},{7,5},{8,10},{9,11},{10,... | collective-permute-start | bytes 153608 | tf_op jit(solution)/shard_map/ppermute | solution.py:116
  248.7 3.2 %collective-permute-start.4 = (f32[2,80,80]{1,0,2:T(2,128)S(1)}, f32[2,80,80]{1,0,2:T(2,128)S(1)}, u32[]{:S(2)}, u32[]{:S(2)}) collective-permute-start(f32[2,80,80]{1,0,2:T(2,128)S(1)} %bitcast.200), channel_id=1, source_target_pairs={{0,1},{1,0},{2,3},{3,2},{4,5},{5,4},{6,7},{7,6},{8,9},{9,8},{10,11... | collective-permute-start | bytes 153608 | tf_op jit(solution)/shard_map/ppermute | solution.py:116
  249.2 4.5 %collective-permute-start.6 = (f32[2,80,80]{1,0,2:T(2,128)S(1)}, f32[2,80,80]{1,0,2:T(2,128)S(1)}, u32[]{:S(2)}, u32[]{:S(2)}) collective-permute-start(f32[2,80,80]{1,0,2:T(2,128)S(1)} %bitcast.201), channel_id=1, source_target_pairs={{0,3},{1,2},{2,1},{3,0},{4,7},{5,6},{6,5},{7,4},{8,11},{9,10},{10,... | collective-permute-start | bytes 153608 | tf_op jit(solution)/shard_map/ppermute | solution.py:116
  253.8 15.0 %collective-permute-start.9 = (f32[2,80,80]{1,0,2:T(2,128)S(1)}, f32[2,80,80]{1,0,2:T(2,128)S(1)}, u32[]{:S(2)}, u32[]{:S(2)}) collective-permute-start(f32[2,80,80]{1,0,2:T(2,128)S(1)} %add_add_fusion.1), channel_id=1, source_target_pairs={{0,12},{1,13},{2,14},{3,15},{4,8},{5,9},{6,10},{7,11},{8,4},{9,5},... | collective-permute-start | bytes 153608 | tf_op jit(solution)/shard_map/ppermute | solution.py:116
  265.6 8.3 %collective-permute-start.8 = (f32[2,80,80]{1,0,2:T(2,128)S(1)}, f32[2,80,80]{1,0,2:T(2,128)S(1)}, u32[]{:S(2)}, u32[]{:S(2)}) collective-permute-start(f32[2,80,80]{1,0,2:T(2,128)S(1)} %add_add_fusion.1), channel_id=1, source_target_pairs={{0,8},{1,9},{2,10},{3,11},{4,12},{5,13},{6,14},{7,15},{8,0},{9,1},... | collective-permute-start | bytes 153608 | tf_op jit(solution)/shard_map/ppermute | solution.py:116
  266.2 7.7 %collective-permute-start.7 = (f32[2,80,80]{1,0,2:T(2,128)S(1)}, f32[2,80,80]{1,0,2:T(2,128)S(1)}, u32[]{:S(2)}, u32[]{:S(2)}) collective-permute-start(f32[2,80,80]{1,0,2:T(2,128)S(1)} %add_add_fusion.1), channel_id=1, source_target_pairs={{0,4},{1,5},{2,6},{3,7},{4,0},{5,1},{6,2},{7,3},{8,12},{9,13},{10,... | collective-permute-start | bytes 153608 | tf_op jit(solution)/shard_map/ppermute | solution.py:116

commit v5 on v4

--- a/solution.py
+++ b/solution.py
@@ -23,16 +23,12 @@
 
 def dressing_matrix(elemental, order_row, phase_row):
     cosine, sine = gamma_parts(order_row, phase_row)
-    real, imag = elemental[0].astype(jnp.float32), elemental[1].astype(jnp.float32)
-    plain = jnp.stack([jnp.stack([real, -imag], 1), jnp.stack([imag, real], 1)], 0)
-    turned = jnp.stack([jnp.stack([-imag, -real], 1), jnp.stack([real, -imag], 1)], 0)
-    spins = cosine.shape[0]
-    weights = (
-        cosine[None, :, None, None, :, None] * plain[:, None, :, :, None, :]
-        + sine[None, :, None, None, :, None] * turned[:, None, :, :, None, :]
-    )
-    size = 2 * spins * real.shape[0]
-    return weights.reshape(size, size).astype(jnp.bfloat16)
+    meson = elemental.astype(jnp.float32)
+    kron_re = jnp.kron(cosine, meson[0]) - jnp.kron(sine, meson[1])
+    kron_im = jnp.kron(cosine, meson[1]) + jnp.kron(sine, meson[0])
+    top = jnp.concatenate([kron_re, -kron_im], axis=1)
+    bottom = jnp.concatenate([kron_im, kron_re], axis=1)
+    return jnp.concatenate([top, bottom], axis=0).astype(jnp.bfloat16)
 
 
 def dress(weights, tile_pair):
@@ -151,10 +147,18 @@
     forwards, partners = [], []
     own_forward = {offset: dress(source_own, tiles[half_window + offset]) for offset in received}
     own_backward = {offset: dress(sink_own, tiles[half_window + offset]) for offset in received}
-    centre_slices, received = lax.optimization_barrier((centre_slices, received))
-    for offset, (tile, partner_mesons) in received.items():
-        source_partner = dressing_matrix(partner_mesons[0], gamma_order[0], gamma_phase[0])
-        sink_partner = dressing_matrix(partner_mesons[1], gamma_order[1], gamma_phase[1])
+    partner_weights = {
+        offset: (
+            dressing_matrix(partner_mesons[0], gamma_order[0], gamma_phase[0]),
+            dressing_matrix(partner_mesons[1], gamma_order[1], gamma_phase[1]),
+        )
+        for offset, (_, partner_mesons) in received.items()
+    }
+    centre_slices, partner_tiles = lax.optimization_barrier(
+        (centre_slices, {offset: tile for offset, (tile, _) in received.items()})
+    )
+    for offset, tile in partner_tiles.items():
+        source_partner, sink_partner = partner_weights[offset]
         forwards += [own_forward[offset], dress(source_partner, tile)]
         partners += [dress(sink_partner, tile), own_backward[offset]]
     rest = rest_loops(forwards, partners, shares)

time: 281 us -> 248 us (0.88)
  local copies, waits for them, and re-layouts: 50.5 us -> 34.6 us
  waiting for transfers between devices: 126 us -> 115 us
  other arithmetic: 14.9 us -> 9.71 us
    convert_element_type x6 -> x0, local copies, waits for them, and re-layouts: 19.8 us -> none  [dressing_matrix(): return weights.reshape(size, size).astype(jnp.bfloat16)]
    convert_element_type x8 -> x2, other arithmetic: 11.8 us -> 0.04 us  [dressing_matrix(): meson = elemental.astype(jnp.float32)]
    ppermute x4, waiting for transfers between devices: 37.6 us -> 26.4 us  [shifted(): return lax.ppermute(block, axis, route)]
    unnamed x32 -> x89, local copies, waits for them, and re-layouts: 5.72 us -> 14.3 us
    another operation x12 -> x3, other arithmetic: 0.39 us -> 7.64 us  [dressing_matrix(): jnp.stack([jnp.stack([real, -imag], 1), jnp.stack([imag, real], 1)], 0)]
    another operation x13 -> x0, local copies, waits for them, and re-layouts: 4.57 us -> none  [the longest x6 2.63 us: dressing_matrix(): jnp.stack([jnp.stack([-imag, -real], 1), jnp.stack([real, -imag], 1)], 0)]
    ppermute x4, starting transfers between devices: 6.54 us -> 11 us  [shifted(): return lax.ppermute(block, axis, route)]
    all_to_all x1, starting transfers between devices: 7.39 us -> 3.87 us  [per_device(): lax.all_to_all(centre, 'src', split_axis=0, concat_axis=0, tiled=True)]
  transfers between devices with their start and end apart: 12 -> 12, of which waited for: 9 -> 7; matrix products, arithmetic and copies ran while one was open for 4% -> 11% of each run, Pallas kernels for 0% -> 0%
where the time goes in v5:
time: 248 us; the launch traced here: 247 us
  waiting for transfers between devices  115 us (46%)
  starting transfers between devices  46.6 us (19%)
  local copies, waits for them, and re-layouts  34.6 us (14%)
  matrix products  28.9 us (12%)
  Pallas kernels  11.8 us (5%)
  other arithmetic  9.71 us (4%)
    all_to_all x1, waiting for transfers between devices, per_device(): lax.all_to_all(rest, 'src', split_axis=0, concat_axis=0, tiled=True)  76.6 us
    ppermute x4, waiting for transfers between devices, shifted(): return lax.ppermute(block, axis, route)  26.4 us
    dot_general x10, matrix products, dress(): out = jnp.dot(weights, stacked, preferred_element_type=jnp.float32)  25.6 us
    ppermute x6, starting transfers between devices, all_sum(): lax.ppermute(table, axis, [(i, i ^ digit * stride) for i in range(n)])  19.9 us
    unnamed x89, local copies, waits for them, and re-layouts  14.3 us
    ppermute x6, waiting for transfers between devices, all_sum(): lax.ppermute(table, axis, [(i, i ^ digit * stride) for i in range(n)])  11.9 us
    all_to_all x1, starting transfers between devices, per_device(): lax.all_to_all(rest, 'src', split_axis=0, concat_axis=0, tiled=True)  11.8 us
    ppermute x4, starting transfers between devices, shifted(): return lax.ppermute(block, axis, route)  11 us
  transfers between devices with their start and end apart: 12, of which 7 were waited for; matrix products, arithmetic and copies ran while one was open for 11% of the time, Pallas kernels for 0%

profile of v5, /device:TPU:0, one launch (start us, length us, event | category | flops | bytes accessed | tf_op | source)
XLA Modules:
  0.0 247.1 jit_solution(10869490708008520530)
XLA Ops:
  0.0 0.9 constant_dynamic-update-slice_fusion.1
  0.9 0.9 constant_dynamic-update-slice_fusion
  1.9 6.1 %collective-permute-start.3 = (bf16[2,2,128,128]{3,2,1,0:T(8,128)(2,1)S(1)}, bf16[2,2,128,128]{3,2,1,0:T(8,128)(2,1)S(1)}, u32[]{:S(2)}, u32[]{:S(2)}) collective-permute-start(bf16[2,2,128,128]{3,2,1,0:T(8,128)(2,1)S(1)} %get-tuple-element.52), channel_id=1, source_target_pairs={{2,0},{3,1},{4,2},{5,3},{6,4},{7,5},{8,6},{9,7},{10,8},{11,9},{12,... | collective-permute-start | bytes 393224 | tf_op jit(solution)/shard_map/ppermute | solution.py:13
  7.9 0.8 fusion.73
  8.7 0.8 slice_bitcast_fusion.14
  9.5 4.6 %fusion.81 = (bf16[1,1,2,512,512]{4,3,2,1,0:T(8,128)(2,1)}, bf16[2,512,512]{2,1,0:T(8,128)(2,1)}, bf16[2,512,512]{2,1,0:T(8,128)(2,1)}, bf16[1,1,2,512,512]{4,3,2,1,0:T(8,128)(2,1)S(1)}, bf16[1,1,2,512,512]{4,3,2,1,0:T(8,128)(2,1)}) fusion(bf16[1,5,2,512,512]{4,3,2,1,0:T(8,128)(2,1)} %param.8), kind=kLoop, calls=%fused_computation.169 | loop fusion | bytes 10485760 | tf_op jit(solution)/shard_map/slice | solution.py:148
  14.3 3.2 %negate_convert_fusion = (bf16[4,128,4,128]{3,2,1,0:T(4,128)(2,1)}, bf16[4,128,4,128]{3,2,1,0:T(4,128)(2,1)}, bf16[4,128,4,128]{3,2,1,0:T(4,128)(2,1)S(1)}, bf16...) fusion(f32[128,128]{1,0:T(8,128)S(1)} %get-tuple-element.37, ...), kind=kLoop, calls=%fused_computation.51 | loop fusion | flops 7864320 | bytes 5111936 | tf_op jit(solution)/shard_map/convert.5
  17.5 0.1 copy.66
  17.6 0.1 copy.67
  17.7 3.5 %negate_convert_fusion.2 = (bf16[4,128,4,128]{3,2,1,0:T(4,128)(2,1)}, bf16[4,128,4,128]{3,2,1,0:T(4,128)(2,1)}, bf16[4,128,4,128]{3,2,1,0:T(4,128)(2,1)}, bf16[4...) fusion(f32[128,128]{1,0:T(8,128)S(1)} %get-tuple-element.78, ...), kind=kLoop, calls=%fused_computation.53 | loop fusion | flops 7864320 | bytes 5111936 | tf_op jit(solution)/shard_map/convert.17
  21.6 1.2 convolution_convert_fusion.4
  22.8 1.2 convolution_convert_fusion.5
  24.1 2.2 shard_map.82
  26.3 3.9 %all-to-all-start = ((bf16[16,1,2,32,512]{4,3,2,1,0:T(8,128)(2,1)}), bf16[16,1,2,32,512]{4,3,2,1,0:T(8,128)(2,1)S(1)}, u32[]{:S(2)}, u32[]{:S(2)}) async-start(bf16[16,1,2,32,512]{4,3,2,1,0:T(8,128)(2,1)} %shard_map.82), calls=%async_computation | async-start | bytes 2097152 | tf_op jit(solution)/shard_map/all_to_all | solution.py:146
  30.2 4.4 %collective-permute-start = (bf16[2,512,512]{2,1,0:T(8,128)(2,1)}, bf16[2,512,512]{2,1,0:T(8,128)(2,1)S(1)}, u32[]{:S(2)}, u32[]{:S(2)}) collective-permute-start(bf16[2,512,512]{2,1,0:T(8,128)(2,1)} %get-tuple-element.15), channel_id=1, source_target_pairs={{1,0},{2,1},{3,2},{4,3},{5,4},{6,5},{7,6},{8,7},{9,8},{10,9},{11,1... | collective-permute-start | bytes 3145736 | tf_op jit(solution)/shard_map/ppermute | solution.py:13
  34.6 0.6 collective-permute-start.1
  35.2 4.3 %convolution_convert_fusion = bf16[1024,512]{1,0:T(8,128)(2,1)} fusion(bf16[1024,512]{1,0:T(8,128)(2,1)} %bitcast.219, bf16[512,512]{1,0:T(8,128)(2,1)} %bitcast.230, bf16[512,512]{1,0:T(8,128)(2,1)} %bitcast.224, bf16[512,512]{1,0:T(8,128)(2,1)} %bitcast.227), kind=kOutput, calls=%fused_computation.41 | convolution fusion | flops 1082654720 | bytes 3670016 | tf_op jit(solution)/shard_map/dot_general | solution.py:37
  39.5 2.2 convolution_convert_fusion.2
  41.7 0.9 copy.53
  42.6 0.9 copy.54
  43.6 0.9 copy.55
  44.7 0.9 copy.59
  45.6 0.9 copy.60
  46.5 0.9 copy.61
  47.4 0.9 copy.62
  48.4 0.9 copy.63
  49.2 0.9 copy.64
  50.1 2.2 convolution_convert_fusion.1
  52.3 2.2 convolution_convert_fusion.3
  54.6 16.2 %collective-permute-done = bf16[2,512,512]{2,1,0:T(8,128)(2,1)S(1)} collective-permute-done((bf16[2,512,512]{2,1,0:T(8,128)(2,1)}, bf16[2,512,512]{2,1,0:T(8,128)(2,1)S(1)}, u32[]{:S(2)}, u32[]{:S(2)}) %collective-permute-start) | collective-permute-done | bytes 1048608 | tf_op jit(solution)/shard_map/ppermute | solution.py:13
  70.8 1.1 copy-done.32
  71.9 10.2 %collective-permute-done.1 = bf16[2,512,512]{2,1,0:T(8,128)(2,1)} collective-permute-done((bf16[2,512,512]{2,1,0:T(8,128)(2,1)}, bf16[2,512,512]{2,1,0:T(8,128)(2,1)}, u32[]{:S(2)}, u32[]{:S(2)}) %collective-permute-start.1) | collective-permute-done | bytes 1048608 | tf_op jit(solution)/shard_map/ppermute | solution.py:13
  82.1 4.0 %fusion.32 = bf16[1024,512]{1,0:T(8,128)(2,1)} fusion(bf16[1024,512]{1,0:T(8,128)(2,1)} %bitcast.25, bf16[512,512]{1,0:T(8,128)(2,1)} %bitcast.246, bf16[512,512]{1,0:T(8,128)(2,1)S(1)} %bitcast.243, bf16[512,512]{1,0:T(8,128)(2,1)} %bitcast.245), kind=kOutput, calls=%fused_computation.37 | convolution fusion | flops 1082654720 | bytes 3670016 | tf_op jit(solution)/shard_map/dot_general | solution.py:37
  86.1 3.5 %fusion.38 = bf16[1024,512]{1,0:T(8,128)(2,1)} fusion(bf16[1024,512]{1,0:T(8,128)(2,1)} %bitcast.25, bf16[512,512]{1,0:T(8,128)(2,1)S(1)} %bitcast.252, bf16[512,512]{1,0:T(8,128)(2,1)S(1)} %bitcast.249, bf16[512,512]{1,0:T(8,128)(2,1)S(1)} %bitcast.251), kind=kOutput, calls=%fused_computation.39 | convolution fusion | flops 1082654720 | bytes 3670016 | tf_op jit(solution)/shard_map/dot_general | solution.py:37
  89.7 2.2 fusion.35
  91.9 2.3 fusion.41
  94.2 9.6 %shard_map.83 = bf16[16,4,2,32,512]{4,3,2,1,0:T(8,128)(2,1)} custom-call(bf16[1,2,512,512]{3,2,1,0:T(8,128)(2,1)} %bitcast.267, bf16[1,2,512,512]{3,2,1,0:T(8,128)(2,1)} %bitcast.271, bf16[1,2,512,512]{3,2,1,0:T(8,128)(2,1)} %bitcast.265, bf16[1,2,512,512]{3,2,1,0:T(8,128)(2,1)} %bitcast.269, bf16[1,2,512,512]{3,2,1,0:T(8,128)(2,1)} %bitcast.270, ...), custom_call_target="tpu_custom_call" | custom-call | flops 4294967296 | bytes 12582912 | tf_op jit(solution)/shard_map/pallas_call | solution.py:87
  103.8 11.8 %all-to-all-start.1 = ((bf16[16,4,2,32,512]{4,3,2,1,0:T(8,128)(2,1)}), bf16[16,4,2,32,512]{4,3,2,1,0:T(8,128)(2,1)}, u32[]{:S(2)}, u32[]{:S(2)}) async-start(bf16[16,4,2,32,512]{4,3,2,1,0:T(8,128)(2,1)} %shard_map.83), calls=%async_computation.1 | async-start | bytes 8388608 | tf_op jit(solution)/shard_map/all_to_all | solution.py:165
  115.7 1.1 constant_dynamic-update-slice_fusion.3
  116.8 76.6 %all-to-all-done.1 = bf16[16,4,2,32,512]{4,3,2,1,0:T(8,128)(2,1)} async-done(((bf16[16,4,2,32,512]{4,3,2,1,0:T(8,128)(2,1)}), bf16[16,4,2,32,512]{4,3,2,1,0:T(8,128)(2,1)}, u32[]{:S(2)}, u32[]{:S(2)}) %all-to-all-start.1) | async-done | bytes 4194336 | tf_op jit(solution)/shard_map/all_to_all | solution.py:165
  193.3 4.7 %constant_dynamic-update-slice_fusion.2 = bf16[16,5,2,32,512]{4,3,2,1,0:T(8,128)(2,1)} fusion(bf16[16,5,2,32,512]{4,3,2,1,0:T(8,128)(2,1)} %constant_dynamic-update-slice_fusion.3, bf16[16,4,2,32,512]{4,3,2,1,0:T(8,128)(2,1)} %all-to-all-done.1), kind=kLoop, calls=%fused_computation.119 | loop fusion | bytes 8388608 | tf_op jit(solution)/shard_map/concatenate | solution.py:166
  198.1 3.0 %fusion.80 = (bf16[16,5,1,32,512]{4,3,2,1,0:T(8,128)(2,1)S(1)}, bf16[16,5,1,32,512]{4,3,2,1,0:T(8,128)(2,1)S(1)}) fusion(bf16[16,5,2,32,512]{4,3,2,1,0:T(8,128)(2,1)} %constant_dynamic-update-slice_fusion.2), kind=kLoop, calls=%fused_computation.168 | loop fusion | bytes 10485760 | tf_op jit(solution)/shard_map/slice | solution.py:169
  201.1 1.6 copy.33
  202.7 0.8 fusion.82
  203.5 1.6 copy.34
  205.2 0.8 fusion.83
  206.0 0.8 fusion.45
  206.9 0.8 fusion.44
  207.8 0.7 gather_fusion
  208.5 0.1 copy.12
  208.6 0.7 gather_fusion.1
  209.3 0.8 collective-permute-start.4
  210.1 6.2 %collective-permute-start.5 = (f32[2,80,80]{1,0,2:T(2,128)S(1)}, f32[2,80,80]{1,0,2:T(2,128)S(1)}, u32[]{:S(2)}, u32[]{:S(2)}) collective-permute-start(f32[2,80,80]{1,0,2:T(2,128)S(1)} %bitcast.256), channel_id=1, source_target_pairs={{0,2},{1,3},{2,0},{3,1},{4,6},{5,7},{6,4},{7,5},{8,10},{9,11},{10,... | collective-permute-start | bytes 153608 | tf_op jit(solution)/shard_map/ppermute | solution.py:112
  216.3 2.8 %collective-permute-done.5 = f32[2,80,80]{1,0,2:T(2,128)S(1)} collective-permute-done((f32[2,80,80]{1,0,2:T(2,128)S(1)}, f32[2,80,80]{1,0,2:T(2,128)S(1)}, u32[]{:S(2)}, u32[]{:S(2)}) %collective-permute-start.5) | collective-permute-done | bytes 51232 | tf_op jit(solution)/shard_map/ppermute | solution.py:112
  219.1 1.9 collective-permute-done.6
  221.1 12.1 %collective-permute-start.9 = (f32[2,80,80]{1,0,2:T(2,128)S(1)}, f32[2,80,80]{1,0,2:T(2,128)S(1)}, u32[]{:S(2)}, u32[]{:S(2)}) collective-permute-start(f32[2,80,80]{1,0,2:T(2,128)S(1)} %add_add_fusion.1), channel_id=1, source_target_pairs={{0,12},{1,13},{2,14},{3,15},{4,8},{5,9},{6,10},{7,11},{8,4},{9,5},... | collective-permute-start | bytes 153608 | tf_op jit(solution)/shard_map/ppermute | solution.py:112
  233.2 0.6 collective-permute-start.8
  233.8 0.2 collective-permute-start.7
  234.0 2.0 collective-permute-done.9
  236.1 5.1 %collective-permute-done.8 = f32[2,80,80]{1,0,2:T(2,128)S(1)} collective-permute-done((f32[2,80,80]{1,0,2:T(2,128)S(1)}, f32[2,80,80]{1,0,2:T(2,128)S(1)}, u32[]{:S(2)}, u32[]{:S(2)}) %collective-permute-start.8) | collective-permute-done | bytes 51232 | tf_op jit(solution)/shard_map/ppermute | solution.py:112
  241.2 1.3 copy.13
  242.5 3.7 %gather_fusion.2 = f32[512,2]{1,0:T(8,128)S(1)} fusion(f32[2,80,80]{0,2,1:T(8,128)S(1)} %copy.13, s32[512]{0:T(512)S(1)} %bitcast.196), kind=kCustom, calls=%fused_computation.2 | custom fusion | bytes 12288 | tf_op jit(solution)/shard_map/gather | solution.py:124
  246.2 0.1 multiply_bitcast_fusion
  246.3 0.7 copy.14
  (95 shorter events, 1.1 us)
Async XLA Ops:
  1.9 12.3 %collective-permute-start.3 = (bf16[2,2,128,128]{3,2,1,0:T(8,128)(2,1)S(1)}, bf16[2,2,128,128]{3,2,1,0:T(8,128)(2,1)S(1)}, u32[]{:S(2)}, u32[]{:S(2)}) collective-permute-start(bf16[2,2,128,128]{3,2,1,0:T(8,128)(2,1)S(1)} %get-tuple-element.52), channel_id=1, source_target_pairs={{2,0},{3,1},{4,2},{5,3},{6,4},{7,5},{8,6},{9,7},{10,8},{11,9},{12,... | collective-permute-start | bytes 393224 | tf_op jit(solution)/shard_map/ppermute | solution.py:13
  7.9 6.3 %collective-permute-start.2 = (bf16[2,2,128,128]{3,2,1,0:T(8,128)(2,1)S(1)}, bf16[2,2,128,128]{3,2,1,0:T(8,128)(2,1)S(1)}, u32[]{:S(2)}, u32[]{:S(2)}) collective-permute-start(bf16[2,2,128,128]{3,2,1,0:T(8,128)(2,1)S(1)} %get-tuple-element.52), channel_id=1, source_target_pairs={{1,0},{2,1},{3,2},{4,3},{5,4},{6,5},{7,6},{8,7},{9,8},{10,9},{11,1... | collective-permute-start | bytes 393224 | tf_op jit(solution)/shard_map/ppermute | solution.py:13
  17.5 4.0 %copy-start.10 = (bf16[64,8,4,128]{3,1,2,0:T(8,128)(2,1)}, bf16[64,8,4,128]{3,1,2,0:T(8,128)(2,1)S(1)}, u32[]{:S(2)}) copy-start(bf16[64,8,4,128]{3,1,2,0:T(8,128)(2,1)S(1)} %copy.65) | copy-start | bytes 1572868
  17.6 3.9 %copy-start.12 = (bf16[64,8,4,128]{3,1,2,0:T(8,128)(2,1)}, bf16[64,8,4,128]{3,1,2,0:T(8,128)(2,1)S(1)}, u32[]{:S(2)}) copy-start(bf16[64,8,4,128]{3,1,2,0:T(8,128)(2,1)S(1)} %copy.66) | copy-start | bytes 1572868
  17.7 3.9 %copy-start.14 = (bf16[64,8,4,128]{3,1,2,0:T(8,128)(2,1)}, bf16[64,8,4,128]{3,1,2,0:T(8,128)(2,1)S(1)}, u32[]{:S(2)}) copy-start(bf16[64,8,4,128]{3,1,2,0:T(8,128)(2,1)S(1)} %copy.67) | copy-start | bytes 1572868
  21.3 1.5 copy-start.16
  21.4 1.4 copy-start.18
  21.5 1.3 copy-start.20
  26.3 55.7 %all-to-all-start = ((bf16[16,1,2,32,512]{4,3,2,1,0:T(8,128)(2,1)}), bf16[16,1,2,32,512]{4,3,2,1,0:T(8,128)(2,1)S(1)}, u32[]{:S(2)}, u32[]{:S(2)}) async-start(bf16[16,1,2,32,512]{4,3,2,1,0:T(8,128)(2,1)} %shard_map.82), calls=%async_computation | async-start | bytes 2097152 | tf_op jit(solution)/shard_map/all_to_all | solution.py:146
  30.2 40.6 %collective-permute-start = (bf16[2,512,512]{2,1,0:T(8,128)(2,1)}, bf16[2,512,512]{2,1,0:T(8,128)(2,1)S(1)}, u32[]{:S(2)}, u32[]{:S(2)}) collective-permute-start(bf16[2,512,512]{2,1,0:T(8,128)(2,1)} %get-tuple-element.15), channel_id=1, source_target_pairs={{1,0},{2,1},{3,2},{4,3},{5,4},{6,5},{7,6},{8,7},{9,8},{10,9},{11,1... | collective-permute-start | bytes 3145736 | tf_op jit(solution)/shard_map/ppermute | solution.py:13
  34.6 47.5 %collective-permute-start.1 = (bf16[2,512,512]{2,1,0:T(8,128)(2,1)}, bf16[2,512,512]{2,1,0:T(8,128)(2,1)}, u32[]{:S(2)}, u32[]{:S(2)}) collective-permute-start(bf16[2,512,512]{2,1,0:T(8,128)(2,1)} %get-tuple-element.14), channel_id=1, source_target_pairs={{2,0},{3,1},{4,2},{5,3},{6,4},{7,5},{8,6},{9,7},{10,8},{11,9},{12,... | collective-permute-start | bytes 3145736 | tf_op jit(solution)/shard_map/ppermute | solution.py:13
  35.1 4.3 %copy-start.9 = (bf16[1,1,2,512,512]{4,3,2,1,0:T(8,128)(2,1)S(1)}, bf16[1,1,2,512,512]{4,3,2,1,0:T(8,128)(2,1)}, u32[]{:S(2)}) copy-start(bf16[1,1,2,512,512]{4,3,2,1,0:T(8,128)(2,1)} %get-tuple-element.13) | copy-start | bytes 3145732
  35.1 4.3 %copy-start.17 = (bf16[64,8,4,128]{3,1,2,0:T(8,128)(2,1)S(1)}, bf16[64,8,4,128]{3,1,2,0:T(8,128)(2,1)}, u32[]{:S(2)}) copy-start(bf16[64,8,4,128]{3,1,2,0:T(8,128)(2,1)} %copy-done.16) | copy-start | bytes 1572868
  35.1 4.3 %copy-start.19 = (bf16[64,8,4,128]{3,1,2,0:T(8,128)(2,1)S(1)}, bf16[64,8,4,128]{3,1,2,0:T(8,128)(2,1)}, u32[]{:S(2)}) copy-start(bf16[64,8,4,128]{3,1,2,0:T(8,128)(2,1)} %copy-done.18) | copy-start | bytes 1572868
  35.1 4.3 %copy-start.21 = (bf16[64,8,4,128]{3,1,2,0:T(8,128)(2,1)S(1)}, bf16[64,8,4,128]{3,1,2,0:T(8,128)(2,1)}, u32[]{:S(2)}) copy-start(bf16[64,8,4,128]{3,1,2,0:T(8,128)(2,1)} %copy-done.20) | copy-start | bytes 1572868
  39.5 2.3 copy-start.1
  39.5 3.1 %copy-start = (bf16[4,128,4,128]{3,2,1,0:T(4,128)(2,1)S(1)}, bf16[4,128,4,128]{3,2,1,0:T(4,128)(2,1)}, u32[]{:S(2)}) copy-start(bf16[4,128,4,128]{3,2,1,0:T(4,128)(2,1)} %get-tuple-element.18) | copy-start | bytes 1572868
  42.6 2.1 copy-start.7
  43.6 2.1 copy-start.6
  44.4 2.1 copy-start.5
  44.5 2.9 %copy-start.4 = (bf16[4,128,4,128]{3,2,1,0:T(4,128)(2,1)S(1)}, bf16[4,128,4,128]{3,2,1,0:T(4,128)(2,1)}, u32[]{:S(2)}) copy-start(bf16[4,128,4,128]{3,2,1,0:T(4,128)(2,1)} %get-tuple-element.63) | copy-start | bytes 1572868
  44.6 3.7 %copy-start.3 = (bf16[4,128,4,128]{3,2,1,0:T(4,128)(2,1)S(1)}, bf16[4,128,4,128]{3,2,1,0:T(4,128)(2,1)}, u32[]{:S(2)}) copy-start(bf16[4,128,4,128]{3,2,1,0:T(4,128)(2,1)} %get-tuple-element.64) | copy-start | bytes 1572868
  44.7 4.5 %copy-start.2 = (bf16[4,128,4,128]{3,2,1,0:T(4,128)(2,1)S(1)}, bf16[4,128,4,128]{3,2,1,0:T(4,128)(2,1)}, u32[]{:S(2)}) copy-start(bf16[4,128,4,128]{3,2,1,0:T(4,128)(2,1)} %get-tuple-element.62) | copy-start | bytes 1572868
  45.6 4.5 %copy-start.8 = (bf16[1,1,2,512,512]{4,3,2,1,0:T(8,128)(2,1)S(1)}, bf16[1,1,2,512,512]{4,3,2,1,0:T(8,128)(2,1)}, u32[]{:S(2)}) copy-start(bf16[1,1,2,512,512]{4,3,2,1,0:T(8,128)(2,1)} %get-tuple-element.17) | copy-start | bytes 3145732
  45.6 4.5 %copy-start.11 = (bf16[64,8,4,128]{3,1,2,0:T(8,128)(2,1)S(1)}, bf16[64,8,4,128]{3,1,2,0:T(8,128)(2,1)}, u32[]{:S(2)}) copy-start(bf16[64,8,4,128]{3,1,2,0:T(8,128)(2,1)} %copy-done.10) | copy-start | bytes 1572868
  45.6 4.5 %copy-start.13 = (bf16[64,8,4,128]{3,1,2,0:T(8,128)(2,1)S(1)}, bf16[64,8,4,128]{3,1,2,0:T(8,128)(2,1)}, u32[]{:S(2)}) copy-start(bf16[64,8,4,128]{3,1,2,0:T(8,128)(2,1)} %copy-done.12) | copy-start | bytes 1572868
  45.6 4.5 %copy-start.15 = (bf16[64,8,4,128]{3,1,2,0:T(8,128)(2,1)S(1)}, bf16[64,8,4,128]{3,1,2,0:T(8,128)(2,1)}, u32[]{:S(2)}) copy-start(bf16[64,8,4,128]{3,1,2,0:T(8,128)(2,1)} %copy-done.14) | copy-start | bytes 1572868
  52.3 29.7 %copy-start.22 = (bf16[64,8,4,128]{3,1,2,0:T(8,128)(2,1)S(1)}, bf16[64,8,4,128]{3,1,2,0:T(8,128)(2,1)}, u32[]{:S(2)}) copy-start(bf16[64,8,4,128]{3,1,2,0:T(8,128)(2,1)} %copy.53) | copy-start | bytes 1572868
  70.8 1.1 copy-start.32
  82.1 4.1 %copy-start.25 = (bf16[64,8,4,128]{3,1,2,0:T(8,128)(2,1)S(1)}, bf16[64,8,4,128]{3,1,2,0:T(8,128)(2,1)}, u32[]{:S(2)}) copy-start(bf16[64,8,4,128]{3,1,2,0:T(8,128)(2,1)} %copy.59) | copy-start | bytes 1572868
  82.1 4.1 %copy-start.27 = (bf16[64,8,4,128]{3,1,2,0:T(8,128)(2,1)S(1)}, bf16[64,8,4,128]{3,1,2,0:T(8,128)(2,1)}, u32[]{:S(2)}) copy-start(bf16[64,8,4,128]{3,1,2,0:T(8,128)(2,1)} %copy.60) | copy-start | bytes 1572868
  82.1 4.1 %copy-start.28 = (bf16[64,8,4,128]{3,1,2,0:T(8,128)(2,1)S(1)}, bf16[64,8,4,128]{3,1,2,0:T(8,128)(2,1)}, u32[]{:S(2)}) copy-start(bf16[64,8,4,128]{3,1,2,0:T(8,128)(2,1)} %copy.61) | copy-start | bytes 1572868
  86.1 3.5 %copy-start.33 = (bf16[2,512,512]{2,1,0:T(8,128)(2,1)S(1)}, bf16[2,512,512]{2,1,0:T(8,128)(2,1)}, u32[]{:S(2)}) copy-start(bf16[2,512,512]{2,1,0:T(8,128)(2,1)} %copy-done.32) | copy-start | bytes 3145732
  89.7 2.2 copy-start.23
  89.7 2.2 copy-start.24
  89.7 2.2 copy-start.26
  103.8 11.8 %copy-start.31 = (s32[80]{0:T(128)S(1)}, s32[80]{0:T(128)}, u32[]{:S(2)}) copy-start(s32[80]{0:T(128)} %constant.66) | copy-start | bytes 964
  103.8 89.5 %all-to-all-start.1 = ((bf16[16,4,2,32,512]{4,3,2,1,0:T(8,128)(2,1)}), bf16[16,4,2,32,512]{4,3,2,1,0:T(8,128)(2,1)}, u32[]{:S(2)}, u32[]{:S(2)}) async-start(bf16[16,4,2,32,512]{4,3,2,1,0:T(8,128)(2,1)} %shard_map.83), calls=%async_computation.1 | async-start | bytes 8388608 | tf_op jit(solution)/shard_map/all_to_all | solution.py:165
  206.9 9.4 %copy-start.29 = (s32[2,512]{1,0:T(2,128)S(1)}, s32[2,512]{1,0:T(2,128)}, u32[]{:S(2)}) copy-start(s32[2,512]{1,0:T(2,128)} %param.13) | copy-start | bytes 12292
  206.9 27.1 %copy-start.30 = (s32[512]{0:T(512)S(1)}, s32[512]{0:T(512)}, u32[]{:S(2)}) copy-start(s32[512]{0:T(512)} %param.14) | copy-start | bytes 6148
  209.3 7.0 %collective-permute-start.4 = (f32[2,80,80]{1,0,2:T(2,128)S(1)}, f32[2,80,80]{1,0,2:T(2,128)S(1)}, u32[]{:S(2)}, u32[]{:S(2)}) collective-permute-start(f32[2,80,80]{1,0,2:T(2,128)S(1)} %bitcast.255), channel_id=1, source_target_pairs={{0,1},{1,0},{2,3},{3,2},{4,5},{5,4},{6,7},{7,6},{8,9},{9,8},{10,11... | collective-permute-start | bytes 153608 | tf_op jit(solution)/shard_map/ppermute | solution.py:112
  210.1 9.0 %collective-permute-start.5 = (f32[2,80,80]{1,0,2:T(2,128)S(1)}, f32[2,80,80]{1,0,2:T(2,128)S(1)}, u32[]{:S(2)}, u32[]{:S(2)}) collective-permute-start(f32[2,80,80]{1,0,2:T(2,128)S(1)} %bitcast.256), channel_id=1, source_target_pairs={{0,2},{1,3},{2,0},{3,1},{4,6},{5,7},{6,4},{7,5},{8,10},{9,11},{10,... | collective-permute-start | bytes 153608 | tf_op jit(solution)/shard_map/ppermute | solution.py:112
  216.3 4.7 %collective-permute-start.6 = (f32[2,80,80]{1,0,2:T(2,128)S(1)}, f32[2,80,80]{1,0,2:T(2,128)S(1)}, u32[]{:S(2)}, u32[]{:S(2)}) collective-permute-start(f32[2,80,80]{1,0,2:T(2,128)S(1)} %bitcast.257), channel_id=1, source_target_pairs={{0,3},{1,2},{2,1},{3,0},{4,7},{5,6},{6,5},{7,4},{8,11},{9,10},{10,... | collective-permute-start | bytes 153608 | tf_op jit(solution)/shard_map/ppermute | solution.py:112
  221.1 15.0 %collective-permute-start.9 = (f32[2,80,80]{1,0,2:T(2,128)S(1)}, f32[2,80,80]{1,0,2:T(2,128)S(1)}, u32[]{:S(2)}, u32[]{:S(2)}) collective-permute-start(f32[2,80,80]{1,0,2:T(2,128)S(1)} %add_add_fusion.1), channel_id=1, source_target_pairs={{0,12},{1,13},{2,14},{3,15},{4,8},{5,9},{6,10},{7,11},{8,4},{9,5},... | collective-permute-start | bytes 153608 | tf_op jit(solution)/shard_map/ppermute | solution.py:112
  233.2 8.0 %collective-permute-start.8 = (f32[2,80,80]{1,0,2:T(2,128)S(1)}, f32[2,80,80]{1,0,2:T(2,128)S(1)}, u32[]{:S(2)}, u32[]{:S(2)}) collective-permute-start(f32[2,80,80]{1,0,2:T(2,128)S(1)} %add_add_fusion.1), channel_id=1, source_target_pairs={{0,8},{1,9},{2,10},{3,11},{4,12},{5,13},{6,14},{7,15},{8,0},{9,1},... | collective-permute-start | bytes 153608 | tf_op jit(solution)/shard_map/ppermute | solution.py:112
  233.8 7.4 %collective-permute-start.7 = (f32[2,80,80]{1,0,2:T(2,128)S(1)}, f32[2,80,80]{1,0,2:T(2,128)S(1)}, u32[]{:S(2)}, u32[]{:S(2)}) collective-permute-start(f32[2,80,80]{1,0,2:T(2,128)S(1)} %add_add_fusion.1), channel_id=1, source_target_pairs={{0,4},{1,5},{2,6},{3,7},{4,0},{5,1},{6,2},{7,3},{8,12},{9,13},{10,... | collective-permute-start | bytes 153608 | tf_op jit(solution)/shard_map/ppermute | solution.py:112

commit v6 on v5

--- a/solution.py
+++ b/solution.py
@@ -105,15 +105,10 @@
     n = lax.axis_size(axis)
     if n & (n - 1):
         return lax.psum(table, axis)
-    stride = 1
-    while stride < n:
-        radix = 4 if n % (stride * 4) == 0 else 2
-        received = [
-            lax.ppermute(table, axis, [(i, i ^ (digit * stride)) for i in range(n)]) for digit in range(1, radix)
-        ]
-        for part in received:
-            table = table + part
-        stride *= radix
+    bit = 1
+    while bit < n:
+        table = table + lax.ppermute(table, axis, [(i, i ^ bit) for i in range(n)])
+        bit *= 2
     return table
 
 

time: 248 us -> 247 us (level)
  waiting for transfers between devices: 115 us -> 112 us
    ppermute x6 -> x4, waiting for transfers between devices: 11.9 us -> 8.69 us  [all_sum(): table = table + lax.ppermute(table, axis, [(i, i ^ bit) for i in range(n)])]
    ppermute x6 -> x4, starting transfers between devices: 19.9 us -> 22 us  [all_sum(): table = table + lax.ppermute(table, axis, [(i, i ^ bit) for i in range(n)])]
  transfers between devices with their start and end apart: 12 -> 10, of which waited for: 7 -> 7; matrix products, arithmetic and copies ran while one was open for 11% -> 11% of each run, Pallas kernels for 0% -> 0%
where the time goes in v6:
time: 247 us; the launch traced here: 246 us
  waiting for transfers between devices  112 us (45%)
  starting transfers between devices  48.7 us (20%)
  local copies, waits for them, and re-layouts  34.6 us (14%)
  matrix products  28.8 us (12%)
  Pallas kernels  11.8 us (5%)
  other arithmetic  9.82 us (4%)
    all_to_all x1, waiting for transfers between devices, per_device(): lax.all_to_all(rest, 'src', split_axis=0, concat_axis=0, tiled=True)  76.6 us
    ppermute x4, waiting for transfers between devices, shifted(): return lax.ppermute(block, axis, route)  26.5 us
    dot_general x10, matrix products, dress(): out = jnp.dot(weights, stacked, preferred_element_type=jnp.float32)  25.5 us
    ppermute x4, starting transfers between devices, all_sum(): table = table + lax.ppermute(table, axis, [(i, i ^ bit) for i in range(n)])  22 us
    unnamed x89, local copies, waits for them, and re-layouts  14.3 us
    all_to_all x1, starting transfers between devices, per_device(): lax.all_to_all(rest, 'src', split_axis=0, concat_axis=0, tiled=True)  11.8 us
    ppermute x4, starting transfers between devices, shifted(): return lax.ppermute(block, axis, route)  11 us
    pallas_call x1, Pallas kernels, rest_loops(): pl.pallas_call(rest_loop_kernel, grid=(count,), in_specs=[whole] * (2 * c...  9.6 us
  transfers between devices with their start and end apart: 10, of which 7 were waited for; matrix products, arithmetic and copies ran while one was open for 11% of the time, Pallas kernels for 0%

profile of v6, /device:TPU:0, one launch (start us, length us, event | category | flops | bytes accessed | tf_op | source)
XLA Modules:
  0.0 246.1 jit_solution(6182320233425449627)
XLA Ops:
  0.0 0.9 constant_dynamic-update-slice_fusion.1
  0.9 0.9 constant_dynamic-update-slice_fusion
  1.9 6.1 %collective-permute-start.3 = (bf16[2,2,128,128]{3,2,1,0:T(8,128)(2,1)S(1)}, bf16[2,2,128,128]{3,2,1,0:T(8,128)(2,1)S(1)}, u32[]{:S(2)}, u32[]{:S(2)}) collective-permute-start(bf16[2,2,128,128]{3,2,1,0:T(8,128)(2,1)S(1)} %get-tuple-element.52), channel_id=1, source_target_pairs={{2,0},{3,1},{4,2},{5,3},{6,4},{7,5},{8,6},{9,7},{10,8},{11,9},{12,... | collective-permute-start | bytes 393224 | tf_op jit(solution)/shard_map/ppermute | solution.py:13
  7.9 0.8 fusion.73
  8.7 0.8 slice_bitcast_fusion.14
  9.5 4.6 %fusion.81 = (bf16[1,1,2,512,512]{4,3,2,1,0:T(8,128)(2,1)}, bf16[2,512,512]{2,1,0:T(8,128)(2,1)}, bf16[2,512,512]{2,1,0:T(8,128)(2,1)}, bf16[1,1,2,512,512]{4,3,2,1,0:T(8,128)(2,1)S(1)}, bf16[1,1,2,512,512]{4,3,2,1,0:T(8,128)(2,1)}) fusion(bf16[1,5,2,512,512]{4,3,2,1,0:T(8,128)(2,1)} %param.8), kind=kLoop, calls=%fused_computation.168 | loop fusion | bytes 10485760 | tf_op jit(solution)/shard_map/slice | solution.py:143
  14.3 3.2 %negate_convert_fusion = (bf16[4,128,4,128]{3,2,1,0:T(4,128)(2,1)}, bf16[4,128,4,128]{3,2,1,0:T(4,128)(2,1)}, bf16[4,128,4,128]{3,2,1,0:T(4,128)(2,1)S(1)}, bf16...) fusion(f32[128,128]{1,0:T(8,128)S(1)} %get-tuple-element.37, ...), kind=kLoop, calls=%fused_computation.51 | loop fusion | flops 7864320 | bytes 5111936 | tf_op jit(solution)/shard_map/convert.5
  17.7 0.1 copy.67
  17.8 3.5 %negate_convert_fusion.2 = (bf16[4,128,4,128]{3,2,1,0:T(4,128)(2,1)}, bf16[4,128,4,128]{3,2,1,0:T(4,128)(2,1)}, bf16[4,128,4,128]{3,2,1,0:T(4,128)(2,1)}, bf16[4...) fusion(f32[128,128]{1,0:T(8,128)S(1)} %get-tuple-element.78, ...), kind=kLoop, calls=%fused_computation.53 | loop fusion | flops 7864320 | bytes 5111936 | tf_op jit(solution)/shard_map/convert.17
  21.4 0.1 copy.69
  21.5 0.1 copy.70
  21.6 1.2 convolution_convert_fusion.4
  22.9 1.2 convolution_convert_fusion.5
  24.1 2.2 shard_map.82
  26.4 3.9 %all-to-all-start = ((bf16[16,1,2,32,512]{4,3,2,1,0:T(8,128)(2,1)}), bf16[16,1,2,32,512]{4,3,2,1,0:T(8,128)(2,1)S(1)}, u32[]{:S(2)}, u32[]{:S(2)}) async-start(bf16[16,1,2,32,512]{4,3,2,1,0:T(8,128)(2,1)} %shard_map.82), calls=%async_computation | async-start | bytes 2097152 | tf_op jit(solution)/shard_map/all_to_all | solution.py:141
  30.2 4.4 %collective-permute-start = (bf16[2,512,512]{2,1,0:T(8,128)(2,1)}, bf16[2,512,512]{2,1,0:T(8,128)(2,1)S(1)}, u32[]{:S(2)}, u32[]{:S(2)}) collective-permute-start(bf16[2,512,512]{2,1,0:T(8,128)(2,1)} %get-tuple-element.15), channel_id=1, source_target_pairs={{1,0},{2,1},{3,2},{4,3},{5,4},{6,5},{7,6},{8,7},{9,8},{10,9},{11,1... | collective-permute-start | bytes 3145736 | tf_op jit(solution)/shard_map/ppermute | solution.py:13
  34.6 0.6 collective-permute-start.1
  35.2 4.3 %convolution_convert_fusion = bf16[1024,512]{1,0:T(8,128)(2,1)} fusion(bf16[1024,512]{1,0:T(8,128)(2,1)} %bitcast.214, bf16[512,512]{1,0:T(8,128)(2,1)} %bitcast.225, bf16[512,512]{1,0:T(8,128)(2,1)} %bitcast.219, bf16[512,512]{1,0:T(8,128)(2,1)} %bitcast.222), kind=kOutput, calls=%fused_computation.41 | convolution fusion | flops 1082654720 | bytes 3670016 | tf_op jit(solution)/shard_map/dot_general | solution.py:37
  39.5 2.2 convolution_convert_fusion.2
  41.7 0.9 copy.53
  42.6 0.9 copy.54
  43.5 0.9 copy.55
  44.7 0.9 copy.59
  45.6 0.9 copy.60
  46.5 0.9 copy.61
  47.4 0.9 copy.62
  48.3 0.9 copy.63
  49.2 0.9 copy.64
  50.1 2.2 convolution_convert_fusion.1
  52.3 2.3 convolution_convert_fusion.3
  54.5 16.3 %collective-permute-done = bf16[2,512,512]{2,1,0:T(8,128)(2,1)S(1)} collective-permute-done((bf16[2,512,512]{2,1,0:T(8,128)(2,1)}, bf16[2,512,512]{2,1,0:T(8,128)(2,1)S(1)}, u32[]{:S(2)}, u32[]{:S(2)}) %collective-permute-start) | collective-permute-done | bytes 1048608 | tf_op jit(solution)/shard_map/ppermute | solution.py:13
  70.9 1.0 copy-done.32
  71.9 10.2 %collective-permute-done.1 = bf16[2,512,512]{2,1,0:T(8,128)(2,1)} collective-permute-done((bf16[2,512,512]{2,1,0:T(8,128)(2,1)}, bf16[2,512,512]{2,1,0:T(8,128)(2,1)}, u32[]{:S(2)}, u32[]{:S(2)}) %collective-permute-start.1) | collective-permute-done | bytes 1048608 | tf_op jit(solution)/shard_map/ppermute | solution.py:13
  82.1 4.0 %fusion.32 = bf16[1024,512]{1,0:T(8,128)(2,1)} fusion(bf16[1024,512]{1,0:T(8,128)(2,1)} %bitcast.25, bf16[512,512]{1,0:T(8,128)(2,1)} %bitcast.241, bf16[512,512]{1,0:T(8,128)(2,1)S(1)} %bitcast.238, bf16[512,512]{1,0:T(8,128)(2,1)} %bitcast.240), kind=kOutput, calls=%fused_computation.37 | convolution fusion | flops 1082654720 | bytes 3670016 | tf_op jit(solution)/shard_map/dot_general | solution.py:37
  86.2 3.5 %fusion.38 = bf16[1024,512]{1,0:T(8,128)(2,1)} fusion(bf16[1024,512]{1,0:T(8,128)(2,1)} %bitcast.25, bf16[512,512]{1,0:T(8,128)(2,1)S(1)} %bitcast.247, bf16[512,512]{1,0:T(8,128)(2,1)S(1)} %bitcast.244, bf16[512,512]{1,0:T(8,128)(2,1)S(1)} %bitcast.246), kind=kOutput, calls=%fused_computation.39 | convolution fusion | flops 1082654720 | bytes 3670016 | tf_op jit(solution)/shard_map/dot_general | solution.py:37
  89.7 2.2 fusion.35
  91.9 2.3 fusion.41
  94.2 9.6 %shard_map.83 = bf16[16,4,2,32,512]{4,3,2,1,0:T(8,128)(2,1)} custom-call(bf16[1,2,512,512]{3,2,1,0:T(8,128)(2,1)} %bitcast.255, bf16[1,2,512,512]{3,2,1,0:T(8,128)(2,1)} %bitcast.259, bf16[1,2,512,512]{3,2,1,0:T(8,128)(2,1)} %bitcast.253, bf16[1,2,512,512]{3,2,1,0:T(8,128)(2,1)} %bitcast.257, bf16[1,2,512,512]{3,2,1,0:T(8,128)(2,1)} %bitcast.258, ...), custom_call_target="tpu_custom_call" | custom-call | flops 4294967296 | bytes 12582912 | tf_op jit(solution)/shard_map/pallas_call | solution.py:87
  103.8 11.8 %all-to-all-start.1 = ((bf16[16,4,2,32,512]{4,3,2,1,0:T(8,128)(2,1)}), bf16[16,4,2,32,512]{4,3,2,1,0:T(8,128)(2,1)}, u32[]{:S(2)}, u32[]{:S(2)}) async-start(bf16[16,4,2,32,512]{4,3,2,1,0:T(8,128)(2,1)} %shard_map.83), calls=%async_computation.1 | async-start | bytes 8388608 | tf_op jit(solution)/shard_map/all_to_all | solution.py:160
  115.7 1.1 constant_dynamic-update-slice_fusion.3
  116.8 76.6 %all-to-all-done.1 = bf16[16,4,2,32,512]{4,3,2,1,0:T(8,128)(2,1)} async-done(((bf16[16,4,2,32,512]{4,3,2,1,0:T(8,128)(2,1)}), bf16[16,4,2,32,512]{4,3,2,1,0:T(8,128)(2,1)}, u32[]{:S(2)}, u32[]{:S(2)}) %all-to-all-start.1) | async-done | bytes 4194336 | tf_op jit(solution)/shard_map/all_to_all | solution.py:160
  193.4 4.8 %constant_dynamic-update-slice_fusion.2 = bf16[16,5,2,32,512]{4,3,2,1,0:T(8,128)(2,1)} fusion(bf16[16,5,2,32,512]{4,3,2,1,0:T(8,128)(2,1)} %constant_dynamic-update-slice_fusion.3, bf16[16,4,2,32,512]{4,3,2,1,0:T(8,128)(2,1)} %all-to-all-done.1), kind=kLoop, calls=%fused_computation.117 | loop fusion | bytes 8388608 | tf_op jit(solution)/shard_map/concatenate | solution.py:161
  198.2 3.0 %fusion.80 = (bf16[16,5,1,32,512]{4,3,2,1,0:T(8,128)(2,1)S(1)}, bf16[16,5,1,32,512]{4,3,2,1,0:T(8,128)(2,1)S(1)}) fusion(bf16[16,5,2,32,512]{4,3,2,1,0:T(8,128)(2,1)} %constant_dynamic-update-slice_fusion.2), kind=kLoop, calls=%fused_computation.167 | loop fusion | bytes 10485760 | tf_op jit(solution)/shard_map/slice | solution.py:164
  201.2 1.6 copy.33
  202.8 0.8 fusion.82
  203.7 1.6 copy.34
  205.3 0.8 fusion.83
  206.1 0.8 fusion.45
  207.0 0.8 fusion.44
  207.9 0.7 gather_fusion
  208.6 0.1 copy.12
  208.7 0.7 gather_fusion.1
  209.4 0.8 collective-permute-start.4
  210.2 0.9 collective-permute-done.4
  211.2 6.2 %collective-permute-start.5 = (f32[2,80,80]{1,0,2:T(2,128)S(1)}, f32[2,80,80]{1,0,2:T(2,128)S(1)}, u32[]{:S(2)}, u32[]{:S(2)}) collective-permute-start(f32[2,80,80]{1,0,2:T(2,128)S(1)} %bitcast_add_fusion), channel_id=1, source_target_pairs={{0,2},{1,3},{2,0},{3,1},{4,6},{5,7},{6,4},{7,5},{8,10},{9,11},{10,... | collective-permute-start | bytes 153608 | tf_op jit(solution)/shard_map/ppermute | solution.py:110
  217.4 3.0 %collective-permute-done.5 = f32[2,80,80]{1,0,2:T(2,128)S(1)} collective-permute-done((f32[2,80,80]{1,0,2:T(2,128)S(1)}, f32[2,80,80]{1,0,2:T(2,128)S(1)}, u32[]{:S(2)}, u32[]{:S(2)}) %collective-permute-start.5) | collective-permute-done | bytes 51232 | tf_op jit(solution)/shard_map/ppermute | solution.py:110
  220.5 11.4 %collective-permute-start.6 = (f32[2,80,80]{1,0,2:T(2,128)S(1)}, f32[2,80,80]{1,0,2:T(2,128)S(1)}, u32[]{:S(2)}, u32[]{:S(2)}) collective-permute-start(f32[2,80,80]{1,0,2:T(2,128)S(1)} %add.100), channel_id=1, source_target_pairs={{0,4},{1,5},{2,6},{3,7},{4,0},{5,1},{6,2},{7,3},{8,12},{9,13},{10,... | collective-permute-start | bytes 153608 | tf_op jit(solution)/shard_map/ppermute | solution.py:110
  231.9 2.4 collective-permute-done.6
  234.3 3.5 %collective-permute-start.7 = (f32[2,80,80]{1,0,2:T(2,128)S(1)}, f32[2,80,80]{1,0,2:T(2,128)S(1)}, u32[]{:S(2)}, u32[]{:S(2)}) collective-permute-start(f32[2,80,80]{1,0,2:T(2,128)S(1)} %add.101), channel_id=1, source_target_pairs={{0,8},{1,9},{2,10},{3,11},{4,12},{5,13},{6,14},{7,15},{8,0},{9,1},... | collective-permute-start | bytes 153608 | tf_op jit(solution)/shard_map/ppermute | solution.py:110
  237.8 2.4 collective-permute-done.7
  240.3 1.3 copy.13
  241.6 3.7 %gather_fusion.2 = f32[512,2]{1,0:T(8,128)S(1)} fusion(f32[2,80,80]{0,2,1:T(8,128)S(1)} %copy.13, s32[512]{0:T(512)S(1)} %bitcast.191), kind=kCustom, calls=%fused_computation.2 | custom fusion | bytes 12288 | tf_op jit(solution)/shard_map/gather | solution.py:119
  245.3 0.1 multiply_bitcast_fusion
  245.4 0.7 copy.14
  (93 shorter events, 1.1 us)
Async XLA Ops:
  1.9 12.3 %collective-permute-start.3 = (bf16[2,2,128,128]{3,2,1,0:T(8,128)(2,1)S(1)}, bf16[2,2,128,128]{3,2,1,0:T(8,128)(2,1)S(1)}, u32[]{:S(2)}, u32[]{:S(2)}) collective-permute-start(bf16[2,2,128,128]{3,2,1,0:T(8,128)(2,1)S(1)} %get-tuple-element.52), channel_id=1, source_target_pairs={{2,0},{3,1},{4,2},{5,3},{6,4},{7,5},{8,6},{9,7},{10,8},{11,9},{12,... | collective-permute-start | bytes 393224 | tf_op jit(solution)/shard_map/ppermute | solution.py:13
  7.9 6.3 %collective-permute-start.2 = (bf16[2,2,128,128]{3,2,1,0:T(8,128)(2,1)S(1)}, bf16[2,2,128,128]{3,2,1,0:T(8,128)(2,1)S(1)}, u32[]{:S(2)}, u32[]{:S(2)}) collective-permute-start(bf16[2,2,128,128]{3,2,1,0:T(8,128)(2,1)S(1)} %get-tuple-element.52), channel_id=1, source_target_pairs={{1,0},{2,1},{3,2},{4,3},{5,4},{6,5},{7,6},{8,7},{9,8},{10,9},{11,1... | collective-permute-start | bytes 393224 | tf_op jit(solution)/shard_map/ppermute | solution.py:13
  17.6 4.0 %copy-start.10 = (bf16[64,8,4,128]{3,1,2,0:T(8,128)(2,1)}, bf16[64,8,4,128]{3,1,2,0:T(8,128)(2,1)S(1)}, u32[]{:S(2)}) copy-start(bf16[64,8,4,128]{3,1,2,0:T(8,128)(2,1)S(1)} %copy.65) | copy-start | bytes 1572868
  17.7 3.9 %copy-start.12 = (bf16[64,8,4,128]{3,1,2,0:T(8,128)(2,1)}, bf16[64,8,4,128]{3,1,2,0:T(8,128)(2,1)S(1)}, u32[]{:S(2)}) copy-start(bf16[64,8,4,128]{3,1,2,0:T(8,128)(2,1)S(1)} %copy.66) | copy-start | bytes 1572868
  17.7 3.8 %copy-start.14 = (bf16[64,8,4,128]{3,1,2,0:T(8,128)(2,1)}, bf16[64,8,4,128]{3,1,2,0:T(8,128)(2,1)S(1)}, u32[]{:S(2)}) copy-start(bf16[64,8,4,128]{3,1,2,0:T(8,128)(2,1)S(1)} %copy.67) | copy-start | bytes 1572868
  21.4 1.5 copy-start.16
  21.5 1.4 copy-start.18
  21.6 1.3 copy-start.20
  26.4 55.7 %all-to-all-start = ((bf16[16,1,2,32,512]{4,3,2,1,0:T(8,128)(2,1)}), bf16[16,1,2,32,512]{4,3,2,1,0:T(8,128)(2,1)S(1)}, u32[]{:S(2)}, u32[]{:S(2)}) async-start(bf16[16,1,2,32,512]{4,3,2,1,0:T(8,128)(2,1)} %shard_map.82), calls=%async_computation | async-start | bytes 2097152 | tf_op jit(solution)/shard_map/all_to_all | solution.py:141
  30.2 40.6 %collective-permute-start = (bf16[2,512,512]{2,1,0:T(8,128)(2,1)}, bf16[2,512,512]{2,1,0:T(8,128)(2,1)S(1)}, u32[]{:S(2)}, u32[]{:S(2)}) collective-permute-start(bf16[2,512,512]{2,1,0:T(8,128)(2,1)} %get-tuple-element.15), channel_id=1, source_target_pairs={{1,0},{2,1},{3,2},{4,3},{5,4},{6,5},{7,6},{8,7},{9,8},{10,9},{11,1... | collective-permute-start | bytes 3145736 | tf_op jit(solution)/shard_map/ppermute | solution.py:13
  34.6 47.5 %collective-permute-start.1 = (bf16[2,512,512]{2,1,0:T(8,128)(2,1)}, bf16[2,512,512]{2,1,0:T(8,128)(2,1)}, u32[]{:S(2)}, u32[]{:S(2)}) collective-permute-start(bf16[2,512,512]{2,1,0:T(8,128)(2,1)} %get-tuple-element.14), channel_id=1, source_target_pairs={{2,0},{3,1},{4,2},{5,3},{6,4},{7,5},{8,6},{9,7},{10,8},{11,9},{12,... | collective-permute-start | bytes 3145736 | tf_op jit(solution)/shard_map/ppermute | solution.py:13
  35.2 4.3 %copy-start.9 = (bf16[1,1,2,512,512]{4,3,2,1,0:T(8,128)(2,1)S(1)}, bf16[1,1,2,512,512]{4,3,2,1,0:T(8,128)(2,1)}, u32[]{:S(2)}) copy-start(bf16[1,1,2,512,512]{4,3,2,1,0:T(8,128)(2,1)} %get-tuple-element.13) | copy-start | bytes 3145732
  35.2 4.3 %copy-start.17 = (bf16[64,8,4,128]{3,1,2,0:T(8,128)(2,1)S(1)}, bf16[64,8,4,128]{3,1,2,0:T(8,128)(2,1)}, u32[]{:S(2)}) copy-start(bf16[64,8,4,128]{3,1,2,0:T(8,128)(2,1)} %copy-done.16) | copy-start | bytes 1572868
  35.2 4.3 %copy-start.19 = (bf16[64,8,4,128]{3,1,2,0:T(8,128)(2,1)S(1)}, bf16[64,8,4,128]{3,1,2,0:T(8,128)(2,1)}, u32[]{:S(2)}) copy-start(bf16[64,8,4,128]{3,1,2,0:T(8,128)(2,1)} %copy-done.18) | copy-start | bytes 1572868
  35.2 4.3 %copy-start.21 = (bf16[64,8,4,128]{3,1,2,0:T(8,128)(2,1)S(1)}, bf16[64,8,4,128]{3,1,2,0:T(8,128)(2,1)}, u32[]{:S(2)}) copy-start(bf16[64,8,4,128]{3,1,2,0:T(8,128)(2,1)} %copy-done.20) | copy-start | bytes 1572868
  39.5 2.2 copy-start.1
  39.5 3.1 %copy-start = (bf16[4,128,4,128]{3,2,1,0:T(4,128)(2,1)S(1)}, bf16[4,128,4,128]{3,2,1,0:T(4,128)(2,1)}, u32[]{:S(2)}) copy-start(bf16[4,128,4,128]{3,2,1,0:T(4,128)(2,1)} %get-tuple-element.18) | copy-start | bytes 1572868
  42.6 2.1 copy-start.7
  43.5 2.1 copy-start.6
  44.4 2.1 copy-start.5
  44.5 2.9 %copy-start.4 = (bf16[4,128,4,128]{3,2,1,0:T(4,128)(2,1)S(1)}, bf16[4,128,4,128]{3,2,1,0:T(4,128)(2,1)}, u32[]{:S(2)}) copy-start(bf16[4,128,4,128]{3,2,1,0:T(4,128)(2,1)} %get-tuple-element.63) | copy-start | bytes 1572868
  44.6 3.7 %copy-start.3 = (bf16[4,128,4,128]{3,2,1,0:T(4,128)(2,1)S(1)}, bf16[4,128,4,128]{3,2,1,0:T(4,128)(2,1)}, u32[]{:S(2)}) copy-start(bf16[4,128,4,128]{3,2,1,0:T(4,128)(2,1)} %get-tuple-element.64) | copy-start | bytes 1572868
  44.7 4.5 %copy-start.2 = (bf16[4,128,4,128]{3,2,1,0:T(4,128)(2,1)S(1)}, bf16[4,128,4,128]{3,2,1,0:T(4,128)(2,1)}, u32[]{:S(2)}) copy-start(bf16[4,128,4,128]{3,2,1,0:T(4,128)(2,1)} %get-tuple-element.62) | copy-start | bytes 1572868
  45.6 4.5 %copy-start.8 = (bf16[1,1,2,512,512]{4,3,2,1,0:T(8,128)(2,1)S(1)}, bf16[1,1,2,512,512]{4,3,2,1,0:T(8,128)(2,1)}, u32[]{:S(2)}) copy-start(bf16[1,1,2,512,512]{4,3,2,1,0:T(8,128)(2,1)} %get-tuple-element.17) | copy-start | bytes 3145732
  45.6 4.5 %copy-start.11 = (bf16[64,8,4,128]{3,1,2,0:T(8,128)(2,1)S(1)}, bf16[64,8,4,128]{3,1,2,0:T(8,128)(2,1)}, u32[]{:S(2)}) copy-start(bf16[64,8,4,128]{3,1,2,0:T(8,128)(2,1)} %copy-done.10) | copy-start | bytes 1572868
  45.6 4.5 %copy-start.13 = (bf16[64,8,4,128]{3,1,2,0:T(8,128)(2,1)S(1)}, bf16[64,8,4,128]{3,1,2,0:T(8,128)(2,1)}, u32[]{:S(2)}) copy-start(bf16[64,8,4,128]{3,1,2,0:T(8,128)(2,1)} %copy-done.12) | copy-start | bytes 1572868
  45.6 4.5 %copy-start.15 = (bf16[64,8,4,128]{3,1,2,0:T(8,128)(2,1)S(1)}, bf16[64,8,4,128]{3,1,2,0:T(8,128)(2,1)}, u32[]{:S(2)}) copy-start(bf16[64,8,4,128]{3,1,2,0:T(8,128)(2,1)} %copy-done.14) | copy-start | bytes 1572868
  52.3 29.8 %copy-start.22 = (bf16[64,8,4,128]{3,1,2,0:T(8,128)(2,1)S(1)}, bf16[64,8,4,128]{3,1,2,0:T(8,128)(2,1)}, u32[]{:S(2)}) copy-start(bf16[64,8,4,128]{3,1,2,0:T(8,128)(2,1)} %copy.53) | copy-start | bytes 1572868
  70.8 1.1 copy-start.32
  82.1 4.1 %copy-start.25 = (bf16[64,8,4,128]{3,1,2,0:T(8,128)(2,1)S(1)}, bf16[64,8,4,128]{3,1,2,0:T(8,128)(2,1)}, u32[]{:S(2)}) copy-start(bf16[64,8,4,128]{3,1,2,0:T(8,128)(2,1)} %copy.59) | copy-start | bytes 1572868
  82.1 4.1 %copy-start.27 = (bf16[64,8,4,128]{3,1,2,0:T(8,128)(2,1)S(1)}, bf16[64,8,4,128]{3,1,2,0:T(8,128)(2,1)}, u32[]{:S(2)}) copy-start(bf16[64,8,4,128]{3,1,2,0:T(8,128)(2,1)} %copy.60) | copy-start | bytes 1572868
  82.1 4.1 %copy-start.28 = (bf16[64,8,4,128]{3,1,2,0:T(8,128)(2,1)S(1)}, bf16[64,8,4,128]{3,1,2,0:T(8,128)(2,1)}, u32[]{:S(2)}) copy-start(bf16[64,8,4,128]{3,1,2,0:T(8,128)(2,1)} %copy.61) | copy-start | bytes 1572868
  86.2 3.6 %copy-start.33 = (bf16[2,512,512]{2,1,0:T(8,128)(2,1)S(1)}, bf16[2,512,512]{2,1,0:T(8,128)(2,1)}, u32[]{:S(2)}) copy-start(bf16[2,512,512]{2,1,0:T(8,128)(2,1)} %copy-done.32) | copy-start | bytes 3145732
  89.7 2.2 copy-start.23
  89.7 2.2 copy-start.24
  89.7 2.2 copy-start.26
  103.8 11.9 %copy-start.31 = (s32[80]{0:T(128)S(1)}, s32[80]{0:T(128)}, u32[]{:S(2)}) copy-start(s32[80]{0:T(128)} %constant.66) | copy-start | bytes 964
  103.8 89.5 %all-to-all-start.1 = ((bf16[16,4,2,32,512]{4,3,2,1,0:T(8,128)(2,1)}), bf16[16,4,2,32,512]{4,3,2,1,0:T(8,128)(2,1)}, u32[]{:S(2)}, u32[]{:S(2)}) async-start(bf16[16,4,2,32,512]{4,3,2,1,0:T(8,128)(2,1)} %shard_map.83), calls=%async_computation.1 | async-start | bytes 8388608 | tf_op jit(solution)/shard_map/all_to_all | solution.py:160
  207.0 24.9 %copy-start.29 = (s32[2,512]{1,0:T(2,128)S(1)}, s32[2,512]{1,0:T(2,128)}, u32[]{:S(2)}) copy-start(s32[2,512]{1,0:T(2,128)} %param.13) | copy-start | bytes 12292
  207.0 30.8 %copy-start.30 = (s32[512]{0:T(512)S(1)}, s32[512]{0:T(512)}, u32[]{:S(2)}) copy-start(s32[512]{0:T(512)} %param.14) | copy-start | bytes 6148
  209.4 1.8 collective-permute-start.4
  211.2 9.2 %collective-permute-start.5 = (f32[2,80,80]{1,0,2:T(2,128)S(1)}, f32[2,80,80]{1,0,2:T(2,128)S(1)}, u32[]{:S(2)}, u32[]{:S(2)}) collective-permute-start(f32[2,80,80]{1,0,2:T(2,128)S(1)} %bitcast_add_fusion), channel_id=1, source_target_pairs={{0,2},{1,3},{2,0},{3,1},{4,6},{5,7},{6,4},{7,5},{8,10},{9,11},{10,... | collective-permute-start | bytes 153608 | tf_op jit(solution)/shard_map/ppermute | solution.py:110
  220.5 13.8 %collective-permute-start.6 = (f32[2,80,80]{1,0,2:T(2,128)S(1)}, f32[2,80,80]{1,0,2:T(2,128)S(1)}, u32[]{:S(2)}, u32[]{:S(2)}) collective-permute-start(f32[2,80,80]{1,0,2:T(2,128)S(1)} %add.100), channel_id=1, source_target_pairs={{0,4},{1,5},{2,6},{3,7},{4,0},{5,1},{6,2},{7,3},{8,12},{9,13},{10,... | collective-permute-start | bytes 153608 | tf_op jit(solution)/shard_map/ppermute | solution.py:110
  234.3 5.9 %collective-permute-start.7 = (f32[2,80,80]{1,0,2:T(2,128)S(1)}, f32[2,80,80]{1,0,2:T(2,128)S(1)}, u32[]{:S(2)}, u32[]{:S(2)}) collective-permute-start(f32[2,80,80]{1,0,2:T(2,128)S(1)} %add.101), channel_id=1, source_target_pairs={{0,8},{1,9},{2,10},{3,11},{4,12},{5,13},{6,14},{7,15},{8,0},{9,1},... | collective-permute-start | bytes 153608 | tf_op jit(solution)/shard_map/ppermute | solution.py:110

commit v7 on v6

--- a/solution.py
+++ b/solution.py
@@ -135,30 +135,15 @@
         )
     source_own = dressing_matrix(mesons[0], gamma_order[0], gamma_phase[0])
     sink_own = dressing_matrix(mesons[1], gamma_order[1], gamma_phase[1])
-    centre = open_loops(
-        dress(source_own, tiles[half_window])[None], dress(sink_own, tiles[half_window])[None], shares
-    )
-    centre_slices = lax.all_to_all(centre, "src", split_axis=0, concat_axis=0, tiled=True)
-    forwards, partners = [], []
-    own_forward = {offset: dress(source_own, tiles[half_window + offset]) for offset in received}
-    own_backward = {offset: dress(sink_own, tiles[half_window + offset]) for offset in received}
-    partner_weights = {
-        offset: (
-            dressing_matrix(partner_mesons[0], gamma_order[0], gamma_phase[0]),
-            dressing_matrix(partner_mesons[1], gamma_order[1], gamma_phase[1]),
-        )
-        for offset, (_, partner_mesons) in received.items()
-    }
-    centre_slices, partner_tiles = lax.optimization_barrier(
-        (centre_slices, {offset: tile for offset, (tile, _) in received.items()})
-    )
-    for offset, tile in partner_tiles.items():
-        source_partner, sink_partner = partner_weights[offset]
-        forwards += [own_forward[offset], dress(source_partner, tile)]
-        partners += [dress(sink_partner, tile), own_backward[offset]]
-    rest = rest_loops(forwards, partners, shares)
-    rest_slices = lax.all_to_all(rest, "src", split_axis=0, concat_axis=0, tiled=True)
-    slices = jnp.concatenate([centre_slices, rest_slices], axis=1)
+    forwards = [dress(source_own, tiles[half_window])]
+    partners = [dress(sink_own, tiles[half_window])]
+    for offset, (tile, partner_mesons) in received.items():
+        source_partner = dressing_matrix(partner_mesons[0], gamma_order[0], gamma_phase[0])
+        sink_partner = dressing_matrix(partner_mesons[1], gamma_order[1], gamma_phase[1])
+        forwards += [dress(source_own, tiles[half_window + offset]), dress(source_partner, tile)]
+        partners += [dress(sink_partner, tile), dress(sink_own, tiles[half_window + offset])]
+    loops = rest_loops(forwards, partners, shares)
+    slices = lax.all_to_all(loops, "src", split_axis=0, concat_axis=0, tiled=True)
     block_count = slices.shape[0] * slices.shape[1]
     real_flat = slices[:, :, 0].reshape(block_count, -1)
     imag_flat = slices[:, :, 1].reshape(block_count, -1)

time: 247 us -> 216 us (0.87)
  local copies, waits for them, and re-layouts: 34.6 us -> 18 us
  starting transfers between devices: 48.7 us -> 40.2 us
  matrix products: 28.8 us -> 25.8 us
  other arithmetic: 9.82 us -> 7.01 us
    all_to_all x2 -> x1, waiting for transfers between devices: 76.6 us -> 95.9 us  [per_device(): lax.all_to_all(loops, 'src', split_axis=0, concat_axis=0, tiled=True)]
    ppermute x4, waiting for transfers between devices: 26.5 us -> 8.67 us  [shifted(): return lax.ppermute(block, axis, route)]
    all_to_all x2 -> x1, starting transfers between devices: 15.7 us -> 6.15 us  [per_device(): lax.all_to_all(loops, 'src', split_axis=0, concat_axis=0, tiled=True)]
    unnamed x89 -> x30, local copies, waits for them, and re-layouts: 14.3 us -> 4.75 us
    concatenate x1 -> x0, local copies, waits for them, and re-layouts: 4.83 us -> none  [per_device(): slices = jnp.concatenate([centre_slices, rest_slices], axis=1)]
    slice x1 -> x0, local copies, waits for them, and re-layouts: 4.59 us -> none  [per_device(): tiles[half_window + offset]]
    ppermute x4, starting transfers between devices: 22 us -> 26.2 us  [all_sum(): table = table + lax.ppermute(table, axis, [(i, i ^ bit) for i in range(n)])]
    ppermute x4, starting transfers between devices: 11 us -> 7.86 us  [shifted(): return lax.ppermute(block, axis, route)]
  transfers between devices with their start and end apart: 10 -> 9, of which waited for: 7 -> 7; matrix products, arithmetic and copies ran while one was open for 11% -> 13% of each run, Pallas kernels for 0% -> 0%
where the time goes in v7:
time: 216 us
  waiting for transfers between devices  113 us (52%)
  starting transfers between devices  40.2 us (19%)
  matrix products  25.8 us (12%)
  local copies, waits for them, and re-layouts  18 us (8%)
  Pallas kernels  11.5 us (5%)
  other arithmetic  7.01 us (3%)
    all_to_all x1, waiting for transfers between devices, per_device(): lax.all_to_all(loops, 'src', split_axis=0, concat_axis=0, tiled=True)  95.9 us
    ppermute x4, starting transfers between devices, all_sum(): table = table + lax.ppermute(table, axis, [(i, i ^ bit) for i in range(n)])  26.2 us
    dot_general x10, matrix products, dress(): out = jnp.dot(weights, stacked, preferred_element_type=jnp.float32)  22.5 us
    pallas_call x1, Pallas kernels, rest_loops(): pl.pallas_call(rest_loop_kernel, grid=(count,), in_specs=[whole] * (2 * c...  11.5 us
    ppermute x4, waiting for transfers between devices, all_sum(): table = table + lax.ppermute(table, axis, [(i, i ^ bit) for i in range(n)])  8.69 us
    ppermute x4, waiting for transfers between devices, shifted(): return lax.ppermute(block, axis, route)  8.67 us
    ppermute x4, starting transfers between devices, shifted(): return lax.ppermute(block, axis, route)  7.86 us
    all_to_all x1, starting transfers between devices, per_device(): lax.all_to_all(loops, 'src', split_axis=0, concat_axis=0, tiled=True)  6.15 us
  transfers between devices with their start and end apart: 9, of which 7 were waited for; matrix products, arithmetic and copies ran while one was open for 13% of the time, Pallas kernels for 0%

profile of v7, /device:TPU:0, one launch (start us, length us, event | category | flops | bytes accessed | tf_op | source)
XLA Modules:
  0.0 216.2 jit_solution(4216889031401823744)
XLA Ops:
  0.0 0.9 constant_dynamic-update-slice_fusion.1
  0.9 0.9 fusion.81
  1.9 6.1 %collective-permute-start.2 = (bf16[2,2,128,128]{3,2,1,0:T(8,128)(2,1)S(1)}, bf16[2,2,128,128]{3,2,1,0:T(8,128)(2,1)S(1)}, u32[]{:S(2)}, u32[]{:S(2)}) collective-permute-start(bf16[2,2,128,128]{3,2,1,0:T(8,128)(2,1)S(1)} %get-tuple-element.47), channel_id=1, source_target_pairs={{2,0},{3,1},{4,2},{5,3},{6,4},{7,5},{8,6},{9,7},{10,8},{11,9},{12,... | collective-permute-start | bytes 393224 | tf_op jit(solution)/shard_map/ppermute | solution.py:13
  8.0 3.1 %slice_bitcast_fusion = (bf16[2,512,512]{2,1,0:T(8,128)(2,1)S(1)}, bf16[2,512,512]{2,1,0:T(8,128)(2,1)S(1)}, bf16[1,1,2,512,512]{4,3,2,1,0:T(8,128)(2,1)S(1)}, b...) fusion(bf16[1,5,2,512,512]{4,3,2,1,0:T(8,128)(2,1)} %param.8), kind=kLoop, calls=%fused_computation.66 | loop fusion | bytes 10485760 | tf_op jit(solution)/shard_map/squeeze | solution.py:133
  11.0 1.1 collective-permute-start.3
  12.2 0.7 collective-permute-start.1
  12.9 0.1 fusion.63
  13.1 2.3 %negate_convert_fusion = (bf16[4,128,4,128]{3,2,1,0:T(4,128)(2,1)S(1)}, bf16[4,128,4,128]{3,2,1,0:T(4,128)(2,1)S(1)}, bf16[4,128,4,128]{3,2,1,0:T(4,128)(2,1)S(1...) fusion(f32[128,128]{1,0:T(8,128)S(1)} %get-tuple-element.31, ...), kind=kLoop, calls=%fused_computation.51 | loop fusion | flops 7864320 | bytes 5111936 | tf_op jit(solution)/shard_map/convert.5
  15.5 0.1 copy.59
  15.6 0.1 copy.60
  15.6 0.1 copy.61
  15.7 2.2 %convolution_convert_fusion = bf16[1024,512]{1,0:T(8,128)(2,1)} fusion(bf16[1024,512]{1,0:T(8,128)(2,1)S(1)} %bitcast.214, bf16[512,512]{1,0:T(8,128)(2,1)S(1)} %bitcast.222, bf16[512,512]{1,0:T(8,128)(2,1)S(1)} %bitcast.216, bf16[512,512]{1,0:T(8,128)(2,1)S(1)} %bitcast.219), kind=kOutput, calls=%fused_computation.41 | convolution fusion | flops 1082654720 | bytes 3670016 | tf_op jit(solution)/shard_map/dot_general | solution.py:37
  18.0 2.3 %convolution_convert_fusion.1 = bf16[1024,512]{1,0:T(8,128)(2,1)} fusion(bf16[1024,512]{1,0:T(8,128)(2,1)S(1)} %bitcast.212, bf16[512,512]{1,0:T(8,128)(2,1)S(1)} %bitcast.223, bf16[512,512]{1,0:T(8,128)(2,1)S(1)} %bitcast.217, bf16[512,512]{1,0:T(8,128)(2,1)S(1)} %bitcast.220), kind=kOutput, calls=%fused_computation.42 | convolution fusion | flops 1082654720 | bytes 3670016 | tf_op jit(solution)/shard_map/dot_general | solution.py:37
  20.2 2.3 %negate_convert_fusion.3 = (bf16[4,128,4,128]{3,2,1,0:T(4,128)(2,1)S(1)}, bf16[4,128,4,128]{3,2,1,0:T(4,128)(2,1)S(1)}, bf16[4,128,4,128]{3,2,1,0:T(4,128)(2,1)S...) fusion(f32[128,128]{1,0:T(8,128)S(1)} %get-tuple-element.72, ...), kind=kLoop, calls=%fused_computation.54 | loop fusion | flops 7864320 | bytes 5111936 | tf_op jit(solution)/shard_map/convert.23
  22.6 0.1 copy.68
  22.7 0.1 copy.69
  22.7 0.1 copy.70
  22.8 2.3 %convolution_convert_fusion.3 = bf16[1024,512]{1,0:T(8,128)(2,1)} fusion(bf16[1024,512]{1,0:T(8,128)(2,1)S(1)} %bitcast.215, bf16[512,512]{1,0:T(8,128)(2,1)S(1)} %bitcast.243, bf16[512,512]{1,0:T(8,128)(2,1)S(1)} %bitcast.237, bf16[512,512]{1,0:T(8,128)(2,1)S(1)} %bitcast.240), kind=kOutput, calls=%fused_computation.44 | convolution fusion | flops 1082654720 | bytes 3670016 | tf_op jit(solution)/shard_map/dot_general | solution.py:37
  25.1 2.2 %convolution_convert_fusion.4 = bf16[1024,512]{1,0:T(8,128)(2,1)} fusion(bf16[1024,512]{1,0:T(8,128)(2,1)S(1)} %bitcast.213, bf16[512,512]{1,0:T(8,128)(2,1)S(1)} %bitcast.244, bf16[512,512]{1,0:T(8,128)(2,1)S(1)} %bitcast.238, bf16[512,512]{1,0:T(8,128)(2,1)S(1)} %bitcast.241), kind=kOutput, calls=%fused_computation.45 | convolution fusion | flops 1082654720 | bytes 3670016 | tf_op jit(solution)/shard_map/dot_general | solution.py:37
  27.3 2.2 %convolution_convert_fusion.2 = bf16[1024,512]{1,0:T(8,128)(2,1)} fusion(bf16[1024,512]{1,0:T(8,128)(2,1)S(1)} %bitcast.210, bf16[512,512]{1,0:T(8,128)(2,1)S(1)} %bitcast.224, bf16[512,512]{1,0:T(8,128)(2,1)S(1)} %bitcast.218, bf16[512,512]{1,0:T(8,128)(2,1)S(1)} %bitcast.221), kind=kOutput, calls=%fused_computation.43 | convolution fusion | flops 1082654720 | bytes 3670016 | tf_op jit(solution)/shard_map/dot_general | solution.py:37
  29.5 2.2 %convolution_convert_fusion.5 = bf16[1024,512]{1,0:T(8,128)(2,1)} fusion(bf16[1024,512]{1,0:T(8,128)(2,1)S(1)} %bitcast.211, bf16[512,512]{1,0:T(8,128)(2,1)S(1)} %bitcast.245, bf16[512,512]{1,0:T(8,128)(2,1)S(1)} %bitcast.239, bf16[512,512]{1,0:T(8,128)(2,1)S(1)} %bitcast.242), kind=kOutput, calls=%fused_computation.46 | convolution fusion | flops 1082654720 | bytes 3670016 | tf_op jit(solution)/shard_map/dot_general | solution.py:37
  31.8 0.1 copy.53
  31.8 0.1 copy.54
  31.9 0.1 copy.55
  32.0 0.1 copy.56
  32.1 0.1 copy.57
  32.2 0.1 copy.58
  32.3 0.1 copy.62
  32.4 0.1 copy.63
  32.5 0.1 copy.64
  32.5 0.1 copy.65
  32.6 0.1 copy.66
  32.7 0.1 copy.67
  32.8 3.9 %collective-permute-done.3 = bf16[2,512,512]{2,1,0:T(8,128)(2,1)S(1)} collective-permute-done((bf16[2,512,512]{2,1,0:T(8,128)(2,1)S(1)}, bf16[2,512,512]{2,1,0:T(8,128)(2,1)S(1)}, u32[]{:S(2)}, u32[]{:S(2)}) %collective-permute-start.3) | collective-permute-done | bytes 1048608 | tf_op jit(solution)/shard_map/ppermute | solution.py:13
  36.7 2.2 %fusion.32 = bf16[1024,512]{1,0:T(8,128)(2,1)} fusion(bf16[1024,512]{1,0:T(8,128)(2,1)S(1)} %bitcast.250, bf16[512,512]{1,0:T(8,128)(2,1)S(1)} %bitcast.231, bf16[512,512]{1,0:T(8,128)(2,1)S(1)} %bitcast.228, bf16[512,512]{1,0:T(8,128)(2,1)S(1)} %bitcast.229), kind=kOutput, calls=%fused_computation.37 | convolution fusion | flops 1082654720 | bytes 3670016 | tf_op jit(solution)/shard_map/dot_general | solution.py:37
  38.9 2.2 %fusion.38 = bf16[1024,512]{1,0:T(8,128)(2,1)} fusion(bf16[1024,512]{1,0:T(8,128)(2,1)S(1)} %bitcast.251, bf16[512,512]{1,0:T(8,128)(2,1)S(1)} %bitcast.236, bf16[512,512]{1,0:T(8,128)(2,1)S(1)} %bitcast.234, bf16[512,512]{1,0:T(8,128)(2,1)S(1)} %bitcast.235), kind=kOutput, calls=%fused_computation.39 | convolution fusion | flops 1082654720 | bytes 3670016 | tf_op jit(solution)/shard_map/dot_general | solution.py:37
  41.1 4.8 %collective-permute-done.1 = bf16[2,512,512]{2,1,0:T(8,128)(2,1)S(1)} collective-permute-done((bf16[2,512,512]{2,1,0:T(8,128)(2,1)S(1)}, bf16[2,512,512]{2,1,0:T(8,128)(2,1)S(1)}, u32[]{:S(2)}, u32[]{:S(2)}) %collective-permute-start.1) | collective-permute-done | bytes 1048608 | tf_op jit(solution)/shard_map/ppermute | solution.py:13
  45.9 2.2 %fusion.35 = bf16[1024,512]{1,0:T(8,128)(2,1)} fusion(bf16[1024,512]{1,0:T(8,128)(2,1)S(1)} %bitcast.248, bf16[512,512]{1,0:T(8,128)(2,1)S(1)} %bitcast.227, bf16[512,512]{1,0:T(8,128)(2,1)S(1)} %bitcast.225, bf16[512,512]{1,0:T(8,128)(2,1)S(1)} %bitcast.226), kind=kOutput, calls=%fused_computation.38 | convolution fusion | flops 1082654720 | bytes 3670016 | tf_op jit(solution)/shard_map/dot_general | solution.py:37
  48.2 2.3 %fusion.41 = bf16[1024,512]{1,0:T(8,128)(2,1)} fusion(bf16[1024,512]{1,0:T(8,128)(2,1)S(1)} %bitcast.249, bf16[512,512]{1,0:T(8,128)(2,1)S(1)} %bitcast.233, bf16[512,512]{1,0:T(8,128)(2,1)S(1)} %bitcast.230, bf16[512,512]{1,0:T(8,128)(2,1)S(1)} %bitcast.232), kind=kOutput, calls=%fused_computation.40 | convolution fusion | flops 1082654720 | bytes 3670016 | tf_op jit(solution)/shard_map/dot_general | solution.py:37
  50.5 11.5 %shard_map.82 = bf16[16,5,2,32,512]{4,3,2,1,0:T(8,128)(2,1)} custom-call(bf16[1,2,512,512]{3,2,1,0:T(8,128)(2,1)} %bitcast.257, bf16[1,2,512,512]{3,2,1,0:T(8,128)(2,1)} %bitcast.255, bf16[1,2,512,512]{3,2,1,0:T(8,128)(2,1)} %bitcast.261, bf16[1,2,512,512]{3,2,1,0:T(8,128)(2,1)} %bitcast.254, bf16[1,2,512,512]{3,2,1,0:T(8,128)(2,1)} %bitcast.259, ...), custom_call_target="tpu_custom_call" | custom-call | flops 5368709120 | bytes 15728640 | tf_op jit(solution)/shard_map/pallas_call | solution.py:87
  62.0 6.2 %all-to-all-start = ((bf16[16,5,2,32,512]{4,3,2,1,0:T(8,128)(2,1)}), bf16[16,5,2,32,512]{4,3,2,1,0:T(8,128)(2,1)}, u32[]{:S(2)}, u32[]{:S(2)}) async-start(bf16[16,5,2,32,512]{4,3,2,1,0:T(8,128)(2,1)} %shard_map.82), calls=%async_computation | async-start | bytes 10485760 | tf_op jit(solution)/shard_map/all_to_all | solution.py:146
  68.2 95.9 %all-to-all-done = bf16[16,5,2,32,512]{4,3,2,1,0:T(8,128)(2,1)} async-done(((bf16[16,5,2,32,512]{4,3,2,1,0:T(8,128)(2,1)}), bf16[16,5,2,32,512]{4,3,2,1,0:T(8,128)(2,1)}, u32[]{:S(2)}, u32[]{:S(2)}) %all-to-all-start) | async-done | bytes 5242912 | tf_op jit(solution)/shard_map/all_to_all | solution.py:146
  164.1 3.0 %fusion.80 = (bf16[16,5,1,32,512]{4,3,2,1,0:T(8,128)(2,1)S(1)}, bf16[16,5,1,32,512]{4,3,2,1,0:T(8,128)(2,1)S(1)}) fusion(bf16[16,5,2,32,512]{4,3,2,1,0:T(8,128)(2,1)} %all-to-all-done), kind=kLoop, calls=%fused_computation.165 | loop fusion | bytes 10485760 | tf_op jit(solution)/shard_map/slice | solution.py:149
  167.1 1.6 copy.33
  168.7 0.8 fusion.82
  169.6 1.6 copy.34
  171.2 0.8 fusion.83
  172.0 0.8 fusion.45
  172.9 0.8 fusion.44
  173.8 0.7 gather_fusion
  174.5 0.1 copy.12
  174.6 0.7 gather_fusion.1
  175.3 0.8 collective-permute-start.4
  176.1 0.9 collective-permute-done.4
  177.1 7.6 %collective-permute-start.5 = (f32[2,80,80]{1,0,2:T(2,128)S(1)}, f32[2,80,80]{1,0,2:T(2,128)S(1)}, u32[]{:S(2)}, u32[]{:S(2)}) collective-permute-start(f32[2,80,80]{1,0,2:T(2,128)S(1)} %bitcast_add_fusion), channel_id=1, source_target_pairs={{0,2},{1,3},{2,0},{3,1},{4,6},{5,7},{6,4},{7,5},{8,10},{9,11},{10,... | collective-permute-start | bytes 153608 | tf_op jit(solution)/shard_map/ppermute | solution.py:110
  184.7 3.0 %collective-permute-done.5 = f32[2,80,80]{1,0,2:T(2,128)S(1)} collective-permute-done((f32[2,80,80]{1,0,2:T(2,128)S(1)}, f32[2,80,80]{1,0,2:T(2,128)S(1)}, u32[]{:S(2)}, u32[]{:S(2)}) %collective-permute-start.5) | collective-permute-done | bytes 51232 | tf_op jit(solution)/shard_map/ppermute | solution.py:110
  187.8 14.2 %collective-permute-start.6 = (f32[2,80,80]{1,0,2:T(2,128)S(1)}, f32[2,80,80]{1,0,2:T(2,128)S(1)}, u32[]{:S(2)}, u32[]{:S(2)}) collective-permute-start(f32[2,80,80]{1,0,2:T(2,128)S(1)} %add.100), channel_id=1, source_target_pairs={{0,4},{1,5},{2,6},{3,7},{4,0},{5,1},{6,2},{7,3},{8,12},{9,13},{10,... | collective-permute-start | bytes 153608 | tf_op jit(solution)/shard_map/ppermute | solution.py:110
  202.0 2.4 %collective-permute-done.6 = f32[2,80,80]{1,0,2:T(2,128)S(1)} collective-permute-done((f32[2,80,80]{1,0,2:T(2,128)S(1)}, f32[2,80,80]{1,0,2:T(2,128)S(1)}, u32[]{:S(2)}, u32[]{:S(2)}) %collective-permute-start.6) | collective-permute-done | bytes 51232 | tf_op jit(solution)/shard_map/ppermute | solution.py:110
  204.4 3.5 %collective-permute-start.7 = (f32[2,80,80]{1,0,2:T(2,128)S(1)}, f32[2,80,80]{1,0,2:T(2,128)S(1)}, u32[]{:S(2)}, u32[]{:S(2)}) collective-permute-start(f32[2,80,80]{1,0,2:T(2,128)S(1)} %add.101), channel_id=1, source_target_pairs={{0,8},{1,9},{2,10},{3,11},{4,12},{5,13},{6,14},{7,15},{8,0},{9,1},... | collective-permute-start | bytes 153608 | tf_op jit(solution)/shard_map/ppermute | solution.py:110
  207.9 2.4 %collective-permute-done.7 = f32[2,80,80]{1,0,2:T(2,128)S(1)} collective-permute-done((f32[2,80,80]{1,0,2:T(2,128)S(1)}, f32[2,80,80]{1,0,2:T(2,128)S(1)}, u32[]{:S(2)}, u32[]{:S(2)}) %collective-permute-start.7) | collective-permute-done | bytes 51232 | tf_op jit(solution)/shard_map/ppermute | solution.py:110
  210.4 1.3 copy.13
  211.7 3.7 %gather_fusion.2 = f32[512,2]{1,0:T(8,128)S(1)} fusion(f32[2,80,80]{0,2,1:T(8,128)S(1)} %copy.13, s32[512]{0:T(512)S(1)} %bitcast.189), kind=kCustom, calls=%fused_computation.2 | custom fusion | bytes 12288 | tf_op jit(solution)/shard_map/gather | solution.py:119
  215.4 0.1 multiply_bitcast_fusion
  215.5 0.7 copy.14
  (30 shorter events, 0.4 us)
Async XLA Ops:
  1.9 11.0 %copy-start.2 = (s32[2,4]{1,0:T(2,128)S(1)}, s32[2,4]{1,0:T(2,128)}, u32[]{:S(2)}) copy-start(s32[2,4]{1,0:T(2,128)} %param.12) | copy-start | bytes 100
  1.9 11.0 %copy-start.3 = (s32[2,4]{1,0:T(2,128)S(1)}, s32[2,4]{1,0:T(2,128)}, u32[]{:S(2)}) copy-start(s32[2,4]{1,0:T(2,128)} %param.11) | copy-start | bytes 100
  1.9 11.1 %collective-permute-start.2 = (bf16[2,2,128,128]{3,2,1,0:T(8,128)(2,1)S(1)}, bf16[2,2,128,128]{3,2,1,0:T(8,128)(2,1)S(1)}, u32[]{:S(2)}, u32[]{:S(2)}) collective-permute-start(bf16[2,2,128,128]{3,2,1,0:T(8,128)(2,1)S(1)} %get-tuple-element.47), channel_id=1, source_target_pairs={{2,0},{3,1},{4,2},{5,3},{6,4},{7,5},{8,6},{9,7},{10,8},{11,9},{12,... | collective-permute-start | bytes 393224 | tf_op jit(solution)/shard_map/ppermute | solution.py:13
  8.0 5.1 %collective-permute-start = (bf16[2,2,128,128]{3,2,1,0:T(8,128)(2,1)S(1)}, bf16[2,2,128,128]{3,2,1,0:T(8,128)(2,1)S(1)}, u32[]{:S(2)}, u32[]{:S(2)}) collective-permute-start(bf16[2,2,128,128]{3,2,1,0:T(8,128)(2,1)S(1)} %get-tuple-element.47), channel_id=1, source_target_pairs={{1,0},{2,1},{3,2},{4,3},{5,4},{6,5},{7,6},{8,7},{9,8},{10,9},{11,1... | collective-permute-start | bytes 393224 | tf_op jit(solution)/shard_map/ppermute | solution.py:13
  11.0 25.6 %collective-permute-start.3 = (bf16[2,512,512]{2,1,0:T(8,128)(2,1)S(1)}, bf16[2,512,512]{2,1,0:T(8,128)(2,1)S(1)}, u32[]{:S(2)}, u32[]{:S(2)}) collective-permute-start(bf16[2,512,512]{2,1,0:T(8,128)(2,1)S(1)} %get-tuple-element.7), channel_id=1, source_target_pairs={{2,0},{3,1},{4,2},{5,3},{6,4},{7,5},{8,6},{9,7},{10,8},{11,9},{12,... | collective-permute-start | bytes 3145736 | tf_op jit(solution)/shard_map/ppermute | solution.py:13
  12.2 33.8 %collective-permute-start.1 = (bf16[2,512,512]{2,1,0:T(8,128)(2,1)S(1)}, bf16[2,512,512]{2,1,0:T(8,128)(2,1)S(1)}, u32[]{:S(2)}, u32[]{:S(2)}) collective-permute-start(bf16[2,512,512]{2,1,0:T(8,128)(2,1)S(1)} %get-tuple-element.8), channel_id=1, source_target_pairs={{1,0},{2,1},{3,2},{4,3},{5,4},{6,5},{7,6},{8,7},{9,8},{10,9},{11,1... | collective-permute-start | bytes 3145736 | tf_op jit(solution)/shard_map/ppermute | solution.py:13
  62.0 6.2 %copy-start.4 = (s32[80]{0:T(128)S(1)}, s32[80]{0:T(128)}, u32[]{:S(2)}) copy-start(s32[80]{0:T(128)} %constant.66) | copy-start | bytes 964
  62.0 102.1 %all-to-all-start = ((bf16[16,5,2,32,512]{4,3,2,1,0:T(8,128)(2,1)}), bf16[16,5,2,32,512]{4,3,2,1,0:T(8,128)(2,1)}, u32[]{:S(2)}, u32[]{:S(2)}) async-start(bf16[16,5,2,32,512]{4,3,2,1,0:T(8,128)(2,1)} %shard_map.82), calls=%async_computation | async-start | bytes 10485760 | tf_op jit(solution)/shard_map/all_to_all | solution.py:146
  172.9 29.1 %copy-start = (s32[2,512]{1,0:T(2,128)S(1)}, s32[2,512]{1,0:T(2,128)}, u32[]{:S(2)}) copy-start(s32[2,512]{1,0:T(2,128)} %param.13) | copy-start | bytes 12292
  172.9 35.0 %copy-start.1 = (s32[512]{0:T(512)S(1)}, s32[512]{0:T(512)}, u32[]{:S(2)}) copy-start(s32[512]{0:T(512)} %param.14) | copy-start | bytes 6148
  175.3 1.8 collective-permute-start.4
  177.1 10.6 %collective-permute-start.5 = (f32[2,80,80]{1,0,2:T(2,128)S(1)}, f32[2,80,80]{1,0,2:T(2,128)S(1)}, u32[]{:S(2)}, u32[]{:S(2)}) collective-permute-start(f32[2,80,80]{1,0,2:T(2,128)S(1)} %bitcast_add_fusion), channel_id=1, source_target_pairs={{0,2},{1,3},{2,0},{3,1},{4,6},{5,7},{6,4},{7,5},{8,10},{9,11},{10,... | collective-permute-start | bytes 153608 | tf_op jit(solution)/shard_map/ppermute | solution.py:110
  187.8 16.6 %collective-permute-start.6 = (f32[2,80,80]{1,0,2:T(2,128)S(1)}, f32[2,80,80]{1,0,2:T(2,128)S(1)}, u32[]{:S(2)}, u32[]{:S(2)}) collective-permute-start(f32[2,80,80]{1,0,2:T(2,128)S(1)} %add.100), channel_id=1, source_target_pairs={{0,4},{1,5},{2,6},{3,7},{4,0},{5,1},{6,2},{7,3},{8,12},{9,13},{10,... | collective-permute-start | bytes 153608 | tf_op jit(solution)/shard_map/ppermute | solution.py:110
  204.4 5.9 %collective-permute-start.7 = (f32[2,80,80]{1,0,2:T(2,128)S(1)}, f32[2,80,80]{1,0,2:T(2,128)S(1)}, u32[]{:S(2)}, u32[]{:S(2)}) collective-permute-start(f32[2,80,80]{1,0,2:T(2,128)S(1)} %add.101), channel_id=1, source_target_pairs={{0,8},{1,9},{2,10},{3,11},{4,12},{5,13},{6,14},{7,15},{8,0},{9,1},... | collective-permute-start | bytes 153608 | tf_op jit(solution)/shard_map/ppermute | solution.py:110

commit v8 on v7

--- a/solution.py
+++ b/solution.py
@@ -144,25 +144,34 @@
         partners += [dress(sink_partner, tile), dress(sink_own, tiles[half_window + offset])]
     loops = rest_loops(forwards, partners, shares)
     slices = lax.all_to_all(loops, "src", split_axis=0, concat_axis=0, tiled=True)
-    block_count = slices.shape[0] * slices.shape[1]
-    real_flat = slices[:, :, 0].reshape(block_count, -1)
-    imag_flat = slices[:, :, 1].reshape(block_count, -1)
+    sources, slots, _, rows, order = slices.shape
+    block_count = sources * slots
+    pieces = slices.reshape(2 * block_count, rows, order)
+    grams = lax.dot_general(pieces, pieces, (((1, 2), (1, 2)), ((), ())), preferred_element_type=jnp.float32)
+    grams = grams.reshape(block_count, 2, block_count, 2)
     trace_table = jnp.stack(
-        [
-            inner_product(real_flat, real_flat) - inner_product(imag_flat, imag_flat),
-            inner_product(real_flat, imag_flat) + inner_product(imag_flat, real_flat),
-        ]
+        [grams[:, 0, :, 0] - grams[:, 1, :, 1], grams[:, 0, :, 1] + grams[:, 1, :, 0]]
     )
-    place = np.zeros(block_count, np.int32)
-    for source in range(shares):
-        place[source * window + half_window] = source * window
+    canonical_of_row = np.zeros(block_count, np.int32)
+    for source in range(sources):
+        canonical_of_row[source * window] = source * window + half_window
         for offset in range(1, half_window + 1):
-            place[source * window + half_window + offset] = source * window + 2 * offset - 1
-            place[((source + offset) % shares) * window + half_window - offset] = source * window + 2 * offset
-    canonical = jnp.asarray(place)
-    trace_table = trace_table[:, canonical][:, :, canonical]
+            canonical_of_row[source * window + 2 * offset - 1] = source * window + half_window + offset
+            canonical_of_row[source * window + 2 * offset] = ((source + offset) % sources) * window + half_window - offset
+    row_of_canonical = jnp.asarray(np.argsort(canonical_of_row).astype(np.int32))
+    trace_table = trace_table[:, row_of_canonical][:, :, row_of_canonical]
     summed = all_sum(trace_table, "src")
     return select_diagrams(summed, diagram_blocks, diagram_codes)
+
+
+def select_rows(trace_table, canonical_of_row, block_pairs, codes):
+    signs = 1 - 2 * (codes % 2)
+    scales = 1 + codes // 2
+    weight = (signs * scales).astype(jnp.float32)
+    first = (block_pairs[0][:, None] == canonical_of_row[None, :]).astype(jnp.float32)
+    second = (block_pairs[1][:, None] == canonical_of_row[None, :]).astype(jnp.float32)
+    picked = jnp.einsum("dp,cpq->cdq", first, trace_table, precision=lax.Precision.HIGHEST)
+    return jnp.sum(picked * second[None], axis=-1) * weight[None, :]
 
 
 def solution(mesh):

time: 216 us -> 228 us (1.056)
  matrix products: 25.8 us -> 43.6 us
  local copies, waits for them, and re-layouts: 18 us -> 11.8 us
    dot_general x4 -> x1, matrix products: 3.31 us -> 21.2 us  [per_device(): lax.dot_general(pieces, pieces, (((1, 2), (1, 2)), ((), ())), preferred_e...]
    unnamed x30 -> x28, local copies, waits for them, and re-layouts: 4.75 us -> 1.45 us
    slice x1 -> x0, local copies, waits for them, and re-layouts: 2.99 us -> none  [per_device(): imag_flat = slices[:, :, 1].reshape(block_count, -1)]
  transfers between devices with their start and end apart: 9 -> 9, of which waited for: 7 -> 7; matrix products, arithmetic and copies ran while one was open for 13% -> 12% of each run, Pallas kernels for 0% -> 0%
where the time goes in v8:
time: 228 us
  waiting for transfers between devices  113 us (50%)
  matrix products  43.6 us (19%)
  starting transfers between devices  40.2 us (18%)
  local copies, waits for them, and re-layouts  11.8 us (5%)
  Pallas kernels  11.5 us (5%)
  other arithmetic  7.02 us (3%)
    all_to_all x1, waiting for transfers between devices, per_device(): lax.all_to_all(loops, 'src', split_axis=0, concat_axis=0, tiled=True)  95.9 us
    ppermute x4, starting transfers between devices, all_sum(): table = table + lax.ppermute(table, axis, [(i, i ^ bit) for i in range(n)])  26.2 us
    dot_general x10, matrix products, dress(): out = jnp.dot(weights, stacked, preferred_element_type=jnp.float32)  22.5 us
    dot_general x1, matrix products, per_device(): lax.dot_general(pieces, pieces, (((1, 2), (1, 2)), ((), ())), preferred_e...  21.2 us
    pallas_call x1, Pallas kernels, rest_loops(): pl.pallas_call(rest_loop_kernel, grid=(count,), in_specs=[whole] * (2 * c...  11.5 us
    ppermute x4, waiting for transfers between devices, all_sum(): table = table + lax.ppermute(table, axis, [(i, i ^ bit) for i in range(n)])  8.69 us
    ppermute x4, waiting for transfers between devices, shifted(): return lax.ppermute(block, axis, route)  8.67 us
    ppermute x4, starting transfers between devices, shifted(): return lax.ppermute(block, axis, route)  7.86 us
  transfers between devices with their start and end apart: 9, of which 7 were waited for; matrix products, arithmetic and copies ran while one was open for 12% of the time, Pallas kernels for 0%

profile of v8, /device:TPU:0, one launch (start us, length us, event | category | flops | bytes accessed | tf_op | source)
XLA Modules:
  0.0 227.8 jit_solution(7472011172968016476)
XLA Ops:
  0.0 0.9 constant_dynamic-update-slice_fusion.1
  0.9 0.9 fusion.89
  1.9 0.0 copy-start.2
  1.9 0.0 copy-start.3
  1.9 6.1 %collective-permute-start.2 = (bf16[2,2,128,128]{3,2,1,0:T(8,128)(2,1)S(1)}, bf16[2,2,128,128]{3,2,1,0:T(8,128)(2,1)S(1)}, u32[]{:S(2)}, u32[]{:S(2)}) collective-permute-start(bf16[2,2,128,128]{3,2,1,0:T(8,128)(2,1)S(1)} %get-tuple-element.47), channel_id=1, source_target_pairs={{2,0},{3,1},{4,2},{5,3},{6,4},{7,5},{8,6},{9,7},{10,8},{11,9},{12,... | collective-permute-start | bytes 393224 | tf_op jit(solution)/shard_map/ppermute | solution.py:13
  8.0 0.0 collective-permute-start
  8.0 3.1 %slice_bitcast_fusion = (bf16[2,512,512]{2,1,0:T(8,128)(2,1)S(1)}, bf16[2,512,512]{2,1,0:T(8,128)(2,1)S(1)}, bf16[1,1,2,512,512]{4,3,2,1,0:T(8,128)(2,1)S(1)}, b...) fusion(bf16[1,5,2,512,512]{4,3,2,1,0:T(8,128)(2,1)} %param.8), kind=kLoop, calls=%fused_computation.67 | loop fusion | bytes 10485760 | tf_op jit(solution)/shard_map/squeeze | solution.py:133
  11.0 1.1 collective-permute-start.3
  12.2 0.7 collective-permute-start.1
  12.8 0.0 copy-done.2
  12.9 0.1 fusion.72
  13.0 0.0 collective-permute-done.2
  13.0 0.0 collective-permute-done
  13.1 2.3 %negate_convert_fusion = (bf16[4,128,4,128]{3,2,1,0:T(4,128)(2,1)S(1)}, bf16[4,128,4,128]{3,2,1,0:T(4,128)(2,1)S(1)}, bf16[4,128,4,128]{3,2,1,0:T(4,128)(2,1)S(1...) fusion(f32[128,128]{1,0:T(8,128)S(1)} %get-tuple-element.31, ...), kind=kLoop, calls=%fused_computation.52 | loop fusion | flops 7864320 | bytes 5111936 | tf_op jit(solution)/shard_map/convert.5
  15.5 0.1 copy.75
  15.6 0.1 copy.76
  15.6 0.1 copy.77
  15.7 2.2 convolution_convert_fusion
  18.0 2.3 convolution_convert_fusion.1
  20.2 2.3 %negate_convert_fusion.3 = (bf16[4,128,4,128]{3,2,1,0:T(4,128)(2,1)S(1)}, bf16[4,128,4,128]{3,2,1,0:T(4,128)(2,1)S(1)}, bf16[4,128,4,128]{3,2,1,0:T(4,128)(2,1)S...) fusion(f32[128,128]{1,0:T(8,128)S(1)} %get-tuple-element.72, ...), kind=kLoop, calls=%fused_computation.55 | loop fusion | flops 7864320 | bytes 5111936 | tf_op jit(solution)/shard_map/convert.23
  22.6 0.1 copy.84
  22.7 0.1 copy.85
  22.7 0.1 copy.86
  22.8 2.3 %convolution_convert_fusion.3 = bf16[1024,512]{1,0:T(8,128)(2,1)} fusion(bf16[1024,512]{1,0:T(8,128)(2,1)S(1)} %bitcast.204, bf16[512,512]{1,0:T(8,128)(2,1)S(1)} %bitcast.232, bf16[512,512]{1,0:T(8,128)(2,1)S(1)} %bitcast.226, bf16[512,512]{1,0:T(8,128)(2,1)S(1)} %bitcast.229), kind=kOutput, calls=%fused_computation.48 | convolution fusion | flops 1082654720 | bytes 3670016 | tf_op jit(solution)/shard_map/dot_general | solution.py:37
  25.1 2.2 convolution_convert_fusion.4
  27.3 2.2 convolution_convert_fusion.2
  29.5 2.2 convolution_convert_fusion.5
  31.8 0.1 copy.69
  31.8 0.1 copy.70
  31.9 0.1 copy.71
  32.0 0.1 copy.72
  32.1 0.1 copy.73
  32.2 0.1 copy.74
  32.3 0.1 copy.78
  32.4 0.1 copy.79
  32.5 0.1 copy.80
  32.5 0.1 copy.81
  32.6 0.1 copy.82
  32.7 0.1 copy.83
  32.8 3.9 %collective-permute-done.3 = bf16[2,512,512]{2,1,0:T(8,128)(2,1)S(1)} collective-permute-done((bf16[2,512,512]{2,1,0:T(8,128)(2,1)S(1)}, bf16[2,512,512]{2,1,0:T(8,128)(2,1)S(1)}, u32[]{:S(2)}, u32[]{:S(2)}) %collective-permute-start.3) | collective-permute-done | bytes 1048608 | tf_op jit(solution)/shard_map/ppermute | solution.py:13
  36.7 2.2 fusion.36
  38.9 2.2 fusion.42
  41.1 4.8 %collective-permute-done.1 = bf16[2,512,512]{2,1,0:T(8,128)(2,1)S(1)} collective-permute-done((bf16[2,512,512]{2,1,0:T(8,128)(2,1)S(1)}, bf16[2,512,512]{2,1,0:T(8,128)(2,1)S(1)}, u32[]{:S(2)}, u32[]{:S(2)}) %collective-permute-start.1) | collective-permute-done | bytes 1048608 | tf_op jit(solution)/shard_map/ppermute | solution.py:13
  45.9 2.2 fusion.39
  48.2 2.3 %fusion.45 = bf16[1024,512]{1,0:T(8,128)(2,1)} fusion(bf16[1024,512]{1,0:T(8,128)(2,1)S(1)} %bitcast.238, bf16[512,512]{1,0:T(8,128)(2,1)S(1)} %bitcast.222, bf16[512,512]{1,0:T(8,128)(2,1)S(1)} %bitcast.219, bf16[512,512]{1,0:T(8,128)(2,1)S(1)} %bitcast.221), kind=kOutput, calls=%fused_computation.44 | convolution fusion | flops 1082654720 | bytes 3670016 | tf_op jit(solution)/shard_map/dot_general | solution.py:37
  50.5 11.5 %shard_map.82 = bf16[16,5,2,32,512]{4,3,2,1,0:T(8,128)(2,1)} custom-call(bf16[1,2,512,512]{3,2,1,0:T(8,128)(2,1)} %bitcast.246, bf16[1,2,512,512]{3,2,1,0:T(8,128)(2,1)} %bitcast.244, bf16[1,2,512,512]{3,2,1,0:T(8,128)(2,1)} %bitcast.250, bf16[1,2,512,512]{3,2,1,0:T(8,128)(2,1)} %bitcast.243, bf16[1,2,512,512]{3,2,1,0:T(8,128)(2,1)} %bitcast.248, ...), custom_call_target="tpu_custom_call" | custom-call | flops 5368709120 | bytes 15728640 | tf_op jit(solution)/shard_map/pallas_call | solution.py:87
  62.0 6.2 %all-to-all-start = ((bf16[16,5,2,32,512]{4,3,2,1,0:T(8,128)(2,1)}), bf16[16,5,2,32,512]{4,3,2,1,0:T(8,128)(2,1)}, u32[]{:S(2)}, u32[]{:S(2)}) async-start(bf16[16,5,2,32,512]{4,3,2,1,0:T(8,128)(2,1)} %shard_map.82), calls=%async_computation | async-start | bytes 10485760 | tf_op jit(solution)/shard_map/all_to_all | solution.py:146
  68.2 95.9 %all-to-all-done = bf16[16,5,2,32,512]{4,3,2,1,0:T(8,128)(2,1)} async-done(((bf16[16,5,2,32,512]{4,3,2,1,0:T(8,128)(2,1)}), bf16[16,5,2,32,512]{4,3,2,1,0:T(8,128)(2,1)}, u32[]{:S(2)}, u32[]{:S(2)}) %all-to-all-start) | async-done | bytes 5242912 | tf_op jit(solution)/shard_map/all_to_all | solution.py:146
  164.1 21.2 %fusion.48 = f32[80,2,80,2]{2,0,3,1:T(8,128)S(1)} fusion(bf16[80,2,32,512]{3,2,1,0:T(8,128)(2,1)} %bitcast.35, bf16[80,2,32,512,1]{3,2,1,0,4:T(8,128)(2,1)} %bitcast.36), kind=kOutput, calls=%fused_computation.51 | convolution fusion | flops 838860800 | bytes 10588160 | tf_op jit(solution)/shard_map/dot_general | solution.py:150
  185.4 0.7 gather_fusion
  186.0 0.1 copy.16
  186.2 0.7 gather_fusion.1
  186.8 0.8 collective-permute-start.4
  187.7 0.9 collective-permute-done.4
  188.6 7.7 %collective-permute-start.5 = (f32[2,80,80]{1,0,2:T(2,128)S(1)}, f32[2,80,80]{1,0,2:T(2,128)S(1)}, u32[]{:S(2)}, u32[]{:S(2)}) collective-permute-start(f32[2,80,80]{1,0,2:T(2,128)S(1)} %bitcast_add_fusion), channel_id=1, source_target_pairs={{0,2},{1,3},{2,0},{3,1},{4,6},{5,7},{6,4},{7,5},{8,10},{9,11},{10,... | collective-permute-start | bytes 153608 | tf_op jit(solution)/shard_map/ppermute | solution.py:110
  196.3 3.0 %collective-permute-done.5 = f32[2,80,80]{1,0,2:T(2,128)S(1)} collective-permute-done((f32[2,80,80]{1,0,2:T(2,128)S(1)}, f32[2,80,80]{1,0,2:T(2,128)S(1)}, u32[]{:S(2)}, u32[]{:S(2)}) %collective-permute-start.5) | collective-permute-done | bytes 51232 | tf_op jit(solution)/shard_map/ppermute | solution.py:110
  199.3 14.2 %collective-permute-start.6 = (f32[2,80,80]{1,0,2:T(2,128)S(1)}, f32[2,80,80]{1,0,2:T(2,128)S(1)}, u32[]{:S(2)}, u32[]{:S(2)}) collective-permute-start(f32[2,80,80]{1,0,2:T(2,128)S(1)} %add.111), channel_id=1, source_target_pairs={{0,4},{1,5},{2,6},{3,7},{4,0},{5,1},{6,2},{7,3},{8,12},{9,13},{10,... | collective-permute-start | bytes 153608 | tf_op jit(solution)/shard_map/ppermute | solution.py:110
  213.5 2.4 %collective-permute-done.6 = f32[2,80,80]{1,0,2:T(2,128)S(1)} collective-permute-done((f32[2,80,80]{1,0,2:T(2,128)S(1)}, f32[2,80,80]{1,0,2:T(2,128)S(1)}, u32[]{:S(2)}, u32[]{:S(2)}) %collective-permute-start.6) | collective-permute-done | bytes 51232 | tf_op jit(solution)/shard_map/ppermute | solution.py:110
  216.0 3.5 %collective-permute-start.7 = (f32[2,80,80]{1,0,2:T(2,128)S(1)}, f32[2,80,80]{1,0,2:T(2,128)S(1)}, u32[]{:S(2)}, u32[]{:S(2)}) collective-permute-start(f32[2,80,80]{1,0,2:T(2,128)S(1)} %add.112), channel_id=1, source_target_pairs={{0,8},{1,9},{2,10},{3,11},{4,12},{5,13},{6,14},{7,15},{8,0},{9,1},... | collective-permute-start | bytes 153608 | tf_op jit(solution)/shard_map/ppermute | solution.py:110
  219.5 2.4 %collective-permute-done.7 = f32[2,80,80]{1,0,2:T(2,128)S(1)} collective-permute-done((f32[2,80,80]{1,0,2:T(2,128)S(1)}, f32[2,80,80]{1,0,2:T(2,128)S(1)}, u32[]{:S(2)}, u32[]{:S(2)}) %collective-permute-start.7) | collective-permute-done | bytes 51232 | tf_op jit(solution)/shard_map/ppermute | solution.py:110
  221.9 1.3 copy.17
  223.2 3.7 %gather_fusion.2 = f32[512,2]{1,0:T(8,128)S(1)} fusion(f32[2,80,80]{0,2,1:T(8,128)S(1)} %copy.17, s32[512]{0:T(512)S(1)} %bitcast.180), kind=kCustom, calls=%fused_computation.2 | custom fusion | bytes 12288 | tf_op jit(solution)/shard_map/gather | solution.py:119
  226.9 0.1 multiply_bitcast_fusion
  227.1 0.7 copy.18
  (25 shorter events, 0.4 us)
Async XLA Ops:
  1.9 11.0 %copy-start.2 = (s32[2,4]{1,0:T(2,128)S(1)}, s32[2,4]{1,0:T(2,128)}, u32[]{:S(2)}) copy-start(s32[2,4]{1,0:T(2,128)} %param.12) | copy-start | bytes 100
  1.9 11.0 %copy-start.3 = (s32[2,4]{1,0:T(2,128)S(1)}, s32[2,4]{1,0:T(2,128)}, u32[]{:S(2)}) copy-start(s32[2,4]{1,0:T(2,128)} %param.11) | copy-start | bytes 100
  1.9 11.1 %collective-permute-start.2 = (bf16[2,2,128,128]{3,2,1,0:T(8,128)(2,1)S(1)}, bf16[2,2,128,128]{3,2,1,0:T(8,128)(2,1)S(1)}, u32[]{:S(2)}, u32[]{:S(2)}) collective-permute-start(bf16[2,2,128,128]{3,2,1,0:T(8,128)(2,1)S(1)} %get-tuple-element.47), channel_id=1, source_target_pairs={{2,0},{3,1},{4,2},{5,3},{6,4},{7,5},{8,6},{9,7},{10,8},{11,9},{12,... | collective-permute-start | bytes 393224 | tf_op jit(solution)/shard_map/ppermute | solution.py:13
  8.0 5.1 %collective-permute-start = (bf16[2,2,128,128]{3,2,1,0:T(8,128)(2,1)S(1)}, bf16[2,2,128,128]{3,2,1,0:T(8,128)(2,1)S(1)}, u32[]{:S(2)}, u32[]{:S(2)}) collective-permute-start(bf16[2,2,128,128]{3,2,1,0:T(8,128)(2,1)S(1)} %get-tuple-element.47), channel_id=1, source_target_pairs={{1,0},{2,1},{3,2},{4,3},{5,4},{6,5},{7,6},{8,7},{9,8},{10,9},{11,1... | collective-permute-start | bytes 393224 | tf_op jit(solution)/shard_map/ppermute | solution.py:13
  11.0 25.6 %collective-permute-start.3 = (bf16[2,512,512]{2,1,0:T(8,128)(2,1)S(1)}, bf16[2,512,512]{2,1,0:T(8,128)(2,1)S(1)}, u32[]{:S(2)}, u32[]{:S(2)}) collective-permute-start(bf16[2,512,512]{2,1,0:T(8,128)(2,1)S(1)} %get-tuple-element.5), channel_id=1, source_target_pairs={{2,0},{3,1},{4,2},{5,3},{6,4},{7,5},{8,6},{9,7},{10,8},{11,9},{12,... | collective-permute-start | bytes 3145736 | tf_op jit(solution)/shard_map/ppermute | solution.py:13
  12.2 33.8 %collective-permute-start.1 = (bf16[2,512,512]{2,1,0:T(8,128)(2,1)S(1)}, bf16[2,512,512]{2,1,0:T(8,128)(2,1)S(1)}, u32[]{:S(2)}, u32[]{:S(2)}) collective-permute-start(bf16[2,512,512]{2,1,0:T(8,128)(2,1)S(1)} %get-tuple-element.6), channel_id=1, source_target_pairs={{1,0},{2,1},{3,2},{4,3},{5,4},{6,5},{7,6},{8,7},{9,8},{10,9},{11,1... | collective-permute-start | bytes 3145736 | tf_op jit(solution)/shard_map/ppermute | solution.py:13
  62.0 6.2 %copy-start.4 = (s32[80]{0:T(128)S(1)}, s32[80]{0:T(128)}, u32[]{:S(2)}) copy-start(s32[80]{0:T(128)} %constant.66) | copy-start | bytes 964
  62.0 102.1 %all-to-all-start = ((bf16[16,5,2,32,512]{4,3,2,1,0:T(8,128)(2,1)}), bf16[16,5,2,32,512]{4,3,2,1,0:T(8,128)(2,1)}, u32[]{:S(2)}, u32[]{:S(2)}) async-start(bf16[16,5,2,32,512]{4,3,2,1,0:T(8,128)(2,1)} %shard_map.82), calls=%async_computation | async-start | bytes 10485760 | tf_op jit(solution)/shard_map/all_to_all | solution.py:146
  164.1 49.4 %copy-start = (s32[2,512]{1,0:T(2,128)S(1)}, s32[2,512]{1,0:T(2,128)}, u32[]{:S(2)}) copy-start(s32[2,512]{1,0:T(2,128)} %param.13) | copy-start | bytes 12292
  164.1 55.4 %copy-start.1 = (s32[512]{0:T(512)S(1)}, s32[512]{0:T(512)}, u32[]{:S(2)}) copy-start(s32[512]{0:T(512)} %param.14) | copy-start | bytes 6148
  186.8 1.8 collective-permute-start.4
  188.6 10.6 %collective-permute-start.5 = (f32[2,80,80]{1,0,2:T(2,128)S(1)}, f32[2,80,80]{1,0,2:T(2,128)S(1)}, u32[]{:S(2)}, u32[]{:S(2)}) collective-permute-start(f32[2,80,80]{1,0,2:T(2,128)S(1)} %bitcast_add_fusion), channel_id=1, source_target_pairs={{0,2},{1,3},{2,0},{3,1},{4,6},{5,7},{6,4},{7,5},{8,10},{9,11},{10,... | collective-permute-start | bytes 153608 | tf_op jit(solution)/shard_map/ppermute | solution.py:110
  199.3 16.6 %collective-permute-start.6 = (f32[2,80,80]{1,0,2:T(2,128)S(1)}, f32[2,80,80]{1,0,2:T(2,128)S(1)}, u32[]{:S(2)}, u32[]{:S(2)}) collective-permute-start(f32[2,80,80]{1,0,2:T(2,128)S(1)} %add.111), channel_id=1, source_target_pairs={{0,4},{1,5},{2,6},{3,7},{4,0},{5,1},{6,2},{7,3},{8,12},{9,13},{10,... | collective-permute-start | bytes 153608 | tf_op jit(solution)/shard_map/ppermute | solution.py:110
  216.0 5.9 %collective-permute-start.7 = (f32[2,80,80]{1,0,2:T(2,128)S(1)}, f32[2,80,80]{1,0,2:T(2,128)S(1)}, u32[]{:S(2)}, u32[]{:S(2)}) collective-permute-start(f32[2,80,80]{1,0,2:T(2,128)S(1)} %add.112), channel_id=1, source_target_pairs={{0,8},{1,9},{2,10},{3,11},{4,12},{5,13},{6,14},{7,15},{8,0},{9,1},... | collective-permute-start | bytes 153608 | tf_op jit(solution)/shard_map/ppermute | solution.py:110

commit v9 on v7

--- a/solution.py
+++ b/solution.py
@@ -116,7 +116,11 @@
     signs = 1 - 2 * (codes % 2)
     scales = 1 + codes // 2
     weight = (signs * scales).astype(jnp.float32)
-    return trace_table[:, block_pairs[0], block_pairs[1]] * weight[None, :]
+    blocks = jnp.arange(trace_table.shape[1], dtype=jnp.int32)
+    first = (block_pairs[0][:, None] == blocks[None, :]).astype(jnp.float32)
+    second = (block_pairs[1][:, None] == blocks[None, :]).astype(jnp.float32)
+    picked = jnp.einsum("dp,cpq->cdq", first, trace_table, precision=lax.Precision.HIGHEST)
+    return jnp.sum(picked * second[None], axis=-1) * weight[None, :]
 
 
 def per_device(

time: 216 us -> 212 us (0.981)
  local copies, waits for them, and re-layouts: 18 us -> 12.4 us
    gather x1 -> x0, local copies, waits for them, and re-layouts: 3.67 us -> none  [select_diagrams(): return trace_table[:, block_pairs[0], block_pairs[1]] * weight[None, :]]
where the time goes in v9:
time: 212 us; the launch traced here: 211 us
  waiting for transfers between devices  113 us (53%)
  starting transfers between devices  40.2 us (19%)
  matrix products  26.1 us (12%)
  local copies, waits for them, and re-layouts  12.4 us (6%)
  Pallas kernels  11.5 us (5%)
  other arithmetic  7.48 us (4%)
    all_to_all x1, waiting for transfers between devices, per_device(): lax.all_to_all(loops, 'src', split_axis=0, concat_axis=0, tiled=True)  95.9 us
    ppermute x4, starting transfers between devices, all_sum(): table = table + lax.ppermute(table, axis, [(i, i ^ bit) for i in range(n)])  26.2 us
    dot_general x10, matrix products, dress(): out = jnp.dot(weights, stacked, preferred_element_type=jnp.float32)  22.5 us
    pallas_call x1, Pallas kernels, rest_loops(): pl.pallas_call(rest_loop_kernel, grid=(count,), in_specs=[whole] * (2 * c...  11.5 us
    ppermute x4, waiting for transfers between devices, all_sum(): table = table + lax.ppermute(table, axis, [(i, i ^ bit) for i in range(n)])  8.68 us
    ppermute x4, waiting for transfers between devices, shifted(): return lax.ppermute(block, axis, route)  8.63 us
    ppermute x4, starting transfers between devices, shifted(): return lax.ppermute(block, axis, route)  7.86 us
    all_to_all x1, starting transfers between devices, per_device(): lax.all_to_all(loops, 'src', split_axis=0, concat_axis=0, tiled=True)  6.16 us
  transfers between devices with their start and end apart: 9, of which 7 were waited for; matrix products, arithmetic and copies ran while one was open for 13% of the time, Pallas kernels for 0%

profile of v9, /device:TPU:0, one launch (start us, length us, event | category | flops | bytes accessed | tf_op | source)
XLA Modules:
  0.0 211.3 jit_solution(10182938905500378217)
XLA Ops:
  0.0 0.9 constant_dynamic-update-slice_fusion.1
  0.9 0.9 fusion.83
  1.9 0.0 copy-start.2
  1.9 0.0 copy-start.3
  1.9 6.1 %collective-permute-start.2 = (bf16[2,2,128,128]{3,2,1,0:T(8,128)(2,1)S(1)}, bf16[2,2,128,128]{3,2,1,0:T(8,128)(2,1)S(1)}, u32[]{:S(2)}, u32[]{:S(2)}) collective-permute-start(bf16[2,2,128,128]{3,2,1,0:T(8,128)(2,1)S(1)} %get-tuple-element.47), channel_id=1, source_target_pairs={{2,0},{3,1},{4,2},{5,3},{6,4},{7,5},{8,6},{9,7},{10,8},{11,9},{12,... | collective-permute-start | bytes 393224 | tf_op jit(solution)/shard_map/ppermute | solution.py:13
  8.0 3.1 %slice_bitcast_fusion = (bf16[2,512,512]{2,1,0:T(8,128)(2,1)S(1)}, bf16[2,512,512]{2,1,0:T(8,128)(2,1)S(1)}, bf16[1,1,2,512,512]{4,3,2,1,0:T(8,128)(2,1)S(1)}, b...) fusion(bf16[1,5,2,512,512]{4,3,2,1,0:T(8,128)(2,1)} %param.8), kind=kLoop, calls=%fused_computation.68 | loop fusion | bytes 10485760 | tf_op jit(solution)/shard_map/squeeze | solution.py:137
  11.0 1.1 collective-permute-start.3
  12.2 0.7 collective-permute-start.1
  12.9 0.1 fusion.65
  13.1 2.3 %negate_convert_fusion = (bf16[4,128,4,128]{3,2,1,0:T(4,128)(2,1)S(1)}, bf16[4,128,4,128]{3,2,1,0:T(4,128)(2,1)S(1)}, bf16[4,128,4,128]{3,2,1,0:T(4,128)(2,1)S(1...) fusion(f32[128,128]{1,0:T(8,128)S(1)} %get-tuple-element.31, ...), kind=kLoop, calls=%fused_computation.53 | loop fusion | flops 7864320 | bytes 5111936 | tf_op jit(solution)/shard_map/convert.5
  15.5 0.1 copy.59
  15.6 0.1 copy.60
  15.6 0.1 copy.61
  15.7 2.3 %convolution_convert_fusion = bf16[1024,512]{1,0:T(8,128)(2,1)} fusion(bf16[1024,512]{1,0:T(8,128)(2,1)S(1)} %bitcast.217, bf16[512,512]{1,0:T(8,128)(2,1)S(1)} %bitcast.225, bf16[512,512]{1,0:T(8,128)(2,1)S(1)} %bitcast.219, bf16[512,512]{1,0:T(8,128)(2,1)S(1)} %bitcast.222), kind=kOutput, calls=%fused_computation.40 | convolution fusion | flops 1082654720 | bytes 3670016 | tf_op jit(solution)/shard_map/dot_general | solution.py:37
  18.0 2.3 %convolution_convert_fusion.1 = bf16[1024,512]{1,0:T(8,128)(2,1)} fusion(bf16[1024,512]{1,0:T(8,128)(2,1)S(1)} %bitcast.215, bf16[512,512]{1,0:T(8,128)(2,1)S(1)} %bitcast.226, bf16[512,512]{1,0:T(8,128)(2,1)S(1)} %bitcast.220, bf16[512,512]{1,0:T(8,128)(2,1)S(1)} %bitcast.223), kind=kOutput, calls=%fused_computation.41 | convolution fusion | flops 1082654720 | bytes 3670016 | tf_op jit(solution)/shard_map/dot_general | solution.py:37
  20.2 2.3 %negate_convert_fusion.3 = (bf16[4,128,4,128]{3,2,1,0:T(4,128)(2,1)S(1)}, bf16[4,128,4,128]{3,2,1,0:T(4,128)(2,1)S(1)}, bf16[4,128,4,128]{3,2,1,0:T(4,128)(2,1)S...) fusion(f32[128,128]{1,0:T(8,128)S(1)} %get-tuple-element.74, ...), kind=kLoop, calls=%fused_computation.56 | loop fusion | flops 7864320 | bytes 5111936 | tf_op jit(solution)/shard_map/convert.23
  22.6 0.1 copy.68
  22.7 0.1 copy.69
  22.8 0.1 copy.70
  22.8 2.3 %convolution_convert_fusion.3 = bf16[1024,512]{1,0:T(8,128)(2,1)} fusion(bf16[1024,512]{1,0:T(8,128)(2,1)S(1)} %bitcast.218, bf16[512,512]{1,0:T(8,128)(2,1)S(1)} %bitcast.246, bf16[512,512]{1,0:T(8,128)(2,1)S(1)} %bitcast.240, bf16[512,512]{1,0:T(8,128)(2,1)S(1)} %bitcast.243), kind=kOutput, calls=%fused_computation.43 | convolution fusion | flops 1082654720 | bytes 3670016 | tf_op jit(solution)/shard_map/dot_general | solution.py:37
  25.2 2.2 %convolution_convert_fusion.4 = bf16[1024,512]{1,0:T(8,128)(2,1)} fusion(bf16[1024,512]{1,0:T(8,128)(2,1)S(1)} %bitcast.216, bf16[512,512]{1,0:T(8,128)(2,1)S(1)} %bitcast.247, bf16[512,512]{1,0:T(8,128)(2,1)S(1)} %bitcast.241, bf16[512,512]{1,0:T(8,128)(2,1)S(1)} %bitcast.244), kind=kOutput, calls=%fused_computation.44 | convolution fusion | flops 1082654720 | bytes 3670016 | tf_op jit(solution)/shard_map/dot_general | solution.py:37
  27.4 2.2 %convolution_convert_fusion.2 = bf16[1024,512]{1,0:T(8,128)(2,1)} fusion(bf16[1024,512]{1,0:T(8,128)(2,1)S(1)} %bitcast.213, bf16[512,512]{1,0:T(8,128)(2,1)S(1)} %bitcast.227, bf16[512,512]{1,0:T(8,128)(2,1)S(1)} %bitcast.221, bf16[512,512]{1,0:T(8,128)(2,1)S(1)} %bitcast.224), kind=kOutput, calls=%fused_computation.42 | convolution fusion | flops 1082654720 | bytes 3670016 | tf_op jit(solution)/shard_map/dot_general | solution.py:37
  29.6 2.2 %convolution_convert_fusion.5 = bf16[1024,512]{1,0:T(8,128)(2,1)} fusion(bf16[1024,512]{1,0:T(8,128)(2,1)S(1)} %bitcast.214, bf16[512,512]{1,0:T(8,128)(2,1)S(1)} %bitcast.248, bf16[512,512]{1,0:T(8,128)(2,1)S(1)} %bitcast.242, bf16[512,512]{1,0:T(8,128)(2,1)S(1)} %bitcast.245), kind=kOutput, calls=%fused_computation.45 | convolution fusion | flops 1082654720 | bytes 3670016 | tf_op jit(solution)/shard_map/dot_general | solution.py:37
  31.8 0.1 copy.53
  31.9 0.1 copy.54
  32.0 0.1 copy.55
  32.1 0.1 copy.56
  32.1 0.1 copy.57
  32.2 0.1 copy.58
  32.3 0.1 copy.62
  32.4 0.1 copy.63
  32.5 0.1 copy.64
  32.6 0.1 copy.65
  32.7 0.1 copy.66
  32.8 0.1 copy.67
  32.8 3.8 %collective-permute-done.3 = bf16[2,512,512]{2,1,0:T(8,128)(2,1)S(1)} collective-permute-done((bf16[2,512,512]{2,1,0:T(8,128)(2,1)S(1)}, bf16[2,512,512]{2,1,0:T(8,128)(2,1)S(1)}, u32[]{:S(2)}, u32[]{:S(2)}) %collective-permute-start.3) | collective-permute-done | bytes 1048608 | tf_op jit(solution)/shard_map/ppermute | solution.py:13
  36.7 2.2 %fusion.32 = bf16[1024,512]{1,0:T(8,128)(2,1)} fusion(bf16[1024,512]{1,0:T(8,128)(2,1)S(1)} %bitcast.255, bf16[512,512]{1,0:T(8,128)(2,1)S(1)} %bitcast.234, bf16[512,512]{1,0:T(8,128)(2,1)S(1)} %bitcast.231, bf16[512,512]{1,0:T(8,128)(2,1)S(1)} %bitcast.232), kind=kOutput, calls=%fused_computation.36 | convolution fusion | flops 1082654720 | bytes 3670016 | tf_op jit(solution)/shard_map/dot_general | solution.py:37
  38.9 2.2 %fusion.38 = bf16[1024,512]{1,0:T(8,128)(2,1)} fusion(bf16[1024,512]{1,0:T(8,128)(2,1)S(1)} %bitcast.256, bf16[512,512]{1,0:T(8,128)(2,1)S(1)} %bitcast.239, bf16[512,512]{1,0:T(8,128)(2,1)S(1)} %bitcast.237, bf16[512,512]{1,0:T(8,128)(2,1)S(1)} %bitcast.238), kind=kOutput, calls=%fused_computation.38 | convolution fusion | flops 1082654720 | bytes 3670016 | tf_op jit(solution)/shard_map/dot_general | solution.py:37
  41.1 4.8 %collective-permute-done.1 = bf16[2,512,512]{2,1,0:T(8,128)(2,1)S(1)} collective-permute-done((bf16[2,512,512]{2,1,0:T(8,128)(2,1)S(1)}, bf16[2,512,512]{2,1,0:T(8,128)(2,1)S(1)}, u32[]{:S(2)}, u32[]{:S(2)}) %collective-permute-start.1) | collective-permute-done | bytes 1048608 | tf_op jit(solution)/shard_map/ppermute | solution.py:13
  45.9 2.3 %fusion.35 = bf16[1024,512]{1,0:T(8,128)(2,1)} fusion(bf16[1024,512]{1,0:T(8,128)(2,1)S(1)} %bitcast.253, bf16[512,512]{1,0:T(8,128)(2,1)S(1)} %bitcast.230, bf16[512,512]{1,0:T(8,128)(2,1)S(1)} %bitcast.228, bf16[512,512]{1,0:T(8,128)(2,1)S(1)} %bitcast.229), kind=kOutput, calls=%fused_computation.37 | convolution fusion | flops 1082654720 | bytes 3670016 | tf_op jit(solution)/shard_map/dot_general | solution.py:37
  48.2 2.3 %fusion.41 = bf16[1024,512]{1,0:T(8,128)(2,1)} fusion(bf16[1024,512]{1,0:T(8,128)(2,1)S(1)} %bitcast.254, bf16[512,512]{1,0:T(8,128)(2,1)S(1)} %bitcast.236, bf16[512,512]{1,0:T(8,128)(2,1)S(1)} %bitcast.233, bf16[512,512]{1,0:T(8,128)(2,1)S(1)} %bitcast.235), kind=kOutput, calls=%fused_computation.39 | convolution fusion | flops 1082654720 | bytes 3670016 | tf_op jit(solution)/shard_map/dot_general | solution.py:37
  50.5 11.5 %shard_map.82 = bf16[16,5,2,32,512]{4,3,2,1,0:T(8,128)(2,1)} custom-call(bf16[1,2,512,512]{3,2,1,0:T(8,128)(2,1)} %bitcast.262, bf16[1,2,512,512]{3,2,1,0:T(8,128)(2,1)} %bitcast.260, bf16[1,2,512,512]{3,2,1,0:T(8,128)(2,1)} %bitcast.266, bf16[1,2,512,512]{3,2,1,0:T(8,128)(2,1)} %bitcast.259, bf16[1,2,512,512]{3,2,1,0:T(8,128)(2,1)} %bitcast.264, ...), custom_call_target="tpu_custom_call" | custom-call | flops 5368709120 | bytes 15728640 | tf_op jit(solution)/shard_map/pallas_call | solution.py:87
  62.0 6.2 %all-to-all-start = ((bf16[16,5,2,32,512]{4,3,2,1,0:T(8,128)(2,1)}), bf16[16,5,2,32,512]{4,3,2,1,0:T(8,128)(2,1)}, u32[]{:S(2)}, u32[]{:S(2)}) async-start(bf16[16,5,2,32,512]{4,3,2,1,0:T(8,128)(2,1)} %shard_map.82), calls=%async_computation | async-start | bytes 10485760 | tf_op jit(solution)/shard_map/all_to_all | solution.py:150
  68.2 95.9 %all-to-all-done = bf16[16,5,2,32,512]{4,3,2,1,0:T(8,128)(2,1)} async-done(((bf16[16,5,2,32,512]{4,3,2,1,0:T(8,128)(2,1)}), bf16[16,5,2,32,512]{4,3,2,1,0:T(8,128)(2,1)}, u32[]{:S(2)}, u32[]{:S(2)}) %all-to-all-start) | async-done | bytes 5242912 | tf_op jit(solution)/shard_map/all_to_all | solution.py:150
  164.1 3.0 %fusion.82 = (bf16[16,5,1,32,512]{4,3,2,1,0:T(8,128)(2,1)S(1)}, bf16[16,5,1,32,512]{4,3,2,1,0:T(8,128)(2,1)S(1)}) fusion(bf16[16,5,2,32,512]{4,3,2,1,0:T(8,128)(2,1)} %all-to-all-done), kind=kLoop, calls=%fused_computation.166 | loop fusion | bytes 10485760 | tf_op jit(solution)/shard_map/slice | solution.py:153
  167.1 1.6 copy.31
  168.8 0.8 fusion.85
  169.6 1.6 copy.32
  171.2 0.8 fusion.86
  172.1 0.8 fusion.47
  172.9 0.8 fusion.46
  173.8 0.7 gather_fusion
  174.5 0.1 copy.11
  174.6 0.7 gather_fusion.1
  175.3 0.8 collective-permute-start.4
  176.2 0.9 collective-permute-done.4
  177.1 7.6 %collective-permute-start.5 = (f32[2,80,80]{1,0,2:T(2,128)S(1)}, f32[2,80,80]{1,0,2:T(2,128)S(1)}, u32[]{:S(2)}, u32[]{:S(2)}) collective-permute-start(f32[2,80,80]{1,0,2:T(2,128)S(1)} %bitcast_add_fusion), channel_id=1, source_target_pairs={{0,2},{1,3},{2,0},{3,1},{4,6},{5,7},{6,4},{7,5},{8,10},{9,11},{10,... | collective-permute-start | bytes 153608 | tf_op jit(solution)/shard_map/ppermute | solution.py:110
  184.8 3.0 %collective-permute-done.5 = f32[2,80,80]{1,0,2:T(2,128)S(1)} collective-permute-done((f32[2,80,80]{1,0,2:T(2,128)S(1)}, f32[2,80,80]{1,0,2:T(2,128)S(1)}, u32[]{:S(2)}, u32[]{:S(2)}) %collective-permute-start.5) | collective-permute-done | bytes 51232 | tf_op jit(solution)/shard_map/ppermute | solution.py:110
  187.8 14.2 %collective-permute-start.6 = (f32[2,80,80]{1,0,2:T(2,128)S(1)}, f32[2,80,80]{1,0,2:T(2,128)S(1)}, u32[]{:S(2)}, u32[]{:S(2)}) collective-permute-start(f32[2,80,80]{1,0,2:T(2,128)S(1)} %add.80), channel_id=1, source_target_pairs={{0,4},{1,5},{2,6},{3,7},{4,0},{5,1},{6,2},{7,3},{8,12},{9,13},{10,... | collective-permute-start | bytes 153608 | tf_op jit(solution)/shard_map/ppermute | solution.py:110
  202.0 2.4 %collective-permute-done.6 = f32[2,80,80]{1,0,2:T(2,128)S(1)} collective-permute-done((f32[2,80,80]{1,0,2:T(2,128)S(1)}, f32[2,80,80]{1,0,2:T(2,128)S(1)}, u32[]{:S(2)}, u32[]{:S(2)}) %collective-permute-start.6) | collective-permute-done | bytes 51232 | tf_op jit(solution)/shard_map/ppermute | solution.py:110
  204.4 3.5 %collective-permute-start.7 = (f32[2,80,80]{1,0,2:T(2,128)S(1)}, f32[2,80,80]{1,0,2:T(2,128)S(1)}, u32[]{:S(2)}, u32[]{:S(2)}) collective-permute-start(f32[2,80,80]{1,0,2:T(2,128)S(1)} %add.81), channel_id=1, source_target_pairs={{0,8},{1,9},{2,10},{3,11},{4,12},{5,13},{6,14},{7,15},{8,0},{9,1},... | collective-permute-start | bytes 153608 | tf_op jit(solution)/shard_map/ppermute | solution.py:110
  208.0 2.4 %collective-permute-done.7 = f32[2,80,80]{1,0,2:T(2,128)S(1)} collective-permute-done((f32[2,80,80]{1,0,2:T(2,128)S(1)}, f32[2,80,80]{1,0,2:T(2,128)S(1)}, u32[]{:S(2)}, u32[]{:S(2)}) %collective-permute-start.7) | collective-permute-done | bytes 51232 | tf_op jit(solution)/shard_map/ppermute | solution.py:110
  210.4 0.3 fusion.45
  210.7 0.6 broadcast_multiply_fusion
  (29 shorter events, 0.4 us)
Async XLA Ops:
  1.9 11.0 %copy-start.2 = (s32[2,4]{1,0:T(2,128)S(1)}, s32[2,4]{1,0:T(2,128)}, u32[]{:S(2)}) copy-start(s32[2,4]{1,0:T(2,128)} %param.12) | copy-start | bytes 100
  1.9 11.0 %copy-start.3 = (s32[2,4]{1,0:T(2,128)S(1)}, s32[2,4]{1,0:T(2,128)}, u32[]{:S(2)}) copy-start(s32[2,4]{1,0:T(2,128)} %param.11) | copy-start | bytes 100
  1.9 11.1 %collective-permute-start.2 = (bf16[2,2,128,128]{3,2,1,0:T(8,128)(2,1)S(1)}, bf16[2,2,128,128]{3,2,1,0:T(8,128)(2,1)S(1)}, u32[]{:S(2)}, u32[]{:S(2)}) collective-permute-start(bf16[2,2,128,128]{3,2,1,0:T(8,128)(2,1)S(1)} %get-tuple-element.47), channel_id=1, source_target_pairs={{2,0},{3,1},{4,2},{5,3},{6,4},{7,5},{8,6},{9,7},{10,8},{11,9},{12,... | collective-permute-start | bytes 393224 | tf_op jit(solution)/shard_map/ppermute | solution.py:13
  8.0 5.1 %collective-permute-start = (bf16[2,2,128,128]{3,2,1,0:T(8,128)(2,1)S(1)}, bf16[2,2,128,128]{3,2,1,0:T(8,128)(2,1)S(1)}, u32[]{:S(2)}, u32[]{:S(2)}) collective-permute-start(bf16[2,2,128,128]{3,2,1,0:T(8,128)(2,1)S(1)} %get-tuple-element.47), channel_id=1, source_target_pairs={{1,0},{2,1},{3,2},{4,3},{5,4},{6,5},{7,6},{8,7},{9,8},{10,9},{11,1... | collective-permute-start | bytes 393224 | tf_op jit(solution)/shard_map/ppermute | solution.py:13
  11.0 25.6 %collective-permute-start.3 = (bf16[2,512,512]{2,1,0:T(8,128)(2,1)S(1)}, bf16[2,512,512]{2,1,0:T(8,128)(2,1)S(1)}, u32[]{:S(2)}, u32[]{:S(2)}) collective-permute-start(bf16[2,512,512]{2,1,0:T(8,128)(2,1)S(1)} %get-tuple-element.7), channel_id=1, source_target_pairs={{2,0},{3,1},{4,2},{5,3},{6,4},{7,5},{8,6},{9,7},{10,8},{11,9},{12,... | collective-permute-start | bytes 3145736 | tf_op jit(solution)/shard_map/ppermute | solution.py:13
  12.2 33.8 %collective-permute-start.1 = (bf16[2,512,512]{2,1,0:T(8,128)(2,1)S(1)}, bf16[2,512,512]{2,1,0:T(8,128)(2,1)S(1)}, u32[]{:S(2)}, u32[]{:S(2)}) collective-permute-start(bf16[2,512,512]{2,1,0:T(8,128)(2,1)S(1)} %get-tuple-element.8), channel_id=1, source_target_pairs={{1,0},{2,1},{3,2},{4,3},{5,4},{6,5},{7,6},{8,7},{9,8},{10,9},{11,1... | collective-permute-start | bytes 3145736 | tf_op jit(solution)/shard_map/ppermute | solution.py:13
  62.0 6.2 %copy-start.4 = (s32[80]{0:T(128)S(1)}, s32[80]{0:T(128)}, u32[]{:S(2)}) copy-start(s32[80]{0:T(128)} %constant.52) | copy-start | bytes 964
  62.0 102.1 %all-to-all-start = ((bf16[16,5,2,32,512]{4,3,2,1,0:T(8,128)(2,1)}), bf16[16,5,2,32,512]{4,3,2,1,0:T(8,128)(2,1)}, u32[]{:S(2)}, u32[]{:S(2)}) async-start(bf16[16,5,2,32,512]{4,3,2,1,0:T(8,128)(2,1)} %shard_map.82), calls=%async_computation | async-start | bytes 10485760 | tf_op jit(solution)/shard_map/all_to_all | solution.py:150
  172.9 11.9 %copy-start = (s32[2,512]{1,0:T(2,128)S(1)}, s32[2,512]{1,0:T(2,128)}, u32[]{:S(2)}) copy-start(s32[2,512]{1,0:T(2,128)} %param.13) | copy-start | bytes 12292
  172.9 35.0 %copy-start.1 = (s32[512]{0:T(512)S(1)}, s32[512]{0:T(512)}, u32[]{:S(2)}) copy-start(s32[512]{0:T(512)} %param.14) | copy-start | bytes 6148
  175.3 1.8 collective-permute-start.4
  177.1 10.6 %collective-permute-start.5 = (f32[2,80,80]{1,0,2:T(2,128)S(1)}, f32[2,80,80]{1,0,2:T(2,128)S(1)}, u32[]{:S(2)}, u32[]{:S(2)}) collective-permute-start(f32[2,80,80]{1,0,2:T(2,128)S(1)} %bitcast_add_fusion), channel_id=1, source_target_pairs={{0,2},{1,3},{2,0},{3,1},{4,6},{5,7},{6,4},{7,5},{8,10},{9,11},{10,... | collective-permute-start | bytes 153608 | tf_op jit(solution)/shard_map/ppermute | solution.py:110
  187.8 16.6 %collective-permute-start.6 = (f32[2,80,80]{1,0,2:T(2,128)S(1)}, f32[2,80,80]{1,0,2:T(2,128)S(1)}, u32[]{:S(2)}, u32[]{:S(2)}) collective-permute-start(f32[2,80,80]{1,0,2:T(2,128)S(1)} %add.80), channel_id=1, source_target_pairs={{0,4},{1,5},{2,6},{3,7},{4,0},{5,1},{6,2},{7,3},{8,12},{9,13},{10,... | collective-permute-start | bytes 153608 | tf_op jit(solution)/shard_map/ppermute | solution.py:110
  204.4 5.9 %collective-permute-start.7 = (f32[2,80,80]{1,0,2:T(2,128)S(1)}, f32[2,80,80]{1,0,2:T(2,128)S(1)}, u32[]{:S(2)}, u32[]{:S(2)}) collective-permute-start(f32[2,80,80]{1,0,2:T(2,128)S(1)} %add.81), channel_id=1, source_target_pairs={{0,8},{1,9},{2,10},{3,11},{4,12},{5,13},{6,14},{7,15},{8,0},{9,1},... | collective-permute-start | bytes 153608 | tf_op jit(solution)/shard_map/ppermute | solution.py:110

commit v10 on v9

--- a/solution.py
+++ b/solution.py
@@ -48,24 +48,7 @@
     real = jnp.dot(fr, br, preferred_element_type=jnp.float32) - jnp.dot(fi, bi, preferred_element_type=jnp.float32)
     imag = jnp.dot(fr, bi, preferred_element_type=jnp.float32) + jnp.dot(fi, br, preferred_element_type=jnp.float32)
     out_ref[:, 0, 0] = real.astype(out_ref.dtype).reshape(shares, rows, real.shape[-1])
-    out_ref[:, 0, 1] = imag.astype(out_ref.dtype).reshape(shares, rows, imag.shape[-1])
-
-
-def open_loops(forward, backward, shares):
-    window, _, order, _ = forward.shape
-    rows = order // shares
-    tile = pl.BlockSpec((1, 2, order, order), lambda s: (s, 0, 0, 0))
-    return pl.pallas_call(
-        loop_kernel,
-        grid=(window,),
-        in_specs=[tile, tile],
-        out_specs=pl.BlockSpec((shares, 1, 2, rows, order), lambda s: (0, s, 0, 0, 0)),
-        out_shape=jax.ShapeDtypeStruct((shares, window, 2, rows, order), jnp.bfloat16),
-        compiler_params=pltpu.CompilerParams(vmem_limit_bytes=48 * 1024 * 1024),
-        cost_estimate=pl.CostEstimate(
-            flops=8 * window * order ** 3, transcendentals=0, bytes_accessed=6 * window * order * order * 2
-        ),
-    )(forward, backward)
+    out_ref[:, 1, 0] = imag.astype(out_ref.dtype).reshape(shares, rows, imag.shape[-1])
 
 
 def rest_loop_kernel(*refs):
@@ -88,8 +71,8 @@
         rest_loop_kernel,
         grid=(count,),
         in_specs=[whole] * (2 * count),
-        out_specs=pl.BlockSpec((shares, 1, 2, rows, order), lambda s: (0, s, 0, 0, 0)),
-        out_shape=jax.ShapeDtypeStruct((shares, count, 2, rows, order), jnp.bfloat16),
+        out_specs=pl.BlockSpec((shares, 2, 1, rows, order), lambda s: (0, 0, s, 0, 0)),
+        out_shape=jax.ShapeDtypeStruct((shares, 2, count, rows, order), jnp.bfloat16),
         compiler_params=pltpu.CompilerParams(vmem_limit_bytes=56 * 1024 * 1024),
         cost_estimate=pl.CostEstimate(
             flops=8 * count * order ** 3, transcendentals=0, bytes_accessed=6 * count * order * order * 2
@@ -148,9 +131,9 @@
         partners += [dress(sink_partner, tile), dress(sink_own, tiles[half_window + offset])]
     loops = rest_loops(forwards, partners, shares)
     slices = lax.all_to_all(loops, "src", split_axis=0, concat_axis=0, tiled=True)
-    block_count = slices.shape[0] * slices.shape[1]
-    real_flat = slices[:, :, 0].reshape(block_count, -1)
-    imag_flat = slices[:, :, 1].reshape(block_count, -1)
+    block_count = slices.shape[0] * slices.shape[2]
+    real_flat = slices[:, 0].reshape(block_count, -1)
+    imag_flat = slices[:, 1].reshape(block_count, -1)
     trace_table = jnp.stack(
         [
             inner_product(real_flat, real_flat) - inner_product(imag_flat, imag_flat),

time: 212 us -> 212 us (level)
  no operation moved by 1% of the time
where the time goes in v10:
time: 212 us; the launch traced here: 211 us
  waiting for transfers between devices  113 us (53%)
  starting transfers between devices  40.2 us (19%)
  matrix products  26.1 us (12%)
  local copies, waits for them, and re-layouts  12.4 us (6%)
  Pallas kernels  11.5 us (5%)
  other arithmetic  7.48 us (4%)
    all_to_all x1, waiting for transfers between devices, per_device(): lax.all_to_all(loops, 'src', split_axis=0, concat_axis=0, tiled=True)  95.9 us
    ppermute x4, starting transfers between devices, all_sum(): table = table + lax.ppermute(table, axis, [(i, i ^ bit) for i in range(n)])  26.2 us
    dot_general x10, matrix products, dress(): out = jnp.dot(weights, stacked, preferred_element_type=jnp.float32)  22.5 us
    pallas_call x1, Pallas kernels, rest_loops(): pl.pallas_call(rest_loop_kernel, grid=(count,), in_specs=[whole] * (2 * c...  11.5 us
    ppermute x4, waiting for transfers between devices, all_sum(): table = table + lax.ppermute(table, axis, [(i, i ^ bit) for i in range(n)])  8.68 us
    ppermute x4, waiting for transfers between devices, shifted(): return lax.ppermute(block, axis, route)  8.63 us
    ppermute x4, starting transfers between devices, shifted(): return lax.ppermute(block, axis, route)  7.86 us
    all_to_all x1, starting transfers between devices, per_device(): lax.all_to_all(loops, 'src', split_axis=0, concat_axis=0, tiled=True)  6.16 us
  transfers between devices with their start and end apart: 9, of which 7 were waited for; matrix products, arithmetic and copies ran while one was open for 13% of the time, Pallas kernels for 0%

profile of v10, /device:TPU:0, one launch (start us, length us, event | category | flops | bytes accessed | tf_op | source)
XLA Modules:
  0.0 211.3 jit_solution(334110801454678698)
XLA Ops:
  0.0 0.9 constant_dynamic-update-slice_fusion.1
  0.9 0.9 fusion.83
  1.9 0.0 copy-start.2
  1.9 6.1 %collective-permute-start.2 = (bf16[2,2,128,128]{3,2,1,0:T(8,128)(2,1)S(1)}, bf16[2,2,128,128]{3,2,1,0:T(8,128)(2,1)S(1)}, u32[]{:S(2)}, u32[]{:S(2)}) collective-permute-start(bf16[2,2,128,128]{3,2,1,0:T(8,128)(2,1)S(1)} %get-tuple-element.47), channel_id=1, source_target_pairs={{2,0},{3,1},{4,2},{5,3},{6,4},{7,5},{8,6},{9,7},{10,8},{11,9},{12,... | collective-permute-start | bytes 393224 | tf_op jit(solution)/shard_map/ppermute | solution.py:13
  8.0 3.1 %slice_bitcast_fusion = (bf16[2,512,512]{2,1,0:T(8,128)(2,1)S(1)}, bf16[2,512,512]{2,1,0:T(8,128)(2,1)S(1)}, bf16[1,1,2,512,512]{4,3,2,1,0:T(8,128)(2,1)S(1)}, b...) fusion(bf16[1,5,2,512,512]{4,3,2,1,0:T(8,128)(2,1)} %param.8), kind=kLoop, calls=%fused_computation.68 | loop fusion | bytes 10485760 | tf_op jit(solution)/shard_map/squeeze | solution.py:120
  11.0 1.1 collective-permute-start.3
  12.2 0.7 collective-permute-start.1
  12.9 0.1 fusion.65
  13.1 2.3 %negate_convert_fusion = (bf16[4,128,4,128]{3,2,1,0:T(4,128)(2,1)S(1)}, bf16[4,128,4,128]{3,2,1,0:T(4,128)(2,1)S(1)}, bf16[4,128,4,128]{3,2,1,0:T(4,128)(2,1)S(1...) fusion(f32[128,128]{1,0:T(8,128)S(1)} %get-tuple-element.31, ...), kind=kLoop, calls=%fused_computation.53 | loop fusion | flops 7864320 | bytes 5111936 | tf_op jit(solution)/shard_map/convert.5
  15.5 0.1 copy.59
  15.6 0.1 copy.60
  15.6 0.1 copy.61
  15.7 2.3 %convolution_convert_fusion = bf16[1024,512]{1,0:T(8,128)(2,1)} fusion(bf16[1024,512]{1,0:T(8,128)(2,1)S(1)} %bitcast.217, bf16[512,512]{1,0:T(8,128)(2,1)S(1)} %bitcast.225, bf16[512,512]{1,0:T(8,128)(2,1)S(1)} %bitcast.219, bf16[512,512]{1,0:T(8,128)(2,1)S(1)} %bitcast.222), kind=kOutput, calls=%fused_computation.40 | convolution fusion | flops 1082654720 | bytes 3670016 | tf_op jit(solution)/shard_map/dot_general | solution.py:37
  18.0 2.3 %convolution_convert_fusion.1 = bf16[1024,512]{1,0:T(8,128)(2,1)} fusion(bf16[1024,512]{1,0:T(8,128)(2,1)S(1)} %bitcast.215, bf16[512,512]{1,0:T(8,128)(2,1)S(1)} %bitcast.226, bf16[512,512]{1,0:T(8,128)(2,1)S(1)} %bitcast.220, bf16[512,512]{1,0:T(8,128)(2,1)S(1)} %bitcast.223), kind=kOutput, calls=%fused_computation.41 | convolution fusion | flops 1082654720 | bytes 3670016 | tf_op jit(solution)/shard_map/dot_general | solution.py:37
  20.2 2.3 %negate_convert_fusion.3 = (bf16[4,128,4,128]{3,2,1,0:T(4,128)(2,1)S(1)}, bf16[4,128,4,128]{3,2,1,0:T(4,128)(2,1)S(1)}, bf16[4,128,4,128]{3,2,1,0:T(4,128)(2,1)S...) fusion(f32[128,128]{1,0:T(8,128)S(1)} %get-tuple-element.74, ...), kind=kLoop, calls=%fused_computation.56 | loop fusion | flops 7864320 | bytes 5111936 | tf_op jit(solution)/shard_map/convert.23
  22.6 0.1 copy.68
  22.7 0.1 copy.69
  22.8 0.1 copy.70
  22.8 2.3 %convolution_convert_fusion.3 = bf16[1024,512]{1,0:T(8,128)(2,1)} fusion(bf16[1024,512]{1,0:T(8,128)(2,1)S(1)} %bitcast.218, bf16[512,512]{1,0:T(8,128)(2,1)S(1)} %bitcast.246, bf16[512,512]{1,0:T(8,128)(2,1)S(1)} %bitcast.240, bf16[512,512]{1,0:T(8,128)(2,1)S(1)} %bitcast.243), kind=kOutput, calls=%fused_computation.43 | convolution fusion | flops 1082654720 | bytes 3670016 | tf_op jit(solution)/shard_map/dot_general | solution.py:37
  25.2 2.2 %convolution_convert_fusion.4 = bf16[1024,512]{1,0:T(8,128)(2,1)} fusion(bf16[1024,512]{1,0:T(8,128)(2,1)S(1)} %bitcast.216, bf16[512,512]{1,0:T(8,128)(2,1)S(1)} %bitcast.247, bf16[512,512]{1,0:T(8,128)(2,1)S(1)} %bitcast.241, bf16[512,512]{1,0:T(8,128)(2,1)S(1)} %bitcast.244), kind=kOutput, calls=%fused_computation.44 | convolution fusion | flops 1082654720 | bytes 3670016 | tf_op jit(solution)/shard_map/dot_general | solution.py:37
  27.4 2.2 %convolution_convert_fusion.2 = bf16[1024,512]{1,0:T(8,128)(2,1)} fusion(bf16[1024,512]{1,0:T(8,128)(2,1)S(1)} %bitcast.213, bf16[512,512]{1,0:T(8,128)(2,1)S(1)} %bitcast.227, bf16[512,512]{1,0:T(8,128)(2,1)S(1)} %bitcast.221, bf16[512,512]{1,0:T(8,128)(2,1)S(1)} %bitcast.224), kind=kOutput, calls=%fused_computation.42 | convolution fusion | flops 1082654720 | bytes 3670016 | tf_op jit(solution)/shard_map/dot_general | solution.py:37
  29.6 2.2 %convolution_convert_fusion.5 = bf16[1024,512]{1,0:T(8,128)(2,1)} fusion(bf16[1024,512]{1,0:T(8,128)(2,1)S(1)} %bitcast.214, bf16[512,512]{1,0:T(8,128)(2,1)S(1)} %bitcast.248, bf16[512,512]{1,0:T(8,128)(2,1)S(1)} %bitcast.242, bf16[512,512]{1,0:T(8,128)(2,1)S(1)} %bitcast.245), kind=kOutput, calls=%fused_computation.45 | convolution fusion | flops 1082654720 | bytes 3670016 | tf_op jit(solution)/shard_map/dot_general | solution.py:37
  31.8 0.1 copy.53
  31.9 0.1 copy.54
  32.0 0.1 copy.55
  32.1 0.1 copy.56
  32.1 0.1 copy.57
  32.2 0.1 copy.58
  32.3 0.1 copy.62
  32.4 0.1 copy.63
  32.5 0.1 copy.64
  32.6 0.1 copy.65
  32.7 0.1 copy.66
  32.8 0.1 copy.67
  32.8 3.8 %collective-permute-done.3 = bf16[2,512,512]{2,1,0:T(8,128)(2,1)S(1)} collective-permute-done((bf16[2,512,512]{2,1,0:T(8,128)(2,1)S(1)}, bf16[2,512,512]{2,1,0:T(8,128)(2,1)S(1)}, u32[]{:S(2)}, u32[]{:S(2)}) %collective-permute-start.3) | collective-permute-done | bytes 1048608 | tf_op jit(solution)/shard_map/ppermute | solution.py:13
  36.7 2.2 %fusion.32 = bf16[1024,512]{1,0:T(8,128)(2,1)} fusion(bf16[1024,512]{1,0:T(8,128)(2,1)S(1)} %bitcast.255, bf16[512,512]{1,0:T(8,128)(2,1)S(1)} %bitcast.234, bf16[512,512]{1,0:T(8,128)(2,1)S(1)} %bitcast.231, bf16[512,512]{1,0:T(8,128)(2,1)S(1)} %bitcast.232), kind=kOutput, calls=%fused_computation.36 | convolution fusion | flops 1082654720 | bytes 3670016 | tf_op jit(solution)/shard_map/dot_general | solution.py:37
  38.9 2.2 %fusion.38 = bf16[1024,512]{1,0:T(8,128)(2,1)} fusion(bf16[1024,512]{1,0:T(8,128)(2,1)S(1)} %bitcast.256, bf16[512,512]{1,0:T(8,128)(2,1)S(1)} %bitcast.239, bf16[512,512]{1,0:T(8,128)(2,1)S(1)} %bitcast.237, bf16[512,512]{1,0:T(8,128)(2,1)S(1)} %bitcast.238), kind=kOutput, calls=%fused_computation.38 | convolution fusion | flops 1082654720 | bytes 3670016 | tf_op jit(solution)/shard_map/dot_general | solution.py:37
  41.1 4.8 %collective-permute-done.1 = bf16[2,512,512]{2,1,0:T(8,128)(2,1)S(1)} collective-permute-done((bf16[2,512,512]{2,1,0:T(8,128)(2,1)S(1)}, bf16[2,512,512]{2,1,0:T(8,128)(2,1)S(1)}, u32[]{:S(2)}, u32[]{:S(2)}) %collective-permute-start.1) | collective-permute-done | bytes 1048608 | tf_op jit(solution)/shard_map/ppermute | solution.py:13
  45.9 2.3 %fusion.35 = bf16[1024,512]{1,0:T(8,128)(2,1)} fusion(bf16[1024,512]{1,0:T(8,128)(2,1)S(1)} %bitcast.253, bf16[512,512]{1,0:T(8,128)(2,1)S(1)} %bitcast.230, bf16[512,512]{1,0:T(8,128)(2,1)S(1)} %bitcast.228, bf16[512,512]{1,0:T(8,128)(2,1)S(1)} %bitcast.229), kind=kOutput, calls=%fused_computation.37 | convolution fusion | flops 1082654720 | bytes 3670016 | tf_op jit(solution)/shard_map/dot_general | solution.py:37
  48.2 2.3 %fusion.41 = bf16[1024,512]{1,0:T(8,128)(2,1)} fusion(bf16[1024,512]{1,0:T(8,128)(2,1)S(1)} %bitcast.254, bf16[512,512]{1,0:T(8,128)(2,1)S(1)} %bitcast.236, bf16[512,512]{1,0:T(8,128)(2,1)S(1)} %bitcast.233, bf16[512,512]{1,0:T(8,128)(2,1)S(1)} %bitcast.235), kind=kOutput, calls=%fused_computation.39 | convolution fusion | flops 1082654720 | bytes 3670016 | tf_op jit(solution)/shard_map/dot_general | solution.py:37
  50.5 11.5 %shard_map.82 = bf16[16,2,5,32,512]{4,3,2,1,0:T(8,128)(2,1)} custom-call(bf16[1,2,512,512]{3,2,1,0:T(8,128)(2,1)} %bitcast.262, bf16[1,2,512,512]{3,2,1,0:T(8,128)(2,1)} %bitcast.260, bf16[1,2,512,512]{3,2,1,0:T(8,128)(2,1)} %bitcast.266, bf16[1,2,512,512]{3,2,1,0:T(8,128)(2,1)} %bitcast.259, bf16[1,2,512,512]{3,2,1,0:T(8,128)(2,1)} %bitcast.264, ...), custom_call_target="tpu_custom_call" | custom-call | flops 5368709120 | bytes 15728640 | tf_op jit(solution)/shard_map/pallas_call | solution.py:70
  62.0 6.2 %all-to-all-start = ((bf16[16,2,5,32,512]{4,3,2,1,0:T(8,128)(2,1)}), bf16[16,2,5,32,512]{4,3,2,1,0:T(8,128)(2,1)}, u32[]{:S(2)}, u32[]{:S(2)}) async-start(bf16[16,2,5,32,512]{4,3,2,1,0:T(8,128)(2,1)} %shard_map.82), calls=%async_computation | async-start | bytes 10485760 | tf_op jit(solution)/shard_map/all_to_all | solution.py:133
  68.2 95.9 %all-to-all-done = bf16[16,2,5,32,512]{4,3,2,1,0:T(8,128)(2,1)} async-done(((bf16[16,2,5,32,512]{4,3,2,1,0:T(8,128)(2,1)}), bf16[16,2,5,32,512]{4,3,2,1,0:T(8,128)(2,1)}, u32[]{:S(2)}, u32[]{:S(2)}) %all-to-all-start) | async-done | bytes 5242912 | tf_op jit(solution)/shard_map/all_to_all | solution.py:133
  164.1 3.0 %fusion.82 = (bf16[16,1,5,32,512]{4,3,2,1,0:T(8,128)(2,1)S(1)}, bf16[16,1,5,32,512]{4,3,2,1,0:T(8,128)(2,1)S(1)}) fusion(bf16[16,2,5,32,512]{4,3,2,1,0:T(8,128)(2,1)} %all-to-all-done), kind=kLoop, calls=%fused_computation.166 | loop fusion | bytes 10485760 | tf_op jit(solution)/shard_map/slice | solution.py:136
  167.1 1.6 copy.31
  168.8 0.8 fusion.85
  169.6 1.6 copy.32
  171.2 0.8 fusion.86
  172.1 0.8 fusion.47
  172.9 0.0 copy-start
  172.9 0.8 fusion.46
  173.9 0.7 gather_fusion
  174.5 0.1 copy.11
  174.6 0.7 gather_fusion.1
  175.3 0.8 collective-permute-start.4
  176.2 0.9 collective-permute-done.4
  177.1 7.6 %collective-permute-start.5 = (f32[2,80,80]{1,0,2:T(2,128)S(1)}, f32[2,80,80]{1,0,2:T(2,128)S(1)}, u32[]{:S(2)}, u32[]{:S(2)}) collective-permute-start(f32[2,80,80]{1,0,2:T(2,128)S(1)} %bitcast_add_fusion), channel_id=1, source_target_pairs={{0,2},{1,3},{2,0},{3,1},{4,6},{5,7},{6,4},{7,5},{8,10},{9,11},{10,... | collective-permute-start | bytes 153608 | tf_op jit(solution)/shard_map/ppermute | solution.py:93
  184.8 3.0 %collective-permute-done.5 = f32[2,80,80]{1,0,2:T(2,128)S(1)} collective-permute-done((f32[2,80,80]{1,0,2:T(2,128)S(1)}, f32[2,80,80]{1,0,2:T(2,128)S(1)}, u32[]{:S(2)}, u32[]{:S(2)}) %collective-permute-start.5) | collective-permute-done | bytes 51232 | tf_op jit(solution)/shard_map/ppermute | solution.py:93
  187.8 14.2 %collective-permute-start.6 = (f32[2,80,80]{1,0,2:T(2,128)S(1)}, f32[2,80,80]{1,0,2:T(2,128)S(1)}, u32[]{:S(2)}, u32[]{:S(2)}) collective-permute-start(f32[2,80,80]{1,0,2:T(2,128)S(1)} %add.80), channel_id=1, source_target_pairs={{0,4},{1,5},{2,6},{3,7},{4,0},{5,1},{6,2},{7,3},{8,12},{9,13},{10,... | collective-permute-start | bytes 153608 | tf_op jit(solution)/shard_map/ppermute | solution.py:93
  202.0 2.4 %collective-permute-done.6 = f32[2,80,80]{1,0,2:T(2,128)S(1)} collective-permute-done((f32[2,80,80]{1,0,2:T(2,128)S(1)}, f32[2,80,80]{1,0,2:T(2,128)S(1)}, u32[]{:S(2)}, u32[]{:S(2)}) %collective-permute-start.6) | collective-permute-done | bytes 51232 | tf_op jit(solution)/shard_map/ppermute | solution.py:93
  204.5 3.5 %collective-permute-start.7 = (f32[2,80,80]{1,0,2:T(2,128)S(1)}, f32[2,80,80]{1,0,2:T(2,128)S(1)}, u32[]{:S(2)}, u32[]{:S(2)}) collective-permute-start(f32[2,80,80]{1,0,2:T(2,128)S(1)} %add.81), channel_id=1, source_target_pairs={{0,8},{1,9},{2,10},{3,11},{4,12},{5,13},{6,14},{7,15},{8,0},{9,1},... | collective-permute-start | bytes 153608 | tf_op jit(solution)/shard_map/ppermute | solution.py:93
  208.0 2.4 %collective-permute-done.7 = f32[2,80,80]{1,0,2:T(2,128)S(1)} collective-permute-done((f32[2,80,80]{1,0,2:T(2,128)S(1)}, f32[2,80,80]{1,0,2:T(2,128)S(1)}, u32[]{:S(2)}, u32[]{:S(2)}) %collective-permute-start.7) | collective-permute-done | bytes 51232 | tf_op jit(solution)/shard_map/ppermute | solution.py:93
  210.4 0.3 fusion.45
  210.7 0.6 broadcast_multiply_fusion
  (29 shorter events, 0.4 us)
Async XLA Ops:
  1.9 11.0 %copy-start.2 = (s32[2,4]{1,0:T(2,128)S(1)}, s32[2,4]{1,0:T(2,128)}, u32[]{:S(2)}) copy-start(s32[2,4]{1,0:T(2,128)} %param.12) | copy-start | bytes 100
  1.9 11.0 %copy-start.3 = (s32[2,4]{1,0:T(2,128)S(1)}, s32[2,4]{1,0:T(2,128)}, u32[]{:S(2)}) copy-start(s32[2,4]{1,0:T(2,128)} %param.11) | copy-start | bytes 100
  1.9 11.1 %collective-permute-start.2 = (bf16[2,2,128,128]{3,2,1,0:T(8,128)(2,1)S(1)}, bf16[2,2,128,128]{3,2,1,0:T(8,128)(2,1)S(1)}, u32[]{:S(2)}, u32[]{:S(2)}) collective-permute-start(bf16[2,2,128,128]{3,2,1,0:T(8,128)(2,1)S(1)} %get-tuple-element.47), channel_id=1, source_target_pairs={{2,0},{3,1},{4,2},{5,3},{6,4},{7,5},{8,6},{9,7},{10,8},{11,9},{12,... | collective-permute-start | bytes 393224 | tf_op jit(solution)/shard_map/ppermute | solution.py:13
  8.0 5.1 %collective-permute-start = (bf16[2,2,128,128]{3,2,1,0:T(8,128)(2,1)S(1)}, bf16[2,2,128,128]{3,2,1,0:T(8,128)(2,1)S(1)}, u32[]{:S(2)}, u32[]{:S(2)}) collective-permute-start(bf16[2,2,128,128]{3,2,1,0:T(8,128)(2,1)S(1)} %get-tuple-element.47), channel_id=1, source_target_pairs={{1,0},{2,1},{3,2},{4,3},{5,4},{6,5},{7,6},{8,7},{9,8},{10,9},{11,1... | collective-permute-start | bytes 393224 | tf_op jit(solution)/shard_map/ppermute | solution.py:13
  11.0 25.6 %collective-permute-start.3 = (bf16[2,512,512]{2,1,0:T(8,128)(2,1)S(1)}, bf16[2,512,512]{2,1,0:T(8,128)(2,1)S(1)}, u32[]{:S(2)}, u32[]{:S(2)}) collective-permute-start(bf16[2,512,512]{2,1,0:T(8,128)(2,1)S(1)} %get-tuple-element.7), channel_id=1, source_target_pairs={{2,0},{3,1},{4,2},{5,3},{6,4},{7,5},{8,6},{9,7},{10,8},{11,9},{12,... | collective-permute-start | bytes 3145736 | tf_op jit(solution)/shard_map/ppermute | solution.py:13
  12.2 33.8 %collective-permute-start.1 = (bf16[2,512,512]{2,1,0:T(8,128)(2,1)S(1)}, bf16[2,512,512]{2,1,0:T(8,128)(2,1)S(1)}, u32[]{:S(2)}, u32[]{:S(2)}) collective-permute-start(bf16[2,512,512]{2,1,0:T(8,128)(2,1)S(1)} %get-tuple-element.8), channel_id=1, source_target_pairs={{1,0},{2,1},{3,2},{4,3},{5,4},{6,5},{7,6},{8,7},{9,8},{10,9},{11,1... | collective-permute-start | bytes 3145736 | tf_op jit(solution)/shard_map/ppermute | solution.py:13
  62.0 6.2 %copy-start.4 = (s32[80]{0:T(128)S(1)}, s32[80]{0:T(128)}, u32[]{:S(2)}) copy-start(s32[80]{0:T(128)} %constant.52) | copy-start | bytes 964
  62.0 102.1 %all-to-all-start = ((bf16[16,2,5,32,512]{4,3,2,1,0:T(8,128)(2,1)}), bf16[16,2,5,32,512]{4,3,2,1,0:T(8,128)(2,1)}, u32[]{:S(2)}, u32[]{:S(2)}) async-start(bf16[16,2,5,32,512]{4,3,2,1,0:T(8,128)(2,1)} %shard_map.82), calls=%async_computation | async-start | bytes 10485760 | tf_op jit(solution)/shard_map/all_to_all | solution.py:133
  172.9 11.9 %copy-start = (s32[2,512]{1,0:T(2,128)S(1)}, s32[2,512]{1,0:T(2,128)}, u32[]{:S(2)}) copy-start(s32[2,512]{1,0:T(2,128)} %param.13) | copy-start | bytes 12292
  172.9 35.0 %copy-start.1 = (s32[512]{0:T(512)S(1)}, s32[512]{0:T(512)}, u32[]{:S(2)}) copy-start(s32[512]{0:T(512)} %param.14) | copy-start | bytes 6148
  175.3 1.8 collective-permute-start.4
  177.1 10.6 %collective-permute-start.5 = (f32[2,80,80]{1,0,2:T(2,128)S(1)}, f32[2,80,80]{1,0,2:T(2,128)S(1)}, u32[]{:S(2)}, u32[]{:S(2)}) collective-permute-start(f32[2,80,80]{1,0,2:T(2,128)S(1)} %bitcast_add_fusion), channel_id=1, source_target_pairs={{0,2},{1,3},{2,0},{3,1},{4,6},{5,7},{6,4},{7,5},{8,10},{9,11},{10,... | collective-permute-start | bytes 153608 | tf_op jit(solution)/shard_map/ppermute | solution.py:93
  187.8 16.6 %collective-permute-start.6 = (f32[2,80,80]{1,0,2:T(2,128)S(1)}, f32[2,80,80]{1,0,2:T(2,128)S(1)}, u32[]{:S(2)}, u32[]{:S(2)}) collective-permute-start(f32[2,80,80]{1,0,2:T(2,128)S(1)} %add.80), channel_id=1, source_target_pairs={{0,4},{1,5},{2,6},{3,7},{4,0},{5,1},{6,2},{7,3},{8,12},{9,13},{10,... | collective-permute-start | bytes 153608 | tf_op jit(solution)/shard_map/ppermute | solution.py:93
  204.5 5.9 %collective-permute-start.7 = (f32[2,80,80]{1,0,2:T(2,128)S(1)}, f32[2,80,80]{1,0,2:T(2,128)S(1)}, u32[]{:S(2)}, u32[]{:S(2)}) collective-permute-start(f32[2,80,80]{1,0,2:T(2,128)S(1)} %add.81), channel_id=1, source_target_pairs={{0,8},{1,9},{2,10},{3,11},{4,12},{5,13},{6,14},{7,15},{8,0},{9,1},... | collective-permute-start | bytes 153608 | tf_op jit(solution)/shard_map/ppermute | solution.py:93

commit v11 on v10

--- a/solution.py
+++ b/solution.py
@@ -35,6 +35,14 @@
     order = tile_pair.shape[-1]
     stacked = tile_pair.reshape(2 * order, order)
     out = jnp.dot(weights, stacked, preferred_element_type=jnp.float32)
+    return out.astype(jnp.bfloat16).reshape(2, order, order)
+
+
+def dress_parts(weights, real, imag):
+    order = real.shape[-1]
+    out = jnp.dot(weights[:, :order], real, preferred_element_type=jnp.float32) + jnp.dot(
+        weights[:, order:], imag, preferred_element_type=jnp.float32
+    )
     return out.astype(jnp.bfloat16).reshape(2, order, order)
 
 
@@ -117,7 +125,7 @@
     received = {}
     for offset in range(1, half_window + 1):
         received[offset] = (
-            shifted(tiles[half_window - offset], "src", -offset),
+            [shifted(tiles[half_window - offset, part], "src", -offset) for part in range(2)],
             shifted(mesons, "src", -offset),
         )
     source_own = dressing_matrix(mesons[0], gamma_order[0], gamma_phase[0])
@@ -127,8 +135,8 @@
     for offset, (tile, partner_mesons) in received.items():
         source_partner = dressing_matrix(partner_mesons[0], gamma_order[0], gamma_phase[0])
         sink_partner = dressing_matrix(partner_mesons[1], gamma_order[1], gamma_phase[1])
-        forwards += [dress(source_own, tiles[half_window + offset]), dress(source_partner, tile)]
-        partners += [dress(sink_partner, tile), dress(sink_own, tiles[half_window + offset])]
+        forwards += [dress(source_own, tiles[half_window + offset]), dress_parts(source_partner, *tile)]
+        partners += [dress_parts(sink_partner, *tile), dress(sink_own, tiles[half_window + offset])]
     loops = rest_loops(forwards, partners, shares)
     slices = lax.all_to_all(loops, "src", split_axis=0, concat_axis=0, tiled=True)
     block_count = slices.shape[0] * slices.shape[2]

time: 212 us -> 215 us (1.014)
    dot_general x0 -> x8, matrix products: none -> 9.75 us  [the longest x4 6.94 us: dress_parts(): jnp.dot(weights[:, :order], real, preferred_element_type=jnp.float32)]
    dot_general x10 -> x6, matrix products: 22.5 us -> 13.4 us  [dress(): out = jnp.dot(weights, stacked, preferred_element_type=jnp.float32)]
    slice x0 -> x1, local copies, waits for them, and re-layouts: none -> 2.23 us  [per_device(): tiles[half_window + offset]]
    ppermute x4 -> x6, starting transfers between devices: 7.86 us -> 9.25 us  [shifted(): return lax.ppermute(block, axis, route)]
    ppermute x4 -> x6, waiting for transfers between devices: 8.63 us -> 8.1 us  [shifted(): return lax.ppermute(block, axis, route)]
  transfers between devices with their start and end apart: 9 -> 11, of which waited for: 7 -> 7; matrix products, arithmetic and copies ran while one was open for 13% -> 15% of each run, Pallas kernels for 0% -> 0%
where the time goes in v11:
time: 215 us
  waiting for transfers between devices  113 us (53%)
  starting transfers between devices  41.6 us (19%)
  matrix products  26.8 us (12%)
  local copies, waits for them, and re-layouts  13.2 us (6%)
  Pallas kernels  11.5 us (5%)
  other arithmetic  8.74 us (4%)
    all_to_all x1, waiting for transfers between devices, per_device(): lax.all_to_all(loops, 'src', split_axis=0, concat_axis=0, tiled=True)  95.9 us
    ppermute x4, starting transfers between devices, all_sum(): table = table + lax.ppermute(table, axis, [(i, i ^ bit) for i in range(n)])  26.2 us
    dot_general x6, matrix products, dress(): out = jnp.dot(weights, stacked, preferred_element_type=jnp.float32)  13.4 us
    pallas_call x1, Pallas kernels, rest_loops(): pl.pallas_call(rest_loop_kernel, grid=(count,), in_specs=[whole] * (2 * c...  11.5 us
    ppermute x6, starting transfers between devices, shifted(): return lax.ppermute(block, axis, route)  9.25 us
    ppermute x4, waiting for transfers between devices, all_sum(): table = table + lax.ppermute(table, axis, [(i, i ^ bit) for i in range(n)])  8.68 us
    ppermute x6, waiting for transfers between devices, shifted(): return lax.ppermute(block, axis, route)  8.1 us
    dot_general x4, matrix products, dress_parts(): jnp.dot(weights[:, :order], real, preferred_element_type=jnp.float32)  6.94 us
  transfers between devices with their start and end apart: 11, of which 7 were waited for; matrix products, arithmetic and copies ran while one was open for 15% of the time, Pallas kernels for 0%

profile of v11, /device:TPU:0, one launch (start us, length us, event | category | flops | bytes accessed | tf_op | source)
XLA Modules:
  0.0 215.0 jit_solution(3291503567648423203)
XLA Ops:
  0.0 0.9 constant_dynamic-update-slice_fusion.1
  0.9 0.9 fusion.48
  1.9 6.1 %collective-permute-start.3 = (bf16[2,2,128,128]{3,2,1,0:T(8,128)(2,1)S(1)}, bf16[2,2,128,128]{3,2,1,0:T(8,128)(2,1)S(1)}, u32[]{:S(2)}, u32[]{:S(2)}) collective-permute-start(bf16[2,2,128,128]{3,2,1,0:T(8,128)(2,1)S(1)} %get-tuple-element.49), channel_id=1, source_target_pairs={{2,0},{3,1},{4,2},{5,3},{6,4},{7,5},{8,6},{9,7},{10,8},{11,9},{12,... | collective-permute-start | bytes 393224 | tf_op jit(solution)/shard_map/ppermute | solution.py:13
  7.9 1.7 slice_bitcast_fusion.1
  9.6 1.1 collective-permute-start.4
  10.7 0.8 collective-permute-start.5
  11.6 2.2 %fusion.47 = (bf16[1,1,2,512,512]{4,3,2,1,0:T(8,128)(2,1)S(1)}, bf16[1,1,2,512,512]{4,3,2,1,0:T(8,128)(2,1)S(1)}, bf16[1,1,2,512,512]{4,3,2,1,0:T(8,128)(2,1)S(1)}) fusion(bf16[1,5,2,512,512]{4,3,2,1,0:T(8,128)(2,1)} %param.8), kind=kLoop, calls=%fused_computation.149 | loop fusion | bytes 6291456 | tf_op jit(solution)/shard_map/slice | solution.py:138
  14.0 1.2 collective-permute-start.1
  15.3 2.3 %negate_convert_fusion = (bf16[4,128,4,128]{3,2,1,0:T(4,128)(2,1)S(1)}, bf16[4,128,4,128]{3,2,1,0:T(4,128)(2,1)S(1)}, bf16[4,128,4,128]{3,2,1,0:T(4,128)(2,1)S(1...) fusion(f32[128,128]{1,0:T(8,128)S(1)} %get-tuple-element.33, ...), kind=kLoop, calls=%fused_computation.37 | loop fusion | flops 7864320 | bytes 5111936 | tf_op jit(solution)/shard_map/convert.5
  17.7 0.1 copy.61
  17.8 0.1 copy.59
  17.9 2.2 %convolution_convert_fusion.1 = bf16[1024,512]{1,0:T(8,128)(2,1)} fusion(bf16[1024,512]{1,0:T(8,128)(2,1)S(1)} %bitcast.237, bf16[512,512]{1,0:T(8,128)(2,1)S(1)} %bitcast.252, bf16[512,512]{1,0:T(8,128)(2,1)S(1)} %bitcast.255, bf16[512,512]{1,0:T(8,128)(2,1)S(1)} %bitcast.258), kind=kOutput, calls=%fused_computation.13 | convolution fusion | flops 1082654720 | bytes 3670016 | tf_op jit(solution)/shard_map/dot_general | solution.py:37
  20.2 2.3 %convolution_convert_fusion = bf16[1024,512]{1,0:T(8,128)(2,1)} fusion(bf16[1024,512]{1,0:T(8,128)(2,1)S(1)} %bitcast.235, bf16[512,512]{1,0:T(8,128)(2,1)S(1)} %bitcast.253, bf16[512,512]{1,0:T(8,128)(2,1)S(1)} %bitcast.256, bf16[512,512]{1,0:T(8,128)(2,1)S(1)} %bitcast.259), kind=kOutput, calls=%fused_computation.12 | convolution fusion | flops 1082654720 | bytes 3670016 | tf_op jit(solution)/shard_map/dot_general | solution.py:37
  22.4 2.3 %negate_convert_fusion.3 = (bf16[4,128,4,128]{3,2,1,0:T(4,128)(2,1)S(1)}, bf16[4,128,4,128]{3,2,1,0:T(4,128)(2,1)S(1)}, bf16[4,128,4,128]{3,2,1,0:T(4,128)(2,1)S...) fusion(f32[128,128]{1,0:T(8,128)S(1)} %get-tuple-element.76, ...), kind=kLoop, calls=%fused_computation.40 | loop fusion | flops 7864320 | bytes 5111936 | tf_op jit(solution)/shard_map/convert.23
  24.8 0.1 copy.70
  24.8 0.1 copy.68
  25.0 2.2 %convolution_convert_fusion.4 = bf16[1024,512]{1,0:T(8,128)(2,1)} fusion(bf16[1024,512]{1,0:T(8,128)(2,1)S(1)} %bitcast.238, bf16[512,512]{1,0:T(8,128)(2,1)S(1)} %bitcast.243, bf16[512,512]{1,0:T(8,128)(2,1)S(1)} %bitcast.246, bf16[512,512]{1,0:T(8,128)(2,1)S(1)} %bitcast.249), kind=kOutput, calls=%fused_computation.16 | convolution fusion | flops 1082654720 | bytes 3670016 | tf_op jit(solution)/shard_map/dot_general | solution.py:37
  27.2 2.3 %convolution_convert_fusion.3 = bf16[1024,512]{1,0:T(8,128)(2,1)} fusion(bf16[1024,512]{1,0:T(8,128)(2,1)S(1)} %bitcast.236, bf16[512,512]{1,0:T(8,128)(2,1)S(1)} %bitcast.244, bf16[512,512]{1,0:T(8,128)(2,1)S(1)} %bitcast.247, bf16[512,512]{1,0:T(8,128)(2,1)S(1)} %bitcast.250), kind=kOutput, calls=%fused_computation.15 | convolution fusion | flops 1082654720 | bytes 3670016 | tf_op jit(solution)/shard_map/dot_general | solution.py:37
  29.6 0.1 copy.53
  29.8 0.1 copy.58
  29.9 0.1 copy.56
  30.0 2.2 %convolution_convert_fusion.2 = bf16[1024,512]{1,0:T(8,128)(2,1)} fusion(bf16[1024,512]{1,0:T(8,128)(2,1)S(1)} %bitcast.233, bf16[512,512]{1,0:T(8,128)(2,1)S(1)} %bitcast.254, bf16[512,512]{1,0:T(8,128)(2,1)S(1)} %bitcast.257, bf16[512,512]{1,0:T(8,128)(2,1)S(1)} %bitcast.260), kind=kOutput, calls=%fused_computation.14 | convolution fusion | flops 1082654720 | bytes 3670016 | tf_op jit(solution)/shard_map/dot_general | solution.py:37
  32.3 0.1 copy.62
  32.4 0.1 copy.64
  32.5 0.1 copy.67
  32.7 0.1 copy.66
  32.8 0.3 maximum_maximum_fusion.5
  33.1 0.3 maximum_maximum_fusion.4
  33.4 0.3 maximum_maximum_fusion.2
  33.7 0.3 maximum_maximum_fusion.1
  34.1 2.2 %convolution_convert_fusion.5 = bf16[1024,512]{1,0:T(8,128)(2,1)} fusion(bf16[1024,512]{1,0:T(8,128)(2,1)S(1)} %bitcast.234, bf16[512,512]{1,0:T(8,128)(2,1)S(1)} %bitcast.245, bf16[512,512]{1,0:T(8,128)(2,1)S(1)} %bitcast.248, bf16[512,512]{1,0:T(8,128)(2,1)S(1)} %bitcast.251), kind=kOutput, calls=%fused_computation.17 | convolution fusion | flops 1082654720 | bytes 3670016 | tf_op jit(solution)/shard_map/dot_general | solution.py:37
  36.3 3.9 %collective-permute-done.2 = bf16[512,512]{1,0:T(8,128)(2,1)S(1)} collective-permute-done((bf16[512,512]{1,0:T(8,128)(2,1)S(1)}, bf16[512,512]{1,0:T(8,128)(2,1)S(1)}, u32[]{:S(2)}, u32[]{:S(2)}) %collective-permute-start.2) | collective-permute-done | bytes 524320 | tf_op jit(solution)/shard_map/ppermute | solution.py:13
  40.2 0.7 fusion.7
  40.9 0.7 fusion.13
  41.6 4.2 %collective-permute-done.1 = bf16[512,512]{1,0:T(8,128)(2,1)S(1)} collective-permute-done((bf16[512,512]{1,0:T(8,128)(2,1)S(1)}, bf16[512,512]{1,0:T(8,128)(2,1)S(1)}, u32[]{:S(2)}, u32[]{:S(2)}) %collective-permute-start.1) | collective-permute-done | bytes 524320 | tf_op jit(solution)/shard_map/ppermute | solution.py:13
  45.8 1.7 add_convert_fusion.1
  47.5 0.7 fusion.4
  48.2 0.7 fusion.10
  48.9 1.8 add_convert_fusion.3
  50.7 1.7 add_convert_fusion
  52.4 1.7 add_convert_fusion.2
  54.2 11.5 %shard_map.82 = bf16[16,2,5,32,512]{4,3,2,1,0:T(8,128)(2,1)} custom-call(bf16[1,2,512,512]{3,2,1,0:T(8,128)(2,1)} %bitcast.270, bf16[1,2,512,512]{3,2,1,0:T(8,128)(2,1)} %bitcast.267, bf16[1,2,512,512]{3,2,1,0:T(8,128)(2,1)} %bitcast.240, bf16[1,2,512,512]{3,2,1,0:T(8,128)(2,1)} %bitcast.268, bf16[1,2,512,512]{3,2,1,0:T(8,128)(2,1)} %bitcast.242, ...), custom_call_target="tpu_custom_call" | custom-call | flops 5368709120 | bytes 15728640 | tf_op jit(solution)/shard_map/pallas_call | solution.py:78
  65.7 6.2 %all-to-all-start = ((bf16[16,2,5,32,512]{4,3,2,1,0:T(8,128)(2,1)}), bf16[16,2,5,32,512]{4,3,2,1,0:T(8,128)(2,1)}, u32[]{:S(2)}, u32[]{:S(2)}) async-start(bf16[16,2,5,32,512]{4,3,2,1,0:T(8,128)(2,1)} %shard_map.82), calls=%async_computation | async-start | bytes 10485760 | tf_op jit(solution)/shard_map/all_to_all | solution.py:141
  71.9 95.9 %all-to-all-done = bf16[16,2,5,32,512]{4,3,2,1,0:T(8,128)(2,1)} async-done(((bf16[16,2,5,32,512]{4,3,2,1,0:T(8,128)(2,1)}), bf16[16,2,5,32,512]{4,3,2,1,0:T(8,128)(2,1)}, u32[]{:S(2)}, u32[]{:S(2)}) %all-to-all-start) | async-done | bytes 5242912 | tf_op jit(solution)/shard_map/all_to_all | solution.py:141
  167.8 3.0 %fusion.46 = (bf16[16,1,5,32,512]{4,3,2,1,0:T(8,128)(2,1)S(1)}, bf16[16,1,5,32,512]{4,3,2,1,0:T(8,128)(2,1)S(1)}) fusion(bf16[16,2,5,32,512]{4,3,2,1,0:T(8,128)(2,1)} %all-to-all-done), kind=kLoop, calls=%fused_computation.148 | loop fusion | bytes 10485760 | tf_op jit(solution)/shard_map/slice | solution.py:144
  170.8 1.6 copy.32
  172.4 1.6 copy.31
  174.1 0.8 fusion.50
  174.9 0.8 fusion.51
  175.7 0.8 fusion.2
  176.6 0.8 fusion.3
  177.5 0.7 gather_fusion
  178.2 0.1 copy.11
  178.3 0.7 gather_fusion.1
  179.0 0.8 collective-permute-start.6
  179.8 0.9 collective-permute-done.6
  180.8 7.7 %collective-permute-start.7 = (f32[2,80,80]{1,0,2:T(2,128)S(1)}, f32[2,80,80]{1,0,2:T(2,128)S(1)}, u32[]{:S(2)}, u32[]{:S(2)}) collective-permute-start(f32[2,80,80]{1,0,2:T(2,128)S(1)} %bitcast_add_fusion), channel_id=1, source_target_pairs={{0,2},{1,3},{2,0},{3,1},{4,6},{5,7},{6,4},{7,5},{8,10},{9,11},{10,... | collective-permute-start | bytes 153608 | tf_op jit(solution)/shard_map/ppermute | solution.py:101
  188.4 3.0 %collective-permute-done.7 = f32[2,80,80]{1,0,2:T(2,128)S(1)} collective-permute-done((f32[2,80,80]{1,0,2:T(2,128)S(1)}, f32[2,80,80]{1,0,2:T(2,128)S(1)}, u32[]{:S(2)}, u32[]{:S(2)}) %collective-permute-start.7) | collective-permute-done | bytes 51232 | tf_op jit(solution)/shard_map/ppermute | solution.py:101
  191.4 14.2 %collective-permute-start.8 = (f32[2,80,80]{1,0,2:T(2,128)S(1)}, f32[2,80,80]{1,0,2:T(2,128)S(1)}, u32[]{:S(2)}, u32[]{:S(2)}) collective-permute-start(f32[2,80,80]{1,0,2:T(2,128)S(1)} %add.96), channel_id=1, source_target_pairs={{0,4},{1,5},{2,6},{3,7},{4,0},{5,1},{6,2},{7,3},{8,12},{9,13},{10,... | collective-permute-start | bytes 153608 | tf_op jit(solution)/shard_map/ppermute | solution.py:101
  205.7 2.4 %collective-permute-done.8 = f32[2,80,80]{1,0,2:T(2,128)S(1)} collective-permute-done((f32[2,80,80]{1,0,2:T(2,128)S(1)}, f32[2,80,80]{1,0,2:T(2,128)S(1)}, u32[]{:S(2)}, u32[]{:S(2)}) %collective-permute-start.8) | collective-permute-done | bytes 51232 | tf_op jit(solution)/shard_map/ppermute | solution.py:101
  208.1 3.5 %collective-permute-start.9 = (f32[2,80,80]{1,0,2:T(2,128)S(1)}, f32[2,80,80]{1,0,2:T(2,128)S(1)}, u32[]{:S(2)}, u32[]{:S(2)}) collective-permute-start(f32[2,80,80]{1,0,2:T(2,128)S(1)} %add.97), channel_id=1, source_target_pairs={{0,8},{1,9},{2,10},{3,11},{4,12},{5,13},{6,14},{7,15},{8,0},{9,1},... | collective-permute-start | bytes 153608 | tf_op jit(solution)/shard_map/ppermute | solution.py:101
  211.6 2.4 %collective-permute-done.9 = f32[2,80,80]{1,0,2:T(2,128)S(1)} collective-permute-done((f32[2,80,80]{1,0,2:T(2,128)S(1)}, f32[2,80,80]{1,0,2:T(2,128)S(1)}, u32[]{:S(2)}, u32[]{:S(2)}) %collective-permute-start.9) | collective-permute-done | bytes 51232 | tf_op jit(solution)/shard_map/ppermute | solution.py:101
  214.1 0.3 fusion.1
  214.4 0.6 broadcast_multiply_fusion
  (42 shorter events, 1.1 us)
Async XLA Ops:
  1.9 12.1 %collective-permute-start.3 = (bf16[2,2,128,128]{3,2,1,0:T(8,128)(2,1)S(1)}, bf16[2,2,128,128]{3,2,1,0:T(8,128)(2,1)S(1)}, u32[]{:S(2)}, u32[]{:S(2)}) collective-permute-start(bf16[2,2,128,128]{3,2,1,0:T(8,128)(2,1)S(1)} %get-tuple-element.49), channel_id=1, source_target_pairs={{2,0},{3,1},{4,2},{5,3},{6,4},{7,5},{8,6},{9,7},{10,8},{11,9},{12,... | collective-permute-start | bytes 393224 | tf_op jit(solution)/shard_map/ppermute | solution.py:13
  7.9 7.3 %collective-permute-start = (bf16[2,2,128,128]{3,2,1,0:T(8,128)(2,1)S(1)}, bf16[2,2,128,128]{3,2,1,0:T(8,128)(2,1)S(1)}, u32[]{:S(2)}, u32[]{:S(2)}) collective-permute-start(bf16[2,2,128,128]{3,2,1,0:T(8,128)(2,1)S(1)} %get-tuple-element.49), channel_id=1, source_target_pairs={{1,0},{2,1},{3,2},{4,3},{5,4},{6,5},{7,6},{8,7},{9,8},{10,9},{11,1... | collective-permute-start | bytes 393224 | tf_op jit(solution)/shard_map/ppermute | solution.py:13
  9.6 41.1 %collective-permute-start.4 = (bf16[512,512]{1,0:T(8,128)(2,1)S(1)}, bf16[512,512]{1,0:T(8,128)(2,1)S(1)}, u32[]{:S(2)}, u32[]{:S(2)}) collective-permute-start(bf16[512,512]{1,0:T(8,128)(2,1)S(1)} %get-tuple-element.7), channel_id=1, source_target_pairs={{2,0},{3,1},{4,2},{5,3},{6,4},{7,5},{8,6},{9,7},{10,8},{11,9},{12,... | collective-permute-start | bytes 1572872 | tf_op jit(solution)/shard_map/ppermute | solution.py:13
  10.7 36.8 %collective-permute-start.5 = (bf16[512,512]{1,0:T(8,128)(2,1)S(1)}, bf16[512,512]{1,0:T(8,128)(2,1)S(1)}, u32[]{:S(2)}, u32[]{:S(2)}) collective-permute-start(bf16[512,512]{1,0:T(8,128)(2,1)S(1)} %get-tuple-element.8), channel_id=1, source_target_pairs={{2,0},{3,1},{4,2},{5,3},{6,4},{7,5},{8,6},{9,7},{10,8},{11,9},{12,... | collective-permute-start | bytes 1572872 | tf_op jit(solution)/shard_map/ppermute | solution.py:13
  11.6 2.3 %copy-start.3 = (s32[2,4]{1,0:T(2,128)S(1)}, s32[2,4]{1,0:T(2,128)}, u32[]{:S(2)}) copy-start(s32[2,4]{1,0:T(2,128)} %param.11) | copy-start | bytes 100
  11.6 2.3 %copy-start.2 = (s32[2,4]{1,0:T(2,128)S(1)}, s32[2,4]{1,0:T(2,128)}, u32[]{:S(2)}) copy-start(s32[2,4]{1,0:T(2,128)} %param.12) | copy-start | bytes 100
  11.6 28.6 %collective-permute-start.2 = (bf16[512,512]{1,0:T(8,128)(2,1)S(1)}, bf16[512,512]{1,0:T(8,128)(2,1)S(1)}, u32[]{:S(2)}, u32[]{:S(2)}) collective-permute-start(bf16[512,512]{1,0:T(8,128)(2,1)S(1)} %get-tuple-element.9), channel_id=1, source_target_pairs={{1,0},{2,1},{3,2},{4,3},{5,4},{6,5},{7,6},{8,7},{9,8},{10,9},{11,1... | collective-permute-start | bytes 1572872 | tf_op jit(solution)/shard_map/ppermute | solution.py:13
  14.0 31.8 %collective-permute-start.1 = (bf16[512,512]{1,0:T(8,128)(2,1)S(1)}, bf16[512,512]{1,0:T(8,128)(2,1)S(1)}, u32[]{:S(2)}, u32[]{:S(2)}) collective-permute-start(bf16[512,512]{1,0:T(8,128)(2,1)S(1)} %get-tuple-element.10), channel_id=1, source_target_pairs={{1,0},{2,1},{3,2},{4,3},{5,4},{6,5},{7,6},{8,7},{9,8},{10,9},{11,1... | collective-permute-start | bytes 1572872 | tf_op jit(solution)/shard_map/ppermute | solution.py:13
  65.7 6.2 %copy-start.4 = (s32[80]{0:T(128)S(1)}, s32[80]{0:T(128)}, u32[]{:S(2)}) copy-start(s32[80]{0:T(128)} %constant.52) | copy-start | bytes 964
  65.7 102.1 %all-to-all-start = ((bf16[16,2,5,32,512]{4,3,2,1,0:T(8,128)(2,1)}), bf16[16,2,5,32,512]{4,3,2,1,0:T(8,128)(2,1)}, u32[]{:S(2)}, u32[]{:S(2)}) async-start(bf16[16,2,5,32,512]{4,3,2,1,0:T(8,128)(2,1)} %shard_map.82), calls=%async_computation | async-start | bytes 10485760 | tf_op jit(solution)/shard_map/all_to_all | solution.py:141
  176.6 11.9 %copy-start = (s32[2,512]{1,0:T(2,128)S(1)}, s32[2,512]{1,0:T(2,128)}, u32[]{:S(2)}) copy-start(s32[2,512]{1,0:T(2,128)} %param.13) | copy-start | bytes 12292
  176.6 35.0 %copy-start.1 = (s32[512]{0:T(512)S(1)}, s32[512]{0:T(512)}, u32[]{:S(2)}) copy-start(s32[512]{0:T(512)} %param.14) | copy-start | bytes 6148
  179.0 1.8 collective-permute-start.6
  180.8 10.6 %collective-permute-start.7 = (f32[2,80,80]{1,0,2:T(2,128)S(1)}, f32[2,80,80]{1,0,2:T(2,128)S(1)}, u32[]{:S(2)}, u32[]{:S(2)}) collective-permute-start(f32[2,80,80]{1,0,2:T(2,128)S(1)} %bitcast_add_fusion), channel_id=1, source_target_pairs={{0,2},{1,3},{2,0},{3,1},{4,6},{5,7},{6,4},{7,5},{8,10},{9,11},{10,... | collective-permute-start | bytes 153608 | tf_op jit(solution)/shard_map/ppermute | solution.py:101
  191.4 16.6 %collective-permute-start.8 = (f32[2,80,80]{1,0,2:T(2,128)S(1)}, f32[2,80,80]{1,0,2:T(2,128)S(1)}, u32[]{:S(2)}, u32[]{:S(2)}) collective-permute-start(f32[2,80,80]{1,0,2:T(2,128)S(1)} %add.96), channel_id=1, source_target_pairs={{0,4},{1,5},{2,6},{3,7},{4,0},{5,1},{6,2},{7,3},{8,12},{9,13},{10,... | collective-permute-start | bytes 153608 | tf_op jit(solution)/shard_map/ppermute | solution.py:101
  208.1 5.9 %collective-permute-start.9 = (f32[2,80,80]{1,0,2:T(2,128)S(1)}, f32[2,80,80]{1,0,2:T(2,128)S(1)}, u32[]{:S(2)}, u32[]{:S(2)}) collective-permute-start(f32[2,80,80]{1,0,2:T(2,128)S(1)} %add.97), channel_id=1, source_target_pairs={{0,8},{1,9},{2,10},{3,11},{4,12},{5,13},{6,14},{7,15},{8,0},{9,1},... | collective-permute-start | bytes 153608 | tf_op jit(solution)/shard_map/ppermute | solution.py:101

commit v12 on v10

--- a/solution.py
+++ b/solution.py
@@ -45,8 +45,9 @@
     bi = backward_ref[0, 1]
     shares = out_ref.shape[0]
     rows = out_ref.shape[3]
-    real = jnp.dot(fr, br, preferred_element_type=jnp.float32) - jnp.dot(fi, bi, preferred_element_type=jnp.float32)
-    imag = jnp.dot(fr, bi, preferred_element_type=jnp.float32) + jnp.dot(fi, br, preferred_element_type=jnp.float32)
+    joined = jnp.concatenate([fr, fi], axis=1)
+    real = jnp.dot(joined, jnp.concatenate([br, -bi], axis=0), preferred_element_type=jnp.float32)
+    imag = jnp.dot(joined, jnp.concatenate([bi, br], axis=0), preferred_element_type=jnp.float32)
     out_ref[:, 0, 0] = real.astype(out_ref.dtype).reshape(shares, rows, real.shape[-1])
     out_ref[:, 1, 0] = imag.astype(out_ref.dtype).reshape(shares, rows, imag.shape[-1])
 

time: 212 us -> 212 us (level)
  no operation moved by 1% of the time
where the time goes in v12:
time: 212 us; the launch traced here: 211 us
  waiting for transfers between devices  113 us (53%)
  starting transfers between devices  40.2 us (19%)
  matrix products  26.1 us (12%)
  local copies, waits for them, and re-layouts  12.4 us (6%)
  Pallas kernels  11.5 us (5%)
  other arithmetic  7.48 us (4%)
    all_to_all x1, waiting for transfers between devices, per_device(): lax.all_to_all(loops, 'src', split_axis=0, concat_axis=0, tiled=True)  95.9 us
    ppermute x4, starting transfers between devices, all_sum(): table = table + lax.ppermute(table, axis, [(i, i ^ bit) for i in range(n)])  26.2 us
    dot_general x10, matrix products, dress(): out = jnp.dot(weights, stacked, preferred_element_type=jnp.float32)  22.5 us
    pallas_call x1, Pallas kernels, rest_loops(): pl.pallas_call(rest_loop_kernel, grid=(count,), in_specs=[whole] * (2 * c...  11.5 us
    ppermute x4, waiting for transfers between devices, all_sum(): table = table + lax.ppermute(table, axis, [(i, i ^ bit) for i in range(n)])  8.68 us
    ppermute x4, waiting for transfers between devices, shifted(): return lax.ppermute(block, axis, route)  8.63 us
    ppermute x4, starting transfers between devices, shifted(): return lax.ppermute(block, axis, route)  7.86 us
    all_to_all x1, starting transfers between devices, per_device(): lax.all_to_all(loops, 'src', split_axis=0, concat_axis=0, tiled=True)  6.16 us
  transfers between devices with their start and end apart: 9, of which 7 were waited for; matrix products, arithmetic and copies ran while one was open for 13% of the time, Pallas kernels for 0%

profile of v12, /device:TPU:0, one launch (start us, length us, event | category | flops | bytes accessed | tf_op | source)
XLA Modules:
  0.0 211.3 jit_solution(4582080544970165767)
XLA Ops:
  0.0 0.9 constant_dynamic-update-slice_fusion.1
  0.9 0.9 fusion.83
  1.9 0.0 copy-start.2
  1.9 0.0 copy-start.3
  1.9 6.1 %collective-permute-start.2 = (bf16[2,2,128,128]{3,2,1,0:T(8,128)(2,1)S(1)}, bf16[2,2,128,128]{3,2,1,0:T(8,128)(2,1)S(1)}, u32[]{:S(2)}, u32[]{:S(2)}) collective-permute-start(bf16[2,2,128,128]{3,2,1,0:T(8,128)(2,1)S(1)} %get-tuple-element.47), channel_id=1, source_target_pairs={{2,0},{3,1},{4,2},{5,3},{6,4},{7,5},{8,6},{9,7},{10,8},{11,9},{12,... | collective-permute-start | bytes 393224 | tf_op jit(solution)/shard_map/ppermute | solution.py:13
  8.0 3.1 %slice_bitcast_fusion = (bf16[2,512,512]{2,1,0:T(8,128)(2,1)S(1)}, bf16[2,512,512]{2,1,0:T(8,128)(2,1)S(1)}, bf16[1,1,2,512,512]{4,3,2,1,0:T(8,128)(2,1)S(1)}, b...) fusion(bf16[1,5,2,512,512]{4,3,2,1,0:T(8,128)(2,1)} %param.8), kind=kLoop, calls=%fused_computation.68 | loop fusion | bytes 10485760 | tf_op jit(solution)/shard_map/squeeze | solution.py:121
  11.0 1.1 collective-permute-start.3
  12.2 0.7 collective-permute-start.1
  12.9 0.1 fusion.65
  13.1 2.3 %negate_convert_fusion = (bf16[4,128,4,128]{3,2,1,0:T(4,128)(2,1)S(1)}, bf16[4,128,4,128]{3,2,1,0:T(4,128)(2,1)S(1)}, bf16[4,128,4,128]{3,2,1,0:T(4,128)(2,1)S(1...) fusion(f32[128,128]{1,0:T(8,128)S(1)} %get-tuple-element.31, ...), kind=kLoop, calls=%fused_computation.53 | loop fusion | flops 7864320 | bytes 5111936 | tf_op jit(solution)/shard_map/convert.5
  15.5 0.1 copy.59
  15.6 0.1 copy.60
  15.6 0.1 copy.61
  15.7 2.3 %convolution_convert_fusion = bf16[1024,512]{1,0:T(8,128)(2,1)} fusion(bf16[1024,512]{1,0:T(8,128)(2,1)S(1)} %bitcast.217, bf16[512,512]{1,0:T(8,128)(2,1)S(1)} %bitcast.225, bf16[512,512]{1,0:T(8,128)(2,1)S(1)} %bitcast.219, bf16[512,512]{1,0:T(8,128)(2,1)S(1)} %bitcast.222), kind=kOutput, calls=%fused_computation.40 | convolution fusion | flops 1082654720 | bytes 3670016 | tf_op jit(solution)/shard_map/dot_general | solution.py:37
  18.0 2.3 %convolution_convert_fusion.1 = bf16[1024,512]{1,0:T(8,128)(2,1)} fusion(bf16[1024,512]{1,0:T(8,128)(2,1)S(1)} %bitcast.215, bf16[512,512]{1,0:T(8,128)(2,1)S(1)} %bitcast.226, bf16[512,512]{1,0:T(8,128)(2,1)S(1)} %bitcast.220, bf16[512,512]{1,0:T(8,128)(2,1)S(1)} %bitcast.223), kind=kOutput, calls=%fused_computation.41 | convolution fusion | flops 1082654720 | bytes 3670016 | tf_op jit(solution)/shard_map/dot_general | solution.py:37
  20.2 2.3 %negate_convert_fusion.3 = (bf16[4,128,4,128]{3,2,1,0:T(4,128)(2,1)S(1)}, bf16[4,128,4,128]{3,2,1,0:T(4,128)(2,1)S(1)}, bf16[4,128,4,128]{3,2,1,0:T(4,128)(2,1)S...) fusion(f32[128,128]{1,0:T(8,128)S(1)} %get-tuple-element.74, ...), kind=kLoop, calls=%fused_computation.56 | loop fusion | flops 7864320 | bytes 5111936 | tf_op jit(solution)/shard_map/convert.23
  22.6 0.1 copy.68
  22.7 0.1 copy.69
  22.8 0.1 copy.70
  22.8 2.3 %convolution_convert_fusion.3 = bf16[1024,512]{1,0:T(8,128)(2,1)} fusion(bf16[1024,512]{1,0:T(8,128)(2,1)S(1)} %bitcast.218, bf16[512,512]{1,0:T(8,128)(2,1)S(1)} %bitcast.246, bf16[512,512]{1,0:T(8,128)(2,1)S(1)} %bitcast.240, bf16[512,512]{1,0:T(8,128)(2,1)S(1)} %bitcast.243), kind=kOutput, calls=%fused_computation.43 | convolution fusion | flops 1082654720 | bytes 3670016 | tf_op jit(solution)/shard_map/dot_general | solution.py:37
  25.2 2.2 %convolution_convert_fusion.4 = bf16[1024,512]{1,0:T(8,128)(2,1)} fusion(bf16[1024,512]{1,0:T(8,128)(2,1)S(1)} %bitcast.216, bf16[512,512]{1,0:T(8,128)(2,1)S(1)} %bitcast.247, bf16[512,512]{1,0:T(8,128)(2,1)S(1)} %bitcast.241, bf16[512,512]{1,0:T(8,128)(2,1)S(1)} %bitcast.244), kind=kOutput, calls=%fused_computation.44 | convolution fusion | flops 1082654720 | bytes 3670016 | tf_op jit(solution)/shard_map/dot_general | solution.py:37
  27.4 2.2 %convolution_convert_fusion.2 = bf16[1024,512]{1,0:T(8,128)(2,1)} fusion(bf16[1024,512]{1,0:T(8,128)(2,1)S(1)} %bitcast.213, bf16[512,512]{1,0:T(8,128)(2,1)S(1)} %bitcast.227, bf16[512,512]{1,0:T(8,128)(2,1)S(1)} %bitcast.221, bf16[512,512]{1,0:T(8,128)(2,1)S(1)} %bitcast.224), kind=kOutput, calls=%fused_computation.42 | convolution fusion | flops 1082654720 | bytes 3670016 | tf_op jit(solution)/shard_map/dot_general | solution.py:37
  29.6 2.2 %convolution_convert_fusion.5 = bf16[1024,512]{1,0:T(8,128)(2,1)} fusion(bf16[1024,512]{1,0:T(8,128)(2,1)S(1)} %bitcast.214, bf16[512,512]{1,0:T(8,128)(2,1)S(1)} %bitcast.248, bf16[512,512]{1,0:T(8,128)(2,1)S(1)} %bitcast.242, bf16[512,512]{1,0:T(8,128)(2,1)S(1)} %bitcast.245), kind=kOutput, calls=%fused_computation.45 | convolution fusion | flops 1082654720 | bytes 3670016 | tf_op jit(solution)/shard_map/dot_general | solution.py:37
  31.8 0.1 copy.53
  31.9 0.1 copy.54
  32.0 0.1 copy.55
  32.1 0.1 copy.56
  32.1 0.1 copy.57
  32.2 0.1 copy.58
  32.3 0.1 copy.62
  32.4 0.1 copy.63
  32.5 0.1 copy.64
  32.6 0.1 copy.65
  32.7 0.1 copy.66
  32.8 0.1 copy.67
  32.8 3.8 %collective-permute-done.3 = bf16[2,512,512]{2,1,0:T(8,128)(2,1)S(1)} collective-permute-done((bf16[2,512,512]{2,1,0:T(8,128)(2,1)S(1)}, bf16[2,512,512]{2,1,0:T(8,128)(2,1)S(1)}, u32[]{:S(2)}, u32[]{:S(2)}) %collective-permute-start.3) | collective-permute-done | bytes 1048608 | tf_op jit(solution)/shard_map/ppermute | solution.py:13
  36.7 2.2 %fusion.32 = bf16[1024,512]{1,0:T(8,128)(2,1)} fusion(bf16[1024,512]{1,0:T(8,128)(2,1)S(1)} %bitcast.255, bf16[512,512]{1,0:T(8,128)(2,1)S(1)} %bitcast.234, bf16[512,512]{1,0:T(8,128)(2,1)S(1)} %bitcast.231, bf16[512,512]{1,0:T(8,128)(2,1)S(1)} %bitcast.232), kind=kOutput, calls=%fused_computation.36 | convolution fusion | flops 1082654720 | bytes 3670016 | tf_op jit(solution)/shard_map/dot_general | solution.py:37
  38.9 2.2 %fusion.38 = bf16[1024,512]{1,0:T(8,128)(2,1)} fusion(bf16[1024,512]{1,0:T(8,128)(2,1)S(1)} %bitcast.256, bf16[512,512]{1,0:T(8,128)(2,1)S(1)} %bitcast.239, bf16[512,512]{1,0:T(8,128)(2,1)S(1)} %bitcast.237, bf16[512,512]{1,0:T(8,128)(2,1)S(1)} %bitcast.238), kind=kOutput, calls=%fused_computation.38 | convolution fusion | flops 1082654720 | bytes 3670016 | tf_op jit(solution)/shard_map/dot_general | solution.py:37
  41.1 4.8 %collective-permute-done.1 = bf16[2,512,512]{2,1,0:T(8,128)(2,1)S(1)} collective-permute-done((bf16[2,512,512]{2,1,0:T(8,128)(2,1)S(1)}, bf16[2,512,512]{2,1,0:T(8,128)(2,1)S(1)}, u32[]{:S(2)}, u32[]{:S(2)}) %collective-permute-start.1) | collective-permute-done | bytes 1048608 | tf_op jit(solution)/shard_map/ppermute | solution.py:13
  45.9 2.3 %fusion.35 = bf16[1024,512]{1,0:T(8,128)(2,1)} fusion(bf16[1024,512]{1,0:T(8,128)(2,1)S(1)} %bitcast.253, bf16[512,512]{1,0:T(8,128)(2,1)S(1)} %bitcast.230, bf16[512,512]{1,0:T(8,128)(2,1)S(1)} %bitcast.228, bf16[512,512]{1,0:T(8,128)(2,1)S(1)} %bitcast.229), kind=kOutput, calls=%fused_computation.37 | convolution fusion | flops 1082654720 | bytes 3670016 | tf_op jit(solution)/shard_map/dot_general | solution.py:37
  48.2 2.3 %fusion.41 = bf16[1024,512]{1,0:T(8,128)(2,1)} fusion(bf16[1024,512]{1,0:T(8,128)(2,1)S(1)} %bitcast.254, bf16[512,512]{1,0:T(8,128)(2,1)S(1)} %bitcast.236, bf16[512,512]{1,0:T(8,128)(2,1)S(1)} %bitcast.233, bf16[512,512]{1,0:T(8,128)(2,1)S(1)} %bitcast.235), kind=kOutput, calls=%fused_computation.39 | convolution fusion | flops 1082654720 | bytes 3670016 | tf_op jit(solution)/shard_map/dot_general | solution.py:37
  50.5 11.5 %shard_map.82 = bf16[16,2,5,32,512]{4,3,2,1,0:T(8,128)(2,1)} custom-call(bf16[1,2,512,512]{3,2,1,0:T(8,128)(2,1)} %bitcast.262, bf16[1,2,512,512]{3,2,1,0:T(8,128)(2,1)} %bitcast.260, bf16[1,2,512,512]{3,2,1,0:T(8,128)(2,1)} %bitcast.266, bf16[1,2,512,512]{3,2,1,0:T(8,128)(2,1)} %bitcast.259, bf16[1,2,512,512]{3,2,1,0:T(8,128)(2,1)} %bitcast.264, ...), custom_call_target="tpu_custom_call" | custom-call | flops 5368709120 | bytes 15728640 | tf_op jit(solution)/shard_map/pallas_call | solution.py:71
  62.0 6.2 %all-to-all-start = ((bf16[16,2,5,32,512]{4,3,2,1,0:T(8,128)(2,1)}), bf16[16,2,5,32,512]{4,3,2,1,0:T(8,128)(2,1)}, u32[]{:S(2)}, u32[]{:S(2)}) async-start(bf16[16,2,5,32,512]{4,3,2,1,0:T(8,128)(2,1)} %shard_map.82), calls=%async_computation | async-start | bytes 10485760 | tf_op jit(solution)/shard_map/all_to_all | solution.py:134
  68.2 95.9 %all-to-all-done = bf16[16,2,5,32,512]{4,3,2,1,0:T(8,128)(2,1)} async-done(((bf16[16,2,5,32,512]{4,3,2,1,0:T(8,128)(2,1)}), bf16[16,2,5,32,512]{4,3,2,1,0:T(8,128)(2,1)}, u32[]{:S(2)}, u32[]{:S(2)}) %all-to-all-start) | async-done | bytes 5242912 | tf_op jit(solution)/shard_map/all_to_all | solution.py:134
  164.1 3.0 %fusion.82 = (bf16[16,1,5,32,512]{4,3,2,1,0:T(8,128)(2,1)S(1)}, bf16[16,1,5,32,512]{4,3,2,1,0:T(8,128)(2,1)S(1)}) fusion(bf16[16,2,5,32,512]{4,3,2,1,0:T(8,128)(2,1)} %all-to-all-done), kind=kLoop, calls=%fused_computation.166 | loop fusion | bytes 10485760 | tf_op jit(solution)/shard_map/slice | solution.py:137
  167.1 1.6 copy.31
  168.8 0.8 fusion.85
  169.6 1.6 copy.32
  171.2 0.8 fusion.86
  172.1 0.8 fusion.47
  172.9 0.8 fusion.46
  173.8 0.7 gather_fusion
  174.5 0.1 copy.11
  174.6 0.7 gather_fusion.1
  175.3 0.8 collective-permute-start.4
  176.1 0.9 collective-permute-done.4
  177.1 7.7 %collective-permute-start.5 = (f32[2,80,80]{1,0,2:T(2,128)S(1)}, f32[2,80,80]{1,0,2:T(2,128)S(1)}, u32[]{:S(2)}, u32[]{:S(2)}) collective-permute-start(f32[2,80,80]{1,0,2:T(2,128)S(1)} %bitcast_add_fusion), channel_id=1, source_target_pairs={{0,2},{1,3},{2,0},{3,1},{4,6},{5,7},{6,4},{7,5},{8,10},{9,11},{10,... | collective-permute-start | bytes 153608 | tf_op jit(solution)/shard_map/ppermute | solution.py:94
  184.8 3.0 %collective-permute-done.5 = f32[2,80,80]{1,0,2:T(2,128)S(1)} collective-permute-done((f32[2,80,80]{1,0,2:T(2,128)S(1)}, f32[2,80,80]{1,0,2:T(2,128)S(1)}, u32[]{:S(2)}, u32[]{:S(2)}) %collective-permute-start.5) | collective-permute-done | bytes 51232 | tf_op jit(solution)/shard_map/ppermute | solution.py:94
  187.8 14.2 %collective-permute-start.6 = (f32[2,80,80]{1,0,2:T(2,128)S(1)}, f32[2,80,80]{1,0,2:T(2,128)S(1)}, u32[]{:S(2)}, u32[]{:S(2)}) collective-permute-start(f32[2,80,80]{1,0,2:T(2,128)S(1)} %add.80), channel_id=1, source_target_pairs={{0,4},{1,5},{2,6},{3,7},{4,0},{5,1},{6,2},{7,3},{8,12},{9,13},{10,... | collective-permute-start | bytes 153608 | tf_op jit(solution)/shard_map/ppermute | solution.py:94
  202.0 2.4 %collective-permute-done.6 = f32[2,80,80]{1,0,2:T(2,128)S(1)} collective-permute-done((f32[2,80,80]{1,0,2:T(2,128)S(1)}, f32[2,80,80]{1,0,2:T(2,128)S(1)}, u32[]{:S(2)}, u32[]{:S(2)}) %collective-permute-start.6) | collective-permute-done | bytes 51232 | tf_op jit(solution)/shard_map/ppermute | solution.py:94
  204.4 3.5 %collective-permute-start.7 = (f32[2,80,80]{1,0,2:T(2,128)S(1)}, f32[2,80,80]{1,0,2:T(2,128)S(1)}, u32[]{:S(2)}, u32[]{:S(2)}) collective-permute-start(f32[2,80,80]{1,0,2:T(2,128)S(1)} %add.81), channel_id=1, source_target_pairs={{0,8},{1,9},{2,10},{3,11},{4,12},{5,13},{6,14},{7,15},{8,0},{9,1},... | collective-permute-start | bytes 153608 | tf_op jit(solution)/shard_map/ppermute | solution.py:94
  208.0 2.4 %collective-permute-done.7 = f32[2,80,80]{1,0,2:T(2,128)S(1)} collective-permute-done((f32[2,80,80]{1,0,2:T(2,128)S(1)}, f32[2,80,80]{1,0,2:T(2,128)S(1)}, u32[]{:S(2)}, u32[]{:S(2)}) %collective-permute-start.7) | collective-permute-done | bytes 51232 | tf_op jit(solution)/shard_map/ppermute | solution.py:94
  210.4 0.3 fusion.45
  210.7 0.6 broadcast_multiply_fusion
  (29 shorter events, 0.4 us)
Async XLA Ops:
  1.9 11.0 %copy-start.2 = (s32[2,4]{1,0:T(2,128)S(1)}, s32[2,4]{1,0:T(2,128)}, u32[]{:S(2)}) copy-start(s32[2,4]{1,0:T(2,128)} %param.12) | copy-start | bytes 100
  1.9 11.0 %copy-start.3 = (s32[2,4]{1,0:T(2,128)S(1)}, s32[2,4]{1,0:T(2,128)}, u32[]{:S(2)}) copy-start(s32[2,4]{1,0:T(2,128)} %param.11) | copy-start | bytes 100
  1.9 11.1 %collective-permute-start.2 = (bf16[2,2,128,128]{3,2,1,0:T(8,128)(2,1)S(1)}, bf16[2,2,128,128]{3,2,1,0:T(8,128)(2,1)S(1)}, u32[]{:S(2)}, u32[]{:S(2)}) collective-permute-start(bf16[2,2,128,128]{3,2,1,0:T(8,128)(2,1)S(1)} %get-tuple-element.47), channel_id=1, source_target_pairs={{2,0},{3,1},{4,2},{5,3},{6,4},{7,5},{8,6},{9,7},{10,8},{11,9},{12,... | collective-permute-start | bytes 393224 | tf_op jit(solution)/shard_map/ppermute | solution.py:13
  8.0 5.1 %collective-permute-start = (bf16[2,2,128,128]{3,2,1,0:T(8,128)(2,1)S(1)}, bf16[2,2,128,128]{3,2,1,0:T(8,128)(2,1)S(1)}, u32[]{:S(2)}, u32[]{:S(2)}) collective-permute-start(bf16[2,2,128,128]{3,2,1,0:T(8,128)(2,1)S(1)} %get-tuple-element.47), channel_id=1, source_target_pairs={{1,0},{2,1},{3,2},{4,3},{5,4},{6,5},{7,6},{8,7},{9,8},{10,9},{11,1... | collective-permute-start | bytes 393224 | tf_op jit(solution)/shard_map/ppermute | solution.py:13
  11.0 25.6 %collective-permute-start.3 = (bf16[2,512,512]{2,1,0:T(8,128)(2,1)S(1)}, bf16[2,512,512]{2,1,0:T(8,128)(2,1)S(1)}, u32[]{:S(2)}, u32[]{:S(2)}) collective-permute-start(bf16[2,512,512]{2,1,0:T(8,128)(2,1)S(1)} %get-tuple-element.7), channel_id=1, source_target_pairs={{2,0},{3,1},{4,2},{5,3},{6,4},{7,5},{8,6},{9,7},{10,8},{11,9},{12,... | collective-permute-start | bytes 3145736 | tf_op jit(solution)/shard_map/ppermute | solution.py:13
  12.2 33.8 %collective-permute-start.1 = (bf16[2,512,512]{2,1,0:T(8,128)(2,1)S(1)}, bf16[2,512,512]{2,1,0:T(8,128)(2,1)S(1)}, u32[]{:S(2)}, u32[]{:S(2)}) collective-permute-start(bf16[2,512,512]{2,1,0:T(8,128)(2,1)S(1)} %get-tuple-element.8), channel_id=1, source_target_pairs={{1,0},{2,1},{3,2},{4,3},{5,4},{6,5},{7,6},{8,7},{9,8},{10,9},{11,1... | collective-permute-start | bytes 3145736 | tf_op jit(solution)/shard_map/ppermute | solution.py:13
  62.0 6.2 %copy-start.4 = (s32[80]{0:T(128)S(1)}, s32[80]{0:T(128)}, u32[]{:S(2)}) copy-start(s32[80]{0:T(128)} %constant.52) | copy-start | bytes 964
  62.0 102.1 %all-to-all-start = ((bf16[16,2,5,32,512]{4,3,2,1,0:T(8,128)(2,1)}), bf16[16,2,5,32,512]{4,3,2,1,0:T(8,128)(2,1)}, u32[]{:S(2)}, u32[]{:S(2)}) async-start(bf16[16,2,5,32,512]{4,3,2,1,0:T(8,128)(2,1)} %shard_map.82), calls=%async_computation | async-start | bytes 10485760 | tf_op jit(solution)/shard_map/all_to_all | solution.py:134
  172.9 11.9 %copy-start = (s32[2,512]{1,0:T(2,128)S(1)}, s32[2,512]{1,0:T(2,128)}, u32[]{:S(2)}) copy-start(s32[2,512]{1,0:T(2,128)} %param.13) | copy-start | bytes 12292
  172.9 35.0 %copy-start.1 = (s32[512]{0:T(512)S(1)}, s32[512]{0:T(512)}, u32[]{:S(2)}) copy-start(s32[512]{0:T(512)} %param.14) | copy-start | bytes 6148
  175.3 1.8 collective-permute-start.4
  177.1 10.6 %collective-permute-start.5 = (f32[2,80,80]{1,0,2:T(2,128)S(1)}, f32[2,80,80]{1,0,2:T(2,128)S(1)}, u32[]{:S(2)}, u32[]{:S(2)}) collective-permute-start(f32[2,80,80]{1,0,2:T(2,128)S(1)} %bitcast_add_fusion), channel_id=1, source_target_pairs={{0,2},{1,3},{2,0},{3,1},{4,6},{5,7},{6,4},{7,5},{8,10},{9,11},{10,... | collective-permute-start | bytes 153608 | tf_op jit(solution)/shard_map/ppermute | solution.py:94
  187.8 16.6 %collective-permute-start.6 = (f32[2,80,80]{1,0,2:T(2,128)S(1)}, f32[2,80,80]{1,0,2:T(2,128)S(1)}, u32[]{:S(2)}, u32[]{:S(2)}) collective-permute-start(f32[2,80,80]{1,0,2:T(2,128)S(1)} %add.80), channel_id=1, source_target_pairs={{0,4},{1,5},{2,6},{3,7},{4,0},{5,1},{6,2},{7,3},{8,12},{9,13},{10,... | collective-permute-start | bytes 153608 | tf_op jit(solution)/shard_map/ppermute | solution.py:94
  204.4 5.9 %collective-permute-start.7 = (f32[2,80,80]{1,0,2:T(2,128)S(1)}, f32[2,80,80]{1,0,2:T(2,128)S(1)}, u32[]{:S(2)}, u32[]{:S(2)}) collective-permute-start(f32[2,80,80]{1,0,2:T(2,128)S(1)} %add.81), channel_id=1, source_target_pairs={{0,8},{1,9},{2,10},{3,11},{4,12},{5,13},{6,14},{7,15},{8,0},{9,1},... | collective-permute-start | bytes 153608 | tf_op jit(solution)/shard_map/ppermute | solution.py:94

commit v13 on v12

--- a/solution.py
+++ b/solution.py
@@ -38,11 +38,7 @@
     return out.astype(jnp.bfloat16).reshape(2, order, order)
 
 
-def loop_kernel(forward_ref, backward_ref, out_ref):
-    fr = forward_ref[0, 0]
-    fi = forward_ref[0, 1]
-    br = backward_ref[0, 0]
-    bi = backward_ref[0, 1]
+def loop_body(fr, fi, br, bi, out_ref):
     shares = out_ref.shape[0]
     rows = out_ref.shape[3]
     joined = jnp.concatenate([fr, fi], axis=1)
@@ -53,32 +49,54 @@
 
 
 def rest_loop_kernel(*refs):
-    count = (len(refs) - 1) // 2
-    forward_refs, partner_refs, out_ref = refs[:count], refs[count:-1], refs[-1]
+    count = (len(refs) - 4) // 2
+    forward_hbm, partner_hbm = refs[:count], refs[count : 2 * count]
+    out_ref, forward_buf, partner_buf, sems = refs[2 * count :]
     step = pl.program_id(0)
+
+    def copies(index):
+        return (
+            pltpu.make_async_copy(forward_hbm[index], forward_buf.at[index], sems.at[0, index]),
+            pltpu.make_async_copy(partner_hbm[index], partner_buf.at[index], sems.at[1, index]),
+        )
+
+    @pl.when(step == 0)
+    def _():
+        for index in range(count):
+            for copy in copies(index):
+                copy.start()
+
     for index in range(count):
 
         @pl.when(step == index)
         def _():
-            loop_kernel(forward_refs[index], partner_refs[index], out_ref)
+            for copy in copies(index):
+                copy.wait()
+            loop_body(
+                forward_buf[index, 0], forward_buf[index, 1], partner_buf[index, 0], partner_buf[index, 1], out_ref
+            )
 
 
 def rest_loops(forwards, partners, shares):
     count = len(forwards)
     _, order, _ = forwards[0].shape
     rows = order // shares
-    whole = pl.BlockSpec((1, 2, order, order), lambda s: (0, 0, 0, 0))
     return pl.pallas_call(
         rest_loop_kernel,
         grid=(count,),
-        in_specs=[whole] * (2 * count),
+        in_specs=[pl.BlockSpec(memory_space=pl.ANY)] * (2 * count),
         out_specs=pl.BlockSpec((shares, 2, 1, rows, order), lambda s: (0, 0, s, 0, 0)),
         out_shape=jax.ShapeDtypeStruct((shares, 2, count, rows, order), jnp.bfloat16),
+        scratch_shapes=[
+            pltpu.VMEM((count, 2, order, order), jnp.bfloat16),
+            pltpu.VMEM((count, 2, order, order), jnp.bfloat16),
+            pltpu.SemaphoreType.DMA((2, count)),
+        ],
         compiler_params=pltpu.CompilerParams(vmem_limit_bytes=56 * 1024 * 1024),
         cost_estimate=pl.CostEstimate(
             flops=8 * count * order ** 3, transcendentals=0, bytes_accessed=6 * count * order * order * 2
         ),
-    )(*[tile[None] for tile in forwards], *[tile[None] for tile in partners])
+    )(*forwards, *partners)
 
 
 def inner_product(left, right):

time: 212 us -> 209 us (0.986)
  Pallas kernels: 11.5 us -> 9.06 us
    pallas_call x1, Pallas kernels: 11.5 us -> 9.06 us  [rest_loops(): pl.pallas_call(rest_loop_kernel, grid=(count,), in_specs=[pl.BlockSpec(me...]
where the time goes in v13:
time: 209 us
  waiting for transfers between devices  113 us (54%)
  starting transfers between devices  40.1 us (19%)
  matrix products  26.1 us (12%)
  local copies, waits for them, and re-layouts  12.4 us (6%)
  Pallas kernels  9.06 us (4%)
  other arithmetic  7.48 us (4%)
    all_to_all x1, waiting for transfers between devices, per_device(): lax.all_to_all(loops, 'src', split_axis=0, concat_axis=0, tiled=True)  95.9 us
    ppermute x4, starting transfers between devices, all_sum(): table = table + lax.ppermute(table, axis, [(i, i ^ bit) for i in range(n)])  26.2 us
    dot_general x10, matrix products, dress(): out = jnp.dot(weights, stacked, preferred_element_type=jnp.float32)  22.5 us
    pallas_call x1, Pallas kernels, rest_loops(): pl.pallas_call(rest_loop_kernel, grid=(count,), in_specs=[pl.BlockSpec(me...  9.06 us
    ppermute x4, waiting for transfers between devices, all_sum(): table = table + lax.ppermute(table, axis, [(i, i ^ bit) for i in range(n)])  8.68 us
    ppermute x4, waiting for transfers between devices, shifted(): return lax.ppermute(block, axis, route)  8.63 us
    ppermute x4, starting transfers between devices, shifted(): return lax.ppermute(block, axis, route)  7.86 us
    all_to_all x1, starting transfers between devices, per_device(): lax.all_to_all(loops, 'src', split_axis=0, concat_axis=0, tiled=True)  6.04 us
  transfers between devices with their start and end apart: 9, of which 7 were waited for; matrix products, arithmetic and copies ran while one was open for 13% of the time, Pallas kernels for 0%

profile of v13, /device:TPU:0, one launch (start us, length us, event | category | flops | bytes accessed | tf_op | source)
XLA Modules:
  0.0 208.8 jit_solution(17002305338312124591)
XLA Ops:
  0.0 0.9 constant_dynamic-update-slice_fusion.1
  0.9 0.9 fusion.83
  1.9 0.0 copy-start.2
  1.9 6.1 %collective-permute-start.2 = (bf16[2,2,128,128]{3,2,1,0:T(8,128)(2,1)S(1)}, bf16[2,2,128,128]{3,2,1,0:T(8,128)(2,1)S(1)}, u32[]{:S(2)}, u32[]{:S(2)}) collective-permute-start(bf16[2,2,128,128]{3,2,1,0:T(8,128)(2,1)S(1)} %get-tuple-element.47), channel_id=1, source_target_pairs={{2,0},{3,1},{4,2},{5,3},{6,4},{7,5},{8,6},{9,7},{10,8},{11,9},{12,... | collective-permute-start | bytes 393224 | tf_op jit(solution)/shard_map/ppermute | solution.py:13
  8.0 3.1 %slice_bitcast_fusion = (bf16[2,512,512]{2,1,0:T(8,128)(2,1)S(1)}, bf16[2,512,512]{2,1,0:T(8,128)(2,1)S(1)}, bf16[1,1,2,512,512]{4,3,2,1,0:T(8,128)(2,1)S(1)}, b...) fusion(bf16[1,5,2,512,512]{4,3,2,1,0:T(8,128)(2,1)} %param.8), kind=kLoop, calls=%fused_computation.68 | loop fusion | bytes 10485760 | tf_op jit(solution)/shard_map/squeeze | solution.py:139
  11.0 1.1 collective-permute-start.3
  12.2 0.7 collective-permute-start.1
  12.9 0.1 fusion.65
  13.1 2.3 %negate_convert_fusion = (bf16[4,128,4,128]{3,2,1,0:T(4,128)(2,1)S(1)}, bf16[4,128,4,128]{3,2,1,0:T(4,128)(2,1)S(1)}, bf16[4,128,4,128]{3,2,1,0:T(4,128)(2,1)S(1...) fusion(f32[128,128]{1,0:T(8,128)S(1)} %get-tuple-element.31, ...), kind=kLoop, calls=%fused_computation.53 | loop fusion | flops 7864320 | bytes 5111936 | tf_op jit(solution)/shard_map/convert.5
  15.5 0.1 copy.59
  15.6 0.1 copy.60
  15.6 0.1 copy.61
  15.7 2.3 %convolution_convert_fusion = bf16[1024,512]{1,0:T(8,128)(2,1)} fusion(bf16[1024,512]{1,0:T(8,128)(2,1)S(1)} %bitcast.217, bf16[512,512]{1,0:T(8,128)(2,1)S(1)} %bitcast.225, bf16[512,512]{1,0:T(8,128)(2,1)S(1)} %bitcast.219, bf16[512,512]{1,0:T(8,128)(2,1)S(1)} %bitcast.222), kind=kOutput, calls=%fused_computation.40 | convolution fusion | flops 1082654720 | bytes 3670016 | tf_op jit(solution)/shard_map/dot_general | solution.py:37
  18.0 2.3 %convolution_convert_fusion.1 = bf16[1024,512]{1,0:T(8,128)(2,1)} fusion(bf16[1024,512]{1,0:T(8,128)(2,1)S(1)} %bitcast.215, bf16[512,512]{1,0:T(8,128)(2,1)S(1)} %bitcast.226, bf16[512,512]{1,0:T(8,128)(2,1)S(1)} %bitcast.220, bf16[512,512]{1,0:T(8,128)(2,1)S(1)} %bitcast.223), kind=kOutput, calls=%fused_computation.41 | convolution fusion | flops 1082654720 | bytes 3670016 | tf_op jit(solution)/shard_map/dot_general | solution.py:37
  20.2 2.3 %negate_convert_fusion.3 = (bf16[4,128,4,128]{3,2,1,0:T(4,128)(2,1)S(1)}, bf16[4,128,4,128]{3,2,1,0:T(4,128)(2,1)S(1)}, bf16[4,128,4,128]{3,2,1,0:T(4,128)(2,1)S...) fusion(f32[128,128]{1,0:T(8,128)S(1)} %get-tuple-element.74, ...), kind=kLoop, calls=%fused_computation.56 | loop fusion | flops 7864320 | bytes 5111936 | tf_op jit(solution)/shard_map/convert.23
  22.6 0.1 copy.68
  22.7 0.1 copy.69
  22.8 0.1 copy.70
  22.8 2.3 %convolution_convert_fusion.3 = bf16[1024,512]{1,0:T(8,128)(2,1)} fusion(bf16[1024,512]{1,0:T(8,128)(2,1)S(1)} %bitcast.218, bf16[512,512]{1,0:T(8,128)(2,1)S(1)} %bitcast.246, bf16[512,512]{1,0:T(8,128)(2,1)S(1)} %bitcast.240, bf16[512,512]{1,0:T(8,128)(2,1)S(1)} %bitcast.243), kind=kOutput, calls=%fused_computation.43 | convolution fusion | flops 1082654720 | bytes 3670016 | tf_op jit(solution)/shard_map/dot_general | solution.py:37
  25.2 2.2 %convolution_convert_fusion.4 = bf16[1024,512]{1,0:T(8,128)(2,1)} fusion(bf16[1024,512]{1,0:T(8,128)(2,1)S(1)} %bitcast.216, bf16[512,512]{1,0:T(8,128)(2,1)S(1)} %bitcast.247, bf16[512,512]{1,0:T(8,128)(2,1)S(1)} %bitcast.241, bf16[512,512]{1,0:T(8,128)(2,1)S(1)} %bitcast.244), kind=kOutput, calls=%fused_computation.44 | convolution fusion | flops 1082654720 | bytes 3670016 | tf_op jit(solution)/shard_map/dot_general | solution.py:37
  27.4 2.2 %convolution_convert_fusion.2 = bf16[1024,512]{1,0:T(8,128)(2,1)} fusion(bf16[1024,512]{1,0:T(8,128)(2,1)S(1)} %bitcast.213, bf16[512,512]{1,0:T(8,128)(2,1)S(1)} %bitcast.227, bf16[512,512]{1,0:T(8,128)(2,1)S(1)} %bitcast.221, bf16[512,512]{1,0:T(8,128)(2,1)S(1)} %bitcast.224), kind=kOutput, calls=%fused_computation.42 | convolution fusion | flops 1082654720 | bytes 3670016 | tf_op jit(solution)/shard_map/dot_general | solution.py:37
  29.6 2.2 %convolution_convert_fusion.5 = bf16[1024,512]{1,0:T(8,128)(2,1)} fusion(bf16[1024,512]{1,0:T(8,128)(2,1)S(1)} %bitcast.214, bf16[512,512]{1,0:T(8,128)(2,1)S(1)} %bitcast.248, bf16[512,512]{1,0:T(8,128)(2,1)S(1)} %bitcast.242, bf16[512,512]{1,0:T(8,128)(2,1)S(1)} %bitcast.245), kind=kOutput, calls=%fused_computation.45 | convolution fusion | flops 1082654720 | bytes 3670016 | tf_op jit(solution)/shard_map/dot_general | solution.py:37
  31.8 0.1 copy.53
  31.9 0.1 copy.54
  32.0 0.1 copy.55
  32.1 0.1 copy.56
  32.1 0.1 copy.57
  32.2 0.1 copy.58
  32.3 0.1 copy.62
  32.4 0.1 copy.63
  32.5 0.1 copy.64
  32.6 0.1 copy.65
  32.7 0.1 copy.66
  32.8 0.1 copy.67
  32.8 3.8 %collective-permute-done.3 = bf16[2,512,512]{2,1,0:T(8,128)(2,1)S(1)} collective-permute-done((bf16[2,512,512]{2,1,0:T(8,128)(2,1)S(1)}, bf16[2,512,512]{2,1,0:T(8,128)(2,1)S(1)}, u32[]{:S(2)}, u32[]{:S(2)}) %collective-permute-start.3) | collective-permute-done | bytes 1048608 | tf_op jit(solution)/shard_map/ppermute | solution.py:13
  36.7 2.2 %fusion.32 = bf16[1024,512]{1,0:T(8,128)(2,1)} fusion(bf16[1024,512]{1,0:T(8,128)(2,1)S(1)} %bitcast.255, bf16[512,512]{1,0:T(8,128)(2,1)S(1)} %bitcast.234, bf16[512,512]{1,0:T(8,128)(2,1)S(1)} %bitcast.231, bf16[512,512]{1,0:T(8,128)(2,1)S(1)} %bitcast.232), kind=kOutput, calls=%fused_computation.36 | convolution fusion | flops 1082654720 | bytes 3670016 | tf_op jit(solution)/shard_map/dot_general | solution.py:37
  38.9 2.2 %fusion.38 = bf16[1024,512]{1,0:T(8,128)(2,1)} fusion(bf16[1024,512]{1,0:T(8,128)(2,1)S(1)} %bitcast.256, bf16[512,512]{1,0:T(8,128)(2,1)S(1)} %bitcast.239, bf16[512,512]{1,0:T(8,128)(2,1)S(1)} %bitcast.237, bf16[512,512]{1,0:T(8,128)(2,1)S(1)} %bitcast.238), kind=kOutput, calls=%fused_computation.38 | convolution fusion | flops 1082654720 | bytes 3670016 | tf_op jit(solution)/shard_map/dot_general | solution.py:37
  41.1 4.8 %collective-permute-done.1 = bf16[2,512,512]{2,1,0:T(8,128)(2,1)S(1)} collective-permute-done((bf16[2,512,512]{2,1,0:T(8,128)(2,1)S(1)}, bf16[2,512,512]{2,1,0:T(8,128)(2,1)S(1)}, u32[]{:S(2)}, u32[]{:S(2)}) %collective-permute-start.1) | collective-permute-done | bytes 1048608 | tf_op jit(solution)/shard_map/ppermute | solution.py:13
  45.9 2.3 %fusion.35 = bf16[1024,512]{1,0:T(8,128)(2,1)} fusion(bf16[1024,512]{1,0:T(8,128)(2,1)S(1)} %bitcast.253, bf16[512,512]{1,0:T(8,128)(2,1)S(1)} %bitcast.230, bf16[512,512]{1,0:T(8,128)(2,1)S(1)} %bitcast.228, bf16[512,512]{1,0:T(8,128)(2,1)S(1)} %bitcast.229), kind=kOutput, calls=%fused_computation.37 | convolution fusion | flops 1082654720 | bytes 3670016 | tf_op jit(solution)/shard_map/dot_general | solution.py:37
  48.2 2.3 %fusion.41 = bf16[1024,512]{1,0:T(8,128)(2,1)} fusion(bf16[1024,512]{1,0:T(8,128)(2,1)S(1)} %bitcast.254, bf16[512,512]{1,0:T(8,128)(2,1)S(1)} %bitcast.236, bf16[512,512]{1,0:T(8,128)(2,1)S(1)} %bitcast.233, bf16[512,512]{1,0:T(8,128)(2,1)S(1)} %bitcast.235), kind=kOutput, calls=%fused_computation.39 | convolution fusion | flops 1082654720 | bytes 3670016 | tf_op jit(solution)/shard_map/dot_general | solution.py:37
  50.5 9.1 %shard_map.82 = bf16[16,2,5,32,512]{4,3,2,1,0:T(8,128)(2,1)} custom-call(bf16[2,512,512]{2,1,0:T(8,128)(2,1)} %bitcast.262, bf16[2,512,512]{2,1,0:T(8,128)(2,1)} %bitcast.260, bf16[2,512,512]{2,1,0:T(8,128)(2,1)} %bitcast.266, bf16[2,512,512]{2,1,0:T(8,128)(2,1)} %bitcast.259, bf16[2,512,512]{2,1,0:T(8,128)(2,1)} %bitcast.264, ...), custom_call_target="tpu_custom_call" | custom-call | flops 5368709120 | bytes 15728640 | tf_op jit(solution)/shard_map/pallas_call | solution.py:84
  59.6 0.0 copy-start.4
  59.6 6.0 %all-to-all-start = ((bf16[16,2,5,32,512]{4,3,2,1,0:T(8,128)(2,1)}), bf16[16,2,5,32,512]{4,3,2,1,0:T(8,128)(2,1)}, u32[]{:S(2)}, u32[]{:S(2)}) async-start(bf16[16,2,5,32,512]{4,3,2,1,0:T(8,128)(2,1)} %shard_map.82), calls=%async_computation | async-start | bytes 10485760 | tf_op jit(solution)/shard_map/all_to_all | solution.py:152
  65.7 95.9 %all-to-all-done = bf16[16,2,5,32,512]{4,3,2,1,0:T(8,128)(2,1)} async-done(((bf16[16,2,5,32,512]{4,3,2,1,0:T(8,128)(2,1)}), bf16[16,2,5,32,512]{4,3,2,1,0:T(8,128)(2,1)}, u32[]{:S(2)}, u32[]{:S(2)}) %all-to-all-start) | async-done | bytes 5242912 | tf_op jit(solution)/shard_map/all_to_all | solution.py:152
  161.6 3.0 %fusion.82 = (bf16[16,1,5,32,512]{4,3,2,1,0:T(8,128)(2,1)S(1)}, bf16[16,1,5,32,512]{4,3,2,1,0:T(8,128)(2,1)S(1)}) fusion(bf16[16,2,5,32,512]{4,3,2,1,0:T(8,128)(2,1)} %all-to-all-done), kind=kLoop, calls=%fused_computation.166 | loop fusion | bytes 10485760 | tf_op jit(solution)/shard_map/slice | solution.py:155
  164.6 1.6 copy.31
  166.2 0.8 fusion.85
  167.0 1.6 copy.32
  168.7 0.8 fusion.86
  169.5 0.8 fusion.47
  170.4 0.8 fusion.46
  171.3 0.7 gather_fusion
  172.0 0.1 copy.11
  172.1 0.7 gather_fusion.1
  172.8 0.8 collective-permute-start.4
  173.6 0.9 collective-permute-done.4
  174.6 7.6 %collective-permute-start.5 = (f32[2,80,80]{1,0,2:T(2,128)S(1)}, f32[2,80,80]{1,0,2:T(2,128)S(1)}, u32[]{:S(2)}, u32[]{:S(2)}) collective-permute-start(f32[2,80,80]{1,0,2:T(2,128)S(1)} %bitcast_add_fusion), channel_id=1, source_target_pairs={{0,2},{1,3},{2,0},{3,1},{4,6},{5,7},{6,4},{7,5},{8,10},{9,11},{10,... | collective-permute-start | bytes 153608 | tf_op jit(solution)/shard_map/ppermute | solution.py:112
  182.2 3.0 %collective-permute-done.5 = f32[2,80,80]{1,0,2:T(2,128)S(1)} collective-permute-done((f32[2,80,80]{1,0,2:T(2,128)S(1)}, f32[2,80,80]{1,0,2:T(2,128)S(1)}, u32[]{:S(2)}, u32[]{:S(2)}) %collective-permute-start.5) | collective-permute-done | bytes 51232 | tf_op jit(solution)/shard_map/ppermute | solution.py:112
  185.2 14.2 %collective-permute-start.6 = (f32[2,80,80]{1,0,2:T(2,128)S(1)}, f32[2,80,80]{1,0,2:T(2,128)S(1)}, u32[]{:S(2)}, u32[]{:S(2)}) collective-permute-start(f32[2,80,80]{1,0,2:T(2,128)S(1)} %add.80), channel_id=1, source_target_pairs={{0,4},{1,5},{2,6},{3,7},{4,0},{5,1},{6,2},{7,3},{8,12},{9,13},{10,... | collective-permute-start | bytes 153608 | tf_op jit(solution)/shard_map/ppermute | solution.py:112
  199.5 2.4 %collective-permute-done.6 = f32[2,80,80]{1,0,2:T(2,128)S(1)} collective-permute-done((f32[2,80,80]{1,0,2:T(2,128)S(1)}, f32[2,80,80]{1,0,2:T(2,128)S(1)}, u32[]{:S(2)}, u32[]{:S(2)}) %collective-permute-start.6) | collective-permute-done | bytes 51232 | tf_op jit(solution)/shard_map/ppermute | solution.py:112
  201.9 3.5 %collective-permute-start.7 = (f32[2,80,80]{1,0,2:T(2,128)S(1)}, f32[2,80,80]{1,0,2:T(2,128)S(1)}, u32[]{:S(2)}, u32[]{:S(2)}) collective-permute-start(f32[2,80,80]{1,0,2:T(2,128)S(1)} %add.81), channel_id=1, source_target_pairs={{0,8},{1,9},{2,10},{3,11},{4,12},{5,13},{6,14},{7,15},{8,0},{9,1},... | collective-permute-start | bytes 153608 | tf_op jit(solution)/shard_map/ppermute | solution.py:112
  205.4 2.4 %collective-permute-done.7 = f32[2,80,80]{1,0,2:T(2,128)S(1)} collective-permute-done((f32[2,80,80]{1,0,2:T(2,128)S(1)}, f32[2,80,80]{1,0,2:T(2,128)S(1)}, u32[]{:S(2)}, u32[]{:S(2)}) %collective-permute-start.7) | collective-permute-done | bytes 51232 | tf_op jit(solution)/shard_map/ppermute | solution.py:112
  207.9 0.3 fusion.45
  208.2 0.6 broadcast_multiply_fusion
  (29 shorter events, 0.4 us)
Async XLA Ops:
  1.9 11.0 %copy-start.2 = (s32[2,4]{1,0:T(2,128)S(1)}, s32[2,4]{1,0:T(2,128)}, u32[]{:S(2)}) copy-start(s32[2,4]{1,0:T(2,128)} %param.12) | copy-start | bytes 100
  1.9 11.0 %copy-start.3 = (s32[2,4]{1,0:T(2,128)S(1)}, s32[2,4]{1,0:T(2,128)}, u32[]{:S(2)}) copy-start(s32[2,4]{1,0:T(2,128)} %param.11) | copy-start | bytes 100
  1.9 11.1 %collective-permute-start.2 = (bf16[2,2,128,128]{3,2,1,0:T(8,128)(2,1)S(1)}, bf16[2,2,128,128]{3,2,1,0:T(8,128)(2,1)S(1)}, u32[]{:S(2)}, u32[]{:S(2)}) collective-permute-start(bf16[2,2,128,128]{3,2,1,0:T(8,128)(2,1)S(1)} %get-tuple-element.47), channel_id=1, source_target_pairs={{2,0},{3,1},{4,2},{5,3},{6,4},{7,5},{8,6},{9,7},{10,8},{11,9},{12,... | collective-permute-start | bytes 393224 | tf_op jit(solution)/shard_map/ppermute | solution.py:13
  8.0 5.1 %collective-permute-start = (bf16[2,2,128,128]{3,2,1,0:T(8,128)(2,1)S(1)}, bf16[2,2,128,128]{3,2,1,0:T(8,128)(2,1)S(1)}, u32[]{:S(2)}, u32[]{:S(2)}) collective-permute-start(bf16[2,2,128,128]{3,2,1,0:T(8,128)(2,1)S(1)} %get-tuple-element.47), channel_id=1, source_target_pairs={{1,0},{2,1},{3,2},{4,3},{5,4},{6,5},{7,6},{8,7},{9,8},{10,9},{11,1... | collective-permute-start | bytes 393224 | tf_op jit(solution)/shard_map/ppermute | solution.py:13
  11.0 25.6 %collective-permute-start.3 = (bf16[2,512,512]{2,1,0:T(8,128)(2,1)S(1)}, bf16[2,512,512]{2,1,0:T(8,128)(2,1)S(1)}, u32[]{:S(2)}, u32[]{:S(2)}) collective-permute-start(bf16[2,512,512]{2,1,0:T(8,128)(2,1)S(1)} %get-tuple-element.7), channel_id=1, source_target_pairs={{2,0},{3,1},{4,2},{5,3},{6,4},{7,5},{8,6},{9,7},{10,8},{11,9},{12,... | collective-permute-start | bytes 3145736 | tf_op jit(solution)/shard_map/ppermute | solution.py:13
  12.2 33.8 %collective-permute-start.1 = (bf16[2,512,512]{2,1,0:T(8,128)(2,1)S(1)}, bf16[2,512,512]{2,1,0:T(8,128)(2,1)S(1)}, u32[]{:S(2)}, u32[]{:S(2)}) collective-permute-start(bf16[2,512,512]{2,1,0:T(8,128)(2,1)S(1)} %get-tuple-element.8), channel_id=1, source_target_pairs={{1,0},{2,1},{3,2},{4,3},{5,4},{6,5},{7,6},{8,7},{9,8},{10,9},{11,1... | collective-permute-start | bytes 3145736 | tf_op jit(solution)/shard_map/ppermute | solution.py:13
  59.6 6.1 %copy-start.4 = (s32[80]{0:T(128)S(1)}, s32[80]{0:T(128)}, u32[]{:S(2)}) copy-start(s32[80]{0:T(128)} %constant.52) | copy-start | bytes 964
  59.6 102.0 %all-to-all-start = ((bf16[16,2,5,32,512]{4,3,2,1,0:T(8,128)(2,1)}), bf16[16,2,5,32,512]{4,3,2,1,0:T(8,128)(2,1)}, u32[]{:S(2)}, u32[]{:S(2)}) async-start(bf16[16,2,5,32,512]{4,3,2,1,0:T(8,128)(2,1)} %shard_map.82), calls=%async_computation | async-start | bytes 10485760 | tf_op jit(solution)/shard_map/all_to_all | solution.py:152
  170.4 11.9 %copy-start = (s32[2,512]{1,0:T(2,128)S(1)}, s32[2,512]{1,0:T(2,128)}, u32[]{:S(2)}) copy-start(s32[2,512]{1,0:T(2,128)} %param.13) | copy-start | bytes 12292
  170.4 35.0 %copy-start.1 = (s32[512]{0:T(512)S(1)}, s32[512]{0:T(512)}, u32[]{:S(2)}) copy-start(s32[512]{0:T(512)} %param.14) | copy-start | bytes 6148
  172.8 1.8 collective-permute-start.4
  174.6 10.6 %collective-permute-start.5 = (f32[2,80,80]{1,0,2:T(2,128)S(1)}, f32[2,80,80]{1,0,2:T(2,128)S(1)}, u32[]{:S(2)}, u32[]{:S(2)}) collective-permute-start(f32[2,80,80]{1,0,2:T(2,128)S(1)} %bitcast_add_fusion), channel_id=1, source_target_pairs={{0,2},{1,3},{2,0},{3,1},{4,6},{5,7},{6,4},{7,5},{8,10},{9,11},{10,... | collective-permute-start | bytes 153608 | tf_op jit(solution)/shard_map/ppermute | solution.py:112
  185.2 16.6 %collective-permute-start.6 = (f32[2,80,80]{1,0,2:T(2,128)S(1)}, f32[2,80,80]{1,0,2:T(2,128)S(1)}, u32[]{:S(2)}, u32[]{:S(2)}) collective-permute-start(f32[2,80,80]{1,0,2:T(2,128)S(1)} %add.80), channel_id=1, source_target_pairs={{0,4},{1,5},{2,6},{3,7},{4,0},{5,1},{6,2},{7,3},{8,12},{9,13},{10,... | collective-permute-start | bytes 153608 | tf_op jit(solution)/shard_map/ppermute | solution.py:112
  201.9 5.9 %collective-permute-start.7 = (f32[2,80,80]{1,0,2:T(2,128)S(1)}, f32[2,80,80]{1,0,2:T(2,128)S(1)}, u32[]{:S(2)}, u32[]{:S(2)}) collective-permute-start(f32[2,80,80]{1,0,2:T(2,128)S(1)} %add.81), channel_id=1, source_target_pairs={{0,8},{1,9},{2,10},{3,11},{4,12},{5,13},{6,14},{7,15},{8,0},{9,1},... | collective-permute-start | bytes 153608 | tf_op jit(solution)/shard_map/ppermute | solution.py:112

commit v14 on v13

--- a/solution.py
+++ b/solution.py
@@ -38,20 +38,23 @@
     return out.astype(jnp.bfloat16).reshape(2, order, order)
 
 
-def loop_body(fr, fi, br, bi, out_ref):
-    shares = out_ref.shape[0]
-    rows = out_ref.shape[3]
+def loop_body(fr, fi, br, bi, out_refs):
+    shares = out_refs[0].shape[0]
+    rows = out_refs[0].shape[3]
     joined = jnp.concatenate([fr, fi], axis=1)
     real = jnp.dot(joined, jnp.concatenate([br, -bi], axis=0), preferred_element_type=jnp.float32)
     imag = jnp.dot(joined, jnp.concatenate([bi, br], axis=0), preferred_element_type=jnp.float32)
-    out_ref[:, 0, 0] = real.astype(out_ref.dtype).reshape(shares, rows, real.shape[-1])
-    out_ref[:, 1, 0] = imag.astype(out_ref.dtype).reshape(shares, rows, imag.shape[-1])
+    real = real.astype(jnp.bfloat16).reshape(shares, len(out_refs), rows, real.shape[-1])
+    imag = imag.astype(jnp.bfloat16).reshape(shares, len(out_refs), rows, imag.shape[-1])
+    for half, out_ref in enumerate(out_refs):
+        out_ref[:, 0, 0] = real[:, half]
+        out_ref[:, 1, 0] = imag[:, half]
 
 
 def rest_loop_kernel(*refs):
-    count = (len(refs) - 4) // 2
+    count = (len(refs) - 5) // 2
     forward_hbm, partner_hbm = refs[:count], refs[count : 2 * count]
-    out_ref, forward_buf, partner_buf, sems = refs[2 * count :]
+    out_refs, (forward_buf, partner_buf, sems) = refs[2 * count : 2 * count + 2], refs[2 * count + 2 :]
     step = pl.program_id(0)
 
     def copies(index):
@@ -73,20 +76,21 @@
             for copy in copies(index):
                 copy.wait()
             loop_body(
-                forward_buf[index, 0], forward_buf[index, 1], partner_buf[index, 0], partner_buf[index, 1], out_ref
+                forward_buf[index, 0], forward_buf[index, 1], partner_buf[index, 0], partner_buf[index, 1], out_refs
             )
 
 
 def rest_loops(forwards, partners, shares):
     count = len(forwards)
     _, order, _ = forwards[0].shape
-    rows = order // shares
+    rows = order // shares // 2
+    half = jax.ShapeDtypeStruct((shares, 2, count, rows, order), jnp.bfloat16)
     return pl.pallas_call(
         rest_loop_kernel,
         grid=(count,),
         in_specs=[pl.BlockSpec(memory_space=pl.ANY)] * (2 * count),
-        out_specs=pl.BlockSpec((shares, 2, 1, rows, order), lambda s: (0, 0, s, 0, 0)),
-        out_shape=jax.ShapeDtypeStruct((shares, 2, count, rows, order), jnp.bfloat16),
+        out_specs=[pl.BlockSpec((shares, 2, 1, rows, order), lambda s: (0, 0, s, 0, 0))] * 2,
+        out_shape=[half, half],
         scratch_shapes=[
             pltpu.VMEM((count, 2, order, order), jnp.bfloat16),
             pltpu.VMEM((count, 2, order, order), jnp.bfloat16),
@@ -148,17 +152,18 @@
         sink_partner = dressing_matrix(partner_mesons[1], gamma_order[1], gamma_phase[1])
         forwards += [dress(source_own, tiles[half_window + offset]), dress(source_partner, tile)]
         partners += [dress(sink_partner, tile), dress(sink_own, tiles[half_window + offset])]
-    loops = rest_loops(forwards, partners, shares)
-    slices = lax.all_to_all(loops, "src", split_axis=0, concat_axis=0, tiled=True)
-    block_count = slices.shape[0] * slices.shape[2]
-    real_flat = slices[:, 0].reshape(block_count, -1)
-    imag_flat = slices[:, 1].reshape(block_count, -1)
-    trace_table = jnp.stack(
-        [
-            inner_product(real_flat, real_flat) - inner_product(imag_flat, imag_flat),
-            inner_product(real_flat, imag_flat) + inner_product(imag_flat, real_flat),
-        ]
-    )
+    trace_table = 0
+    for loops in rest_loops(forwards, partners, shares):
+        slices = lax.all_to_all(loops, "src", split_axis=0, concat_axis=0, tiled=True)
+        block_count = slices.shape[0] * slices.shape[2]
+        real_flat = slices[:, 0].reshape(block_count, -1)
+        imag_flat = slices[:, 1].reshape(block_count, -1)
+        trace_table = trace_table + jnp.stack(
+            [
+                inner_product(real_flat, real_flat) - inner_product(imag_flat, imag_flat),
+                inner_product(real_flat, imag_flat) + inner_product(imag_flat, real_flat),
+            ]
+        )
     place = np.zeros(block_count, np.int32)
     for source in range(shares):
         place[source * window + half_window] = source * window

time: 209 us -> 211 us (level)
  blocking collectives: 0 us -> 64.6 us
  waiting for transfers between devices: 113 us -> 62 us
  starting transfers between devices: 40.1 us -> 28.8 us
    all_to_all x0 -> x1, blocking collectives: none -> 64.6 us  [per_device(): lax.all_to_all(loops, 'src', split_axis=0, concat_axis=0, tiled=True)]
    all_to_all x1, waiting for transfers between devices: 95.9 us -> 44.7 us  [per_device(): lax.all_to_all(loops, 'src', split_axis=0, concat_axis=0, tiled=True)]
    ppermute x4, starting transfers between devices: 26.2 us -> 15.7 us  [all_sum(): table = table + lax.ppermute(table, axis, [(i, i ^ bit) for i in range(n)])]
    unnamed x30 -> x32, local copies, waits for them, and re-layouts: 4.75 us -> 4.63 us
    another operation x3 -> x2, other arithmetic: 4.68 us -> 4.67 us
  transfers between devices with their start and end apart: 9 -> 9, of which waited for: 7 -> 7; matrix products, arithmetic and copies ran while one was open for 13% -> 16% of each run, Pallas kernels for 0% -> 0%
where the time goes in v14:
time: 211 us
  blocking collectives  64.6 us (31%)
  waiting for transfers between devices  62 us (29%)
  starting transfers between devices  28.8 us (14%)
  matrix products  26.7 us (13%)
  local copies, waits for them, and re-layouts  11.5 us (5%)
  Pallas kernels  9.14 us (4%)
  other arithmetic  7.49 us (4%)
    all_to_all x1, blocking collectives, per_device(): lax.all_to_all(loops, 'src', split_axis=0, concat_axis=0, tiled=True)  64.6 us
    all_to_all x1, waiting for transfers between devices, per_device(): lax.all_to_all(loops, 'src', split_axis=0, concat_axis=0, tiled=True)  44.7 us
    dot_general x10, matrix products, dress(): out = jnp.dot(weights, stacked, preferred_element_type=jnp.float32)  22.5 us
    ppermute x4, starting transfers between devices, all_sum(): table = table + lax.ppermute(table, axis, [(i, i ^ bit) for i in range(n)])  15.7 us
    pallas_call x1, Pallas kernels, rest_loops(): pl.pallas_call(rest_loop_kernel, grid=(count,), in_specs=[pl.BlockSpec(me...  9.14 us
    ppermute x4, waiting for transfers between devices, all_sum(): table = table + lax.ppermute(table, axis, [(i, i ^ bit) for i in range(n)])  8.68 us
    ppermute x4, waiting for transfers between devices, shifted(): return lax.ppermute(block, axis, route)  8.65 us
    ppermute x4, starting transfers between devices, shifted(): return lax.ppermute(block, axis, route)  7.86 us
  transfers between devices with their start and end apart: 9, of which 7 were waited for; matrix products, arithmetic and copies ran while one was open for 16% of the time, Pallas kernels for 0%

profile of v14, /device:TPU:0, one launch (start us, length us, event | category | flops | bytes accessed | tf_op | source)
XLA Modules:
  0.0 210.7 jit_solution(12181354546412863352)
XLA Ops:
  0.0 0.9 constant_dynamic-update-slice_fusion.1
  0.9 0.9 fusion.86
  1.9 6.1 %collective-permute-start.2 = (bf16[2,2,128,128]{3,2,1,0:T(8,128)(2,1)S(1)}, bf16[2,2,128,128]{3,2,1,0:T(8,128)(2,1)S(1)}, u32[]{:S(2)}, u32[]{:S(2)}) collective-permute-start(bf16[2,2,128,128]{3,2,1,0:T(8,128)(2,1)S(1)} %get-tuple-element.53), channel_id=1, source_target_pairs={{2,0},{3,1},{4,2},{5,3},{6,4},{7,5},{8,6},{9,7},{10,8},{11,9},{12,... | collective-permute-start | bytes 393224 | tf_op jit(solution)/shard_map/ppermute | solution.py:13
  8.0 3.1 %slice_bitcast_fusion = (bf16[2,512,512]{2,1,0:T(8,128)(2,1)S(1)}, bf16[2,512,512]{2,1,0:T(8,128)(2,1)S(1)}, bf16[1,1,2,512,512]{4,3,2,1,0:T(8,128)(2,1)S(1)}, b...) fusion(bf16[1,5,2,512,512]{4,3,2,1,0:T(8,128)(2,1)} %param.8), kind=kLoop, calls=%fused_computation.72 | loop fusion | bytes 10485760 | tf_op jit(solution)/shard_map/squeeze | solution.py:143
  11.0 1.1 collective-permute-start.3
  12.2 0.7 collective-permute-start.1
  13.1 2.3 %negate_convert_fusion = (bf16[4,128,4,128]{3,2,1,0:T(4,128)(2,1)S(1)}, bf16[4,128,4,128]{3,2,1,0:T(4,128)(2,1)S(1)}, bf16[4,128,4,128]{3,2,1,0:T(4,128)(2,1)S(1...) fusion(f32[128,128]{1,0:T(8,128)S(1)} %get-tuple-element.37, ...), kind=kLoop, calls=%fused_computation.57 | loop fusion | flops 7864320 | bytes 5111936 | tf_op jit(solution)/shard_map/convert.5
  15.5 0.1 copy.61
  15.6 0.1 copy.62
  15.7 2.3 %convolution_convert_fusion = bf16[1024,512]{1,0:T(8,128)(2,1)} fusion(bf16[1024,512]{1,0:T(8,128)(2,1)S(1)} %bitcast.243, bf16[512,512]{1,0:T(8,128)(2,1)S(1)} %bitcast.251, bf16[512,512]{1,0:T(8,128)(2,1)S(1)} %bitcast.245, bf16[512,512]{1,0:T(8,128)(2,1)S(1)} %bitcast.248), kind=kOutput, calls=%fused_computation.40 | convolution fusion | flops 1082654720 | bytes 3670016 | tf_op jit(solution)/shard_map/dot_general | solution.py:37
  18.0 2.3 %convolution_convert_fusion.1 = bf16[1024,512]{1,0:T(8,128)(2,1)} fusion(bf16[1024,512]{1,0:T(8,128)(2,1)S(1)} %bitcast.241, bf16[512,512]{1,0:T(8,128)(2,1)S(1)} %bitcast.252, bf16[512,512]{1,0:T(8,128)(2,1)S(1)} %bitcast.246, bf16[512,512]{1,0:T(8,128)(2,1)S(1)} %bitcast.249), kind=kOutput, calls=%fused_computation.41 | convolution fusion | flops 1082654720 | bytes 3670016 | tf_op jit(solution)/shard_map/dot_general | solution.py:37
  20.2 2.3 %negate_convert_fusion.3 = (bf16[4,128,4,128]{3,2,1,0:T(4,128)(2,1)S(1)}, bf16[4,128,4,128]{3,2,1,0:T(4,128)(2,1)S(1)}, bf16[4,128,4,128]{3,2,1,0:T(4,128)(2,1)S...) fusion(f32[128,128]{1,0:T(8,128)S(1)} %get-tuple-element.80, ...), kind=kLoop, calls=%fused_computation.60 | loop fusion | flops 7864320 | bytes 5111936 | tf_op jit(solution)/shard_map/convert.23
  22.6 0.1 copy.70
  22.7 0.1 copy.71
  22.8 2.3 %convolution_convert_fusion.3 = bf16[1024,512]{1,0:T(8,128)(2,1)} fusion(bf16[1024,512]{1,0:T(8,128)(2,1)S(1)} %bitcast.244, bf16[512,512]{1,0:T(8,128)(2,1)S(1)} %bitcast.272, bf16[512,512]{1,0:T(8,128)(2,1)S(1)} %bitcast.266, bf16[512,512]{1,0:T(8,128)(2,1)S(1)} %bitcast.269), kind=kOutput, calls=%fused_computation.43 | convolution fusion | flops 1082654720 | bytes 3670016 | tf_op jit(solution)/shard_map/dot_general | solution.py:37
  25.1 2.2 %convolution_convert_fusion.4 = bf16[1024,512]{1,0:T(8,128)(2,1)} fusion(bf16[1024,512]{1,0:T(8,128)(2,1)S(1)} %bitcast.242, bf16[512,512]{1,0:T(8,128)(2,1)S(1)} %bitcast.273, bf16[512,512]{1,0:T(8,128)(2,1)S(1)} %bitcast.267, bf16[512,512]{1,0:T(8,128)(2,1)S(1)} %bitcast.270), kind=kOutput, calls=%fused_computation.44 | convolution fusion | flops 1082654720 | bytes 3670016 | tf_op jit(solution)/shard_map/dot_general | solution.py:37
  27.3 2.2 %convolution_convert_fusion.2 = bf16[1024,512]{1,0:T(8,128)(2,1)} fusion(bf16[1024,512]{1,0:T(8,128)(2,1)S(1)} %bitcast.239, bf16[512,512]{1,0:T(8,128)(2,1)S(1)} %bitcast.253, bf16[512,512]{1,0:T(8,128)(2,1)S(1)} %bitcast.247, bf16[512,512]{1,0:T(8,128)(2,1)S(1)} %bitcast.250), kind=kOutput, calls=%fused_computation.42 | convolution fusion | flops 1082654720 | bytes 3670016 | tf_op jit(solution)/shard_map/dot_general | solution.py:37
  29.6 2.2 %convolution_convert_fusion.5 = bf16[1024,512]{1,0:T(8,128)(2,1)} fusion(bf16[1024,512]{1,0:T(8,128)(2,1)S(1)} %bitcast.240, bf16[512,512]{1,0:T(8,128)(2,1)S(1)} %bitcast.274, bf16[512,512]{1,0:T(8,128)(2,1)S(1)} %bitcast.268, bf16[512,512]{1,0:T(8,128)(2,1)S(1)} %bitcast.271), kind=kOutput, calls=%fused_computation.45 | convolution fusion | flops 1082654720 | bytes 3670016 | tf_op jit(solution)/shard_map/dot_general | solution.py:37
  31.9 0.1 copy.56
  31.9 0.1 copy.57
  32.0 0.1 copy.58
  32.1 0.1 copy.59
  32.3 0.1 copy.64
  32.5 0.1 copy.66
  32.6 0.1 copy.67
  32.6 0.1 copy.68
  32.7 0.1 copy.69
  32.8 3.8 %collective-permute-done.3 = bf16[2,512,512]{2,1,0:T(8,128)(2,1)S(1)} collective-permute-done((bf16[2,512,512]{2,1,0:T(8,128)(2,1)S(1)}, bf16[2,512,512]{2,1,0:T(8,128)(2,1)S(1)}, u32[]{:S(2)}, u32[]{:S(2)}) %collective-permute-start.3) | collective-permute-done | bytes 1048608 | tf_op jit(solution)/shard_map/ppermute | solution.py:13
  36.7 2.2 %fusion.32 = bf16[1024,512]{1,0:T(8,128)(2,1)} fusion(bf16[1024,512]{1,0:T(8,128)(2,1)S(1)} %bitcast.281, bf16[512,512]{1,0:T(8,128)(2,1)S(1)} %bitcast.260, bf16[512,512]{1,0:T(8,128)(2,1)S(1)} %bitcast.257, bf16[512,512]{1,0:T(8,128)(2,1)S(1)} %bitcast.258), kind=kOutput, calls=%fused_computation.36 | convolution fusion | flops 1082654720 | bytes 3670016 | tf_op jit(solution)/shard_map/dot_general | solution.py:37
  38.9 2.2 %fusion.38 = bf16[1024,512]{1,0:T(8,128)(2,1)} fusion(bf16[1024,512]{1,0:T(8,128)(2,1)S(1)} %bitcast.282, bf16[512,512]{1,0:T(8,128)(2,1)S(1)} %bitcast.265, bf16[512,512]{1,0:T(8,128)(2,1)S(1)} %bitcast.263, bf16[512,512]{1,0:T(8,128)(2,1)S(1)} %bitcast.264), kind=kOutput, calls=%fused_computation.38 | convolution fusion | flops 1082654720 | bytes 3670016 | tf_op jit(solution)/shard_map/dot_general | solution.py:37
  41.1 4.8 %collective-permute-done.1 = bf16[2,512,512]{2,1,0:T(8,128)(2,1)S(1)} collective-permute-done((bf16[2,512,512]{2,1,0:T(8,128)(2,1)S(1)}, bf16[2,512,512]{2,1,0:T(8,128)(2,1)S(1)}, u32[]{:S(2)}, u32[]{:S(2)}) %collective-permute-start.1) | collective-permute-done | bytes 1048608 | tf_op jit(solution)/shard_map/ppermute | solution.py:13
  45.9 2.3 %fusion.35 = bf16[1024,512]{1,0:T(8,128)(2,1)} fusion(bf16[1024,512]{1,0:T(8,128)(2,1)S(1)} %bitcast.279, bf16[512,512]{1,0:T(8,128)(2,1)S(1)} %bitcast.256, bf16[512,512]{1,0:T(8,128)(2,1)S(1)} %bitcast.254, bf16[512,512]{1,0:T(8,128)(2,1)S(1)} %bitcast.255), kind=kOutput, calls=%fused_computation.37 | convolution fusion | flops 1082654720 | bytes 3670016 | tf_op jit(solution)/shard_map/dot_general | solution.py:37
  48.2 2.3 %fusion.41 = bf16[1024,512]{1,0:T(8,128)(2,1)} fusion(bf16[1024,512]{1,0:T(8,128)(2,1)S(1)} %bitcast.280, bf16[512,512]{1,0:T(8,128)(2,1)S(1)} %bitcast.262, bf16[512,512]{1,0:T(8,128)(2,1)S(1)} %bitcast.259, bf16[512,512]{1,0:T(8,128)(2,1)S(1)} %bitcast.261), kind=kOutput, calls=%fused_computation.39 | convolution fusion | flops 1082654720 | bytes 3670016 | tf_op jit(solution)/shard_map/dot_general | solution.py:37
  50.5 9.1 %shard_map.82 = (bf16[16,2,5,16,512]{4,3,2,1,0:T(8,128)(2,1)}, bf16[16,2,5,16,512]{4,3,2,1,0:T(8,128)(2,1)}) custom-call(bf16[2,512,512]{2,1,0:T(8,128)(2,1)} %bitcast.288, bf16[2,512,512]{2,1,0:T(8,128)(2,1)} %bitcast.286, bf16[2,512,512]{2,1,0:T(8,128)(2,1)} %bitcast.292, bf16[2,512,512]{2,1,0:T(8,128)(2,1)} %bitcast.285, bf16[2,512,512]{2,1,0:T(8,128)(2,1)} %bitcast.290, ...), custom_call_target="tpu_custom_call" | custom-call | flops 5368709120 | bytes 15728640 | tf_op jit(solution)/shard_map/pallas_call | solution.py:88
  59.7 64.6 %all_to_all.10 = bf16[16,2,5,16,512]{4,3,2,1,0:T(8,128)(2,1)} all-to-all(bf16[16,2,5,16,512]{4,3,2,1,0:T(8,128)(2,1)} %get-tuple-element.8), channel_id=1, replica_groups=mesh['groups'=2,'src'=16] {'src'}, dimensions={0} | all-to-all | bytes 5242880 | tf_op jit(solution)/shard_map/all_to_all | solution.py:157
  124.3 5.3 %all-to-all-start = ((bf16[16,2,5,16,512]{4,3,2,1,0:T(8,128)(2,1)}), bf16[16,2,5,16,512]{4,3,2,1,0:T(8,128)(2,1)S(1)}, u32[]{:S(2)}, u32[]{:S(2)}) async-start(bf16[16,2,5,16,512]{4,3,2,1,0:T(8,128)(2,1)} %get-tuple-element.7), calls=%async_computation | async-start | bytes 5242880 | tf_op jit(solution)/shard_map/all_to_all | solution.py:157
  129.6 2.0 fusion.84
  131.6 0.8 copy.33
  132.4 0.8 copy.34
  133.2 0.5 fusion.90
  133.7 0.5 fusion.47
  134.2 0.5 fusion.91
  134.7 0.5 fusion.46
  135.2 44.7 %all-to-all-done = bf16[16,2,5,16,512]{4,3,2,1,0:T(8,128)(2,1)S(1)} async-done(((bf16[16,2,5,16,512]{4,3,2,1,0:T(8,128)(2,1)}), bf16[16,2,5,16,512]{4,3,2,1,0:T(8,128)(2,1)S(1)}, u32[]{:S(2)}, u32[]{:S(2)}) %all-to-all-start) | async-done | bytes 2621472 | tf_op jit(solution)/shard_map/all_to_all | solution.py:157
  179.8 0.2 fusion.85
  180.1 0.8 copy.31
  180.9 0.5 fusion.88
  181.4 0.8 copy.32
  182.2 0.5 fusion.89
  182.7 0.5 fusion.49
  183.2 0.5 fusion.48
  183.8 0.7 gather_fusion
  184.4 0.1 copy.11
  184.6 0.7 gather_fusion.1
  185.2 0.8 collective-permute-start.4
  186.1 0.9 collective-permute-done.4
  187.0 4.1 %collective-permute-start.5 = (f32[2,80,80]{1,0,2:T(2,128)S(1)}, f32[2,80,80]{1,0,2:T(2,128)S(1)}, u32[]{:S(2)}, u32[]{:S(2)}) collective-permute-start(f32[2,80,80]{1,0,2:T(2,128)S(1)} %bitcast_add_fusion), channel_id=1, source_target_pairs={{0,2},{1,3},{2,0},{3,1},{4,6},{5,7},{6,4},{7,5},{8,10},{9,11},{10,... | collective-permute-start | bytes 153608 | tf_op jit(solution)/shard_map/ppermute | solution.py:116
  191.2 3.0 %collective-permute-done.5 = f32[2,80,80]{1,0,2:T(2,128)S(1)} collective-permute-done((f32[2,80,80]{1,0,2:T(2,128)S(1)}, f32[2,80,80]{1,0,2:T(2,128)S(1)}, u32[]{:S(2)}, u32[]{:S(2)}) %collective-permute-start.5) | collective-permute-done | bytes 51232 | tf_op jit(solution)/shard_map/ppermute | solution.py:116
  194.2 7.2 %collective-permute-start.6 = (f32[2,80,80]{1,0,2:T(2,128)S(1)}, f32[2,80,80]{1,0,2:T(2,128)S(1)}, u32[]{:S(2)}, u32[]{:S(2)}) collective-permute-start(f32[2,80,80]{1,0,2:T(2,128)S(1)} %add.88), channel_id=1, source_target_pairs={{0,4},{1,5},{2,6},{3,7},{4,0},{5,1},{6,2},{7,3},{8,12},{9,13},{10,... | collective-permute-start | bytes 153608 | tf_op jit(solution)/shard_map/ppermute | solution.py:116
  201.4 2.4 %collective-permute-done.6 = f32[2,80,80]{1,0,2:T(2,128)S(1)} collective-permute-done((f32[2,80,80]{1,0,2:T(2,128)S(1)}, f32[2,80,80]{1,0,2:T(2,128)S(1)}, u32[]{:S(2)}, u32[]{:S(2)}) %collective-permute-start.6) | collective-permute-done | bytes 51232 | tf_op jit(solution)/shard_map/ppermute | solution.py:116
  203.8 3.5 %collective-permute-start.7 = (f32[2,80,80]{1,0,2:T(2,128)S(1)}, f32[2,80,80]{1,0,2:T(2,128)S(1)}, u32[]{:S(2)}, u32[]{:S(2)}) collective-permute-start(f32[2,80,80]{1,0,2:T(2,128)S(1)} %add.89), channel_id=1, source_target_pairs={{0,8},{1,9},{2,10},{3,11},{4,12},{5,13},{6,14},{7,15},{8,0},{9,1},... | collective-permute-start | bytes 153608 | tf_op jit(solution)/shard_map/ppermute | solution.py:116
  207.4 2.4 %collective-permute-done.7 = f32[2,80,80]{1,0,2:T(2,128)S(1)} collective-permute-done((f32[2,80,80]{1,0,2:T(2,128)S(1)}, f32[2,80,80]{1,0,2:T(2,128)S(1)}, u32[]{:S(2)}, u32[]{:S(2)}) %collective-permute-start.7) | collective-permute-done | bytes 51232 | tf_op jit(solution)/shard_map/ppermute | solution.py:116
  209.8 0.3 fusion.45
  210.1 0.6 broadcast_multiply_fusion
  (37 shorter events, 0.9 us)
Async XLA Ops:
  1.9 11.0 %copy-start.2 = (s32[2,4]{1,0:T(2,128)S(1)}, s32[2,4]{1,0:T(2,128)}, u32[]{:S(2)}) copy-start(s32[2,4]{1,0:T(2,128)} %param.12) | copy-start | bytes 100
  1.9 11.0 %copy-start.3 = (s32[2,4]{1,0:T(2,128)S(1)}, s32[2,4]{1,0:T(2,128)}, u32[]{:S(2)}) copy-start(s32[2,4]{1,0:T(2,128)} %param.11) | copy-start | bytes 100
  1.9 11.1 %collective-permute-start.2 = (bf16[2,2,128,128]{3,2,1,0:T(8,128)(2,1)S(1)}, bf16[2,2,128,128]{3,2,1,0:T(8,128)(2,1)S(1)}, u32[]{:S(2)}, u32[]{:S(2)}) collective-permute-start(bf16[2,2,128,128]{3,2,1,0:T(8,128)(2,1)S(1)} %get-tuple-element.53), channel_id=1, source_target_pairs={{2,0},{3,1},{4,2},{5,3},{6,4},{7,5},{8,6},{9,7},{10,8},{11,9},{12,... | collective-permute-start | bytes 393224 | tf_op jit(solution)/shard_map/ppermute | solution.py:13
  8.0 5.1 %collective-permute-start = (bf16[2,2,128,128]{3,2,1,0:T(8,128)(2,1)S(1)}, bf16[2,2,128,128]{3,2,1,0:T(8,128)(2,1)S(1)}, u32[]{:S(2)}, u32[]{:S(2)}) collective-permute-start(bf16[2,2,128,128]{3,2,1,0:T(8,128)(2,1)S(1)} %get-tuple-element.53), channel_id=1, source_target_pairs={{1,0},{2,1},{3,2},{4,3},{5,4},{6,5},{7,6},{8,7},{9,8},{10,9},{11,1... | collective-permute-start | bytes 393224 | tf_op jit(solution)/shard_map/ppermute | solution.py:13
  11.0 25.6 %collective-permute-start.3 = (bf16[2,512,512]{2,1,0:T(8,128)(2,1)S(1)}, bf16[2,512,512]{2,1,0:T(8,128)(2,1)S(1)}, u32[]{:S(2)}, u32[]{:S(2)}) collective-permute-start(bf16[2,512,512]{2,1,0:T(8,128)(2,1)S(1)} %get-tuple-element.9), channel_id=1, source_target_pairs={{2,0},{3,1},{4,2},{5,3},{6,4},{7,5},{8,6},{9,7},{10,8},{11,9},{12,... | collective-permute-start | bytes 3145736 | tf_op jit(solution)/shard_map/ppermute | solution.py:13
  12.2 33.8 %collective-permute-start.1 = (bf16[2,512,512]{2,1,0:T(8,128)(2,1)S(1)}, bf16[2,512,512]{2,1,0:T(8,128)(2,1)S(1)}, u32[]{:S(2)}, u32[]{:S(2)}) collective-permute-start(bf16[2,512,512]{2,1,0:T(8,128)(2,1)S(1)} %get-tuple-element.10), channel_id=1, source_target_pairs={{1,0},{2,1},{3,2},{4,3},{5,4},{6,5},{7,6},{8,7},{9,8},{10,9},{11,1... | collective-permute-start | bytes 3145736 | tf_op jit(solution)/shard_map/ppermute | solution.py:13
  124.3 5.3 %copy-start.4 = (s32[80]{0:T(128)S(1)}, s32[80]{0:T(128)}, u32[]{:S(2)}) copy-start(s32[80]{0:T(128)} %constant.52) | copy-start | bytes 964
  124.3 55.5 %all-to-all-start = ((bf16[16,2,5,16,512]{4,3,2,1,0:T(8,128)(2,1)}), bf16[16,2,5,16,512]{4,3,2,1,0:T(8,128)(2,1)S(1)}, u32[]{:S(2)}, u32[]{:S(2)}) async-start(bf16[16,2,5,16,512]{4,3,2,1,0:T(8,128)(2,1)} %get-tuple-element.7), calls=%async_computation | async-start | bytes 5242880 | tf_op jit(solution)/shard_map/all_to_all | solution.py:157
  183.2 8.0 %copy-start = (s32[2,512]{1,0:T(2,128)S(1)}, s32[2,512]{1,0:T(2,128)}, u32[]{:S(2)}) copy-start(s32[2,512]{1,0:T(2,128)} %param.13) | copy-start | bytes 12292
  183.2 24.2 %copy-start.1 = (s32[512]{0:T(512)S(1)}, s32[512]{0:T(512)}, u32[]{:S(2)}) copy-start(s32[512]{0:T(512)} %param.14) | copy-start | bytes 6148
  185.2 1.8 collective-permute-start.4
  187.0 7.1 %collective-permute-start.5 = (f32[2,80,80]{1,0,2:T(2,128)S(1)}, f32[2,80,80]{1,0,2:T(2,128)S(1)}, u32[]{:S(2)}, u32[]{:S(2)}) collective-permute-start(f32[2,80,80]{1,0,2:T(2,128)S(1)} %bitcast_add_fusion), channel_id=1, source_target_pairs={{0,2},{1,3},{2,0},{3,1},{4,6},{5,7},{6,4},{7,5},{8,10},{9,11},{10,... | collective-permute-start | bytes 153608 | tf_op jit(solution)/shard_map/ppermute | solution.py:116
  194.2 9.6 %collective-permute-start.6 = (f32[2,80,80]{1,0,2:T(2,128)S(1)}, f32[2,80,80]{1,0,2:T(2,128)S(1)}, u32[]{:S(2)}, u32[]{:S(2)}) collective-permute-start(f32[2,80,80]{1,0,2:T(2,128)S(1)} %add.88), channel_id=1, source_target_pairs={{0,4},{1,5},{2,6},{3,7},{4,0},{5,1},{6,2},{7,3},{8,12},{9,13},{10,... | collective-permute-start | bytes 153608 | tf_op jit(solution)/shard_map/ppermute | solution.py:116
  203.8 5.9 %collective-permute-start.7 = (f32[2,80,80]{1,0,2:T(2,128)S(1)}, f32[2,80,80]{1,0,2:T(2,128)S(1)}, u32[]{:S(2)}, u32[]{:S(2)}) collective-permute-start(f32[2,80,80]{1,0,2:T(2,128)S(1)} %add.89), channel_id=1, source_target_pairs={{0,8},{1,9},{2,10},{3,11},{4,12},{5,13},{6,14},{7,15},{8,0},{9,1},... | collective-permute-start | bytes 153608 | tf_op jit(solution)/shard_map/ppermute | solution.py:116

commit v15 on v13

--- a/solution.py
+++ b/solution.py
@@ -1,3 +1,5 @@
+import functools
+
 import jax
 import numpy as np
 import jax.numpy as jnp
@@ -48,10 +50,9 @@
     out_ref[:, 1, 0] = imag.astype(out_ref.dtype).reshape(shares, rows, imag.shape[-1])
 
 
-def rest_loop_kernel(*refs):
-    count = (len(refs) - 4) // 2
+def rest_loop_kernel(count, *refs):
     forward_hbm, partner_hbm = refs[:count], refs[count : 2 * count]
-    out_ref, forward_buf, partner_buf, sems = refs[2 * count :]
+    out_ref, forward_buf, partner_buf, sems = refs[-4:]
     step = pl.program_id(0)
 
     def copies(index):
@@ -77,26 +78,28 @@
             )
 
 
-def rest_loops(forwards, partners, shares):
+def rest_loops(forwards, partners, shares, total, first_slot, into=None):
     count = len(forwards)
     _, order, _ = forwards[0].shape
     rows = order // shares
+    operands = [*forwards, *partners] + ([] if into is None else [into])
     return pl.pallas_call(
-        rest_loop_kernel,
+        functools.partial(rest_loop_kernel, count),
         grid=(count,),
-        in_specs=[pl.BlockSpec(memory_space=pl.ANY)] * (2 * count),
-        out_specs=pl.BlockSpec((shares, 2, 1, rows, order), lambda s: (0, 0, s, 0, 0)),
-        out_shape=jax.ShapeDtypeStruct((shares, 2, count, rows, order), jnp.bfloat16),
+        in_specs=[pl.BlockSpec(memory_space=pl.ANY)] * len(operands),
+        out_specs=pl.BlockSpec((shares, 2, 1, rows, order), lambda s: (0, 0, s + first_slot, 0, 0)),
+        out_shape=jax.ShapeDtypeStruct((shares, 2, total, rows, order), jnp.bfloat16),
         scratch_shapes=[
             pltpu.VMEM((count, 2, order, order), jnp.bfloat16),
             pltpu.VMEM((count, 2, order, order), jnp.bfloat16),
             pltpu.SemaphoreType.DMA((2, count)),
         ],
+        input_output_aliases={} if into is None else {2 * count: 0},
         compiler_params=pltpu.CompilerParams(vmem_limit_bytes=56 * 1024 * 1024),
         cost_estimate=pl.CostEstimate(
             flops=8 * count * order ** 3, transcendentals=0, bytes_accessed=6 * count * order * order * 2
         ),
-    )(*forwards, *partners)
+    )(*operands)
 
 
 def inner_product(left, right):
@@ -148,7 +151,8 @@
         sink_partner = dressing_matrix(partner_mesons[1], gamma_order[1], gamma_phase[1])
         forwards += [dress(source_own, tiles[half_window + offset]), dress(source_partner, tile)]
         partners += [dress(sink_partner, tile), dress(sink_own, tiles[half_window + offset])]
-    loops = rest_loops(forwards, partners, shares)
+    loops = rest_loops(forwards[:1], partners[:1], shares, window, 0)
+    loops = rest_loops(forwards[1:], partners[1:], shares, window, 1, into=loops)
     slices = lax.all_to_all(loops, "src", split_axis=0, concat_axis=0, tiled=True)
     block_count = slices.shape[0] * slices.shape[2]
     real_flat = slices[:, 0].reshape(block_count, -1)

time: 209 us -> 211 us (level)
  waiting for transfers between devices: 113 us -> 108 us
  matrix products: 26.1 us -> 31 us
  Pallas kernels: 9.06 us -> 11.5 us
    ppermute x4, waiting for transfers between devices: 8.63 us -> 3.25 us  [shifted(): return lax.ppermute(block, axis, route)]
    dot_general x10, matrix products: 22.5 us -> 27.4 us  [dress(): out = jnp.dot(weights, stacked, preferred_element_type=jnp.float32)]
    squeeze x1 -> x0, local copies, waits for them, and re-layouts: 3.08 us -> none  [per_device(): tiles[half_window - offset]]
    slice x0 -> x1, local copies, waits for them, and re-layouts: none -> 3.01 us  [per_device(): forwards = [dress(source_own, tiles[half_window])]]
    pallas_call x1 -> x2, Pallas kernels: 9.06 us -> 11.5 us  [rest_loops(): pl.pallas_call(functools.partial(rest_loop_kernel, count), grid=(count,),...]
    unnamed x30 -> x32, local copies, waits for them, and re-layouts: 4.75 us -> 5.55 us
  transfers between devices with their start and end apart: 9 -> 9, of which waited for: 7 -> 6; matrix products, arithmetic and copies ran while one was open for 13% -> 15% of each run, Pallas kernels for 0% -> 2%
where the time goes in v15:
time: 211 us
  waiting for transfers between devices  108 us (51%)
  starting transfers between devices  39.5 us (19%)
  matrix products  31 us (15%)
  local copies, waits for them, and re-layouts  13.1 us (6%)
  Pallas kernels  11.5 us (5%)
  other arithmetic  7.48 us (4%)
    all_to_all x1, waiting for transfers between devices, per_device(): lax.all_to_all(loops, 'src', split_axis=0, concat_axis=0, tiled=True)  95.9 us
    dot_general x10, matrix products, dress(): out = jnp.dot(weights, stacked, preferred_element_type=jnp.float32)  27.4 us
    ppermute x4, starting transfers between devices, all_sum(): table = table + lax.ppermute(table, axis, [(i, i ^ bit) for i in range(n)])  26.2 us
    pallas_call x2, Pallas kernels, rest_loops(): pl.pallas_call(functools.partial(rest_loop_kernel, count), grid=(count,),...  11.5 us
    ppermute x4, waiting for transfers between devices, all_sum(): table = table + lax.ppermute(table, axis, [(i, i ^ bit) for i in range(n)])  8.68 us
    ppermute x4, starting transfers between devices, shifted(): return lax.ppermute(block, axis, route)  8.14 us
    unnamed x32, local copies, waits for them, and re-layouts  5.55 us
    all_to_all x1, starting transfers between devices, per_device(): lax.all_to_all(loops, 'src', split_axis=0, concat_axis=0, tiled=True)  5.14 us
  transfers between devices with their start and end apart: 9, of which 6 were waited for; matrix products, arithmetic and copies ran while one was open for 15% of the time, Pallas kernels for 2%

profile of v15, /device:TPU:0, one launch (start us, length us, event | category | flops | bytes accessed | tf_op | source)
XLA Modules:
  0.0 210.9 jit_solution(10569377923253028706)
XLA Ops:
  0.0 0.9 constant_dynamic-update-slice_fusion.1
  0.9 0.9 fusion.84
  1.9 6.1 %collective-permute-start.2 = (bf16[2,2,128,128]{3,2,1,0:T(8,128)(2,1)S(1)}, bf16[2,2,128,128]{3,2,1,0:T(8,128)(2,1)S(1)}, u32[]{:S(2)}, u32[]{:S(2)}) collective-permute-start(bf16[2,2,128,128]{3,2,1,0:T(8,128)(2,1)S(1)} %get-tuple-element.47), channel_id=1, source_target_pairs={{2,0},{3,1},{4,2},{5,3},{6,4},{7,5},{8,6},{9,7},{10,8},{11,9},{12,... | collective-permute-start | bytes 393224 | tf_op jit(solution)/shard_map/ppermute | solution.py:15
  8.0 3.0 %fusion.83 = (bf16[1,1,2,512,512]{4,3,2,1,0:T(8,128)(2,1)S(1)}, bf16[1,1,2,512,512]{4,3,2,1,0:T(8,128)(2,1)S(1)}, bf16[2,512,512]{2,1,0:T(8,128)(2,1)S(1)}, bf16...) fusion(bf16[1,5,2,512,512]{4,3,2,1,0:T(8,128)(2,1)} %param.8), kind=kLoop, calls=%fused_computation.167 | loop fusion | bytes 10485760 | tf_op jit(solution)/shard_map/slice | solution.py:147
  11.0 0.7 collective-permute-start.1
  11.6 1.4 collective-permute-start.3
  13.1 0.1 fusion.65
  13.3 2.3 %negate_convert_fusion.3 = (bf16[4,128,4,128]{3,2,1,0:T(4,128)(2,1)S(1)}, bf16[4,128,4,128]{3,2,1,0:T(4,128)(2,1)S(1)}, bf16[4,128,4,128]{3,2,1,0:T(4,128)(2,1)S...) fusion(f32[128,128]{1,0:T(8,128)S(1)} %get-tuple-element.74, ...), kind=kLoop, calls=%fused_computation.56 | loop fusion | flops 7864320 | bytes 5111936 | tf_op jit(solution)/shard_map/convert.23
  15.7 0.1 copy.71
  15.8 0.1 copy.69
  15.9 0.1 copy.70
  15.9 2.2 %convolution_convert_fusion.5 = bf16[1024,512]{1,0:T(8,128)(2,1)} fusion(bf16[1024,512]{1,0:T(8,128)(2,1)S(1)} %bitcast.217, bf16[512,512]{1,0:T(8,128)(2,1)S(1)} %bitcast.229, bf16[512,512]{1,0:T(8,128)(2,1)S(1)} %bitcast.232, bf16[512,512]{1,0:T(8,128)(2,1)S(1)} %bitcast.236), kind=kOutput, calls=%fused_computation.45 | convolution fusion | flops 1082654720 | bytes 3670016 | tf_op jit(solution)/shard_map/dot_general | solution.py:39
  18.2 2.2 %convolution_convert_fusion.4 = bf16[1024,512]{1,0:T(8,128)(2,1)} fusion(bf16[1024,512]{1,0:T(8,128)(2,1)S(1)} %bitcast.215, bf16[512,512]{1,0:T(8,128)(2,1)S(1)} %bitcast.230, bf16[512,512]{1,0:T(8,128)(2,1)S(1)} %bitcast.233, bf16[512,512]{1,0:T(8,128)(2,1)S(1)} %bitcast.237), kind=kOutput, calls=%fused_computation.44 | convolution fusion | flops 1082654720 | bytes 3670016 | tf_op jit(solution)/shard_map/dot_general | solution.py:39
  20.4 2.3 %negate_convert_fusion = (bf16[4,128,4,128]{3,2,1,0:T(4,128)(2,1)S(1)}, bf16[4,128,4,128]{3,2,1,0:T(4,128)(2,1)S(1)}, bf16[4,128,4,128]{3,2,1,0:T(4,128)(2,1)S(1...) fusion(f32[128,128]{1,0:T(8,128)S(1)} %get-tuple-element.31, ...), kind=kLoop, calls=%fused_computation.53 | loop fusion | flops 7864320 | bytes 5111936 | tf_op jit(solution)/shard_map/convert.5
  22.7 0.1 copy.59
  22.8 0.1 copy.57
  22.9 0.1 copy.58
  23.0 2.3 %convolution_convert_fusion.3 = bf16[1024,512]{1,0:T(8,128)(2,1)} fusion(bf16[1024,512]{1,0:T(8,128)(2,1)S(1)} %bitcast.218, bf16[512,512]{1,0:T(8,128)(2,1)S(1)} %bitcast.250, bf16[512,512]{1,0:T(8,128)(2,1)S(1)} %bitcast.253, bf16[512,512]{1,0:T(8,128)(2,1)S(1)} %bitcast.256), kind=kOutput, calls=%fused_computation.43 | convolution fusion | flops 1082654720 | bytes 3670016 | tf_op jit(solution)/shard_map/dot_general | solution.py:39
  25.3 2.3 %convolution_convert_fusion.2 = bf16[1024,512]{1,0:T(8,128)(2,1)} fusion(bf16[1024,512]{1,0:T(8,128)(2,1)S(1)} %bitcast.216, bf16[512,512]{1,0:T(8,128)(2,1)S(1)} %bitcast.251, bf16[512,512]{1,0:T(8,128)(2,1)S(1)} %bitcast.254, bf16[512,512]{1,0:T(8,128)(2,1)S(1)} %bitcast.257), kind=kOutput, calls=%fused_computation.42 | convolution fusion | flops 1082654720 | bytes 3670016 | tf_op jit(solution)/shard_map/dot_general | solution.py:39
  27.6 2.2 %convolution_convert_fusion.1 = bf16[1024,512]{1,0:T(8,128)(2,1)} fusion(bf16[1024,512]{1,0:T(8,128)(2,1)S(1)} %bitcast.213, bf16[512,512]{1,0:T(8,128)(2,1)S(1)} %bitcast.231, bf16[512,512]{1,0:T(8,128)(2,1)S(1)} %bitcast.234, bf16[512,512]{1,0:T(8,128)(2,1)S(1)} %bitcast.238), kind=kOutput, calls=%fused_computation.41 | convolution fusion | flops 1082654720 | bytes 3670016 | tf_op jit(solution)/shard_map/dot_general | solution.py:39
  29.8 2.3 %convolution_convert_fusion = bf16[1024,512]{1,0:T(8,128)(2,1)} fusion(bf16[1024,512]{1,0:T(8,128)(2,1)S(1)} %bitcast.214, bf16[512,512]{1,0:T(8,128)(2,1)S(1)} %bitcast.252, bf16[512,512]{1,0:T(8,128)(2,1)S(1)} %bitcast.255, bf16[512,512]{1,0:T(8,128)(2,1)S(1)} %bitcast.258), kind=kOutput, calls=%fused_computation.40 | convolution fusion | flops 1082654720 | bytes 3670016 | tf_op jit(solution)/shard_map/dot_general | solution.py:39
  32.1 0.1 copy.68
  32.2 0.1 copy.66
  32.3 0.1 copy.67
  32.3 0.1 copy.65
  32.4 0.1 copy.63
  32.5 0.1 copy.64
  32.6 0.1 copy.62
  32.7 0.1 copy.60
  32.8 0.9 copy.61
  33.7 0.1 copy.56
  33.7 0.1 copy.54
  33.8 0.1 copy.55
  33.9 3.8 %shard_map.82.refs_8_ = bf16[16,2,5,32,512]{4,3,2,1,0:T(8,128)(2,1)} custom-call(bf16[2,512,512]{2,1,0:T(8,128)(2,1)} %bitcast.223, bf16[2,512,512]{2,1,0:T(8,128)(2,1)} %bitcast.224), custom_call_target="tpu_custom_call" | custom-call | flops 1073741824 | bytes 3145728 | tf_op jit(solution)/shard_map/pallas_call | solution.py:86
  37.8 3.5 %fusion.41 = bf16[1024,512]{1,0:T(8,128)(2,1)} fusion(bf16[1024,512]{1,0:T(8,128)(2,1)} %bitcast.10, bf16[512,512]{1,0:T(8,128)(2,1)S(1)} %bitcast.241, bf16[512,512]{1,0:T(8,128)(2,1)S(1)} %bitcast.242, bf16[512,512]{1,0:T(8,128)(2,1)S(1)} %bitcast.244), kind=kOutput, calls=%fused_computation.39 | convolution fusion | flops 1082654720 | bytes 3670016 | tf_op jit(solution)/shard_map/dot_general | solution.py:39
  41.3 3.5 %fusion.35 = bf16[1024,512]{1,0:T(8,128)(2,1)} fusion(bf16[1024,512]{1,0:T(8,128)(2,1)} %bitcast.10, bf16[512,512]{1,0:T(8,128)(2,1)S(1)} %bitcast.247, bf16[512,512]{1,0:T(8,128)(2,1)S(1)} %bitcast.248, bf16[512,512]{1,0:T(8,128)(2,1)S(1)} %bitcast.249), kind=kOutput, calls=%fused_computation.37 | convolution fusion | flops 1082654720 | bytes 3670016 | tf_op jit(solution)/shard_map/dot_general | solution.py:39
  44.8 3.2 %collective-permute-done.3 = bf16[2,512,512]{2,1,0:T(8,128)(2,1)} collective-permute-done((bf16[2,512,512]{2,1,0:T(8,128)(2,1)S(1)}, bf16[2,512,512]{2,1,0:T(8,128)(2,1)}, u32[]{:S(2)}, u32[]{:S(2)}) %collective-permute-start.3) | collective-permute-done | bytes 1048608 | tf_op jit(solution)/shard_map/ppermute | solution.py:15
  48.0 3.4 %fusion.38 = bf16[1024,512]{1,0:T(8,128)(2,1)} fusion(bf16[1024,512]{1,0:T(8,128)(2,1)} %bitcast.17, bf16[512,512]{1,0:T(8,128)(2,1)S(1)} %bitcast.235, bf16[512,512]{1,0:T(8,128)(2,1)S(1)} %bitcast.239, bf16[512,512]{1,0:T(8,128)(2,1)S(1)} %bitcast.240), kind=kOutput, calls=%fused_computation.38 | convolution fusion | flops 1082654720 | bytes 3670016 | tf_op jit(solution)/shard_map/dot_general | solution.py:39
  51.4 3.4 %fusion.32 = bf16[1024,512]{1,0:T(8,128)(2,1)} fusion(bf16[1024,512]{1,0:T(8,128)(2,1)} %bitcast.17, bf16[512,512]{1,0:T(8,128)(2,1)S(1)} %bitcast.243, bf16[512,512]{1,0:T(8,128)(2,1)S(1)} %bitcast.245, bf16[512,512]{1,0:T(8,128)(2,1)S(1)} %bitcast.246), kind=kOutput, calls=%fused_computation.36 | convolution fusion | flops 1082654720 | bytes 3670016 | tf_op jit(solution)/shard_map/dot_general | solution.py:39
  54.9 7.7 %shard_map.83 = bf16[16,2,5,32,512]{4,3,2,1,0:T(8,128)(2,1)} custom-call(bf16[2,512,512]{2,1,0:T(8,128)(2,1)} %bitcast.219, bf16[2,512,512]{2,1,0:T(8,128)(2,1)} %bitcast.225, bf16[2,512,512]{2,1,0:T(8,128)(2,1)} %bitcast.220, bf16[2,512,512]{2,1,0:T(8,128)(2,1)} %bitcast.227, bf16[2,512,512]{2,1,0:T(8,128)(2,1)} %bitcast.226, ...), custom_call_target="tpu_custom_call", output_to_operand_aliasing={{}: (8, {})} | custom-call | flops 4294967296 | bytes 12582912 | tf_op jit(solution)/shard_map/pallas_call | solution.py:86
  62.6 0.0 copy-start.5
  62.6 5.1 %all-to-all-start = ((bf16[16,2,5,32,512]{4,3,2,1,0:T(8,128)(2,1)}), bf16[16,2,5,32,512]{4,3,2,1,0:T(8,128)(2,1)}, u32[]{:S(2)}, u32[]{:S(2)}) async-start(bf16[16,2,5,32,512]{4,3,2,1,0:T(8,128)(2,1)} %shard_map.83), calls=%async_computation | async-start | bytes 10485760 | tf_op jit(solution)/shard_map/all_to_all | solution.py:156
  67.8 95.9 %all-to-all-done = bf16[16,2,5,32,512]{4,3,2,1,0:T(8,128)(2,1)} async-done(((bf16[16,2,5,32,512]{4,3,2,1,0:T(8,128)(2,1)}), bf16[16,2,5,32,512]{4,3,2,1,0:T(8,128)(2,1)}, u32[]{:S(2)}, u32[]{:S(2)}) %all-to-all-start) | async-done | bytes 5242912 | tf_op jit(solution)/shard_map/all_to_all | solution.py:156
  163.7 3.0 %fusion.82 = (bf16[16,1,5,32,512]{4,3,2,1,0:T(8,128)(2,1)S(1)}, bf16[16,1,5,32,512]{4,3,2,1,0:T(8,128)(2,1)S(1)}) fusion(bf16[16,2,5,32,512]{4,3,2,1,0:T(8,128)(2,1)} %all-to-all-done), kind=kLoop, calls=%fused_computation.166 | loop fusion | bytes 10485760 | tf_op jit(solution)/shard_map/slice | solution.py:159
  166.7 1.6 copy.32
  168.3 1.6 copy.33
  170.0 0.8 fusion.86
  170.8 0.8 fusion.87
  171.6 0.8 fusion.46
  172.5 0.0 copy-start.1
  172.5 0.8 fusion.47
  173.4 0.7 gather_fusion
  174.1 0.1 copy.12
  174.2 0.7 gather_fusion.1
  174.9 0.8 collective-permute-start.4
  175.7 0.9 collective-permute-done.4
  176.7 7.7 %collective-permute-start.5 = (f32[2,80,80]{1,0,2:T(2,128)S(1)}, f32[2,80,80]{1,0,2:T(2,128)S(1)}, u32[]{:S(2)}, u32[]{:S(2)}) collective-permute-start(f32[2,80,80]{1,0,2:T(2,128)S(1)} %bitcast_add_fusion), channel_id=1, source_target_pairs={{0,2},{1,3},{2,0},{3,1},{4,6},{5,7},{6,4},{7,5},{8,10},{9,11},{10,... | collective-permute-start | bytes 153608 | tf_op jit(solution)/shard_map/ppermute | solution.py:115
  184.3 3.0 %collective-permute-done.5 = f32[2,80,80]{1,0,2:T(2,128)S(1)} collective-permute-done((f32[2,80,80]{1,0,2:T(2,128)S(1)}, f32[2,80,80]{1,0,2:T(2,128)S(1)}, u32[]{:S(2)}, u32[]{:S(2)}) %collective-permute-start.5) | collective-permute-done | bytes 51232 | tf_op jit(solution)/shard_map/ppermute | solution.py:115
  187.3 14.2 %collective-permute-start.6 = (f32[2,80,80]{1,0,2:T(2,128)S(1)}, f32[2,80,80]{1,0,2:T(2,128)S(1)}, u32[]{:S(2)}, u32[]{:S(2)}) collective-permute-start(f32[2,80,80]{1,0,2:T(2,128)S(1)} %add.80), channel_id=1, source_target_pairs={{0,4},{1,5},{2,6},{3,7},{4,0},{5,1},{6,2},{7,3},{8,12},{9,13},{10,... | collective-permute-start | bytes 153608 | tf_op jit(solution)/shard_map/ppermute | solution.py:115
  201.6 2.4 %collective-permute-done.6 = f32[2,80,80]{1,0,2:T(2,128)S(1)} collective-permute-done((f32[2,80,80]{1,0,2:T(2,128)S(1)}, f32[2,80,80]{1,0,2:T(2,128)S(1)}, u32[]{:S(2)}, u32[]{:S(2)}) %collective-permute-start.6) | collective-permute-done | bytes 51232 | tf_op jit(solution)/shard_map/ppermute | solution.py:115
  204.0 3.5 %collective-permute-start.7 = (f32[2,80,80]{1,0,2:T(2,128)S(1)}, f32[2,80,80]{1,0,2:T(2,128)S(1)}, u32[]{:S(2)}, u32[]{:S(2)}) collective-permute-start(f32[2,80,80]{1,0,2:T(2,128)S(1)} %add.81), channel_id=1, source_target_pairs={{0,8},{1,9},{2,10},{3,11},{4,12},{5,13},{6,14},{7,15},{8,0},{9,1},... | collective-permute-start | bytes 153608 | tf_op jit(solution)/shard_map/ppermute | solution.py:115
  207.5 2.4 %collective-permute-done.7 = f32[2,80,80]{1,0,2:T(2,128)S(1)} collective-permute-done((f32[2,80,80]{1,0,2:T(2,128)S(1)}, f32[2,80,80]{1,0,2:T(2,128)S(1)}, u32[]{:S(2)}, u32[]{:S(2)}) %collective-permute-start.7) | collective-permute-done | bytes 51232 | tf_op jit(solution)/shard_map/ppermute | solution.py:115
  210.0 0.3 fusion.45
  210.3 0.6 broadcast_multiply_fusion
  (32 shorter events, 0.4 us)
Async XLA Ops:
  1.9 11.2 %copy-start.3 = (s32[2,4]{1,0:T(2,128)S(1)}, s32[2,4]{1,0:T(2,128)}, u32[]{:S(2)}) copy-start(s32[2,4]{1,0:T(2,128)} %param.12) | copy-start | bytes 100
  1.9 11.2 %copy-start.4 = (s32[2,4]{1,0:T(2,128)S(1)}, s32[2,4]{1,0:T(2,128)}, u32[]{:S(2)}) copy-start(s32[2,4]{1,0:T(2,128)} %param.11) | copy-start | bytes 100
  1.9 11.3 %collective-permute-start.2 = (bf16[2,2,128,128]{3,2,1,0:T(8,128)(2,1)S(1)}, bf16[2,2,128,128]{3,2,1,0:T(8,128)(2,1)S(1)}, u32[]{:S(2)}, u32[]{:S(2)}) collective-permute-start(bf16[2,2,128,128]{3,2,1,0:T(8,128)(2,1)S(1)} %get-tuple-element.47), channel_id=1, source_target_pairs={{2,0},{3,1},{4,2},{5,3},{6,4},{7,5},{8,6},{9,7},{10,8},{11,9},{12,... | collective-permute-start | bytes 393224 | tf_op jit(solution)/shard_map/ppermute | solution.py:15
  8.0 5.3 %collective-permute-start = (bf16[2,2,128,128]{3,2,1,0:T(8,128)(2,1)S(1)}, bf16[2,2,128,128]{3,2,1,0:T(8,128)(2,1)S(1)}, u32[]{:S(2)}, u32[]{:S(2)}) collective-permute-start(bf16[2,2,128,128]{3,2,1,0:T(8,128)(2,1)S(1)} %get-tuple-element.47), channel_id=1, source_target_pairs={{1,0},{2,1},{3,2},{4,3},{5,4},{6,5},{7,6},{8,7},{9,8},{10,9},{11,1... | collective-permute-start | bytes 393224 | tf_op jit(solution)/shard_map/ppermute | solution.py:15
  11.0 26.8 %collective-permute-start.1 = (bf16[2,512,512]{2,1,0:T(8,128)(2,1)S(1)}, bf16[2,512,512]{2,1,0:T(8,128)(2,1)}, u32[]{:S(2)}, u32[]{:S(2)}) collective-permute-start(bf16[2,512,512]{2,1,0:T(8,128)(2,1)S(1)} %get-tuple-element.9), channel_id=1, source_target_pairs={{1,0},{2,1},{3,2},{4,3},{5,4},{6,5},{7,6},{8,7},{9,8},{10,9},{11,1... | collective-permute-start | bytes 3145736 | tf_op jit(solution)/shard_map/ppermute | solution.py:15
  11.6 36.4 %collective-permute-start.3 = (bf16[2,512,512]{2,1,0:T(8,128)(2,1)S(1)}, bf16[2,512,512]{2,1,0:T(8,128)(2,1)}, u32[]{:S(2)}, u32[]{:S(2)}) collective-permute-start(bf16[2,512,512]{2,1,0:T(8,128)(2,1)S(1)} %get-tuple-element.11), channel_id=1, source_target_pairs={{2,0},{3,1},{4,2},{5,3},{6,4},{7,5},{8,6},{9,7},{10,8},{11,9},{12,... | collective-permute-start | bytes 3145736 | tf_op jit(solution)/shard_map/ppermute | solution.py:15
  37.7 3.5 %copy-start = (bf16[64,8,4,128]{3,1,2,0:T(8,128)(2,1)S(1)}, bf16[64,8,4,128]{3,1,2,0:T(8,128)(2,1)}, u32[]{:S(2)}) copy-start(bf16[64,8,4,128]{3,1,2,0:T(8,128)(2,1)} %copy.61) | copy-start | bytes 1572868
  62.6 5.2 %copy-start.5 = (s32[80]{0:T(128)S(1)}, s32[80]{0:T(128)}, u32[]{:S(2)}) copy-start(s32[80]{0:T(128)} %constant.52) | copy-start | bytes 964
  62.6 101.1 %all-to-all-start = ((bf16[16,2,5,32,512]{4,3,2,1,0:T(8,128)(2,1)}), bf16[16,2,5,32,512]{4,3,2,1,0:T(8,128)(2,1)}, u32[]{:S(2)}, u32[]{:S(2)}) async-start(bf16[16,2,5,32,512]{4,3,2,1,0:T(8,128)(2,1)} %shard_map.83), calls=%async_computation | async-start | bytes 10485760 | tf_op jit(solution)/shard_map/all_to_all | solution.py:156
  172.5 11.9 %copy-start.1 = (s32[2,512]{1,0:T(2,128)S(1)}, s32[2,512]{1,0:T(2,128)}, u32[]{:S(2)}) copy-start(s32[2,512]{1,0:T(2,128)} %param.13) | copy-start | bytes 12292
  172.5 35.0 %copy-start.2 = (s32[512]{0:T(512)S(1)}, s32[512]{0:T(512)}, u32[]{:S(2)}) copy-start(s32[512]{0:T(512)} %param.14) | copy-start | bytes 6148
  174.9 1.8 collective-permute-start.4
  176.7 10.6 %collective-permute-start.5 = (f32[2,80,80]{1,0,2:T(2,128)S(1)}, f32[2,80,80]{1,0,2:T(2,128)S(1)}, u32[]{:S(2)}, u32[]{:S(2)}) collective-permute-start(f32[2,80,80]{1,0,2:T(2,128)S(1)} %bitcast_add_fusion), channel_id=1, source_target_pairs={{0,2},{1,3},{2,0},{3,1},{4,6},{5,7},{6,4},{7,5},{8,10},{9,11},{10,... | collective-permute-start | bytes 153608 | tf_op jit(solution)/shard_map/ppermute | solution.py:115
  187.3 16.6 %collective-permute-start.6 = (f32[2,80,80]{1,0,2:T(2,128)S(1)}, f32[2,80,80]{1,0,2:T(2,128)S(1)}, u32[]{:S(2)}, u32[]{:S(2)}) collective-permute-start(f32[2,80,80]{1,0,2:T(2,128)S(1)} %add.80), channel_id=1, source_target_pairs={{0,4},{1,5},{2,6},{3,7},{4,0},{5,1},{6,2},{7,3},{8,12},{9,13},{10,... | collective-permute-start | bytes 153608 | tf_op jit(solution)/shard_map/ppermute | solution.py:115
  204.0 5.9 %collective-permute-start.7 = (f32[2,80,80]{1,0,2:T(2,128)S(1)}, f32[2,80,80]{1,0,2:T(2,128)S(1)}, u32[]{:S(2)}, u32[]{:S(2)}) collective-permute-start(f32[2,80,80]{1,0,2:T(2,128)S(1)} %add.81), channel_id=1, source_target_pairs={{0,8},{1,9},{2,10},{3,11},{4,12},{5,13},{6,14},{7,15},{8,0},{9,1},... | collective-permute-start | bytes 153608 | tf_op jit(solution)/shard_map/ppermute | solution.py:115

commit v16 on v13

--- a/solution.py
+++ b/solution.py
@@ -153,11 +153,9 @@
     block_count = slices.shape[0] * slices.shape[2]
     real_flat = slices[:, 0].reshape(block_count, -1)
     imag_flat = slices[:, 1].reshape(block_count, -1)
+    mixed = inner_product(real_flat, imag_flat)
     trace_table = jnp.stack(
-        [
-            inner_product(real_flat, real_flat) - inner_product(imag_flat, imag_flat),
-            inner_product(real_flat, imag_flat) + inner_product(imag_flat, real_flat),
-        ]
+        [inner_product(real_flat, real_flat) - inner_product(imag_flat, imag_flat), mixed + mixed.T]
     )
     place = np.zeros(block_count, np.int32)
     for source in range(shares):

time: 209 us -> 208 us (level)
  no operation moved by 1% of the time
where the time goes in v16:
time: 208 us
  waiting for transfers between devices  113 us (54%)
  starting transfers between devices  40.1 us (19%)
  matrix products  25.3 us (12%)
  local copies, waits for them, and re-layouts  12.5 us (6%)
  Pallas kernels  9.06 us (4%)
  other arithmetic  7.49 us (4%)
    all_to_all x1, waiting for transfers between devices, per_device(): lax.all_to_all(loops, 'src', split_axis=0, concat_axis=0, tiled=True)  95.9 us
    ppermute x4, starting transfers between devices, all_sum(): table = table + lax.ppermute(table, axis, [(i, i ^ bit) for i in range(n)])  26.2 us
    dot_general x10, matrix products, dress(): out = jnp.dot(weights, stacked, preferred_element_type=jnp.float32)  22.5 us
    pallas_call x1, Pallas kernels, rest_loops(): pl.pallas_call(rest_loop_kernel, grid=(count,), in_specs=[pl.BlockSpec(me...  9.06 us
    ppermute x4, waiting for transfers between devices, all_sum(): table = table + lax.ppermute(table, axis, [(i, i ^ bit) for i in range(n)])  8.68 us
    ppermute x4, waiting for transfers between devices, shifted(): return lax.ppermute(block, axis, route)  8.63 us
    ppermute x4, starting transfers between devices, shifted(): return lax.ppermute(block, axis, route)  7.86 us
    all_to_all x1, starting transfers between devices, per_device(): lax.all_to_all(loops, 'src', split_axis=0, concat_axis=0, tiled=True)  6.04 us
  transfers between devices with their start and end apart: 9, of which 7 were waited for; matrix products, arithmetic and copies ran while one was open for 13% of the time, Pallas kernels for 0%

profile of v16, /device:TPU:0, one launch (start us, length us, event | category | flops | bytes accessed | tf_op | source)
XLA Modules:
  0.0 208.0 jit_solution(12398176027320415844)
XLA Ops:
  0.0 0.9 constant_dynamic-update-slice_fusion.1
  0.9 0.9 fusion.83
  1.9 0.0 copy-start.2
  1.9 6.1 %collective-permute-start.2 = (bf16[2,2,128,128]{3,2,1,0:T(8,128)(2,1)S(1)}, bf16[2,2,128,128]{3,2,1,0:T(8,128)(2,1)S(1)}, u32[]{:S(2)}, u32[]{:S(2)}) collective-permute-start(bf16[2,2,128,128]{3,2,1,0:T(8,128)(2,1)S(1)} %get-tuple-element.47), channel_id=1, source_target_pairs={{2,0},{3,1},{4,2},{5,3},{6,4},{7,5},{8,6},{9,7},{10,8},{11,9},{12,... | collective-permute-start | bytes 393224 | tf_op jit(solution)/shard_map/ppermute | solution.py:13
  8.0 3.1 %slice_bitcast_fusion = (bf16[2,512,512]{2,1,0:T(8,128)(2,1)S(1)}, bf16[2,512,512]{2,1,0:T(8,128)(2,1)S(1)}, bf16[1,1,2,512,512]{4,3,2,1,0:T(8,128)(2,1)S(1)}, b...) fusion(bf16[1,5,2,512,512]{4,3,2,1,0:T(8,128)(2,1)} %param.8), kind=kLoop, calls=%fused_computation.66 | loop fusion | bytes 10485760 | tf_op jit(solution)/shard_map/squeeze | solution.py:139
  11.0 1.1 collective-permute-start.3
  12.2 0.7 collective-permute-start.1
  12.9 0.1 fusion.65
  13.1 2.3 %negate_convert_fusion = (bf16[4,128,4,128]{3,2,1,0:T(4,128)(2,1)S(1)}, bf16[4,128,4,128]{3,2,1,0:T(4,128)(2,1)S(1)}, bf16[4,128,4,128]{3,2,1,0:T(4,128)(2,1)S(1...) fusion(f32[128,128]{1,0:T(8,128)S(1)} %get-tuple-element.31, ...), kind=kLoop, calls=%fused_computation.51 | loop fusion | flops 7864320 | bytes 5111936 | tf_op jit(solution)/shard_map/convert.5
  15.5 0.1 copy.61
  15.6 0.1 copy.62
  15.6 0.1 copy.63
  15.7 2.3 %convolution_convert_fusion = bf16[1024,512]{1,0:T(8,128)(2,1)} fusion(bf16[1024,512]{1,0:T(8,128)(2,1)S(1)} %bitcast.217, bf16[512,512]{1,0:T(8,128)(2,1)S(1)} %bitcast.225, bf16[512,512]{1,0:T(8,128)(2,1)S(1)} %bitcast.219, bf16[512,512]{1,0:T(8,128)(2,1)S(1)} %bitcast.222), kind=kOutput, calls=%fused_computation.40 | convolution fusion | flops 1082654720 | bytes 3670016 | tf_op jit(solution)/shard_map/dot_general | solution.py:37
  18.0 2.3 %convolution_convert_fusion.1 = bf16[1024,512]{1,0:T(8,128)(2,1)} fusion(bf16[1024,512]{1,0:T(8,128)(2,1)S(1)} %bitcast.215, bf16[512,512]{1,0:T(8,128)(2,1)S(1)} %bitcast.226, bf16[512,512]{1,0:T(8,128)(2,1)S(1)} %bitcast.220, bf16[512,512]{1,0:T(8,128)(2,1)S(1)} %bitcast.223), kind=kOutput, calls=%fused_computation.41 | convolution fusion | flops 1082654720 | bytes 3670016 | tf_op jit(solution)/shard_map/dot_general | solution.py:37
  20.2 2.3 %negate_convert_fusion.3 = (bf16[4,128,4,128]{3,2,1,0:T(4,128)(2,1)S(1)}, bf16[4,128,4,128]{3,2,1,0:T(4,128)(2,1)S(1)}, bf16[4,128,4,128]{3,2,1,0:T(4,128)(2,1)S...) fusion(f32[128,128]{1,0:T(8,128)S(1)} %get-tuple-element.74, ...), kind=kLoop, calls=%fused_computation.54 | loop fusion | flops 7864320 | bytes 5111936 | tf_op jit(solution)/shard_map/convert.23
  22.6 0.1 copy.70
  22.7 0.1 copy.71
  22.8 0.1 copy.72
  22.8 2.3 %convolution_convert_fusion.3 = bf16[1024,512]{1,0:T(8,128)(2,1)} fusion(bf16[1024,512]{1,0:T(8,128)(2,1)S(1)} %bitcast.218, bf16[512,512]{1,0:T(8,128)(2,1)S(1)} %bitcast.246, bf16[512,512]{1,0:T(8,128)(2,1)S(1)} %bitcast.240, bf16[512,512]{1,0:T(8,128)(2,1)S(1)} %bitcast.243), kind=kOutput, calls=%fused_computation.43 | convolution fusion | flops 1082654720 | bytes 3670016 | tf_op jit(solution)/shard_map/dot_general | solution.py:37
  25.2 2.2 %convolution_convert_fusion.4 = bf16[1024,512]{1,0:T(8,128)(2,1)} fusion(bf16[1024,512]{1,0:T(8,128)(2,1)S(1)} %bitcast.216, bf16[512,512]{1,0:T(8,128)(2,1)S(1)} %bitcast.247, bf16[512,512]{1,0:T(8,128)(2,1)S(1)} %bitcast.241, bf16[512,512]{1,0:T(8,128)(2,1)S(1)} %bitcast.244), kind=kOutput, calls=%fused_computation.44 | convolution fusion | flops 1082654720 | bytes 3670016 | tf_op jit(solution)/shard_map/dot_general | solution.py:37
  27.4 2.2 %convolution_convert_fusion.2 = bf16[1024,512]{1,0:T(8,128)(2,1)} fusion(bf16[1024,512]{1,0:T(8,128)(2,1)S(1)} %bitcast.213, bf16[512,512]{1,0:T(8,128)(2,1)S(1)} %bitcast.227, bf16[512,512]{1,0:T(8,128)(2,1)S(1)} %bitcast.221, bf16[512,512]{1,0:T(8,128)(2,1)S(1)} %bitcast.224), kind=kOutput, calls=%fused_computation.42 | convolution fusion | flops 1082654720 | bytes 3670016 | tf_op jit(solution)/shard_map/dot_general | solution.py:37
  29.6 2.2 %convolution_convert_fusion.5 = bf16[1024,512]{1,0:T(8,128)(2,1)} fusion(bf16[1024,512]{1,0:T(8,128)(2,1)S(1)} %bitcast.214, bf16[512,512]{1,0:T(8,128)(2,1)S(1)} %bitcast.248, bf16[512,512]{1,0:T(8,128)(2,1)S(1)} %bitcast.242, bf16[512,512]{1,0:T(8,128)(2,1)S(1)} %bitcast.245), kind=kOutput, calls=%fused_computation.45 | convolution fusion | flops 1082654720 | bytes 3670016 | tf_op jit(solution)/shard_map/dot_general | solution.py:37
  31.8 0.1 copy.55
  31.9 0.1 copy.56
  32.0 0.1 copy.57
  32.1 0.1 copy.58
  32.1 0.1 copy.59
  32.2 0.1 copy.60
  32.3 0.1 copy.64
  32.4 0.1 copy.65
  32.5 0.1 copy.66
  32.6 0.1 copy.67
  32.7 0.1 copy.68
  32.8 0.1 copy.69
  32.8 3.8 %collective-permute-done.3 = bf16[2,512,512]{2,1,0:T(8,128)(2,1)S(1)} collective-permute-done((bf16[2,512,512]{2,1,0:T(8,128)(2,1)S(1)}, bf16[2,512,512]{2,1,0:T(8,128)(2,1)S(1)}, u32[]{:S(2)}, u32[]{:S(2)}) %collective-permute-start.3) | collective-permute-done | bytes 1048608 | tf_op jit(solution)/shard_map/ppermute | solution.py:13
  36.7 2.2 %fusion.32 = bf16[1024,512]{1,0:T(8,128)(2,1)} fusion(bf16[1024,512]{1,0:T(8,128)(2,1)S(1)} %bitcast.255, bf16[512,512]{1,0:T(8,128)(2,1)S(1)} %bitcast.234, bf16[512,512]{1,0:T(8,128)(2,1)S(1)} %bitcast.231, bf16[512,512]{1,0:T(8,128)(2,1)S(1)} %bitcast.232), kind=kOutput, calls=%fused_computation.36 | convolution fusion | flops 1082654720 | bytes 3670016 | tf_op jit(solution)/shard_map/dot_general | solution.py:37
  38.9 2.2 %fusion.38 = bf16[1024,512]{1,0:T(8,128)(2,1)} fusion(bf16[1024,512]{1,0:T(8,128)(2,1)S(1)} %bitcast.256, bf16[512,512]{1,0:T(8,128)(2,1)S(1)} %bitcast.239, bf16[512,512]{1,0:T(8,128)(2,1)S(1)} %bitcast.237, bf16[512,512]{1,0:T(8,128)(2,1)S(1)} %bitcast.238), kind=kOutput, calls=%fused_computation.38 | convolution fusion | flops 1082654720 | bytes 3670016 | tf_op jit(solution)/shard_map/dot_general | solution.py:37
  41.1 4.8 %collective-permute-done.1 = bf16[2,512,512]{2,1,0:T(8,128)(2,1)S(1)} collective-permute-done((bf16[2,512,512]{2,1,0:T(8,128)(2,1)S(1)}, bf16[2,512,512]{2,1,0:T(8,128)(2,1)S(1)}, u32[]{:S(2)}, u32[]{:S(2)}) %collective-permute-start.1) | collective-permute-done | bytes 1048608 | tf_op jit(solution)/shard_map/ppermute | solution.py:13
  45.9 2.3 %fusion.35 = bf16[1024,512]{1,0:T(8,128)(2,1)} fusion(bf16[1024,512]{1,0:T(8,128)(2,1)S(1)} %bitcast.253, bf16[512,512]{1,0:T(8,128)(2,1)S(1)} %bitcast.230, bf16[512,512]{1,0:T(8,128)(2,1)S(1)} %bitcast.228, bf16[512,512]{1,0:T(8,128)(2,1)S(1)} %bitcast.229), kind=kOutput, calls=%fused_computation.37 | convolution fusion | flops 1082654720 | bytes 3670016 | tf_op jit(solution)/shard_map/dot_general | solution.py:37
  48.2 2.3 %fusion.41 = bf16[1024,512]{1,0:T(8,128)(2,1)} fusion(bf16[1024,512]{1,0:T(8,128)(2,1)S(1)} %bitcast.254, bf16[512,512]{1,0:T(8,128)(2,1)S(1)} %bitcast.236, bf16[512,512]{1,0:T(8,128)(2,1)S(1)} %bitcast.233, bf16[512,512]{1,0:T(8,128)(2,1)S(1)} %bitcast.235), kind=kOutput, calls=%fused_computation.39 | convolution fusion | flops 1082654720 | bytes 3670016 | tf_op jit(solution)/shard_map/dot_general | solution.py:37
  50.5 9.1 %shard_map.82 = bf16[16,2,5,32,512]{4,3,2,1,0:T(8,128)(2,1)} custom-call(bf16[2,512,512]{2,1,0:T(8,128)(2,1)} %bitcast.262, bf16[2,512,512]{2,1,0:T(8,128)(2,1)} %bitcast.260, bf16[2,512,512]{2,1,0:T(8,128)(2,1)} %bitcast.266, bf16[2,512,512]{2,1,0:T(8,128)(2,1)} %bitcast.259, bf16[2,512,512]{2,1,0:T(8,128)(2,1)} %bitcast.264, ...), custom_call_target="tpu_custom_call" | custom-call | flops 5368709120 | bytes 15728640 | tf_op jit(solution)/shard_map/pallas_call | solution.py:84
  59.6 0.0 copy-start.4
  59.6 6.0 %all-to-all-start = ((bf16[16,2,5,32,512]{4,3,2,1,0:T(8,128)(2,1)}), bf16[16,2,5,32,512]{4,3,2,1,0:T(8,128)(2,1)}, u32[]{:S(2)}, u32[]{:S(2)}) async-start(bf16[16,2,5,32,512]{4,3,2,1,0:T(8,128)(2,1)} %shard_map.82), calls=%async_computation | async-start | bytes 10485760 | tf_op jit(solution)/shard_map/all_to_all | solution.py:152
  65.7 95.9 %all-to-all-done = bf16[16,2,5,32,512]{4,3,2,1,0:T(8,128)(2,1)} async-done(((bf16[16,2,5,32,512]{4,3,2,1,0:T(8,128)(2,1)}), bf16[16,2,5,32,512]{4,3,2,1,0:T(8,128)(2,1)}, u32[]{:S(2)}, u32[]{:S(2)}) %all-to-all-start) | async-done | bytes 5242912 | tf_op jit(solution)/shard_map/all_to_all | solution.py:152
  161.6 3.0 %fusion.82 = (bf16[16,1,5,32,512]{4,3,2,1,0:T(8,128)(2,1)S(1)}, bf16[16,1,5,32,512]{4,3,2,1,0:T(8,128)(2,1)S(1)}) fusion(bf16[16,2,5,32,512]{4,3,2,1,0:T(8,128)(2,1)} %all-to-all-done), kind=kLoop, calls=%fused_computation.166 | loop fusion | bytes 10485760 | tf_op jit(solution)/shard_map/slice | solution.py:155
  164.6 1.6 copy.33
  166.2 0.8 fusion.85
  167.0 1.6 copy.34
  168.7 0.8 fusion.86
  169.5 0.8 fusion.46
  170.4 0.1 copy.11
  170.5 0.7 gather_fusion
  171.2 0.1 copy.13
  171.3 0.7 gather_fusion.1
  172.0 0.8 collective-permute-start.4
  172.9 0.9 collective-permute-done.4
  173.8 7.6 %collective-permute-start.5 = (f32[2,80,80]{1,0,2:T(2,128)S(1)}, f32[2,80,80]{1,0,2:T(2,128)S(1)}, u32[]{:S(2)}, u32[]{:S(2)}) collective-permute-start(f32[2,80,80]{1,0,2:T(2,128)S(1)} %bitcast_add_fusion.1), channel_id=1, source_target_pairs={{0,2},{1,3},{2,0},{3,1},{4,6},{5,7},{6,4},{7,5},{8,10},{9,11},{10,... | collective-permute-start | bytes 153608 | tf_op jit(solution)/shard_map/ppermute | solution.py:112
  181.5 3.0 %collective-permute-done.5 = f32[2,80,80]{1,0,2:T(2,128)S(1)} collective-permute-done((f32[2,80,80]{1,0,2:T(2,128)S(1)}, f32[2,80,80]{1,0,2:T(2,128)S(1)}, u32[]{:S(2)}, u32[]{:S(2)}) %collective-permute-start.5) | collective-permute-done | bytes 51232 | tf_op jit(solution)/shard_map/ppermute | solution.py:112
  184.5 14.2 %collective-permute-start.6 = (f32[2,80,80]{1,0,2:T(2,128)S(1)}, f32[2,80,80]{1,0,2:T(2,128)S(1)}, u32[]{:S(2)}, u32[]{:S(2)}) collective-permute-start(f32[2,80,80]{1,0,2:T(2,128)S(1)} %add.80), channel_id=1, source_target_pairs={{0,4},{1,5},{2,6},{3,7},{4,0},{5,1},{6,2},{7,3},{8,12},{9,13},{10,... | collective-permute-start | bytes 153608 | tf_op jit(solution)/shard_map/ppermute | solution.py:112
  198.7 2.4 %collective-permute-done.6 = f32[2,80,80]{1,0,2:T(2,128)S(1)} collective-permute-done((f32[2,80,80]{1,0,2:T(2,128)S(1)}, f32[2,80,80]{1,0,2:T(2,128)S(1)}, u32[]{:S(2)}, u32[]{:S(2)}) %collective-permute-start.6) | collective-permute-done | bytes 51232 | tf_op jit(solution)/shard_map/ppermute | solution.py:112
  201.2 3.5 %collective-permute-start.7 = (f32[2,80,80]{1,0,2:T(2,128)S(1)}, f32[2,80,80]{1,0,2:T(2,128)S(1)}, u32[]{:S(2)}, u32[]{:S(2)}) collective-permute-start(f32[2,80,80]{1,0,2:T(2,128)S(1)} %add.81), channel_id=1, source_target_pairs={{0,8},{1,9},{2,10},{3,11},{4,12},{5,13},{6,14},{7,15},{8,0},{9,1},... | collective-permute-start | bytes 153608 | tf_op jit(solution)/shard_map/ppermute | solution.py:112
  204.7 2.4 %collective-permute-done.7 = f32[2,80,80]{1,0,2:T(2,128)S(1)} collective-permute-done((f32[2,80,80]{1,0,2:T(2,128)S(1)}, f32[2,80,80]{1,0,2:T(2,128)S(1)}, u32[]{:S(2)}, u32[]{:S(2)}) %collective-permute-start.7) | collective-permute-done | bytes 51232 | tf_op jit(solution)/shard_map/ppermute | solution.py:112
  207.1 0.3 fusion.45
  207.4 0.6 broadcast_multiply_fusion
  (30 shorter events, 0.4 us)
Async XLA Ops:
  1.9 11.0 %copy-start.2 = (s32[2,4]{1,0:T(2,128)S(1)}, s32[2,4]{1,0:T(2,128)}, u32[]{:S(2)}) copy-start(s32[2,4]{1,0:T(2,128)} %param.12) | copy-start | bytes 100
  1.9 11.0 %copy-start.3 = (s32[2,4]{1,0:T(2,128)S(1)}, s32[2,4]{1,0:T(2,128)}, u32[]{:S(2)}) copy-start(s32[2,4]{1,0:T(2,128)} %param.11) | copy-start | bytes 100
  1.9 11.1 %collective-permute-start.2 = (bf16[2,2,128,128]{3,2,1,0:T(8,128)(2,1)S(1)}, bf16[2,2,128,128]{3,2,1,0:T(8,128)(2,1)S(1)}, u32[]{:S(2)}, u32[]{:S(2)}) collective-permute-start(bf16[2,2,128,128]{3,2,1,0:T(8,128)(2,1)S(1)} %get-tuple-element.47), channel_id=1, source_target_pairs={{2,0},{3,1},{4,2},{5,3},{6,4},{7,5},{8,6},{9,7},{10,8},{11,9},{12,... | collective-permute-start | bytes 393224 | tf_op jit(solution)/shard_map/ppermute | solution.py:13
  8.0 5.1 %collective-permute-start = (bf16[2,2,128,128]{3,2,1,0:T(8,128)(2,1)S(1)}, bf16[2,2,128,128]{3,2,1,0:T(8,128)(2,1)S(1)}, u32[]{:S(2)}, u32[]{:S(2)}) collective-permute-start(bf16[2,2,128,128]{3,2,1,0:T(8,128)(2,1)S(1)} %get-tuple-element.47), channel_id=1, source_target_pairs={{1,0},{2,1},{3,2},{4,3},{5,4},{6,5},{7,6},{8,7},{9,8},{10,9},{11,1... | collective-permute-start | bytes 393224 | tf_op jit(solution)/shard_map/ppermute | solution.py:13
  11.0 25.6 %collective-permute-start.3 = (bf16[2,512,512]{2,1,0:T(8,128)(2,1)S(1)}, bf16[2,512,512]{2,1,0:T(8,128)(2,1)S(1)}, u32[]{:S(2)}, u32[]{:S(2)}) collective-permute-start(bf16[2,512,512]{2,1,0:T(8,128)(2,1)S(1)} %get-tuple-element.7), channel_id=1, source_target_pairs={{2,0},{3,1},{4,2},{5,3},{6,4},{7,5},{8,6},{9,7},{10,8},{11,9},{12,... | collective-permute-start | bytes 3145736 | tf_op jit(solution)/shard_map/ppermute | solution.py:13
  12.2 33.8 %collective-permute-start.1 = (bf16[2,512,512]{2,1,0:T(8,128)(2,1)S(1)}, bf16[2,512,512]{2,1,0:T(8,128)(2,1)S(1)}, u32[]{:S(2)}, u32[]{:S(2)}) collective-permute-start(bf16[2,512,512]{2,1,0:T(8,128)(2,1)S(1)} %get-tuple-element.8), channel_id=1, source_target_pairs={{1,0},{2,1},{3,2},{4,3},{5,4},{6,5},{7,6},{8,7},{9,8},{10,9},{11,1... | collective-permute-start | bytes 3145736 | tf_op jit(solution)/shard_map/ppermute | solution.py:13
  59.6 6.1 %copy-start.4 = (s32[80]{0:T(128)S(1)}, s32[80]{0:T(128)}, u32[]{:S(2)}) copy-start(s32[80]{0:T(128)} %constant.52) | copy-start | bytes 964
  59.6 102.0 %all-to-all-start = ((bf16[16,2,5,32,512]{4,3,2,1,0:T(8,128)(2,1)}), bf16[16,2,5,32,512]{4,3,2,1,0:T(8,128)(2,1)}, u32[]{:S(2)}, u32[]{:S(2)}) async-start(bf16[16,2,5,32,512]{4,3,2,1,0:T(8,128)(2,1)} %shard_map.82), calls=%async_computation | async-start | bytes 10485760 | tf_op jit(solution)/shard_map/all_to_all | solution.py:152
  169.5 12.0 %copy-start = (s32[2,512]{1,0:T(2,128)S(1)}, s32[2,512]{1,0:T(2,128)}, u32[]{:S(2)}) copy-start(s32[2,512]{1,0:T(2,128)} %param.13) | copy-start | bytes 12292
  169.5 35.1 %copy-start.1 = (s32[512]{0:T(512)S(1)}, s32[512]{0:T(512)}, u32[]{:S(2)}) copy-start(s32[512]{0:T(512)} %param.14) | copy-start | bytes 6148
  172.0 1.8 collective-permute-start.4
  173.8 10.6 %collective-permute-start.5 = (f32[2,80,80]{1,0,2:T(2,128)S(1)}, f32[2,80,80]{1,0,2:T(2,128)S(1)}, u32[]{:S(2)}, u32[]{:S(2)}) collective-permute-start(f32[2,80,80]{1,0,2:T(2,128)S(1)} %bitcast_add_fusion.1), channel_id=1, source_target_pairs={{0,2},{1,3},{2,0},{3,1},{4,6},{5,7},{6,4},{7,5},{8,10},{9,11},{10,... | collective-permute-start | bytes 153608 | tf_op jit(solution)/shard_map/ppermute | solution.py:112
  184.5 16.6 %collective-permute-start.6 = (f32[2,80,80]{1,0,2:T(2,128)S(1)}, f32[2,80,80]{1,0,2:T(2,128)S(1)}, u32[]{:S(2)}, u32[]{:S(2)}) collective-permute-start(f32[2,80,80]{1,0,2:T(2,128)S(1)} %add.80), channel_id=1, source_target_pairs={{0,4},{1,5},{2,6},{3,7},{4,0},{5,1},{6,2},{7,3},{8,12},{9,13},{10,... | collective-permute-start | bytes 153608 | tf_op jit(solution)/shard_map/ppermute | solution.py:112
  201.2 5.9 %collective-permute-start.7 = (f32[2,80,80]{1,0,2:T(2,128)S(1)}, f32[2,80,80]{1,0,2:T(2,128)S(1)}, u32[]{:S(2)}, u32[]{:S(2)}) collective-permute-start(f32[2,80,80]{1,0,2:T(2,128)S(1)} %add.81), channel_id=1, source_target_pairs={{0,8},{1,9},{2,10},{3,11},{4,12},{5,13},{6,14},{7,15},{8,0},{9,1},... | collective-permute-start | bytes 153608 | tf_op jit(solution)/shard_map/ppermute | solution.py:112
